TPU v7x, 32 devices: a whole 2x2x4 slice. The times are simulated.
32 devices in a mesh: groups: 2 (over y), req: 4 (over z), head: 2 (over x), sub: 2 (over core).
Axes of the slice: x: 2, y: 2, z: 4, core: 2. Of those that a mesh axis runs over, the one named last changes fastest.
Arguments:
- hidden_in: bfloat16 [1024, 8192], P(('groups', 'req')), parts along dimension 0, may hold values from -3 to 3
- q_weight: bfloat16 [8192, 8192], P('req', ('head', 'sub')), may hold values from -0.0625 to 0.0625
- q_gain: float32 [128], replicated, may hold values from 0.1 to 1.9
- key_cache: bfloat16 [8, 1601, 1024], P(('groups', 'req'), None, 'head'), parts along dimension 0, may hold values from -64 to 64
- value_cache: bfloat16 [8, 1601, 1024], P(('groups', 'req'), None, 'head'), parts along dimension 0, may hold values from -8 to 8
- out_weight: bfloat16 [8192, 8192], P(('head', 'sub'), 'req'), may hold values from -0.09375 to 0.09375
- req_image: int32 [1024], P(('groups', 'req')), parts along dimension 0, may hold values from 0 to 3, as said below
- image_count: int32 [1024], P(('groups', 'req')), parts along dimension 0, may hold values from 0 to 1, as said below
- image_home: int32 [8], P('groups'), parts along dimension 0, may hold values from 0 to 3, as said below
Outputs:
- layer_out: bfloat16 [1024, 8192], P(('groups', 'req'), ('head', 'sub')), parts along dimension 0
There are 2 independent parts, one for each index of `groups`. A program takes and returns all parts, laid end to end along the dimension named above; an argument that names none is the same for every part. Nothing has to cross between parts.
Inputs may be any that keep to these rules, and one draw needn't show every extreme that they name: Requests with image_count 0 attend to nothing; in each aligned block of 128 requests at most a quarter have image_count 0. In each aligned block of 128 requests, at most 64 requests with image_count 1 have one and the same value of image_home[req_image]; in every block exactly 64 of them share one value, and that value is the same for all blocks. `image_home`: each cache row holds exactly one image.
All inputs are finite; a program needn't handle non-finite values.
Results may differ from a plain program's by a relative error of at most 0.025.
Values may be sent and summed in bfloat16 or wider, within the bound.
No kernel may reach another device: no remote copies, remote signals or barrier semaphores. Data moves between devices by JAX's collectives and lax.ppermute only.
A program may use at most 128 MiB of HBM per device.

v0:
```python
import jax
import jax.numpy as jnp
from jax import lax
from jax.sharding import PartitionSpec as P

HQ = 64
KVH = 8


def normalize_heads(queries, q_gain, head_dim):
    row_count = queries.shape[0]
    per_head = queries.astype(jnp.float32).reshape(row_count, -1, head_dim)
    inv_rms = lax.rsqrt(jnp.mean(per_head * per_head, axis=2, keepdims=True) + 1e-05)
    return (per_head * inv_rms * q_gain).reshape(row_count, -1).astype(jnp.bfloat16)


def local(
    hidden_in,
    q_weight,
    q_gain,
    key_cache,
    value_cache,
    out_weight,
    req_image,
    image_count,
    image_home,
):
    req_count = lax.axis_size("req")
    local_rows = hidden_in.shape[0]
    q_cols = q_weight.shape[1]
    head_dim = q_gain.shape[0]
    group_size = HQ // KVH
    heads_here = q_cols // head_dim
    spread_cols = lax.all_to_all(hidden_in, "req", split_axis=1, concat_axis=0, tiled=True)
    query_sum = lax.psum_scatter(
        jnp.dot(spread_cols, q_weight, preferred_element_type=jnp.float32).astype(jnp.bfloat16),
        "req",
        scatter_dimension=0,
        tiled=True,
    )
    queries = lax.optimization_barrier(query_sum)
    normalized = normalize_heads(queries, q_gain, head_dim)
    capacity = 2 * local_rows // req_count
    slot_total = req_count * capacity
    table_ids = lax.broadcasted_iota(jnp.int32, (local_rows, image_home.shape[0]), 1)
    home_rows = jnp.sum(jnp.where(req_image[:, None] == table_ids, image_home[None, :], 0), axis=1)
    wanted = image_count == 1
    dest_ids = lax.broadcasted_iota(jnp.int32, (local_rows, req_count), 1)
    to_dest = ((home_rows[:, None] == dest_ids) & wanted[:, None]).astype(jnp.int32)
    earlier = jnp.cumsum(to_dest, axis=0) - to_dest
    position = home_rows * capacity + jnp.sum(earlier * to_dest, axis=1)
    slot_ids = lax.broadcasted_iota(jnp.int32, (slot_total, local_rows), 0)
    dispatch = ((slot_ids == position[None, :]) & wanted[None, :]).astype(jnp.bfloat16)
    outgoing = jnp.dot(dispatch, normalized, preferred_element_type=jnp.float32).astype(
        jnp.bfloat16
    )
    outgoing = outgoing.reshape(req_count, capacity, q_cols)
    kv_count = max(1, heads_here // group_size)
    per_kv = heads_here // kv_count
    sub_index = lax.axis_index("sub")
    kv_first = sub_index * heads_here // group_size
    keys_here = lax.dynamic_slice_in_dim(
        key_cache[0], kv_first * head_dim, kv_count * head_dim, 1
    ).reshape(-1, kv_count, head_dim)
    values_here = lax.dynamic_slice_in_dim(
        value_cache[0], kv_first * head_dim, kv_count * head_dim, 1
    ).reshape(-1, kv_count, head_dim)
    score_scale = head_dim ** (-0.5)
    arrived = lax.all_to_all(outgoing, "req", split_axis=0, concat_axis=0, tiled=True)
    sources = arrived.shape[0]
    slot_count = arrived.shape[1]
    flat_rows = arrived.reshape(sources * slot_count, kv_count, per_kv, head_dim)
    scores = (
        jnp.einsum("mkgd,tkd->kgmt", flat_rows, keys_here, preferred_element_type=jnp.float32)
        * score_scale
    )
    row_peak = jnp.max(scores, axis=3, keepdims=True)
    weights = jnp.exp(scores - row_peak)
    probs = (weights / jnp.sum(weights, axis=3, keepdims=True)).astype(jnp.bfloat16)
    mixed_heads = jnp.einsum(
        "kgmt,tkd->mkgd", probs, values_here, preferred_element_type=jnp.float32
    )
    replies = mixed_heads.astype(jnp.bfloat16).reshape(sources, slot_count, q_cols)
    returned = lax.all_to_all(replies, "req", split_axis=0, concat_axis=0, tiled=True)
    attended = lax.dot_general(
        dispatch,
        returned.reshape(slot_total, q_cols),
        (((0,), (0,)), ((), ())),
        preferred_element_type=jnp.float32,
    ).astype(jnp.bfloat16)
    partial_cols = jnp.dot(
        lax.all_gather(attended, "req", axis=0, tiled=True),
        out_weight,
        preferred_element_type=jnp.float32,
    )
    head_terms = lax.all_to_all(
        partial_cols.astype(jnp.bfloat16), "req", split_axis=0, concat_axis=1, tiled=True
    )
    head_total = lax.psum_scatter(
        head_terms, ("head", "sub"), scatter_dimension=1, tiled=True
    ).astype(jnp.float32)
    out_width = head_total.shape[1]
    column_index = lax.axis_index("head") * lax.axis_size("sub") + lax.axis_index("sub")
    residual = lax.dynamic_slice_in_dim(hidden_in, column_index * out_width, out_width, 1)
    return (residual.astype(jnp.float32) + head_total).astype(jnp.bfloat16)


def solution(mesh):
    in_specs = (
        P(("groups", "req"), None),
        P("req", ("head", "sub")),
        P(),
        P(("groups", "req"), None, "head"),
        P(("groups", "req"), None, "head"),
        P(("head", "sub"), "req"),
        P(("groups", "req")),
        P(("groups", "req")),
        P("groups"),
    )
    out_specs = P(("groups", "req"), ("head", "sub"))
    return jax.shard_map(local, mesh=mesh, in_specs=in_specs, out_specs=out_specs, check_vma=False)
```

profile of v0, /device:TPU:6, one launch (start us, length us, event | category | flops | bytes accessed | tf_op | source)
XLA Modules:
  0.0 353.4 jit_solution(17557983354356708979)
XLA Ops:
  6.5 4.1 %copy.39 = bf16[128,8192]{0,1:T(8,128)(2,1)} copy(bf16[128,8192]{1,0:T(8,128)(2,1)} %param.9) | data formatting | bytes 4194304 | tf_op args[0]
  10.6 53.1 %all_to_all.48 = bf16[128,4,2048]{0,2,1:T(8,128)(2,1)S(1)} all-to-all(bf16[128,4,2048]{0,2,1:T(8,128)(2,1)} %bitcast.58), channel_id=1, replica_groups=mesh['groups'=2,'req'=4,'head'=2,'sub'=2] {'req'}, dimensions={1} | all-to-all | bytes 4194304 | tf_op jit(solution)/shard_map/all_to_all | solution.py:34
  63.7 2.7 copy.40
  66.4 9.9 %convolution_convert_fusion.1 = bf16[512,2048]{1,0:T(8,128)(2,1)} fusion(bf16[512,2048]{1,0:T(8,128)(2,1)} %bitcast.63, bf16[2048,2048]{1,0:T(8,128)(2,1)} %param.10), kind=kOutput, calls=%fused_computation.11 | convolution fusion | flops 4296015872 | bytes 12582912 | tf_op jit(solution)/shard_map/dot_general | solution.py:36
  77.0 42.5 %reduce-scatter.3.cloned.1.call-done = bf16[128,2048]{1,0:T(8,128)(2,1)} async-done(((bf16[512,2048]{1,0:T(8,128)(2,1)}), bf16[128,2048]{1,0:T(8,128)(2,1)}) %reduce-scatter.3.cloned.1.call-update) | async-done | bytes 524304 | tf_op jit(solution)/shard_map/reduce_scatter | solution.py:35
  119.5 1.2 fusion.12
  121.8 1.6 convolution_convert_fusion.2
  123.4 3.5 all-to-all-start.1
  127.1 1.5 constant_dynamic-slice_fusion
  128.7 1.4 copy.38
  130.0 0.7 copy.37
  130.7 22.0 %all-to-all-done.1 = bf16[4,64,2048]{2,1,0:T(8,128)(2,1)S(1)} async-done(((bf16[4,64,2048]{2,1,0:T(8,128)(2,1)}), bf16[4,64,2048]{2,1,0:T(8,128)(2,1)S(1)}, u32[]{:S(2)}, u32[]{:S(2)}) %all-to-all-start.1) | async-done | bytes 1048608 | tf_op jit(solution)/shard_map/all_to_all | solution.py:69
  152.9 14.5 %fusion.34 = (f32[2,8,256]{2,1,0:T(8,128)S(1)}, f32[2,8,256,1601]{2,3,1,0:T(8,128)}) fusion(bf16[1601,2,128,1]{0,2,3,1:T(8,128)(2,1)} %bitcast.67, bf16[256,2,8,128]{3,2,1,0:T(8,128)(2,1)S(1)} %bitcast.65), kind=kOutput, calls=%fused_computation.45 | convolution fusion | flops 1698444800 | bytes 28115456 | tf_op jit(solution)/shard_map/sub | solution.py:78
  167.5 11.1 %fusion.11 = bf16[256,2,8,128]{0,3,2,1:T(8,128)(2,1)S(1)} fusion(bf16[1601,2,128,1]{0,2,3,1:T(8,128)(2,1)S(1)} %bitcast.66, f32[2,8,256,1601]{2,3,1,0:T(8,128)} %get-tuple-element.6, f32[2,8,256]{2,1,0:T(8,128)S(1)} %get-tuple-element.5), kind=kOutput, calls=%fused_computation.15 | convolution fusion | flops 1692409856 | bytes 28115456 | tf_op jit(solution)/shard_map/kgmt,tkd->mkgd/dot_general | solution.py:80
  178.6 1.1 copy.46
  179.7 0.5 reshape.59
  180.2 27.7 %all_to_all.49 = bf16[4,64,2048]{2,1,0:T(8,128)(2,1)S(1)} all-to-all(bf16[4,64,2048]{2,1,0:T(8,128)(2,1)S(1)} %reshape.59), channel_id=1, replica_groups=mesh['groups'=2,'req'=4,'head'=2,'sub'=2] {'req'}, dimensions={0} | all-to-all | bytes 2097152 | tf_op jit(solution)/shard_map/all_to_all | solution.py:84
  207.9 1.1 convolution_convert_fusion.3
  209.1 45.0 %all-gather.2.cloned.1.call-done = bf16[512,2048]{1,0:T(8,128)(2,1)} async-done(((bf16[128,2048]{1,0:T(8,128)(2,1)}), bf16[512,2048]{1,0:T(8,128)(2,1)}) %all-gather.2.cloned.1.call-update) | async-done | bytes 2097168 | tf_op jit(solution)/shard_map/all_gather | solution.py:92
  254.1 8.5 %convolution_convert_fusion = bf16[512,2048]{1,0:T(8,128)(2,1)S(1)} fusion(bf16[512,2048]{1,0:T(8,128)(2,1)} %all-gather.2.cloned.1.call-done, bf16[2048,2048]{1,0:T(8,128)(2,1)} %param.14), kind=kOutput, calls=%fused_computation.10 | convolution fusion | flops 4296015872 | bytes 12582912 | tf_op jit(solution)/shard_map/dot_general | solution.py:91
  262.6 50.9 %all_to_all.50 = bf16[4,128,2048]{2,1,0:T(8,128)(2,1)S(1)} all-to-all(bf16[4,128,2048]{2,1,0:T(8,128)(2,1)S(1)} %bitcast.64), channel_id=1, replica_groups=mesh['groups'=2,'req'=4,'head'=2,'sub'=2] {'req'}, dimensions={0} | all-to-all | bytes 4194304 | tf_op jit(solution)/shard_map/all_to_all | solution.py:96
  313.6 1.5 copy.54
  315.1 29.7 %reduce-scatter.5.cloned.1.call-done = bf16[128,2048]{1,0:T(8,128)(2,1)} async-done(((bf16[128,8192]{1,0:T(8,128)(2,1)}), bf16[128,2048]{1,0:T(8,128)(2,1)}) %reduce-scatter.5.cloned.1.call-update) | async-done | bytes 524304 | tf_op jit(solution)/shard_map/reduce_scatter | solution.py:99
  344.8 2.1 add_convert_fusion
  (32 shorter events, 2.2 us)
Async XLA Ops:
  6.5 70.5 %copy-start = (f32[128]{0:T(128)S(1)}, f32[128]{0:T(128)}, u32[]{:S(2)}) copy-start(f32[128]{0:T(128)} %param.11) | copy-start | bytes 1540
  6.5 113.0 %reduce-scatter.3.cloned.1.call-start = ((), (), s32[]{:S(2)}) async-start(), calls=%async_computation.6 | async-start | bytes 2621440 | tf_op jit(solution)/shard_map/reduce_scatter | solution.py:35
  66.4 9.9 %copy-start.3 = (s32[4]{0:T(128)S(1)}, s32[4]{0:T(128)}, u32[]{:S(2)}) copy-start(s32[4]{0:T(128)} %param.17) | copy-start | bytes 52
  66.4 9.9 %copy-start.4 = (s32[128]{0:T(128)S(1)}, s32[128]{0:T(128)}, u32[]{:S(2)}) copy-start(s32[128]{0:T(128)} %param.15) | copy-start | bytes 1540
  66.4 10.1 %copy-start.5 = (s32[128]{0:T(128)S(1)}, s32[128]{0:T(128)}, u32[]{:S(2)}) copy-start(s32[128]{0:T(128)} %param.16) | copy-start | bytes 1540
  119.5 2.3 copy-start.2
  123.4 29.3 %all-to-all-start.1 = ((bf16[4,64,2048]{2,1,0:T(8,128)(2,1)}), bf16[4,64,2048]{2,1,0:T(8,128)(2,1)S(1)}, u32[]{:S(2)}, u32[]{:S(2)}) async-start(bf16[4,64,2048]{2,1,0:T(8,128)(2,1)} %bitcast.8), calls=%async_computation.2 | async-start | bytes 2097152 | tf_op jit(solution)/shard_map/all_to_all | solution.py:69
  126.9 127.2 %all-gather.2.cloned.1.call-start = ((), (), s32[]{:S(2)}) async-start(), calls=%async_computation.7 | async-start | bytes 2621440 | tf_op jit(solution)/shard_map/all_gather | solution.py:92
  209.1 135.7 %reduce-scatter.5.cloned.1.call-start = ((), (), s32[]{:S(2)}) async-start(), calls=%async_computation.8 | async-start | bytes 2621440 | tf_op jit(solution)/shard_map/reduce_scatter | solution.py:99
  262.6 84.3 %copy-start.1 = (f32[128]{0:T(128)S(1)}, f32[128]{0:T(128)}, u32[]{:S(2)}) copy-start(f32[128]{0:T(128)} %param.11) | copy-start | bytes 1540
Sparse Core Ops, SparseCore 0:
  76.4 43.0 reduce-scatter.2
  209.2 44.8 all-gather.1
  315.2 29.5 reduce-scatter.4
where the time goes:
time: 356 us; the launch traced here: 353 us
  waiting for transfers between devices  139 us (39%)
  blocking collectives  132 us (37%)
  matrix products  46.8 us (13%)
  local copies, waits for them, and re-layouts  14.3 us (4%)
  between operations  13.3 us (4%)
  other arithmetic  4.32 us (1%)
  starting transfers between devices  3.78 us (1%)
    all_to_all x1, blocking collectives, local(): lax.all_to_all(hidden_in, 'req', split_axis=1, concat_axis=0, tiled=True)  53.1 us
    all_to_all x1, blocking collectives, local(): lax.all_to_all(partial_cols.astype(jnp.bfloat16), 'req', split_axis=0, co...  50.9 us
    all_gather x1, waiting for transfers between devices, local(): lax.all_gather(attended, 'req', axis=0, tiled=True)  45 us
    reduce_scatter x1, waiting for transfers between devices, local(): lax.psum_scatter(jnp.dot(spread_cols, q_weight, preferred_element_type=jn...  42.5 us
    reduce_scatter x1, waiting for transfers between devices, local(): lax.psum_scatter(head_terms, ('head', 'sub'), scatter_dimension=1, tiled=...  29.7 us
    all_to_all x1, blocking collectives, local(): lax.all_to_all(replies, 'req', split_axis=0, concat_axis=0, tiled=True)  27.7 us
    all_to_all x1, waiting for transfers between devices, local(): lax.all_to_all(outgoing, 'req', split_axis=0, concat_axis=0, tiled=True)  22 us
    sub x1, matrix products, local(): weights = jnp.exp(scores - row_peak)  14.5 us
  transfers between devices with their start and end apart: 4, of which 4 were waited for; matrix products, arithmetic and copies ran while one was open for 1% of the time, Pallas kernels for 0%

commit v1 on v0

--- a/solution.py
+++ b/solution.py
@@ -31,7 +31,16 @@
     head_dim = q_gain.shape[0]
     group_size = HQ // KVH
     heads_here = q_cols // head_dim
-    spread_cols = lax.all_to_all(hidden_in, "req", split_axis=1, concat_axis=0, tiled=True)
+    sub_count = lax.axis_size("sub")
+    sub_index = lax.axis_index("sub")
+    block_width = hidden_in.shape[1] // req_count
+    part_width = block_width // sub_count
+    by_block = hidden_in.reshape(local_rows, req_count, sub_count, part_width)
+    my_part = lax.dynamic_index_in_dim(by_block, sub_index, axis=2, keepdims=False)
+    spread_part = lax.all_to_all(my_part, "req", split_axis=1, concat_axis=0, tiled=True)
+    spread_cols = lax.all_gather(
+        spread_part.reshape(req_count * local_rows, part_width), "sub", axis=1, tiled=True
+    )
     query_sum = lax.psum_scatter(
         jnp.dot(spread_cols, q_weight, preferred_element_type=jnp.float32).astype(jnp.bfloat16),
         "req",
@@ -57,7 +66,6 @@
     outgoing = outgoing.reshape(req_count, capacity, q_cols)
     kv_count = max(1, heads_here // group_size)
     per_kv = heads_here // kv_count
-    sub_index = lax.axis_index("sub")
     kv_first = sub_index * heads_here // group_size
     keys_here = lax.dynamic_slice_in_dim(
         key_cache[0], kv_first * head_dim, kv_count * head_dim, 1
@@ -92,16 +100,34 @@
         lax.all_gather(attended, "req", axis=0, tiled=True),
         out_weight,
         preferred_element_type=jnp.float32,
+    ).astype(jnp.bfloat16)
+    hs_count = lax.axis_size("head") * sub_count
+    hs_index = lax.axis_index("head") * sub_count + sub_index
+    req_index = lax.axis_index("req")
+    owner_sums = lax.psum_scatter(
+        partial_cols, ("head", "sub"), scatter_dimension=0, tiled=True
     )
-    head_terms = lax.all_to_all(
-        partial_cols.astype(jnp.bfloat16), "req", split_axis=0, concat_axis=1, tiled=True
-    )
-    head_total = lax.psum_scatter(
-        head_terms, ("head", "sub"), scatter_dimension=1, tiled=True
-    ).astype(jnp.float32)
+    per_hs = req_count // hs_count
+    out_block = partial_cols.shape[1]
+    owner_sums = owner_sums.reshape(per_hs, local_rows, out_block)
+    arrived_blocks = []
+    for step in range(per_hs):
+        chunk = lax.dynamic_index_in_dim(
+            owner_sums, (req_index + step) % per_hs, axis=0, keepdims=False
+        )
+        pairs = []
+        for c in range(req_count):
+            for j in range(hs_count):
+                k = j * per_hs + (c + step) % per_hs
+                pairs.append((c * hs_count + j, k * hs_count + c // per_hs))
+        arrived_blocks.append(lax.ppermute(chunk, ("req", "head", "sub"), pairs))
+    stacked = jnp.stack(arrived_blocks)
+    order = (req_index % per_hs - jnp.arange(per_hs)) % per_hs
+    head_total = jnp.take(stacked, order, axis=0)
+    head_total = jnp.transpose(head_total, (1, 0, 2)).reshape(local_rows, per_hs * out_block)
+    head_total = head_total.astype(jnp.float32)
     out_width = head_total.shape[1]
-    column_index = lax.axis_index("head") * lax.axis_size("sub") + lax.axis_index("sub")
-    residual = lax.dynamic_slice_in_dim(hidden_in, column_index * out_width, out_width, 1)
+    residual = lax.dynamic_slice_in_dim(hidden_in, hs_index * out_width, out_width, 1)
     return (residual.astype(jnp.float32) + head_total).astype(jnp.bfloat16)
 
 

time: 356 us -> 318 us (0.89)
  blocking collectives: 132 us -> 58.2 us
  waiting for transfers between devices: 139 us -> 175 us
  starting transfers between devices: 3.78 us -> 9.02 us
  local copies, waits for them, and re-layouts: 14.3 us -> 9.89 us
    all_to_all x2 -> x1, blocking collectives: 104 us -> 30.5 us  [local(): lax.all_to_all(my_part, 'req', split_axis=1, concat_axis=0, tiled=True)]
    ppermute x0 -> x1, waiting for transfers between devices: none -> 24.1 us  [local(): arrived_blocks.append(lax.ppermute(chunk, ('req', 'head', 'sub'), pairs))]
    all_gather x0 -> x1, waiting for transfers between devices: none -> 9.95 us  [local(): lax.all_gather(spread_part.reshape(req_count * local_rows, part_width), '...]
    ppermute x0 -> x1, starting transfers between devices: none -> 5.2 us  [local(): arrived_blocks.append(lax.ppermute(chunk, ('req', 'head', 'sub'), pairs))]
    all_to_all x2 -> x0, local copies, waits for them, and re-layouts: 4.17 us -> none  [the longest x1 2.68 us: local(): lax.all_to_all(hidden_in, 'req', split_axis=1, concat_axis=0, tiled=True)]
  transfers between devices with their start and end apart: 4 -> 6, of which waited for: 4 -> 6; matrix products, arithmetic and copies ran while one was open for 1% -> 1% of each run, Pallas kernels for 0% -> 0%
where the time goes in v1:
time: 318 us
  waiting for transfers between devices  175 us (55%)
  blocking collectives  58.2 us (18%)
  matrix products  48 us (15%)
  between operations  13.4 us (4%)
  local copies, waits for them, and re-layouts  9.89 us (3%)
  starting transfers between devices  9.02 us (3%)
  other arithmetic  4.21 us (1%)
    all_gather x1, waiting for transfers between devices, local(): lax.all_gather(attended, 'req', axis=0, tiled=True)  45 us
    reduce_scatter x1, waiting for transfers between devices, local(): lax.psum_scatter(jnp.dot(spread_cols, q_weight, preferred_element_type=jn...  44.2 us
    all_to_all x1, blocking collectives, local(): lax.all_to_all(my_part, 'req', split_axis=1, concat_axis=0, tiled=True)  30.5 us
    reduce_scatter x1, waiting for transfers between devices, local(): lax.psum_scatter(partial_cols, ('head', 'sub'), scatter_dimension=0, tile...  29.4 us
    all_to_all x1, blocking collectives, local(): lax.all_to_all(replies, 'req', split_axis=0, concat_axis=0, tiled=True)  27.7 us
    ppermute x1, waiting for transfers between devices, local(): arrived_blocks.append(lax.ppermute(chunk, ('req', 'head', 'sub'), pairs))  24.1 us
    all_to_all x1, waiting for transfers between devices, local(): lax.all_to_all(outgoing, 'req', split_axis=0, concat_axis=0, tiled=True)  22 us
    sub x1, matrix products, local(): weights = jnp.exp(scores - row_peak)  14.5 us
  transfers between devices with their start and end apart: 6, of which 6 were waited for; matrix products, arithmetic and copies ran while one was open for 1% of the time, Pallas kernels for 0%

profile of v1, /device:TPU:6, one launch (start us, length us, event | category | flops | bytes accessed | tf_op | source)
XLA Modules:
  0.0 317.6 jit_solution(9231149602611494265)
XLA Ops:
  6.5 3.2 %copy.35 = bf16[128,8192]{0,1:T(8,128)(2,1)S(1)} copy(bf16[128,8192]{1,0:T(8,128)(2,1)} %param.9) | data formatting | bytes 4194304 | tf_op args[0]
  9.9 0.5 copy.36
  10.4 30.5 %all_to_all.25 = bf16[128,4,1024]{2,0,1:T(8,128)(2,1)} all-to-all(bf16[128,4,1024]{2,0,1:T(8,128)(2,1)S(1)} %bitcast.61), channel_id=1, replica_groups=mesh['groups'=2,'req'=4,'head'=2,'sub'=2] {'req'}, dimensions={1} | all-to-all | bytes 2097152 | tf_op jit(solution)/shard_map/all_to_all | solution.py:40
  41.0 9.9 %all-gather.3.cloned.1.call-done = bf16[512,2048]{1,0:T(8,128)(2,1)} async-done(((bf16[512,1024]{1,0:T(8,128)(2,1)}), bf16[512,2048]{1,0:T(8,128)(2,1)}) %all-gather.3.cloned.1.call-update) | async-done | bytes 2097168 | tf_op jit(solution)/shard_map/all_gather | solution.py:41
  51.0 9.8 %convolution_convert_fusion.1 = bf16[512,2048]{1,0:T(8,128)(2,1)} fusion(bf16[512,2048]{1,0:T(8,128)(2,1)} %all-gather.3.cloned.1.call-done, bf16[2048,2048]{1,0:T(8,128)(2,1)} %param.10), kind=kOutput, calls=%fused_computation.11 | convolution fusion | flops 4296015872 | bytes 12582912 | tf_op jit(solution)/shard_map/dot_general | solution.py:45
  61.5 44.2 %reduce-scatter.3.cloned.1.call-done = bf16[128,2048]{1,0:T(8,128)(2,1)} async-done(((bf16[512,2048]{1,0:T(8,128)(2,1)}), bf16[128,2048]{1,0:T(8,128)(2,1)}) %reduce-scatter.3.cloned.1.call-update) | async-done | bytes 524304 | tf_op jit(solution)/shard_map/reduce_scatter | solution.py:44
  105.7 1.2 fusion.12
  108.0 1.6 convolution_convert_fusion.2
  109.6 3.5 %all-to-all-start.1 = ((bf16[4,64,2048]{2,1,0:T(8,128)(2,1)}), bf16[4,64,2048]{2,1,0:T(8,128)(2,1)S(1)}, u32[]{:S(2)}, u32[]{:S(2)}) async-start(bf16[4,64,2048]{2,1,0:T(8,128)(2,1)} %bitcast.10), calls=%async_computation.2 | async-start | bytes 2097152 | tf_op jit(solution)/shard_map/all_to_all | solution.py:77
  113.4 1.5 constant_dynamic-slice_fusion
  114.9 1.4 copy.34
  116.3 0.7 copy.33
  116.9 22.0 %all-to-all-done.1 = bf16[4,64,2048]{2,1,0:T(8,128)(2,1)S(1)} async-done(((bf16[4,64,2048]{2,1,0:T(8,128)(2,1)}), bf16[4,64,2048]{2,1,0:T(8,128)(2,1)S(1)}, u32[]{:S(2)}, u32[]{:S(2)}) %all-to-all-start.1) | async-done | bytes 1048608 | tf_op jit(solution)/shard_map/all_to_all | solution.py:77
  139.2 14.5 %fusion.34 = (f32[2,8,256]{2,1,0:T(8,128)S(1)}, f32[2,8,256,1601]{2,3,1,0:T(8,128)}) fusion(bf16[1601,2,128,1]{0,2,3,1:T(8,128)(2,1)} %bitcast.64, bf16[256,2,8,128]{3,2,1,0:T(8,128)(2,1)S(1)} %bitcast.62), kind=kOutput, calls=%fused_computation.46 | convolution fusion | flops 1698444800 | bytes 28115456 | tf_op jit(solution)/shard_map/sub | solution.py:86
  153.7 11.1 %fusion.11 = bf16[256,2,8,128]{0,3,2,1:T(8,128)(2,1)S(1)} fusion(bf16[1601,2,128,1]{0,2,3,1:T(8,128)(2,1)S(1)} %bitcast.63, f32[2,8,256,1601]{2,3,1,0:T(8,128)} %get-tuple-element.6, f32[2,8,256]{2,1,0:T(8,128)S(1)} %get-tuple-element.5), kind=kOutput, calls=%fused_computation.15 | convolution fusion | flops 1692409856 | bytes 28115456 | tf_op jit(solution)/shard_map/kgmt,tkd->mkgd/dot_general | solution.py:88
  164.8 1.1 copy.42
  166.4 27.7 %all_to_all.26 = bf16[4,64,2048]{2,1,0:T(8,128)(2,1)S(1)} all-to-all(bf16[4,64,2048]{2,1,0:T(8,128)(2,1)S(1)} %reshape.75), channel_id=1, replica_groups=mesh['groups'=2,'req'=4,'head'=2,'sub'=2] {'req'}, dimensions={0} | all-to-all | bytes 2097152 | tf_op jit(solution)/shard_map/all_to_all | solution.py:92
  194.1 1.1 convolution_convert_fusion.3
  195.3 45.0 %all-gather.5.cloned.1.call-done = bf16[512,2048]{1,0:T(8,128)(2,1)} async-done(((bf16[128,2048]{1,0:T(8,128)(2,1)}), bf16[512,2048]{1,0:T(8,128)(2,1)}) %all-gather.5.cloned.1.call-update) | async-done | bytes 2097168 | tf_op jit(solution)/shard_map/all_gather | solution.py:100
  240.3 9.9 %convolution_convert_fusion = bf16[512,2048]{1,0:T(8,128)(2,1)} fusion(bf16[512,2048]{1,0:T(8,128)(2,1)} %all-gather.5.cloned.1.call-done, bf16[2048,2048]{1,0:T(8,128)(2,1)} %param.14), kind=kOutput, calls=%fused_computation.10 | convolution fusion | flops 4296015872 | bytes 12582912 | tf_op jit(solution)/shard_map/dot_general | solution.py:99
  250.2 29.4 %reduce-scatter.5.cloned.1.call-done = bf16[128,2048]{1,0:T(8,128)(2,1)} async-done(((bf16[512,2048]{1,0:T(8,128)(2,1)}), bf16[128,2048]{1,0:T(8,128)(2,1)}) %reduce-scatter.5.cloned.1.call-update) | async-done | bytes 524304 | tf_op jit(solution)/shard_map/reduce_scatter | solution.py:107
  279.7 5.2 %collective-permute-start = (bf16[128,2048]{1,0:T(8,128)(2,1)}, bf16[128,2048]{1,0:T(8,128)(2,1)S(1)}, u32[]{:S(2)}, u32[]{:S(2)}) collective-permute-start(bf16[128,2048]{1,0:T(8,128)(2,1)} %reduce-scatter.5.cloned.1.call-done), channel_id=1, source_target_pairs={{0,0},{1,4},{2,8},{3,12},{4,1},{5,5},{6,9},{7,13},{8,2},{9,6},{10,... | collective-permute-start | bytes 1572872 | tf_op jit(solution)/shard_map/ppermute | solution.py:123
  284.9 24.1 %collective-permute-done = bf16[128,2048]{1,0:T(8,128)(2,1)S(1)} collective-permute-done((bf16[128,2048]{1,0:T(8,128)(2,1)}, bf16[128,2048]{1,0:T(8,128)(2,1)S(1)}, u32[]{:S(2)}, u32[]{:S(2)}) %collective-permute-start) | collective-permute-done | bytes 524320 | tf_op jit(solution)/shard_map/ppermute | solution.py:123
  309.0 2.0 add_convert_fusion
  (36 shorter events, 2.9 us)
Async XLA Ops:
  6.5 54.9 %copy-start = (f32[128]{0:T(128)S(1)}, f32[128]{0:T(128)}, u32[]{:S(2)}) copy-start(f32[128]{0:T(128)} %param.11) | copy-start | bytes 1540
  6.5 44.4 %all-gather.3.cloned.1.call-start = ((), (), s32[]{:S(2)}) async-start(), calls=%async_computation.5 | async-start | bytes 3145728 | tf_op jit(solution)/shard_map/all_gather | solution.py:41
  40.9 19.9 %copy-start.3 = (s32[4]{0:T(128)S(1)}, s32[4]{0:T(128)}, u32[]{:S(2)}) copy-start(s32[4]{0:T(128)} %param.17) | copy-start | bytes 52
  40.9 19.9 %copy-start.4 = (s32[128]{0:T(128)S(1)}, s32[128]{0:T(128)}, u32[]{:S(2)}) copy-start(s32[128]{0:T(128)} %param.15) | copy-start | bytes 1540
  40.9 20.0 %copy-start.5 = (s32[128]{0:T(128)S(1)}, s32[128]{0:T(128)}, u32[]{:S(2)}) copy-start(s32[128]{0:T(128)} %param.16) | copy-start | bytes 1540
  41.0 64.8 %reduce-scatter.3.cloned.1.call-start = ((), (), s32[]{:S(2)}) async-start(), calls=%async_computation.6 | async-start | bytes 2621440 | tf_op jit(solution)/shard_map/reduce_scatter | solution.py:44
  105.7 2.3 copy-start.2
  109.6 29.3 %all-to-all-start.1 = ((bf16[4,64,2048]{2,1,0:T(8,128)(2,1)}), bf16[4,64,2048]{2,1,0:T(8,128)(2,1)S(1)}, u32[]{:S(2)}, u32[]{:S(2)}) async-start(bf16[4,64,2048]{2,1,0:T(8,128)(2,1)} %bitcast.10), calls=%async_computation.2 | async-start | bytes 2097152 | tf_op jit(solution)/shard_map/all_to_all | solution.py:77
  113.1 127.2 %all-gather.5.cloned.1.call-start = ((), (), s32[]{:S(2)}) async-start(), calls=%async_computation.7 | async-start | bytes 2621440 | tf_op jit(solution)/shard_map/all_gather | solution.py:100
  195.3 84.4 %reduce-scatter.5.cloned.1.call-start = ((), (), s32[]{:S(2)}) async-start(), calls=%async_computation.8 | async-start | bytes 2621440 | tf_op jit(solution)/shard_map/reduce_scatter | solution.py:107
  240.3 70.7 %copy-start.1 = (f32[128]{0:T(128)S(1)}, f32[128]{0:T(128)}, u32[]{:S(2)}) copy-start(f32[128]{0:T(128)} %param.11) | copy-start | bytes 1540
  279.7 29.4 %collective-permute-start = (bf16[128,2048]{1,0:T(8,128)(2,1)}, bf16[128,2048]{1,0:T(8,128)(2,1)S(1)}, u32[]{:S(2)}, u32[]{:S(2)}) collective-permute-start(bf16[128,2048]{1,0:T(8,128)(2,1)} %reduce-scatter.5.cloned.1.call-done), channel_id=1, source_target_pairs={{0,0},{1,4},{2,8},{3,12},{4,1},{5,5},{6,9},{7,13},{8,2},{9,6},{10,... | collective-permute-start | bytes 1572872 | tf_op jit(solution)/shard_map/ppermute | solution.py:123
Sparse Core Ops, SparseCore 0:
  41.0 9.8 all-gather.2
  60.9 44.7 reduce-scatter.2
  195.4 44.8 all-gather.4
  250.4 29.2 reduce-scatter.4

commit v2 on v1

--- a/solution.py
+++ b/solution.py
@@ -38,9 +38,18 @@
     by_block = hidden_in.reshape(local_rows, req_count, sub_count, part_width)
     my_part = lax.dynamic_index_in_dim(by_block, sub_index, axis=2, keepdims=False)
     spread_part = lax.all_to_all(my_part, "req", split_axis=1, concat_axis=0, tiled=True)
-    spread_cols = lax.all_gather(
-        spread_part.reshape(req_count * local_rows, part_width), "sub", axis=1, tiled=True
+    spread_part = spread_part.reshape(req_count * local_rows, part_width)
+    spread_cols = jnp.zeros((req_count * local_rows, block_width), spread_part.dtype)
+    spread_cols = lax.dynamic_update_slice_in_dim(
+        spread_cols, spread_part, sub_index * part_width, 1
     )
+    for shift in range(1, sub_count):
+        other_part = lax.ppermute(
+            spread_part, "sub", [(i, (i + shift) % sub_count) for i in range(sub_count)]
+        )
+        spread_cols = lax.dynamic_update_slice_in_dim(
+            spread_cols, other_part, ((sub_index - shift) % sub_count) * part_width, 1
+        )
     query_sum = lax.psum_scatter(
         jnp.dot(spread_cols, q_weight, preferred_element_type=jnp.float32).astype(jnp.bfloat16),
         "req",
@@ -104,9 +113,11 @@
     hs_count = lax.axis_size("head") * sub_count
     hs_index = lax.axis_index("head") * sub_count + sub_index
     req_index = lax.axis_index("req")
-    owner_sums = lax.psum_scatter(
-        partial_cols, ("head", "sub"), scatter_dimension=0, tiled=True
-    )
+    head_count = lax.axis_size("head")
+    by_group = partial_cols.reshape(sub_count, -1, partial_cols.shape[1])
+    owner_sums = lax.psum_scatter(by_group, "sub", scatter_dimension=0, tiled=True)
+    owner_sums = owner_sums.reshape(head_count, -1, partial_cols.shape[1])
+    owner_sums = lax.psum_scatter(owner_sums, "head", scatter_dimension=0, tiled=True)
     per_hs = req_count // hs_count
     out_block = partial_cols.shape[1]
     owner_sums = owner_sums.reshape(per_hs, local_rows, out_block)
@@ -117,9 +128,12 @@
         )
         pairs = []
         for c in range(req_count):
-            for j in range(hs_count):
-                k = j * per_hs + (c + step) % per_hs
-                pairs.append((c * hs_count + j, k * hs_count + c // per_hs))
+            for h in range(head_count):
+                for u in range(sub_count):
+                    j = u * head_count + h
+                    k = j * per_hs + (c + step) % per_hs
+                    src = c * hs_count + h * sub_count + u
+                    pairs.append((src, k * hs_count + c // per_hs))
         arrived_blocks.append(lax.ppermute(chunk, ("req", "head", "sub"), pairs))
     stacked = jnp.stack(arrived_blocks)
     order = (req_index % per_hs - jnp.arange(per_hs)) % per_hs

time: 318 us -> 304 us (0.956); the launches traced: 318 us -> 299 us
  waiting for transfers between devices: 175 us -> 157 us
    all_gather x1 -> x0, waiting for transfers between devices: 9.95 us -> none  [local(): lax.all_gather(spread_part.reshape(req_count * local_rows, part_width), '...]
    ppermute x1, waiting for transfers between devices: 24.1 us -> 14.5 us  [local(): arrived_blocks.append(lax.ppermute(chunk, ('req', 'head', 'sub'), pairs))]
    reduce_scatter x1 -> x2, waiting for transfers between devices: 29.4 us -> 31.1 us  [the longest x1 22.4 us: local(): lax.psum_scatter(owner_sums, 'head', scatter_dimension=0, tiled=True)]
  transfers between devices with their start and end apart: 6 -> 7, of which waited for: 6 -> 7; matrix products, arithmetic and copies ran while one was open for 1% -> 2% of each run, Pallas kernels for 0% -> 0%
where the time goes in v2:
time: 304 us; the launch traced here: 299 us
  waiting for transfers between devices  157 us (52%)
  blocking collectives  58.1 us (19%)
  matrix products  47.3 us (16%)
  between operations  13.4 us (4%)
  local copies, waits for them, and re-layouts  11 us (4%)
  starting transfers between devices  8.11 us (3%)
  other arithmetic  4.14 us (1%)
    all_gather x1, waiting for transfers between devices, local(): lax.all_gather(attended, 'req', axis=0, tiled=True)  45 us
    reduce_scatter x1, waiting for transfers between devices, local(): lax.psum_scatter(jnp.dot(spread_cols, q_weight, preferred_element_type=jn...  41.8 us
    all_to_all x1, blocking collectives, local(): lax.all_to_all(my_part, 'req', split_axis=1, concat_axis=0, tiled=True)  30.4 us
    all_to_all x1, blocking collectives, local(): lax.all_to_all(replies, 'req', split_axis=0, concat_axis=0, tiled=True)  27.7 us
    reduce_scatter x1, waiting for transfers between devices, local(): lax.psum_scatter(owner_sums, 'head', scatter_dimension=0, tiled=True)  22.4 us
    all_to_all x1, waiting for transfers between devices, local(): lax.all_to_all(outgoing, 'req', split_axis=0, concat_axis=0, tiled=True)  22 us
    sub x1, matrix products, local(): weights = jnp.exp(scores - row_peak)  14.5 us
    ppermute x1, waiting for transfers between devices, local(): arrived_blocks.append(lax.ppermute(chunk, ('req', 'head', 'sub'), pairs))  14.5 us
  transfers between devices with their start and end apart: 7, of which 7 were waited for; matrix products, arithmetic and copies ran while one was open for 2% of the time, Pallas kernels for 0%

profile of v2, /device:TPU:6, one launch (start us, length us, event | category | flops | bytes accessed | tf_op | source)
XLA Modules:
  0.0 298.8 jit_solution(3900016634550330122)
XLA Ops:
  6.5 3.2 %copy.35 = bf16[128,8192]{0,1:T(8,128)(2,1)S(1)} copy(bf16[128,8192]{1,0:T(8,128)(2,1)} %param.9) | data formatting | bytes 4194304 | tf_op args[0]
  10.4 30.4 %all_to_all.25 = bf16[128,4,1024]{2,0,1:T(8,128)(2,1)S(1)} all-to-all(bf16[128,4,1024]{2,0,1:T(8,128)(2,1)S(1)} %bitcast.65), channel_id=1, replica_groups=mesh['groups'=2,'req'=4,'head'=2,'sub'=2] {'req'}, dimensions={1} | all-to-all | bytes 2097152 | tf_op jit(solution)/shard_map/all_to_all | solution.py:40
  41.2 2.3 collective-permute-done
  43.6 9.1 %convolution_convert_fusion.1 = bf16[512,2048]{1,0:T(8,128)(2,1)} fusion(bf16[512,2048]{1,0:T(8,128)(2,1)S(1)} %constant_dynamic-update-slice_fusion.1, bf16[2048,2048]{1,0:T(8,128)(2,1)} %param.10), kind=kOutput, calls=%fused_computation.11 | convolution fusion | flops 4296015872 | bytes 12582912 | tf_op jit(solution)/shard_map/dot_general | solution.py:54
  54.0 41.8 %reduce-scatter.4.cloned.1.call-done = bf16[128,2048]{1,0:T(8,128)(2,1)} async-done(((bf16[512,2048]{1,0:T(8,128)(2,1)}), bf16[128,2048]{1,0:T(8,128)(2,1)}) %reduce-scatter.4.cloned.1.call-update) | async-done | bytes 524304 | tf_op jit(solution)/shard_map/reduce_scatter | solution.py:53
  95.8 1.1 fusion.12
  98.0 1.6 convolution_convert_fusion.2
  99.6 3.5 %all-to-all-start.1 = ((bf16[4,64,2048]{2,1,0:T(8,128)(2,1)}), bf16[4,64,2048]{2,1,0:T(8,128)(2,1)S(1)}, u32[]{:S(2)}, u32[]{:S(2)}) async-start(bf16[4,64,2048]{2,1,0:T(8,128)(2,1)} %bitcast.12), calls=%async_computation.2 | async-start | bytes 2097152 | tf_op jit(solution)/shard_map/all_to_all | solution.py:86
  103.4 1.5 constant_dynamic-slice_fusion.1
  104.9 1.4 copy.34
  106.3 0.7 copy.33
  106.9 22.0 %all-to-all-done.1 = bf16[4,64,2048]{2,1,0:T(8,128)(2,1)S(1)} async-done(((bf16[4,64,2048]{2,1,0:T(8,128)(2,1)}), bf16[4,64,2048]{2,1,0:T(8,128)(2,1)S(1)}, u32[]{:S(2)}, u32[]{:S(2)}) %all-to-all-start.1) | async-done | bytes 1048608 | tf_op jit(solution)/shard_map/all_to_all | solution.py:86
  129.2 14.5 %fusion.34 = (f32[2,8,256]{2,1,0:T(8,128)S(1)}, f32[2,8,256,1601]{2,3,1,0:T(8,128)}) fusion(bf16[1601,2,128,1]{0,2,3,1:T(8,128)(2,1)} %bitcast.70, bf16[256,2,8,128]{3,2,1,0:T(8,128)(2,1)S(1)} %bitcast.68), kind=kOutput, calls=%fused_computation.48 | convolution fusion | flops 1698444800 | bytes 28115456 | tf_op jit(solution)/shard_map/sub | solution.py:95
  143.7 11.1 %fusion.11 = bf16[256,2,8,128]{0,3,2,1:T(8,128)(2,1)S(1)} fusion(bf16[1601,2,128,1]{0,2,3,1:T(8,128)(2,1)S(1)} %bitcast.69, f32[2,8,256,1601]{2,3,1,0:T(8,128)} %get-tuple-element.6, f32[2,8,256]{2,1,0:T(8,128)S(1)} %get-tuple-element.5), kind=kOutput, calls=%fused_computation.15 | convolution fusion | flops 1692409856 | bytes 28115456 | tf_op jit(solution)/shard_map/kgmt,tkd->mkgd/dot_general | solution.py:97
  154.8 1.1 copy.42
  156.4 27.7 %all_to_all.26 = bf16[4,64,2048]{2,1,0:T(8,128)(2,1)S(1)} all-to-all(bf16[4,64,2048]{2,1,0:T(8,128)(2,1)S(1)} %reshape.78), channel_id=1, replica_groups=mesh['groups'=2,'req'=4,'head'=2,'sub'=2] {'req'}, dimensions={0} | all-to-all | bytes 2097152 | tf_op jit(solution)/shard_map/all_to_all | solution.py:101
  184.1 1.1 convolution_convert_fusion.3
  185.4 45.0 %all-gather.2.cloned.1.call-done = bf16[512,2048]{1,0:T(8,128)(2,1)} async-done(((bf16[128,2048]{1,0:T(8,128)(2,1)}), bf16[512,2048]{1,0:T(8,128)(2,1)}) %all-gather.2.cloned.1.call-update) | async-done | bytes 2097168 | tf_op jit(solution)/shard_map/all_gather | solution.py:109
  230.4 9.9 %convolution_convert_fusion = bf16[512,2048]{1,0:T(8,128)(2,1)} fusion(bf16[512,2048]{1,0:T(8,128)(2,1)} %all-gather.2.cloned.1.call-done, bf16[2048,2048]{1,0:T(8,128)(2,1)} %param.14), kind=kOutput, calls=%fused_computation.10 | convolution fusion | flops 4296015872 | bytes 12582912 | tf_op jit(solution)/shard_map/dot_general | solution.py:108
  240.3 8.7 %reduce-scatter.6.cloned.1.call-done = bf16[1,256,2048]{2,1,0:T(8,128)(2,1)} async-done(((bf16[2,256,2048]{2,1,0:T(8,128)(2,1)}), bf16[1,256,2048]{2,1,0:T(8,128)(2,1)}) %reduce-scatter.6.cloned.1.call-update) | async-done | bytes 1048592 | tf_op jit(solution)/shard_map/reduce_scatter | solution.py:118
  249.0 22.4 %reduce-scatter.8.cloned.1.call-done = bf16[1,128,2048]{2,1,0:T(8,128)(2,1)} async-done(((bf16[2,128,2048]{2,1,0:T(8,128)(2,1)}), bf16[1,128,2048]{2,1,0:T(8,128)(2,1)}) %reduce-scatter.8.cloned.1.call-update) | async-done | bytes 524304 | tf_op jit(solution)/shard_map/reduce_scatter | solution.py:120
  271.5 4.3 %collective-permute-start.1 = (bf16[128,2048]{1,0:T(8,128)(2,1)}, bf16[128,2048]{1,0:T(8,128)(2,1)S(1)}, u32[]{:S(2)}, u32[]{:S(2)}) collective-permute-start(bf16[128,2048]{1,0:T(8,128)(2,1)} %bitcast.71), channel_id=1, source_target_pairs={{0,0},{1,8},{2,4},{3,12},{4,1},{5,9},{6,5},{7,13},{8,2},{9,10},{10... | collective-permute-start | bytes 1572872 | tf_op jit(solution)/shard_map/ppermute | solution.py:137
  275.8 14.5 %collective-permute-done.1 = bf16[128,2048]{1,0:T(8,128)(2,1)S(1)} collective-permute-done((bf16[128,2048]{1,0:T(8,128)(2,1)}, bf16[128,2048]{1,0:T(8,128)(2,1)S(1)}, u32[]{:S(2)}, u32[]{:S(2)}) %collective-permute-start.1) | collective-permute-done | bytes 524320 | tf_op jit(solution)/shard_map/ppermute | solution.py:137
  290.3 2.0 add_convert_fusion
  (41 shorter events, 4.5 us)
Async XLA Ops:
  6.5 47.5 %copy-start = (f32[128]{0:T(128)S(1)}, f32[128]{0:T(128)}, u32[]{:S(2)}) copy-start(f32[128]{0:T(128)} %param.11) | copy-start | bytes 1540
  6.5 89.3 %reduce-scatter.4.cloned.1.call-start = ((), (), s32[]{:S(2)}) async-start(), calls=%async_computation.6 | async-start | bytes 2621440 | tf_op jit(solution)/shard_map/reduce_scatter | solution.py:53
  40.8 2.7 collective-permute-start
  52.7 0.7 copy-start.3
  52.7 0.7 copy-start.4
  52.7 0.8 copy-start.5
  97.0 1.1 copy-start.2
  99.6 29.3 %all-to-all-start.1 = ((bf16[4,64,2048]{2,1,0:T(8,128)(2,1)}), bf16[4,64,2048]{2,1,0:T(8,128)(2,1)S(1)}, u32[]{:S(2)}, u32[]{:S(2)}) async-start(bf16[4,64,2048]{2,1,0:T(8,128)(2,1)} %bitcast.12), calls=%async_computation.2 | async-start | bytes 2097152 | tf_op jit(solution)/shard_map/all_to_all | solution.py:86
  103.1 127.2 %all-gather.2.cloned.1.call-start = ((), (), s32[]{:S(2)}) async-start(), calls=%async_computation.7 | async-start | bytes 2621440 | tf_op jit(solution)/shard_map/all_gather | solution.py:109
  185.3 63.7 %reduce-scatter.6.cloned.1.call-start = ((), (), s32[]{:S(2)}) async-start(), calls=%async_computation.8 | async-start | bytes 3145728 | tf_op jit(solution)/shard_map/reduce_scatter | solution.py:118
  240.2 52.0 %copy-start.1 = (f32[128]{0:T(128)S(1)}, f32[128]{0:T(128)}, u32[]{:S(2)}) copy-start(f32[128]{0:T(128)} %param.11) | copy-start | bytes 1540
  240.3 31.2 %reduce-scatter.8.cloned.1.call-start = ((), (), s32[]{:S(2)}) async-start(), calls=%async_computation.9 | async-start | bytes 1572864 | tf_op jit(solution)/shard_map/reduce_scatter | solution.py:120
  271.5 18.8 %collective-permute-start.1 = (bf16[128,2048]{1,0:T(8,128)(2,1)}, bf16[128,2048]{1,0:T(8,128)(2,1)S(1)}, u32[]{:S(2)}, u32[]{:S(2)}) collective-permute-start(bf16[128,2048]{1,0:T(8,128)(2,1)} %bitcast.71), channel_id=1, source_target_pairs={{0,0},{1,8},{2,4},{3,12},{4,1},{5,9},{6,5},{7,13},{8,2},{9,10},{10... | collective-permute-start | bytes 1572872 | tf_op jit(solution)/shard_map/ppermute | solution.py:137
Sparse Core Ops, SparseCore 0:
  52.8 42.9 reduce-scatter.3
  185.4 44.8 all-gather.1
  240.4 8.5 reduce-scatter.5
  251.1 20.3 reduce-scatter.7

commit v3 on v2

--- a/solution.py
+++ b/solution.py
@@ -12,6 +12,15 @@
     per_head = queries.astype(jnp.float32).reshape(row_count, -1, head_dim)
     inv_rms = lax.rsqrt(jnp.mean(per_head * per_head, axis=2, keepdims=True) + 1e-05)
     return (per_head * inv_rms * q_gain).reshape(row_count, -1).astype(jnp.bfloat16)
+
+
+def exchange_sum(parts, axis, count, index):
+    total = lax.dynamic_index_in_dim(parts, index, axis=0, keepdims=False).astype(jnp.float32)
+    for shift in range(1, count):
+        outgoing = lax.dynamic_index_in_dim(parts, (index + shift) % count, axis=0, keepdims=False)
+        incoming = lax.ppermute(outgoing, axis, [(i, (i + shift) % count) for i in range(count)])
+        total = total + incoming.astype(jnp.float32)
+    return total.astype(jnp.bfloat16)
 
 
 def local(
@@ -115,9 +124,9 @@
     req_index = lax.axis_index("req")
     head_count = lax.axis_size("head")
     by_group = partial_cols.reshape(sub_count, -1, partial_cols.shape[1])
-    owner_sums = lax.psum_scatter(by_group, "sub", scatter_dimension=0, tiled=True)
+    owner_sums = exchange_sum(by_group, "sub", sub_count, sub_index)
     owner_sums = owner_sums.reshape(head_count, -1, partial_cols.shape[1])
-    owner_sums = lax.psum_scatter(owner_sums, "head", scatter_dimension=0, tiled=True)
+    owner_sums = exchange_sum(owner_sums, "head", head_count, lax.axis_index("head"))
     per_hs = req_count // hs_count
     out_block = partial_cols.shape[1]
     owner_sums = owner_sums.reshape(per_hs, local_rows, out_block)

time: 304 us -> 289 us (0.951)
  waiting for transfers between devices: 157 us -> 144 us
    reduce_scatter x2 -> x0, waiting for transfers between devices: 31.1 us -> none  [the longest x1 22.4 us: local(): lax.psum_scatter(owner_sums, 'head', scatter_dimension=0, tiled=True)]
    ppermute x0 -> x2, waiting for transfers between devices: none -> 16.1 us  [exchange_sum(): lax.ppermute(outgoing, axis, [(i, (i + shift) % count) for i in range(cou...]
where the time goes in v3:
time: 289 us; the launch traced here: 285 us
  waiting for transfers between devices  144 us (50%)
  blocking collectives  58.1 us (20%)
  matrix products  46 us (16%)
  between operations  13.7 us (5%)
  local copies, waits for them, and re-layouts  11.2 us (4%)
  starting transfers between devices  6.38 us (2%)
  other arithmetic  5.88 us (2%)
    all_gather x1, waiting for transfers between devices, local(): lax.all_gather(attended, 'req', axis=0, tiled=True)  45.1 us
    reduce_scatter x1, waiting for transfers between devices, local(): lax.psum_scatter(jnp.dot(spread_cols, q_weight, preferred_element_type=jn...  41.8 us
    all_to_all x1, blocking collectives, local(): lax.all_to_all(my_part, 'req', split_axis=1, concat_axis=0, tiled=True)  30.4 us
    all_to_all x1, blocking collectives, local(): lax.all_to_all(replies, 'req', split_axis=0, concat_axis=0, tiled=True)  27.7 us
    all_to_all x1, waiting for transfers between devices, local(): lax.all_to_all(outgoing, 'req', split_axis=0, concat_axis=0, tiled=True)  22 us
    ppermute x1, waiting for transfers between devices, local(): arrived_blocks.append(lax.ppermute(chunk, ('req', 'head', 'sub'), pairs))  16.6 us
    ppermute x2, waiting for transfers between devices, exchange_sum(): lax.ppermute(outgoing, axis, [(i, (i + shift) % count) for i in range(cou...  16.1 us
    sub x1, matrix products, local(): weights = jnp.exp(scores - row_peak)  14.5 us
  transfers between devices with their start and end apart: 7, of which 7 were waited for; matrix products, arithmetic and copies ran while one was open for 2% of the time, Pallas kernels for 0%

profile of v3, /device:TPU:6, one launch (start us, length us, event | category | flops | bytes accessed | tf_op | source)
XLA Modules:
  0.0 285.1 jit_solution(2909639808181706036)
XLA Ops:
  6.5 3.2 %copy.35 = bf16[128,8192]{0,1:T(8,128)(2,1)S(1)} copy(bf16[128,8192]{1,0:T(8,128)(2,1)} %param.9) | data formatting | bytes 4194304 | tf_op args[0]
  10.4 30.4 %all_to_all.25 = bf16[128,4,1024]{2,0,1:T(8,128)(2,1)S(1)} all-to-all(bf16[128,4,1024]{2,0,1:T(8,128)(2,1)S(1)} %bitcast.76), channel_id=1, replica_groups=mesh['groups'=2,'req'=4,'head'=2,'sub'=2] {'req'}, dimensions={1} | all-to-all | bytes 2097152 | tf_op jit(solution)/shard_map/all_to_all | solution.py:49
  41.2 2.3 collective-permute-done
  43.6 9.1 %convolution_convert_fusion.1 = bf16[512,2048]{1,0:T(8,128)(2,1)} fusion(bf16[512,2048]{1,0:T(8,128)(2,1)S(1)} %constant_dynamic-update-slice_fusion, bf16[2048,2048]{1,0:T(8,128)(2,1)} %param.10), kind=kOutput, calls=%fused_computation.11 | convolution fusion | flops 4296015872 | bytes 12582912 | tf_op jit(solution)/shard_map/dot_general | solution.py:63
  54.0 41.8 %reduce-scatter.2.cloned.1.call-done = bf16[128,2048]{1,0:T(8,128)(2,1)} async-done(((bf16[512,2048]{1,0:T(8,128)(2,1)}), bf16[128,2048]{1,0:T(8,128)(2,1)}) %reduce-scatter.2.cloned.1.call-update) | async-done | bytes 524304 | tf_op jit(solution)/shard_map/reduce_scatter | solution.py:62
  95.8 1.1 fusion.13
  98.0 1.6 convolution_convert_fusion.2
  99.6 3.5 %all-to-all-start.1 = ((bf16[4,64,2048]{2,1,0:T(8,128)(2,1)}), bf16[4,64,2048]{2,1,0:T(8,128)(2,1)S(1)}, u32[]{:S(2)}, u32[]{:S(2)}) async-start(bf16[4,64,2048]{2,1,0:T(8,128)(2,1)} %bitcast.12), calls=%async_computation.2 | async-start | bytes 2097152 | tf_op jit(solution)/shard_map/all_to_all | solution.py:95
  103.4 1.5 constant_dynamic-slice_fusion.1
  104.9 1.4 copy.34
  106.9 22.0 %all-to-all-done.1 = bf16[4,64,2048]{2,1,0:T(8,128)(2,1)S(1)} async-done(((bf16[4,64,2048]{2,1,0:T(8,128)(2,1)}), bf16[4,64,2048]{2,1,0:T(8,128)(2,1)S(1)}, u32[]{:S(2)}, u32[]{:S(2)}) %all-to-all-start.1) | async-done | bytes 1048608 | tf_op jit(solution)/shard_map/all_to_all | solution.py:95
  129.2 14.5 %fusion.36 = (f32[2,8,256]{2,1,0:T(8,128)S(1)}, f32[2,8,256,1601]{2,3,1,0:T(8,128)}) fusion(bf16[1601,2,128,1]{0,2,3,1:T(8,128)(2,1)} %bitcast.81, bf16[256,2,8,128]{3,2,1,0:T(8,128)(2,1)S(1)} %bitcast.79), kind=kOutput, calls=%fused_computation.54 | convolution fusion | flops 1698444800 | bytes 28115456 | tf_op jit(solution)/shard_map/sub | solution.py:104
  143.7 11.1 %fusion.12 = bf16[256,2,8,128]{0,3,2,1:T(8,128)(2,1)S(1)} fusion(bf16[1601,2,128,1]{0,2,3,1:T(8,128)(2,1)S(1)} %bitcast.80, f32[2,8,256,1601]{2,3,1,0:T(8,128)} %get-tuple-element.6, f32[2,8,256]{2,1,0:T(8,128)S(1)} %get-tuple-element.5), kind=kOutput, calls=%fused_computation.17 | convolution fusion | flops 1692409856 | bytes 28115456 | tf_op jit(solution)/shard_map/kgmt,tkd->mkgd/dot_general | solution.py:106
  154.8 1.1 copy.42
  156.4 27.7 %all_to_all.26 = bf16[4,64,2048]{2,1,0:T(8,128)(2,1)S(1)} all-to-all(bf16[4,64,2048]{2,1,0:T(8,128)(2,1)S(1)} %reshape.85), channel_id=1, replica_groups=mesh['groups'=2,'req'=4,'head'=2,'sub'=2] {'req'}, dimensions={0} | all-to-all | bytes 2097152 | tf_op jit(solution)/shard_map/all_to_all | solution.py:110
  184.1 1.1 convolution_convert_fusion.3
  185.3 45.1 %all-gather.2.cloned.1.call-done = bf16[512,2048]{1,0:T(8,128)(2,1)} async-done(((bf16[128,2048]{1,0:T(8,128)(2,1)}), bf16[512,2048]{1,0:T(8,128)(2,1)}) %all-gather.2.cloned.1.call-update) | async-done | bytes 2097168 | tf_op jit(solution)/shard_map/all_gather | solution.py:118
  230.4 8.5 %convolution_convert_fusion = bf16[512,2048]{1,0:T(8,128)(2,1)S(1)} fusion(bf16[512,2048]{1,0:T(8,128)(2,1)} %all-gather.2.cloned.1.call-done, bf16[2048,2048]{1,0:T(8,128)(2,1)} %param.14), kind=kOutput, calls=%fused_computation.10 | convolution fusion | flops 4296015872 | bytes 12582912 | tf_op jit(solution)/shard_map/dot_general | solution.py:117
  239.1 2.8 collective-permute-done.1
  241.9 1.6 fusion.10
  244.2 13.4 %collective-permute-done.2 = bf16[128,2048]{1,0:T(8,128)(2,1)S(1)} collective-permute-done((bf16[128,2048]{1,0:T(8,128)(2,1)S(1)}, bf16[128,2048]{1,0:T(8,128)(2,1)S(1)}, u32[]{:S(2)}, u32[]{:S(2)}) %collective-permute-start.2) | collective-permute-done | bytes 524320 | tf_op jit(solution)/shard_map/ppermute | solution.py:21
  257.7 1.9 collective-permute-start.3
  259.6 16.6 %collective-permute-done.3 = bf16[128,2048]{1,0:T(8,128)(2,1)S(1)} collective-permute-done((bf16[128,2048]{1,0:T(8,128)(2,1)S(1)}, bf16[128,2048]{1,0:T(8,128)(2,1)S(1)}, u32[]{:S(2)}, u32[]{:S(2)}) %collective-permute-start.3) | collective-permute-done | bytes 524320 | tf_op jit(solution)/shard_map/ppermute | solution.py:146
  276.2 2.0 add_convert_fusion
  (43 shorter events, 6.1 us)
Async XLA Ops:
  6.5 47.5 %copy-start = (f32[128]{0:T(128)S(1)}, f32[128]{0:T(128)}, u32[]{:S(2)}) copy-start(f32[128]{0:T(128)} %param.11) | copy-start | bytes 1540
  6.5 89.3 %reduce-scatter.2.cloned.1.call-start = ((), (), s32[]{:S(2)}) async-start(), calls=%async_computation.4 | async-start | bytes 2621440 | tf_op jit(solution)/shard_map/reduce_scatter | solution.py:62
  40.8 2.7 collective-permute-start
  52.7 0.7 copy-start.3
  52.7 0.7 copy-start.4
  52.7 0.8 copy-start.5
  97.0 1.1 copy-start.2
  99.6 29.3 %all-to-all-start.1 = ((bf16[4,64,2048]{2,1,0:T(8,128)(2,1)}), bf16[4,64,2048]{2,1,0:T(8,128)(2,1)S(1)}, u32[]{:S(2)}, u32[]{:S(2)}) async-start(bf16[4,64,2048]{2,1,0:T(8,128)(2,1)} %bitcast.12), calls=%async_computation.2 | async-start | bytes 2097152 | tf_op jit(solution)/shard_map/all_to_all | solution.py:95
  103.1 127.2 %all-gather.2.cloned.1.call-start = ((), (), s32[]{:S(2)}) async-start(), calls=%async_computation.5 | async-start | bytes 2621440 | tf_op jit(solution)/shard_map/all_gather | solution.py:118
  239.0 2.9 %collective-permute-start.1 = (bf16[256,2048]{1,0:T(8,128)(2,1)S(1)}, bf16[256,2048]{1,0:T(8,128)(2,1)}, u32[]{:S(2)}, u32[]{:S(2)}) collective-permute-start(bf16[256,2048]{1,0:T(8,128)(2,1)S(1)} %dynamic-slice_bitcast_fusion), channel_id=1, source_target_pairs={{0,1},{1,0},{2,3},{3,2},{4,5},{5,4},{6,7},{7,6},{8,9},{9,8},{10,11... | collective-permute-start | bytes 3145736 | tf_op jit(solution)/shard_map/ppermute | solution.py:21
  243.5 34.8 %copy-start.1 = (f32[128]{0:T(128)S(1)}, f32[128]{0:T(128)}, u32[]{:S(2)}) copy-start(f32[128]{0:T(128)} %param.11) | copy-start | bytes 1540
  243.5 14.0 %collective-permute-start.2 = (bf16[128,2048]{1,0:T(8,128)(2,1)S(1)}, bf16[128,2048]{1,0:T(8,128)(2,1)S(1)}, u32[]{:S(2)}, u32[]{:S(2)}) collective-permute-start(bf16[128,2048]{1,0:T(8,128)(2,1)S(1)} %dynamic-slice_bitcast_fusion.1), channel_id=1, source_target_pairs={{0,2},{2,0},{1,3},{3,1},{4,6},{6,4},{5,7},{7,5},{8,10},{10,8},{9,1... | collective-permute-start | bytes 1572872 | tf_op jit(solution)/shard_map/ppermute | solution.py:21
  257.7 18.5 %collective-permute-start.3 = (bf16[128,2048]{1,0:T(8,128)(2,1)S(1)}, bf16[128,2048]{1,0:T(8,128)(2,1)S(1)}, u32[]{:S(2)}, u32[]{:S(2)}) collective-permute-start(bf16[128,2048]{1,0:T(8,128)(2,1)S(1)} %fusion.16), channel_id=1, source_target_pairs={{0,0},{1,8},{2,4},{3,12},{4,1},{5,9},{6,5},{7,13},{8,2},{9,10},{10... | collective-permute-start | bytes 1572872 | tf_op jit(solution)/shard_map/ppermute | solution.py:146
Sparse Core Ops, SparseCore 0:
  52.8 42.9 reduce-scatter.1
  185.4 44.8 all-gather.1

commit v4 on v3

--- a/solution.py
+++ b/solution.py
@@ -1,7 +1,10 @@
+import functools
+
 import jax
 import jax.numpy as jnp
 from jax import lax
 from jax.sharding import PartitionSpec as P
+from jax.experimental import pallas as pl
 
 HQ = 64
 KVH = 8
@@ -21,6 +24,52 @@
         incoming = lax.ppermute(outgoing, axis, [(i, (i + shift) % count) for i in range(count)])
         total = total + incoming.astype(jnp.float32)
     return total.astype(jnp.bfloat16)
+
+
+def attend_kernel(q_ref, k_ref, v_ref, o_ref, *, per_kv, head_dim, token_count):
+    keys = k_ref[...]
+    values = v_ref[...]
+    rows = q_ref.shape[0]
+    valid = lax.broadcasted_iota(jnp.int32, (rows, keys.shape[0]), 1) < token_count
+    score_scale = head_dim ** (-0.5)
+    for g in range(per_kv):
+        query = q_ref[:, g * head_dim:(g + 1) * head_dim]
+        scores = lax.dot_general(
+            query, keys, (((1,), (1,)), ((), ())), preferred_element_type=jnp.float32
+        ) * score_scale
+        scores = jnp.where(valid, scores, -jnp.inf)
+        peak = jnp.max(scores, axis=1, keepdims=True)
+        weights = jnp.exp(scores - peak)
+        probs = (weights / jnp.sum(weights, axis=1, keepdims=True)).astype(jnp.bfloat16)
+        mixed = jnp.dot(probs, values, preferred_element_type=jnp.float32)
+        o_ref[:, g * head_dim:(g + 1) * head_dim] = mixed.astype(o_ref.dtype)
+
+
+def attend(rows_in, keys, values, kv_count, per_kv, head_dim, token_count):
+    rows, width = rows_in.shape
+    padded_tokens = keys.shape[0]
+    group_width = per_kv * head_dim
+    kernel = functools.partial(
+        attend_kernel, per_kv=per_kv, head_dim=head_dim, token_count=token_count
+    )
+    flops = 4 * rows * padded_tokens * head_dim * per_kv * kv_count
+    moved = 2 * (2 * rows * width + 2 * padded_tokens * head_dim * kv_count)
+    return pl.pallas_call(
+        kernel,
+        grid=(kv_count,),
+        in_specs=[
+            pl.BlockSpec((rows, group_width), lambda k: (0, k)),
+            pl.BlockSpec((padded_tokens, head_dim), lambda k: (0, k)),
+            pl.BlockSpec((padded_tokens, head_dim), lambda k: (0, k)),
+        ],
+        out_specs=pl.BlockSpec((rows, group_width), lambda k: (0, k)),
+        out_shape=jax.ShapeDtypeStruct((rows, width), jnp.bfloat16),
+        cost_estimate=pl.CostEstimate(
+            flops=flops,
+            transcendentals=rows * padded_tokens * per_kv * kv_count,
+            bytes_accessed=moved,
+        ),
+    )(rows_in, keys, values)
 
 
 def local(
@@ -85,28 +134,22 @@
     kv_count = max(1, heads_here // group_size)
     per_kv = heads_here // kv_count
     kv_first = sub_index * heads_here // group_size
-    keys_here = lax.dynamic_slice_in_dim(
-        key_cache[0], kv_first * head_dim, kv_count * head_dim, 1
-    ).reshape(-1, kv_count, head_dim)
-    values_here = lax.dynamic_slice_in_dim(
-        value_cache[0], kv_first * head_dim, kv_count * head_dim, 1
-    ).reshape(-1, kv_count, head_dim)
-    score_scale = head_dim ** (-0.5)
+    token_count = key_cache.shape[1]
+    padded_tokens = -(-token_count // 128) * 128
+    keys_here = jnp.pad(
+        lax.dynamic_slice_in_dim(key_cache[0], kv_first * head_dim, kv_count * head_dim, 1),
+        ((0, padded_tokens - token_count), (0, 0)),
+    )
+    values_here = jnp.pad(
+        lax.dynamic_slice_in_dim(value_cache[0], kv_first * head_dim, kv_count * head_dim, 1),
+        ((0, padded_tokens - token_count), (0, 0)),
+    )
     arrived = lax.all_to_all(outgoing, "req", split_axis=0, concat_axis=0, tiled=True)
     sources = arrived.shape[0]
     slot_count = arrived.shape[1]
-    flat_rows = arrived.reshape(sources * slot_count, kv_count, per_kv, head_dim)
-    scores = (
-        jnp.einsum("mkgd,tkd->kgmt", flat_rows, keys_here, preferred_element_type=jnp.float32)
-        * score_scale
-    )
-    row_peak = jnp.max(scores, axis=3, keepdims=True)
-    weights = jnp.exp(scores - row_peak)
-    probs = (weights / jnp.sum(weights, axis=3, keepdims=True)).astype(jnp.bfloat16)
-    mixed_heads = jnp.einsum(
-        "kgmt,tkd->mkgd", probs, values_here, preferred_element_type=jnp.float32
-    )
-    replies = mixed_heads.astype(jnp.bfloat16).reshape(sources, slot_count, q_cols)
+    flat_rows = arrived.reshape(sources * slot_count, q_cols)
+    mixed_heads = attend(flat_rows, keys_here, values_here, kv_count, per_kv, head_dim, token_count)
+    replies = mixed_heads.reshape(sources, slot_count, q_cols)
     returned = lax.all_to_all(replies, "req", split_axis=0, concat_axis=0, tiled=True)
     attended = lax.dot_general(
         dispatch,

time: 289 us -> 282 us (0.976)
  matrix products: 46 us -> 20.3 us
  Pallas kernels: 0 us -> 18.2 us
    pallas_call x0 -> x1, Pallas kernels: none -> 18.2 us  [attend(): pl.pallas_call(kernel, grid=(kv_count,), in_specs=[pl.BlockSpec((rows, gr...]
    sub x1 -> x0, matrix products: 14.5 us -> none  [local(): weights = jnp.exp(scores - row_peak)]
    dot_general x1 -> x0, matrix products: 11.1 us -> none  [local(): jnp.einsum('kgmt,tkd->mkgd', probs, values_here, preferred_element_type=j...]
where the time goes in v4:
time: 282 us; the launch traced here: 278 us
  waiting for transfers between devices  144 us (51%)
  blocking collectives  59.1 us (21%)
  matrix products  20.3 us (7%)
  Pallas kernels  18.2 us (6%)
  between operations  13.7 us (5%)
  local copies, waits for them, and re-layouts  9.99 us (4%)
  starting transfers between devices  6.38 us (2%)
  other arithmetic  5.88 us (2%)
    all_gather x1, waiting for transfers between devices, local(): lax.all_gather(attended, 'req', axis=0, tiled=True)  45.1 us
    reduce_scatter x1, waiting for transfers between devices, local(): lax.psum_scatter(jnp.dot(spread_cols, q_weight, preferred_element_type=jn...  41.8 us
    all_to_all x1, blocking collectives, local(): lax.all_to_all(my_part, 'req', split_axis=1, concat_axis=0, tiled=True)  30.4 us
    all_to_all x1, blocking collectives, local(): lax.all_to_all(replies, 'req', split_axis=0, concat_axis=0, tiled=True)  28.7 us
    all_to_all x1, waiting for transfers between devices, local(): lax.all_to_all(outgoing, 'req', split_axis=0, concat_axis=0, tiled=True)  22.4 us
    pallas_call x1, Pallas kernels, attend(): pl.pallas_call(kernel, grid=(kv_count,), in_specs=[pl.BlockSpec((rows, gr...  18.2 us
    ppermute x1, waiting for transfers between devices, local(): arrived_blocks.append(lax.ppermute(chunk, ('req', 'head', 'sub'), pairs))  16.6 us
    ppermute x2, waiting for transfers between devices, exchange_sum(): lax.ppermute(outgoing, axis, [(i, (i + shift) % count) for i in range(cou...  16.1 us
  transfers between devices with their start and end apart: 7, of which 7 were waited for; matrix products, arithmetic and copies ran while one was open for 2% of the time, Pallas kernels for 0%

profile of v4, /device:TPU:6, one launch (start us, length us, event | category | flops | bytes accessed | tf_op | source)
XLA Modules:
  0.0 277.9 jit_solution(15944227682741666032)
XLA Ops:
  6.5 3.2 %copy.15 = bf16[128,8192]{0,1:T(8,128)(2,1)S(1)} copy(bf16[128,8192]{1,0:T(8,128)(2,1)} %param.9) | data formatting | bytes 4194304 | tf_op args[0]
  10.4 30.4 %all_to_all.25 = bf16[128,4,1024]{2,0,1:T(8,128)(2,1)S(1)} all-to-all(bf16[128,4,1024]{2,0,1:T(8,128)(2,1)S(1)} %bitcast.49), channel_id=1, replica_groups=mesh['groups'=2,'req'=4,'head'=2,'sub'=2] {'req'}, dimensions={1} | all-to-all | bytes 2097152 | tf_op jit(solution)/shard_map/all_to_all | solution.py:98
  41.2 2.3 collective-permute-done
  43.6 9.1 %convolution_convert_fusion.1 = bf16[512,2048]{1,0:T(8,128)(2,1)} fusion(bf16[512,2048]{1,0:T(8,128)(2,1)S(1)} %constant_dynamic-update-slice_fusion, bf16[2048,2048]{1,0:T(8,128)(2,1)} %param.10), kind=kOutput, calls=%fused_computation.1 | convolution fusion | flops 4296015872 | bytes 12582912 | tf_op jit(solution)/shard_map/dot_general | solution.py:112
  54.0 41.8 %reduce-scatter.2.cloned.1.call-done = bf16[128,2048]{1,0:T(8,128)(2,1)} async-done(((bf16[512,2048]{1,0:T(8,128)(2,1)}), bf16[128,2048]{1,0:T(8,128)(2,1)}) %reduce-scatter.2.cloned.1.call-update) | async-done | bytes 524304 | tf_op jit(solution)/shard_map/reduce_scatter | solution.py:111
  95.8 1.1 fusion.1
  98.0 1.6 convolution_convert_fusion.2
  99.6 3.5 %all-to-all-start.1 = ((bf16[4,64,2048]{2,1,0:T(8,128)(2,1)}), bf16[4,64,2048]{2,1,0:T(8,128)(2,1)S(1)}, u32[]{:S(2)}, u32[]{:S(2)}) async-start(bf16[4,64,2048]{2,1,0:T(8,128)(2,1)} %bitcast.8), calls=%async_computation.2 | async-start | bytes 2097152 | tf_op jit(solution)/shard_map/all_to_all | solution.py:147
  103.4 1.3 dynamic-slice_bitcast_fusion.1
  104.7 1.0 pad.7.k_ref
  105.6 1.0 pad.8.v_ref
  106.6 22.4 %all-to-all-done.1 = bf16[4,64,2048]{2,1,0:T(8,128)(2,1)S(1)} async-done(((bf16[4,64,2048]{2,1,0:T(8,128)(2,1)}), bf16[4,64,2048]{2,1,0:T(8,128)(2,1)S(1)}, u32[]{:S(2)}, u32[]{:S(2)}) %all-to-all-start.1) | async-done | bytes 1048608 | tf_op jit(solution)/shard_map/all_to_all | solution.py:147
  129.0 1.0 copy-done.2
  129.9 18.2 %shard_map.91 = bf16[256,2048]{1,0:T(8,128)(2,1)} custom-call(bf16[256,2048]{1,0:T(8,128)(2,1)} %bitcast.52, bf16[1664,256]{1,0:T(8,128)(2,1)} %pad.7.k_ref, bf16[1664,256]{1,0:T(8,128)(2,1)} %pad.8.v_ref), custom_call_target="tpu_custom_call" | custom-call | flops 3489660928 | bytes 3801088 | tf_op jit(solution)/shard_map/pallas_call | solution.py:57
  148.2 28.7 %all_to_all.26 = bf16[4,64,2048]{2,1,0:T(8,128)(2,1)S(1)} all-to-all(bf16[4,64,2048]{2,1,0:T(8,128)(2,1)} %bitcast.53), channel_id=1, replica_groups=mesh['groups'=2,'req'=4,'head'=2,'sub'=2] {'req'}, dimensions={0} | all-to-all | bytes 2097152 | tf_op jit(solution)/shard_map/all_to_all | solution.py:153
  176.9 1.1 convolution_convert_fusion.3
  178.1 45.1 %all-gather.2.cloned.1.call-done = bf16[512,2048]{1,0:T(8,128)(2,1)} async-done(((bf16[128,2048]{1,0:T(8,128)(2,1)}), bf16[512,2048]{1,0:T(8,128)(2,1)}) %all-gather.2.cloned.1.call-update) | async-done | bytes 2097168 | tf_op jit(solution)/shard_map/all_gather | solution.py:161
  223.2 8.5 %convolution_convert_fusion = bf16[512,2048]{1,0:T(8,128)(2,1)S(1)} fusion(bf16[512,2048]{1,0:T(8,128)(2,1)} %all-gather.2.cloned.1.call-done, bf16[2048,2048]{1,0:T(8,128)(2,1)} %param.14), kind=kOutput, calls=%fused_computation | convolution fusion | flops 4296015872 | bytes 12582912 | tf_op jit(solution)/shard_map/dot_general | solution.py:160
  231.9 2.8 collective-permute-done.1
  234.7 1.6 fusion
  237.0 13.4 %collective-permute-done.2 = bf16[128,2048]{1,0:T(8,128)(2,1)S(1)} collective-permute-done((bf16[128,2048]{1,0:T(8,128)(2,1)S(1)}, bf16[128,2048]{1,0:T(8,128)(2,1)S(1)}, u32[]{:S(2)}, u32[]{:S(2)}) %collective-permute-start.2) | collective-permute-done | bytes 524320 | tf_op jit(solution)/shard_map/ppermute | solution.py:24
  250.5 1.9 collective-permute-start.3
  252.5 16.6 %collective-permute-done.3 = bf16[128,2048]{1,0:T(8,128)(2,1)S(1)} collective-permute-done((bf16[128,2048]{1,0:T(8,128)(2,1)S(1)}, bf16[128,2048]{1,0:T(8,128)(2,1)S(1)}, u32[]{:S(2)}, u32[]{:S(2)}) %collective-permute-start.3) | collective-permute-done | bytes 524320 | tf_op jit(solution)/shard_map/ppermute | solution.py:189
  269.1 2.0 add_convert_fusion
  (41 shorter events, 4.7 us)
Async XLA Ops:
  6.5 47.5 %copy-start = (f32[128]{0:T(128)S(1)}, f32[128]{0:T(128)}, u32[]{:S(2)}) copy-start(f32[128]{0:T(128)} %param.11) | copy-start | bytes 1540
  6.5 89.3 %reduce-scatter.2.cloned.1.call-start = ((), (), s32[]{:S(2)}) async-start(), calls=%async_computation.4 | async-start | bytes 2621440 | tf_op jit(solution)/shard_map/reduce_scatter | solution.py:111
  40.8 2.7 collective-permute-start
  52.7 0.7 copy-start.4
  52.7 0.7 copy-start.5
  52.7 0.8 copy-start.6
  96.9 1.1 copy-start.1
  98.0 5.4 %copy-start.3 = (bf16[1,1601,512]{2,1,0:T(8,128)(2,1)S(1)}, bf16[1,1601,512]{2,1,0:T(8,128)(2,1)}, u32[]{:S(2)}) copy-start(bf16[1,1601,512]{2,1,0:T(8,128)(2,1)} %param.13) | copy-start | bytes 4918276
  99.6 29.4 %all-to-all-start.1 = ((bf16[4,64,2048]{2,1,0:T(8,128)(2,1)}), bf16[4,64,2048]{2,1,0:T(8,128)(2,1)S(1)}, u32[]{:S(2)}, u32[]{:S(2)}) async-start(bf16[4,64,2048]{2,1,0:T(8,128)(2,1)} %bitcast.8), calls=%async_computation.2 | async-start | bytes 2097152 | tf_op jit(solution)/shard_map/all_to_all | solution.py:147
  103.1 120.1 %all-gather.2.cloned.1.call-start = ((), (), s32[]{:S(2)}) async-start(), calls=%async_computation.5 | async-start | bytes 2621440 | tf_op jit(solution)/shard_map/all_gather | solution.py:161
  129.0 1.0 copy-start.2
  231.8 2.9 %collective-permute-start.1 = (bf16[256,2048]{1,0:T(8,128)(2,1)S(1)}, bf16[256,2048]{1,0:T(8,128)(2,1)}, u32[]{:S(2)}, u32[]{:S(2)}) collective-permute-start(bf16[256,2048]{1,0:T(8,128)(2,1)S(1)} %dynamic-slice_bitcast_fusion), channel_id=1, source_target_pairs={{0,1},{1,0},{2,3},{3,2},{4,5},{5,4},{6,7},{7,6},{8,9},{9,8},{10,11... | collective-permute-start | bytes 3145736 | tf_op jit(solution)/shard_map/ppermute | solution.py:24
  236.4 14.0 %collective-permute-start.2 = (bf16[128,2048]{1,0:T(8,128)(2,1)S(1)}, bf16[128,2048]{1,0:T(8,128)(2,1)S(1)}, u32[]{:S(2)}, u32[]{:S(2)}) collective-permute-start(bf16[128,2048]{1,0:T(8,128)(2,1)S(1)} %dynamic-slice_bitcast_fusion.3), channel_id=1, source_target_pairs={{0,2},{2,0},{1,3},{3,1},{4,6},{6,4},{5,7},{7,5},{8,10},{10,8},{9,1... | collective-permute-start | bytes 1572872 | tf_op jit(solution)/shard_map/ppermute | solution.py:24
  250.5 18.5 %collective-permute-start.3 = (bf16[128,2048]{1,0:T(8,128)(2,1)S(1)}, bf16[128,2048]{1,0:T(8,128)(2,1)S(1)}, u32[]{:S(2)}, u32[]{:S(2)}) collective-permute-start(bf16[128,2048]{1,0:T(8,128)(2,1)S(1)} %fusion.4), channel_id=1, source_target_pairs={{0,0},{1,8},{2,4},{3,12},{4,1},{5,9},{6,5},{7,13},{8,2},{9,10},{10... | collective-permute-start | bytes 1572872 | tf_op jit(solution)/shard_map/ppermute | solution.py:189
Sparse Core Ops, SparseCore 0:
  52.8 42.9 reduce-scatter.1
  178.2 44.9 all-gather.1

commit v5 on v4

--- a/solution.py
+++ b/solution.py
@@ -27,21 +27,37 @@
 
 
 def attend_kernel(q_ref, k_ref, v_ref, o_ref, *, per_kv, head_dim, token_count):
+    padded_tokens = k_ref.shape[0]
+    split = (token_count // 128) * 128
     keys = k_ref[...]
-    values = v_ref[...]
     rows = q_ref.shape[0]
-    valid = lax.broadcasted_iota(jnp.int32, (rows, keys.shape[0]), 1) < token_count
     score_scale = head_dim ** (-0.5)
     for g in range(per_kv):
         query = q_ref[:, g * head_dim:(g + 1) * head_dim]
         scores = lax.dot_general(
             query, keys, (((1,), (1,)), ((), ())), preferred_element_type=jnp.float32
         ) * score_scale
-        scores = jnp.where(valid, scores, -jnp.inf)
-        peak = jnp.max(scores, axis=1, keepdims=True)
-        weights = jnp.exp(scores - peak)
-        probs = (weights / jnp.sum(weights, axis=1, keepdims=True)).astype(jnp.bfloat16)
-        mixed = jnp.dot(probs, values, preferred_element_type=jnp.float32)
+        pieces = [scores[:, :split]] if split else []
+        if split < padded_tokens:
+            tail = scores[:, split:]
+            valid = lax.broadcasted_iota(jnp.int32, tail.shape, 1) < token_count - split
+            pieces.append(jnp.where(valid, tail, -jnp.inf))
+        peak = jnp.max(pieces[0], axis=1, keepdims=True)
+        for piece in pieces[1:]:
+            peak = jnp.maximum(peak, jnp.max(piece, axis=1, keepdims=True))
+        weights = [jnp.exp(piece - peak) for piece in pieces]
+        total = sum(jnp.sum(w, axis=1, keepdims=True) for w in weights)
+        inverse = 1.0 / total
+        mixed = None
+        start = 0
+        for w in weights:
+            width = w.shape[1]
+            probs = (w * inverse).astype(jnp.bfloat16)
+            term = jnp.dot(
+                probs, v_ref[start:start + width, :], preferred_element_type=jnp.float32
+            )
+            mixed = term if mixed is None else mixed + term
+            start += width
         o_ref[:, g * head_dim:(g + 1) * head_dim] = mixed.astype(o_ref.dtype)
 
 

time: 282 us -> 282 us (level)
  no operation moved by 1% of the time
where the time goes in v5:
time: 282 us; the launch traced here: 278 us
  waiting for transfers between devices  144 us (51%)
  blocking collectives  59.1 us (21%)
  matrix products  20.3 us (7%)
  Pallas kernels  18.2 us (6%)
  between operations  13.7 us (5%)
  local copies, waits for them, and re-layouts  9.99 us (4%)
  starting transfers between devices  6.38 us (2%)
  other arithmetic  5.88 us (2%)
    all_gather x1, waiting for transfers between devices, local(): lax.all_gather(attended, 'req', axis=0, tiled=True)  45.1 us
    reduce_scatter x1, waiting for transfers between devices, local(): lax.psum_scatter(jnp.dot(spread_cols, q_weight, preferred_element_type=jn...  41.8 us
    all_to_all x1, blocking collectives, local(): lax.all_to_all(my_part, 'req', split_axis=1, concat_axis=0, tiled=True)  30.4 us
    all_to_all x1, blocking collectives, local(): lax.all_to_all(replies, 'req', split_axis=0, concat_axis=0, tiled=True)  28.7 us
    all_to_all x1, waiting for transfers between devices, local(): lax.all_to_all(outgoing, 'req', split_axis=0, concat_axis=0, tiled=True)  22.4 us
    pallas_call x1, Pallas kernels, attend(): pl.pallas_call(kernel, grid=(kv_count,), in_specs=[pl.BlockSpec((rows, gr...  18.2 us
    ppermute x1, waiting for transfers between devices, local(): arrived_blocks.append(lax.ppermute(chunk, ('req', 'head', 'sub'), pairs))  16.6 us
    ppermute x2, waiting for transfers between devices, exchange_sum(): lax.ppermute(outgoing, axis, [(i, (i + shift) % count) for i in range(cou...  16.1 us
  transfers between devices with their start and end apart: 7, of which 7 were waited for; matrix products, arithmetic and copies ran while one was open for 2% of the time, Pallas kernels for 0%

profile of v5, /device:TPU:6, one launch (start us, length us, event | category | flops | bytes accessed | tf_op | source)
XLA Modules:
  0.0 277.9 jit_solution(5595800701543146608)
XLA Ops:
  6.5 3.2 %copy.15 = bf16[128,8192]{0,1:T(8,128)(2,1)S(1)} copy(bf16[128,8192]{1,0:T(8,128)(2,1)} %param.9) | data formatting | bytes 4194304 | tf_op args[0]
  10.4 30.4 %all_to_all.25 = bf16[128,4,1024]{2,0,1:T(8,128)(2,1)S(1)} all-to-all(bf16[128,4,1024]{2,0,1:T(8,128)(2,1)S(1)} %bitcast.49), channel_id=1, replica_groups=mesh['groups'=2,'req'=4,'head'=2,'sub'=2] {'req'}, dimensions={1} | all-to-all | bytes 2097152 | tf_op jit(solution)/shard_map/all_to_all | solution.py:114
  41.2 2.3 collective-permute-done
  43.6 9.1 %convolution_convert_fusion.1 = bf16[512,2048]{1,0:T(8,128)(2,1)} fusion(bf16[512,2048]{1,0:T(8,128)(2,1)S(1)} %constant_dynamic-update-slice_fusion, bf16[2048,2048]{1,0:T(8,128)(2,1)} %param.10), kind=kOutput, calls=%fused_computation.1 | convolution fusion | flops 4296015872 | bytes 12582912 | tf_op jit(solution)/shard_map/dot_general | solution.py:128
  54.0 41.8 %reduce-scatter.2.cloned.1.call-done = bf16[128,2048]{1,0:T(8,128)(2,1)} async-done(((bf16[512,2048]{1,0:T(8,128)(2,1)}), bf16[128,2048]{1,0:T(8,128)(2,1)}) %reduce-scatter.2.cloned.1.call-update) | async-done | bytes 524304 | tf_op jit(solution)/shard_map/reduce_scatter | solution.py:127
  95.8 1.1 fusion.1
  98.0 1.6 convolution_convert_fusion.2
  99.6 3.5 %all-to-all-start.1 = ((bf16[4,64,2048]{2,1,0:T(8,128)(2,1)}), bf16[4,64,2048]{2,1,0:T(8,128)(2,1)S(1)}, u32[]{:S(2)}, u32[]{:S(2)}) async-start(bf16[4,64,2048]{2,1,0:T(8,128)(2,1)} %bitcast.8), calls=%async_computation.2 | async-start | bytes 2097152 | tf_op jit(solution)/shard_map/all_to_all | solution.py:163
  103.4 1.3 dynamic-slice_bitcast_fusion.1
  104.7 1.0 pad.7.k_ref
  105.6 1.0 pad.8.v_ref
  106.6 22.4 %all-to-all-done.1 = bf16[4,64,2048]{2,1,0:T(8,128)(2,1)S(1)} async-done(((bf16[4,64,2048]{2,1,0:T(8,128)(2,1)}), bf16[4,64,2048]{2,1,0:T(8,128)(2,1)S(1)}, u32[]{:S(2)}, u32[]{:S(2)}) %all-to-all-start.1) | async-done | bytes 1048608 | tf_op jit(solution)/shard_map/all_to_all | solution.py:163
  129.0 1.0 copy-done.2
  129.9 18.2 %shard_map.91 = bf16[256,2048]{1,0:T(8,128)(2,1)} custom-call(bf16[256,2048]{1,0:T(8,128)(2,1)} %bitcast.52, bf16[1664,256]{1,0:T(8,128)(2,1)} %pad.7.k_ref, bf16[1664,256]{1,0:T(8,128)(2,1)} %pad.8.v_ref), custom_call_target="tpu_custom_call" | custom-call | flops 3489660928 | bytes 3801088 | tf_op jit(solution)/shard_map/pallas_call | solution.py:73
  148.1 28.7 %all_to_all.26 = bf16[4,64,2048]{2,1,0:T(8,128)(2,1)S(1)} all-to-all(bf16[4,64,2048]{2,1,0:T(8,128)(2,1)} %bitcast.53), channel_id=1, replica_groups=mesh['groups'=2,'req'=4,'head'=2,'sub'=2] {'req'}, dimensions={0} | all-to-all | bytes 2097152 | tf_op jit(solution)/shard_map/all_to_all | solution.py:169
  176.8 1.1 convolution_convert_fusion.3
  178.0 45.1 %all-gather.2.cloned.1.call-done = bf16[512,2048]{1,0:T(8,128)(2,1)} async-done(((bf16[128,2048]{1,0:T(8,128)(2,1)}), bf16[512,2048]{1,0:T(8,128)(2,1)}) %all-gather.2.cloned.1.call-update) | async-done | bytes 2097168 | tf_op jit(solution)/shard_map/all_gather | solution.py:177
  223.1 8.5 %convolution_convert_fusion = bf16[512,2048]{1,0:T(8,128)(2,1)S(1)} fusion(bf16[512,2048]{1,0:T(8,128)(2,1)} %all-gather.2.cloned.1.call-done, bf16[2048,2048]{1,0:T(8,128)(2,1)} %param.14), kind=kOutput, calls=%fused_computation | convolution fusion | flops 4296015872 | bytes 12582912 | tf_op jit(solution)/shard_map/dot_general | solution.py:176
  231.9 2.8 collective-permute-done.1
  234.6 1.6 fusion
  236.9 13.4 %collective-permute-done.2 = bf16[128,2048]{1,0:T(8,128)(2,1)S(1)} collective-permute-done((bf16[128,2048]{1,0:T(8,128)(2,1)S(1)}, bf16[128,2048]{1,0:T(8,128)(2,1)S(1)}, u32[]{:S(2)}, u32[]{:S(2)}) %collective-permute-start.2) | collective-permute-done | bytes 524320 | tf_op jit(solution)/shard_map/ppermute | solution.py:24
  250.5 1.9 collective-permute-start.3
  252.4 16.6 %collective-permute-done.3 = bf16[128,2048]{1,0:T(8,128)(2,1)S(1)} collective-permute-done((bf16[128,2048]{1,0:T(8,128)(2,1)S(1)}, bf16[128,2048]{1,0:T(8,128)(2,1)S(1)}, u32[]{:S(2)}, u32[]{:S(2)}) %collective-permute-start.3) | collective-permute-done | bytes 524320 | tf_op jit(solution)/shard_map/ppermute | solution.py:205
  269.0 2.0 add_convert_fusion
  (41 shorter events, 4.7 us)
Async XLA Ops:
  6.5 47.5 %copy-start = (f32[128]{0:T(128)S(1)}, f32[128]{0:T(128)}, u32[]{:S(2)}) copy-start(f32[128]{0:T(128)} %param.11) | copy-start | bytes 1540
  6.5 89.3 %reduce-scatter.2.cloned.1.call-start = ((), (), s32[]{:S(2)}) async-start(), calls=%async_computation.4 | async-start | bytes 2621440 | tf_op jit(solution)/shard_map/reduce_scatter | solution.py:127
  40.8 2.7 collective-permute-start
  52.7 0.7 copy-start.4
  52.7 0.7 copy-start.5
  52.7 0.8 copy-start.6
  96.9 1.1 copy-start.1
  98.0 5.4 %copy-start.3 = (bf16[1,1601,512]{2,1,0:T(8,128)(2,1)S(1)}, bf16[1,1601,512]{2,1,0:T(8,128)(2,1)}, u32[]{:S(2)}) copy-start(bf16[1,1601,512]{2,1,0:T(8,128)(2,1)} %param.13) | copy-start | bytes 4918276
  99.6 29.4 %all-to-all-start.1 = ((bf16[4,64,2048]{2,1,0:T(8,128)(2,1)}), bf16[4,64,2048]{2,1,0:T(8,128)(2,1)S(1)}, u32[]{:S(2)}, u32[]{:S(2)}) async-start(bf16[4,64,2048]{2,1,0:T(8,128)(2,1)} %bitcast.8), calls=%async_computation.2 | async-start | bytes 2097152 | tf_op jit(solution)/shard_map/all_to_all | solution.py:163
  103.1 120.0 %all-gather.2.cloned.1.call-start = ((), (), s32[]{:S(2)}) async-start(), calls=%async_computation.5 | async-start | bytes 2621440 | tf_op jit(solution)/shard_map/all_gather | solution.py:177
  129.0 1.0 copy-start.2
  231.8 2.9 %collective-permute-start.1 = (bf16[256,2048]{1,0:T(8,128)(2,1)S(1)}, bf16[256,2048]{1,0:T(8,128)(2,1)}, u32[]{:S(2)}, u32[]{:S(2)}) collective-permute-start(bf16[256,2048]{1,0:T(8,128)(2,1)S(1)} %dynamic-slice_bitcast_fusion), channel_id=1, source_target_pairs={{0,1},{1,0},{2,3},{3,2},{4,5},{5,4},{6,7},{7,6},{8,9},{9,8},{10,11... | collective-permute-start | bytes 3145736 | tf_op jit(solution)/shard_map/ppermute | solution.py:24
  236.3 14.0 %collective-permute-start.2 = (bf16[128,2048]{1,0:T(8,128)(2,1)S(1)}, bf16[128,2048]{1,0:T(8,128)(2,1)S(1)}, u32[]{:S(2)}, u32[]{:S(2)}) collective-permute-start(bf16[128,2048]{1,0:T(8,128)(2,1)S(1)} %dynamic-slice_bitcast_fusion.3), channel_id=1, source_target_pairs={{0,2},{2,0},{1,3},{3,1},{4,6},{6,4},{5,7},{7,5},{8,10},{10,8},{9,1... | collective-permute-start | bytes 1572872 | tf_op jit(solution)/shard_map/ppermute | solution.py:24
  250.5 18.5 %collective-permute-start.3 = (bf16[128,2048]{1,0:T(8,128)(2,1)S(1)}, bf16[128,2048]{1,0:T(8,128)(2,1)S(1)}, u32[]{:S(2)}, u32[]{:S(2)}) collective-permute-start(bf16[128,2048]{1,0:T(8,128)(2,1)S(1)} %fusion.4), channel_id=1, source_target_pairs={{0,0},{1,8},{2,4},{3,12},{4,1},{5,9},{6,5},{7,13},{8,2},{9,10},{10... | collective-permute-start | bytes 1572872 | tf_op jit(solution)/shard_map/ppermute | solution.py:205
Sparse Core Ops, SparseCore 0:
  52.8 42.9 reduce-scatter.1
  178.1 44.9 all-gather.1

commit v6 on v5

--- a/solution.py
+++ b/solution.py
@@ -27,16 +27,14 @@
 
 
 def attend_kernel(q_ref, k_ref, v_ref, o_ref, *, per_kv, head_dim, token_count):
-    padded_tokens = k_ref.shape[0]
+    padded_tokens = k_ref.shape[1]
     split = (token_count // 128) * 128
     keys = k_ref[...]
     rows = q_ref.shape[0]
     score_scale = head_dim ** (-0.5)
     for g in range(per_kv):
         query = q_ref[:, g * head_dim:(g + 1) * head_dim]
-        scores = lax.dot_general(
-            query, keys, (((1,), (1,)), ((), ())), preferred_element_type=jnp.float32
-        ) * score_scale
+        scores = jnp.dot(query, keys, preferred_element_type=jnp.float32) * score_scale
         pieces = [scores[:, :split]] if split else []
         if split < padded_tokens:
             tail = scores[:, split:]
@@ -63,7 +61,7 @@
 
 def attend(rows_in, keys, values, kv_count, per_kv, head_dim, token_count):
     rows, width = rows_in.shape
-    padded_tokens = keys.shape[0]
+    padded_tokens = keys.shape[1]
     group_width = per_kv * head_dim
     kernel = functools.partial(
         attend_kernel, per_kv=per_kv, head_dim=head_dim, token_count=token_count
@@ -75,7 +73,7 @@
         grid=(kv_count,),
         in_specs=[
             pl.BlockSpec((rows, group_width), lambda k: (0, k)),
-            pl.BlockSpec((padded_tokens, head_dim), lambda k: (0, k)),
+            pl.BlockSpec((head_dim, padded_tokens), lambda k: (k, 0)),
             pl.BlockSpec((padded_tokens, head_dim), lambda k: (0, k)),
         ],
         out_specs=pl.BlockSpec((rows, group_width), lambda k: (0, k)),
@@ -164,7 +162,7 @@
     sources = arrived.shape[0]
     slot_count = arrived.shape[1]
     flat_rows = arrived.reshape(sources * slot_count, q_cols)
-    mixed_heads = attend(flat_rows, keys_here, values_here, kv_count, per_kv, head_dim, token_count)
+    mixed_heads = attend(flat_rows, keys_here.T, values_here, kv_count, per_kv, head_dim, token_count)
     replies = mixed_heads.reshape(sources, slot_count, q_cols)
     returned = lax.all_to_all(replies, "req", split_axis=0, concat_axis=0, tiled=True)
     attended = lax.dot_general(

time: 282 us -> 289 us (1.025)
  local copies, waits for them, and re-layouts: 9.99 us -> 15.2 us
where the time goes in v6:
time: 289 us; the launch traced here: 285 us
  waiting for transfers between devices  144 us (50%)
  blocking collectives  59.3 us (21%)
  matrix products  20.4 us (7%)
  Pallas kernels  18.1 us (6%)
  local copies, waits for them, and re-layouts  15.2 us (5%)
  between operations  13.7 us (5%)
  other arithmetic  7.28 us (3%)
  starting transfers between devices  7.1 us (2%)
    all_gather x1, waiting for transfers between devices, local(): lax.all_gather(attended, 'req', axis=0, tiled=True)  45.1 us
    reduce_scatter x1, waiting for transfers between devices, local(): lax.psum_scatter(jnp.dot(spread_cols, q_weight, preferred_element_type=jn...  41.8 us
    all_to_all x1, blocking collectives, local(): lax.all_to_all(my_part, 'req', split_axis=1, concat_axis=0, tiled=True)  30.6 us
    all_to_all x1, blocking collectives, local(): lax.all_to_all(replies, 'req', split_axis=0, concat_axis=0, tiled=True)  28.7 us
    all_to_all x1, waiting for transfers between devices, local(): lax.all_to_all(outgoing, 'req', split_axis=0, concat_axis=0, tiled=True)  21.7 us
    pallas_call x1, Pallas kernels, attend(): pl.pallas_call(kernel, grid=(kv_count,), in_specs=[pl.BlockSpec((rows, gr...  18.1 us
    ppermute x1, waiting for transfers between devices, local(): arrived_blocks.append(lax.ppermute(chunk, ('req', 'head', 'sub'), pairs))  16.6 us
    ppermute x2, waiting for transfers between devices, exchange_sum(): lax.ppermute(outgoing, axis, [(i, (i + shift) % count) for i in range(cou...  16.3 us
  transfers between devices with their start and end apart: 7, of which 7 were waited for; matrix products, arithmetic and copies ran while one was open for 2% of the time, Pallas kernels for 0%

profile of v6, /device:TPU:6, one launch (start us, length us, event | category | flops | bytes accessed | tf_op | source)
XLA Modules:
  0.0 285.1 jit_solution(13007660022522826043)
XLA Ops:
  6.5 4.2 %copy.19 = bf16[128,8192]{0,1:T(8,128)(2,1)} copy(bf16[128,8192]{1,0:T(8,128)(2,1)} %param.9) | data formatting | bytes 4194304 | tf_op args[0]
  10.7 1.3 constant_dynamic-slice_fusion.1
  12.0 1.3 copy.20
  13.3 30.6 %all_to_all.25 = bf16[128,4,1024]{2,0,1:T(8,128)(2,1)S(1)} all-to-all(bf16[128,4,1024]{2,0,1:T(8,128)(2,1)} %bitcast.50), channel_id=1, replica_groups=mesh['groups'=2,'req'=4,'head'=2,'sub'=2] {'req'}, dimensions={1} | all-to-all | bytes 2097152 | tf_op jit(solution)/shard_map/all_to_all | solution.py:112
  44.3 2.4 collective-permute-done
  46.7 1.3 constant_dynamic-update-slice_fusion
  48.1 9.2 %convolution_convert_fusion.1 = bf16[512,2048]{1,0:T(8,128)(2,1)} fusion(bf16[512,2048]{1,0:T(8,128)(2,1)S(1)} %constant_dynamic-update-slice_fusion, bf16[2048,2048]{1,0:T(8,128)(2,1)} %param.10), kind=kOutput, calls=%fused_computation.1 | convolution fusion | flops 4296015872 | bytes 12582912 | tf_op jit(solution)/shard_map/dot_general | solution.py:126
  58.6 41.8 %reduce-scatter.2.cloned.1.call-done = bf16[128,2048]{1,0:T(8,128)(2,1)} async-done(((bf16[512,2048]{1,0:T(8,128)(2,1)}), bf16[128,2048]{1,0:T(8,128)(2,1)}) %reduce-scatter.2.cloned.1.call-update) | async-done | bytes 524304 | tf_op jit(solution)/shard_map/reduce_scatter | solution.py:125
  102.6 1.6 convolution_convert_fusion.2
  104.2 4.2 %all-to-all-start.1 = ((bf16[4,64,2048]{2,1,0:T(8,128)(2,1)}), bf16[4,64,2048]{2,1,0:T(8,128)(2,1)}, u32[]{:S(2)}, u32[]{:S(2)}) async-start(bf16[4,64,2048]{2,1,0:T(8,128)(2,1)} %bitcast.8), calls=%async_computation.2 | async-start | bytes 2097152 | tf_op jit(solution)/shard_map/all_to_all | solution.py:161
  109.5 1.2 dynamic-slice_bitcast_fusion.1
  112.6 21.7 %all-to-all-done.1 = bf16[4,64,2048]{2,1,0:T(8,128)(2,1)} async-done(((bf16[4,64,2048]{2,1,0:T(8,128)(2,1)}), bf16[4,64,2048]{2,1,0:T(8,128)(2,1)}, u32[]{:S(2)}, u32[]{:S(2)}) %all-to-all-start.1) | async-done | bytes 1048608 | tf_op jit(solution)/shard_map/all_to_all | solution.py:161
  134.4 18.1 %shard_map.91 = bf16[256,2048]{1,0:T(8,128)(2,1)} custom-call(bf16[256,2048]{1,0:T(8,128)(2,1)} %bitcast.9.q_ref, bf16[256,1664]{1,0:T(8,128)(2,1)} %pad_bitcast_fusion.k_ref, bf16[1664,256]{1,0:T(8,128)(2,1)} %pad.8.v_ref), custom_call_target="tpu_custom_call" | custom-call | flops 3489660928 | bytes 3801088 | tf_op jit(solution)/shard_map/pallas_call | solution.py:71
  152.5 28.7 %all_to_all.26 = bf16[4,64,2048]{2,1,0:T(8,128)(2,1)S(1)} all-to-all(bf16[4,64,2048]{2,1,0:T(8,128)(2,1)} %bitcast.54), channel_id=1, replica_groups=mesh['groups'=2,'req'=4,'head'=2,'sub'=2] {'req'}, dimensions={0} | all-to-all | bytes 2097152 | tf_op jit(solution)/shard_map/all_to_all | solution.py:167
  182.4 45.1 %all-gather.2.cloned.1.call-done = bf16[512,2048]{1,0:T(8,128)(2,1)} async-done(((bf16[128,2048]{1,0:T(8,128)(2,1)}), bf16[512,2048]{1,0:T(8,128)(2,1)}) %all-gather.2.cloned.1.call-update) | async-done | bytes 2097168 | tf_op jit(solution)/shard_map/all_gather | solution.py:175
  227.5 8.5 %convolution_convert_fusion = bf16[512,2048]{1,0:T(8,128)(2,1)S(1)} fusion(bf16[512,2048]{1,0:T(8,128)(2,1)} %all-gather.2.cloned.1.call-done, bf16[2048,2048]{1,0:T(8,128)(2,1)} %param.14), kind=kOutput, calls=%fused_computation | convolution fusion | flops 4296015872 | bytes 12582912 | tf_op jit(solution)/shard_map/dot_general | solution.py:174
  236.0 1.3 copy-done.2
  237.6 2.8 collective-permute-done.1
  240.3 1.9 fusion
  243.0 13.5 %collective-permute-done.2 = bf16[128,2048]{1,0:T(8,128)(2,1)} collective-permute-done((bf16[128,2048]{1,0:T(8,128)(2,1)S(1)}, bf16[128,2048]{1,0:T(8,128)(2,1)}, u32[]{:S(2)}, u32[]{:S(2)}) %collective-permute-start.2) | collective-permute-done | bytes 524320 | tf_op jit(solution)/shard_map/ppermute | solution.py:24
  256.5 1.2 fusion.4
  257.7 1.9 collective-permute-start.3
  259.6 16.6 %collective-permute-done.3 = bf16[128,2048]{1,0:T(8,128)(2,1)S(1)} collective-permute-done((bf16[128,2048]{1,0:T(8,128)(2,1)S(1)}, bf16[128,2048]{1,0:T(8,128)(2,1)S(1)}, u32[]{:S(2)}, u32[]{:S(2)}) %collective-permute-start.3) | collective-permute-done | bytes 524320 | tf_op jit(solution)/shard_map/ppermute | solution.py:203
  276.2 2.0 add_convert_fusion
  (43 shorter events, 8.8 us)
Async XLA Ops:
  6.5 102.2 %copy-start = (bf16[1,1601,512]{2,1,0:T(8,128)(2,1)S(1)}, bf16[1,1601,512]{2,1,0:T(8,128)(2,1)}, u32[]{:S(2)}) copy-start(bf16[1,1601,512]{2,1,0:T(8,128)(2,1)} %param.12) | copy-start | bytes 4918276
  6.5 93.8 %reduce-scatter.2.cloned.1.call-start = ((), (), s32[]{:S(2)}) async-start(), calls=%async_computation.4 | async-start | bytes 2621440 | tf_op jit(solution)/shard_map/reduce_scatter | solution.py:125
  43.9 2.8 collective-permute-start
  57.2 0.7 copy-start.4
  57.2 0.7 copy-start.5
  57.2 0.8 copy-start.6
  57.2 1.3 copy-start.3
  101.5 1.1 copy-start.1
  104.2 30.1 %all-to-all-start.1 = ((bf16[4,64,2048]{2,1,0:T(8,128)(2,1)}), bf16[4,64,2048]{2,1,0:T(8,128)(2,1)}, u32[]{:S(2)}, u32[]{:S(2)}) async-start(bf16[4,64,2048]{2,1,0:T(8,128)(2,1)} %bitcast.8), calls=%async_computation.2 | async-start | bytes 2097152 | tf_op jit(solution)/shard_map/all_to_all | solution.py:161
  108.5 119.1 %all-gather.2.cloned.1.call-start = ((), (), s32[]{:S(2)}) async-start(), calls=%async_computation.5 | async-start | bytes 2621440 | tf_op jit(solution)/shard_map/all_gather | solution.py:175
  236.0 1.3 copy-start.2
  237.5 2.9 %collective-permute-start.1 = (bf16[256,2048]{1,0:T(8,128)(2,1)S(1)}, bf16[256,2048]{1,0:T(8,128)(2,1)}, u32[]{:S(2)}, u32[]{:S(2)}) collective-permute-start(bf16[256,2048]{1,0:T(8,128)(2,1)S(1)} %dynamic-slice_bitcast_fusion), channel_id=1, source_target_pairs={{0,1},{1,0},{2,3},{3,2},{4,5},{5,4},{6,7},{7,6},{8,9},{9,8},{10,11... | collective-permute-start | bytes 3145736 | tf_op jit(solution)/shard_map/ppermute | solution.py:24
  242.3 14.1 %collective-permute-start.2 = (bf16[128,2048]{1,0:T(8,128)(2,1)S(1)}, bf16[128,2048]{1,0:T(8,128)(2,1)}, u32[]{:S(2)}, u32[]{:S(2)}) collective-permute-start(bf16[128,2048]{1,0:T(8,128)(2,1)S(1)} %dynamic-slice_bitcast_fusion.2), channel_id=1, source_target_pairs={{0,2},{2,0},{1,3},{3,1},{4,6},{6,4},{5,7},{7,5},{8,10},{10,8},{9,1... | collective-permute-start | bytes 1572872 | tf_op jit(solution)/shard_map/ppermute | solution.py:24
  257.7 18.5 %collective-permute-start.3 = (bf16[128,2048]{1,0:T(8,128)(2,1)S(1)}, bf16[128,2048]{1,0:T(8,128)(2,1)S(1)}, u32[]{:S(2)}, u32[]{:S(2)}) collective-permute-start(bf16[128,2048]{1,0:T(8,128)(2,1)S(1)} %fusion.4), channel_id=1, source_target_pairs={{0,0},{1,8},{2,4},{3,12},{4,1},{5,9},{6,5},{7,13},{8,2},{9,10},{10... | collective-permute-start | bytes 1572872 | tf_op jit(solution)/shard_map/ppermute | solution.py:203
Sparse Core Ops, SparseCore 0:
  57.4 42.9 reduce-scatter.1
  182.5 44.9 all-gather.1

commit v7 on v5

--- a/solution.py
+++ b/solution.py
@@ -15,6 +15,15 @@
     per_head = queries.astype(jnp.float32).reshape(row_count, -1, head_dim)
     inv_rms = lax.rsqrt(jnp.mean(per_head * per_head, axis=2, keepdims=True) + 1e-05)
     return (per_head * inv_rms * q_gain).reshape(row_count, -1).astype(jnp.bfloat16)
+
+
+def shift_exchange(blocks, axis, count):
+    arrived = [blocks[0]]
+    for shift in range(1, count):
+        arrived.append(
+            lax.ppermute(blocks[shift], axis, [(i, (i + shift) % count) for i in range(count)])
+        )
+    return jnp.stack(arrived)
 
 
 def exchange_sum(parts, axis, count, index):
@@ -110,8 +119,13 @@
     block_width = hidden_in.shape[1] // req_count
     part_width = block_width // sub_count
     by_block = hidden_in.reshape(local_rows, req_count, sub_count, part_width)
+    req_index = lax.axis_index("req")
     my_part = lax.dynamic_index_in_dim(by_block, sub_index, axis=2, keepdims=False)
-    spread_part = lax.all_to_all(my_part, "req", split_axis=1, concat_axis=0, tiled=True)
+    shift_order = (req_index + jnp.arange(req_count)) % req_count
+    outgoing_parts = jnp.take(jnp.swapaxes(my_part, 0, 1), shift_order, axis=0)
+    arrived_parts = shift_exchange(outgoing_parts, "req", req_count)
+    source_order = (req_index - jnp.arange(req_count)) % req_count
+    spread_part = jnp.take(arrived_parts, source_order, axis=0)
     spread_part = spread_part.reshape(req_count * local_rows, part_width)
     spread_cols = jnp.zeros((req_count * local_rows, block_width), spread_part.dtype)
     spread_cols = lax.dynamic_update_slice_in_dim(
@@ -140,7 +154,9 @@
     dest_ids = lax.broadcasted_iota(jnp.int32, (local_rows, req_count), 1)
     to_dest = ((home_rows[:, None] == dest_ids) & wanted[:, None]).astype(jnp.int32)
     earlier = jnp.cumsum(to_dest, axis=0) - to_dest
-    position = home_rows * capacity + jnp.sum(earlier * to_dest, axis=1)
+    position = ((home_rows - req_index) % req_count) * capacity + jnp.sum(
+        earlier * to_dest, axis=1
+    )
     slot_ids = lax.broadcasted_iota(jnp.int32, (slot_total, local_rows), 0)
     dispatch = ((slot_ids == position[None, :]) & wanted[None, :]).astype(jnp.bfloat16)
     outgoing = jnp.dot(dispatch, normalized, preferred_element_type=jnp.float32).astype(
@@ -160,13 +176,16 @@
         lax.dynamic_slice_in_dim(value_cache[0], kv_first * head_dim, kv_count * head_dim, 1),
         ((0, padded_tokens - token_count), (0, 0)),
     )
-    arrived = lax.all_to_all(outgoing, "req", split_axis=0, concat_axis=0, tiled=True)
+    arrived = shift_exchange(outgoing, "req", req_count)
     sources = arrived.shape[0]
     slot_count = arrived.shape[1]
     flat_rows = arrived.reshape(sources * slot_count, q_cols)
     mixed_heads = attend(flat_rows, keys_here, values_here, kv_count, per_kv, head_dim, token_count)
     replies = mixed_heads.reshape(sources, slot_count, q_cols)
-    returned = lax.all_to_all(replies, "req", split_axis=0, concat_axis=0, tiled=True)
+    returned = shift_exchange(
+        jnp.concatenate([replies[:1], replies[1:][::-1]]), "req", req_count
+    )
+    returned = jnp.concatenate([returned[:1], returned[1:][::-1]])
     attended = lax.dot_general(
         dispatch,
         returned.reshape(slot_total, q_cols),
@@ -180,7 +199,6 @@
     ).astype(jnp.bfloat16)
     hs_count = lax.axis_size("head") * sub_count
     hs_index = lax.axis_index("head") * sub_count + sub_index
-    req_index = lax.axis_index("req")
     head_count = lax.axis_size("head")
     by_group = partial_cols.reshape(sub_count, -1, partial_cols.shape[1])
     owner_sums = exchange_sum(by_group, "sub", sub_count, sub_index)

time: 282 us -> 274 us (0.972)
  blocking collectives: 59.1 us -> 0 us
  waiting for transfers between devices: 144 us -> 184 us
  starting transfers between devices: 6.38 us -> 15.9 us
    ppermute x0 -> x9, waiting for transfers between devices: none -> 61.8 us  [shift_exchange(): lax.ppermute(blocks[shift], axis, [(i, (i + shift) % count) for i in rang...]
    all_to_all x2 -> x0, blocking collectives: 59.1 us -> none  [the longest x1 30.4 us: local(): lax.all_to_all(my_part, 'req', split_axis=1, concat_axis=0, tiled=True)]
    all_to_all x1 -> x0, waiting for transfers between devices: 22.4 us -> none  [local(): lax.all_to_all(outgoing, 'req', split_axis=0, concat_axis=0, tiled=True)]
    ppermute x0 -> x9, starting transfers between devices: none -> 13.1 us  [shift_exchange(): lax.ppermute(blocks[shift], axis, [(i, (i + shift) % count) for i in rang...]
    all_to_all x1 -> x0, starting transfers between devices: 3.51 us -> none  [local(): lax.all_to_all(outgoing, 'req', split_axis=0, concat_axis=0, tiled=True)]
  transfers between devices with their start and end apart: 7 -> 15, of which waited for: 7 -> 12; matrix products, arithmetic and copies ran while one was open for 2% -> 1% of each run, Pallas kernels for 0% -> 0%
where the time goes in v7:
time: 274 us; the launch traced here: 270 us
  waiting for transfers between devices  184 us (67%)
  matrix products  19.3 us (7%)
  Pallas kernels  18.2 us (7%)
  starting transfers between devices  15.9 us (6%)
  between operations  13.8 us (5%)
  local copies, waits for them, and re-layouts  10.5 us (4%)
  other arithmetic  7.69 us (3%)
    ppermute x9, waiting for transfers between devices, shift_exchange(): lax.ppermute(blocks[shift], axis, [(i, (i + shift) % count) for i in rang...  61.8 us
    all_gather x1, waiting for transfers between devices, local(): lax.all_gather(attended, 'req', axis=0, tiled=True)  44.2 us
    reduce_scatter x1, waiting for transfers between devices, local(): lax.psum_scatter(jnp.dot(spread_cols, q_weight, preferred_element_type=jn...  43.1 us
    pallas_call x1, Pallas kernels, attend(): pl.pallas_call(kernel, grid=(kv_count,), in_specs=[pl.BlockSpec((rows, gr...  18.2 us
    ppermute x1, waiting for transfers between devices, local(): arrived_blocks.append(lax.ppermute(chunk, ('req', 'head', 'sub'), pairs))  16.6 us
    ppermute x2, waiting for transfers between devices, exchange_sum(): lax.ppermute(outgoing, axis, [(i, (i + shift) % count) for i in range(cou...  16.1 us
    ppermute x9, starting transfers between devices, shift_exchange(): lax.ppermute(blocks[shift], axis, [(i, (i + shift) % count) for i in rang...  13.1 us
    dot_general x1, matrix products, local(): jnp.dot(spread_cols, q_weight, preferred_element_type=jnp.float32)  9.06 us
  transfers between devices with their start and end apart: 15, of which 12 were waited for; matrix products, arithmetic and copies ran while one was open for 1% of the time, Pallas kernels for 0%

profile of v7, /device:TPU:6, one launch (start us, length us, event | category | flops | bytes accessed | tf_op | source)
XLA Modules:
  0.0 269.5 jit_solution(2051176467986029343)
XLA Ops:
  6.6 3.2 %copy.16 = bf16[128,8192]{0,1:T(8,128)(2,1)S(1)} copy(bf16[128,8192]{1,0:T(8,128)(2,1)} %param.11) | data formatting | bytes 4194304 | tf_op args[0]
  11.3 3.7 %collective-permute-start.2 = (bf16[128,1024]{1,0:T(8,128)(2,1)S(1)}, bf16[128,1024]{1,0:T(8,128)(2,1)S(1)}, u32[]{:S(2)}, u32[]{:S(2)}) collective-permute-start(bf16[128,1024]{1,0:T(8,128)(2,1)S(1)} %get-tuple-element.15), channel_id=1, source_target_pairs={{0,12},{4,0},{8,4},{12,8},{1,13},{5,1},{9,5},{13,9},{2,14},{6,2},{... | collective-permute-start | bytes 786440 | tf_op jit(solution)/shard_map/ppermute | solution.py:24
  16.0 5.7 %collective-permute-done.2 = bf16[128,1024]{1,0:T(8,128)(2,1)S(1)} collective-permute-done((bf16[128,1024]{1,0:T(8,128)(2,1)S(1)}, bf16[128,1024]{1,0:T(8,128)(2,1)S(1)}, u32[]{:S(2)}, u32[]{:S(2)}) %collective-permute-start.2) | collective-permute-done | bytes 262176 | tf_op jit(solution)/shard_map/ppermute | solution.py:24
  21.7 15.6 %collective-permute-done.1 = bf16[128,1024]{1,0:T(8,128)(2,1)S(1)} collective-permute-done((bf16[128,1024]{1,0:T(8,128)(2,1)S(1)}, bf16[128,1024]{1,0:T(8,128)(2,1)S(1)}, u32[]{:S(2)}, u32[]{:S(2)}) %collective-permute-start.1) | collective-permute-done | bytes 262176 | tf_op jit(solution)/shard_map/ppermute | solution.py:24
  38.7 2.2 collective-permute-done.3
  41.0 9.1 %convolution_convert_fusion.1 = bf16[512,2048]{1,0:T(8,128)(2,1)} fusion(bf16[512,2048]{1,0:T(8,128)(2,1)S(1)} %constant_dynamic-update-slice_fusion, bf16[2048,2048]{1,0:T(8,128)(2,1)} %param.12), kind=kOutput, calls=%fused_computation.3 | convolution fusion | flops 4296015872 | bytes 12582912 | tf_op jit(solution)/shard_map/dot_general | solution.py:142
  51.5 43.1 %reduce-scatter.2.cloned.1.call-done = bf16[128,2048]{1,0:T(8,128)(2,1)} async-done(((bf16[512,2048]{1,0:T(8,128)(2,1)}), bf16[128,2048]{1,0:T(8,128)(2,1)}) %reduce-scatter.2.cloned.1.call-update) | async-done | bytes 524304 | tf_op jit(solution)/shard_map/reduce_scatter | solution.py:141
  97.5 1.7 collective-permute-start.6
  99.4 1.9 collective-permute-start.4
  103.4 2.7 collective-permute-done.6
  106.1 16.5 %collective-permute-done.5 = bf16[64,2048]{1,0:T(8,128)(2,1)S(1)} collective-permute-done((bf16[64,2048]{1,0:T(8,128)(2,1)S(1)}, bf16[64,2048]{1,0:T(8,128)(2,1)S(1)}, u32[]{:S(2)}, u32[]{:S(2)}) %collective-permute-start.5) | collective-permute-done | bytes 262176 | tf_op jit(solution)/shard_map/ppermute | solution.py:24
  123.7 18.2 %shard_map.91 = bf16[256,2048]{1,0:T(8,128)(2,1)} custom-call(bf16[256,2048]{1,0:T(8,128)(2,1)} %bitcast.67, bf16[1664,256]{1,0:T(8,128)(2,1)} %pad.7.k_ref, bf16[1664,256]{1,0:T(8,128)(2,1)} %pad.8.v_ref), custom_call_target="tpu_custom_call" | custom-call | flops 3489660928 | bytes 3801088 | tf_op jit(solution)/shard_map/pallas_call | solution.py:82
  143.2 2.6 collective-permute-start.8
  145.8 1.9 collective-permute-start.7
  147.8 3.0 %collective-permute-done.9 = bf16[64,2048]{1,0:T(8,128)(2,1)S(1)} collective-permute-done((bf16[64,2048]{1,0:T(8,128)(2,1)S(1)}, bf16[64,2048]{1,0:T(8,128)(2,1)S(1)}, u32[]{:S(2)}, u32[]{:S(2)}) %collective-permute-start.9) | collective-permute-done | bytes 262176 | tf_op jit(solution)/shard_map/ppermute | solution.py:24
  150.8 18.4 %collective-permute-done.8 = bf16[64,2048]{1,0:T(8,128)(2,1)S(1)} collective-permute-done((bf16[64,2048]{1,0:T(8,128)(2,1)S(1)}, bf16[64,2048]{1,0:T(8,128)(2,1)S(1)}, u32[]{:S(2)}, u32[]{:S(2)}) %collective-permute-start.8) | collective-permute-done | bytes 262176 | tf_op jit(solution)/shard_map/ppermute | solution.py:24
  170.6 44.2 %all-gather.2.cloned.1.call-done = bf16[512,2048]{1,0:T(8,128)(2,1)} async-done(((bf16[128,2048]{1,0:T(8,128)(2,1)}), bf16[512,2048]{1,0:T(8,128)(2,1)}) %all-gather.2.cloned.1.call-update) | async-done | bytes 2097168 | tf_op jit(solution)/shard_map/all_gather | solution.py:196
  214.8 8.5 %convolution_convert_fusion = bf16[512,2048]{1,0:T(8,128)(2,1)S(1)} fusion(bf16[512,2048]{1,0:T(8,128)(2,1)} %all-gather.2.cloned.1.call-done, bf16[2048,2048]{1,0:T(8,128)(2,1)} %param.16), kind=kOutput, calls=%fused_computation.2 | convolution fusion | flops 4296015872 | bytes 12582912 | tf_op jit(solution)/shard_map/dot_general | solution.py:195
  223.5 2.8 %collective-permute-done.10 = bf16[256,2048]{1,0:T(8,128)(2,1)} collective-permute-done((bf16[256,2048]{1,0:T(8,128)(2,1)S(1)}, bf16[256,2048]{1,0:T(8,128)(2,1)}, u32[]{:S(2)}, u32[]{:S(2)}) %collective-permute-start.10) | collective-permute-done | bytes 1048608 | tf_op jit(solution)/shard_map/ppermute | solution.py:33
  226.3 1.6 fusion
  228.6 13.4 %collective-permute-done.11 = bf16[128,2048]{1,0:T(8,128)(2,1)S(1)} collective-permute-done((bf16[128,2048]{1,0:T(8,128)(2,1)S(1)}, bf16[128,2048]{1,0:T(8,128)(2,1)S(1)}, u32[]{:S(2)}, u32[]{:S(2)}) %collective-permute-start.11) | collective-permute-done | bytes 524320 | tf_op jit(solution)/shard_map/ppermute | solution.py:33
  242.1 1.9 collective-permute-start.12
  244.1 16.6 %collective-permute-done.12 = bf16[128,2048]{1,0:T(8,128)(2,1)S(1)} collective-permute-done((bf16[128,2048]{1,0:T(8,128)(2,1)S(1)}, bf16[128,2048]{1,0:T(8,128)(2,1)S(1)}, u32[]{:S(2)}, u32[]{:S(2)}) %collective-permute-start.12) | collective-permute-done | bytes 524320 | tf_op jit(solution)/shard_map/ppermute | solution.py:223
  260.7 2.0 add_convert_fusion
  (72 shorter events, 15.2 us)
Async XLA Ops:
  6.5 44.9 %copy-start = (f32[128]{0:T(128)S(1)}, f32[128]{0:T(128)}, u32[]{:S(2)}) copy-start(f32[128]{0:T(128)} %param.13) | copy-start | bytes 1540
  6.5 88.0 %reduce-scatter.2.cloned.1.call-start = ((), (), s32[]{:S(2)}) async-start(), calls=%async_computation.1 | async-start | bytes 2621440 | tf_op jit(solution)/shard_map/reduce_scatter | solution.py:141
  11.3 10.4 %collective-permute-start.2 = (bf16[128,1024]{1,0:T(8,128)(2,1)S(1)}, bf16[128,1024]{1,0:T(8,128)(2,1)S(1)}, u32[]{:S(2)}, u32[]{:S(2)}) collective-permute-start(bf16[128,1024]{1,0:T(8,128)(2,1)S(1)} %get-tuple-element.15), channel_id=1, source_target_pairs={{0,12},{4,0},{8,4},{12,8},{1,13},{5,1},{9,5},{13,9},{2,14},{6,2},{... | collective-permute-start | bytes 786440 | tf_op jit(solution)/shard_map/ppermute | solution.py:24
  15.0 22.3 %collective-permute-start.1 = (bf16[128,1024]{1,0:T(8,128)(2,1)S(1)}, bf16[128,1024]{1,0:T(8,128)(2,1)S(1)}, u32[]{:S(2)}, u32[]{:S(2)}) collective-permute-start(bf16[128,1024]{1,0:T(8,128)(2,1)S(1)} %get-tuple-element.16), channel_id=1, source_target_pairs={{0,8},{4,12},{8,0},{12,4},{1,9},{5,13},{9,1},{13,5},{2,10},{6,14},... | collective-permute-start | bytes 786440 | tf_op jit(solution)/shard_map/ppermute | solution.py:24
  15.0 22.3 %collective-permute-start = (bf16[128,1024]{1,0:T(8,128)(2,1)S(1)}, bf16[128,1024]{1,0:T(8,128)(2,1)S(1)}, u32[]{:S(2)}, u32[]{:S(2)}) collective-permute-start(bf16[128,1024]{1,0:T(8,128)(2,1)S(1)} %get-tuple-element.17), channel_id=1, source_target_pairs={{0,4},{4,8},{8,12},{12,0},{1,5},{5,9},{9,13},{13,1},{2,6},{6,10},{... | collective-permute-start | bytes 786440 | tf_op jit(solution)/shard_map/ppermute | solution.py:24
  38.2 2.7 %collective-permute-start.3 = (bf16[512,1024]{1,0:T(8,128)(2,1)S(1)}, bf16[512,1024]{1,0:T(8,128)(2,1)S(1)}, u32[]{:S(2)}, u32[]{:S(2)}) collective-permute-start(bf16[512,1024]{1,0:T(8,128)(2,1)S(1)} %bitcast.57), channel_id=1, source_target_pairs={{0,1},{1,0},{2,3},{3,2},{4,5},{5,4},{6,7},{7,6},{8,9},{9,8},{10,11... | collective-permute-start | bytes 3145736 | tf_op jit(solution)/shard_map/ppermute | solution.py:135
  50.1 0.7 copy-start.4
  50.1 0.7 copy-start.5
  50.1 0.8 copy-start.6
  50.1 164.6 %all-gather.2.cloned.1.call-start = ((), (), s32[]{:S(2)}) async-start(), calls=%async_computation.2 | async-start | bytes 2621440 | tf_op jit(solution)/shard_map/all_gather | solution.py:196
  95.7 1.1 copy-start.1
  96.8 4.6 %copy-start.2 = (bf16[1,1601,512]{2,1,0:T(8,128)(2,1)S(1)}, bf16[1,1601,512]{2,1,0:T(8,128)(2,1)}, u32[]{:S(2)}) copy-start(bf16[1,1601,512]{2,1,0:T(8,128)(2,1)} %param.15) | copy-start | bytes 4918276
  96.8 4.5 %copy-start.3 = (bf16[1,1601,512]{2,1,0:T(8,128)(2,1)S(1)}, bf16[1,1601,512]{2,1,0:T(8,128)(2,1)}, u32[]{:S(2)}) copy-start(bf16[1,1601,512]{2,1,0:T(8,128)(2,1)} %param.14) | copy-start | bytes 4918276
  97.5 8.5 %collective-permute-start.6 = (bf16[64,2048]{1,0:T(8,128)(2,1)S(1)}, bf16[64,2048]{1,0:T(8,128)(2,1)S(1)}, u32[]{:S(2)}, u32[]{:S(2)}) collective-permute-start(bf16[64,2048]{1,0:T(8,128)(2,1)S(1)} %get-tuple-element.11), channel_id=1, source_target_pairs={{0,12},{4,0},{8,4},{12,8},{1,13},{5,1},{9,5},{13,9},{2,14},{6,2},{... | collective-permute-start | bytes 786440 | tf_op jit(solution)/shard_map/ppermute | solution.py:24
  99.3 23.3 %collective-permute-start.5 = (bf16[64,2048]{1,0:T(8,128)(2,1)S(1)}, bf16[64,2048]{1,0:T(8,128)(2,1)S(1)}, u32[]{:S(2)}, u32[]{:S(2)}) collective-permute-start(bf16[64,2048]{1,0:T(8,128)(2,1)S(1)} %get-tuple-element.12), channel_id=1, source_target_pairs={{0,8},{4,12},{8,0},{12,4},{1,9},{5,13},{9,1},{13,5},{2,10},{6,14},... | collective-permute-start | bytes 786440 | tf_op jit(solution)/shard_map/ppermute | solution.py:24
  99.4 23.2 %collective-permute-start.4 = (bf16[64,2048]{1,0:T(8,128)(2,1)S(1)}, bf16[64,2048]{1,0:T(8,128)(2,1)S(1)}, u32[]{:S(2)}, u32[]{:S(2)}) collective-permute-start(bf16[64,2048]{1,0:T(8,128)(2,1)S(1)} %get-tuple-element.13), channel_id=1, source_target_pairs={{0,4},{4,8},{8,12},{12,0},{1,5},{5,9},{9,13},{13,1},{2,6},{6,10},{... | collective-permute-start | bytes 786440 | tf_op jit(solution)/shard_map/ppermute | solution.py:24
  143.1 7.6 %collective-permute-start.9 = (bf16[64,2048]{1,0:T(8,128)(2,1)S(1)}, bf16[64,2048]{1,0:T(8,128)(2,1)S(1)}, u32[]{:S(2)}, u32[]{:S(2)}) collective-permute-start(bf16[64,2048]{1,0:T(8,128)(2,1)S(1)} %get-tuple-element.7), channel_id=1, source_target_pairs={{0,12},{4,0},{8,4},{12,8},{1,13},{5,1},{9,5},{13,9},{2,14},{6,2},{... | collective-permute-start | bytes 786440 | tf_op jit(solution)/shard_map/ppermute | solution.py:24
  143.2 25.9 %collective-permute-start.8 = (bf16[64,2048]{1,0:T(8,128)(2,1)S(1)}, bf16[64,2048]{1,0:T(8,128)(2,1)S(1)}, u32[]{:S(2)}, u32[]{:S(2)}) collective-permute-start(bf16[64,2048]{1,0:T(8,128)(2,1)S(1)} %get-tuple-element.8), channel_id=1, source_target_pairs={{0,8},{4,12},{8,0},{12,4},{1,9},{5,13},{9,1},{13,5},{2,10},{6,14},... | collective-permute-start | bytes 786440 | tf_op jit(solution)/shard_map/ppermute | solution.py:24
  145.8 23.3 %collective-permute-start.7 = (bf16[64,2048]{1,0:T(8,128)(2,1)S(1)}, bf16[64,2048]{1,0:T(8,128)(2,1)S(1)}, u32[]{:S(2)}, u32[]{:S(2)}) collective-permute-start(bf16[64,2048]{1,0:T(8,128)(2,1)S(1)} %get-tuple-element.9), channel_id=1, source_target_pairs={{0,4},{4,8},{8,12},{12,0},{1,5},{5,9},{9,13},{13,1},{2,6},{6,10},{... | collective-permute-start | bytes 786440 | tf_op jit(solution)/shard_map/ppermute | solution.py:24
  223.4 2.9 %collective-permute-start.10 = (bf16[256,2048]{1,0:T(8,128)(2,1)S(1)}, bf16[256,2048]{1,0:T(8,128)(2,1)}, u32[]{:S(2)}, u32[]{:S(2)}) collective-permute-start(bf16[256,2048]{1,0:T(8,128)(2,1)S(1)} %dynamic-slice_bitcast_fusion), channel_id=1, source_target_pairs={{0,1},{1,0},{2,3},{3,2},{4,5},{5,4},{6,7},{7,6},{8,9},{9,8},{10,11... | collective-permute-start | bytes 3145736 | tf_op jit(solution)/shard_map/ppermute | solution.py:33
  228.0 14.0 %collective-permute-start.11 = (bf16[128,2048]{1,0:T(8,128)(2,1)S(1)}, bf16[128,2048]{1,0:T(8,128)(2,1)S(1)}, u32[]{:S(2)}, u32[]{:S(2)}) collective-permute-start(bf16[128,2048]{1,0:T(8,128)(2,1)S(1)} %dynamic-slice_bitcast_fusion.3), channel_id=1, source_target_pairs={{0,2},{2,0},{1,3},{3,1},{4,6},{6,4},{5,7},{7,5},{8,10},{10,8},{9,1... | collective-permute-start | bytes 1572872 | tf_op jit(solution)/shard_map/ppermute | solution.py:33
  242.1 18.5 %collective-permute-start.12 = (bf16[128,2048]{1,0:T(8,128)(2,1)S(1)}, bf16[128,2048]{1,0:T(8,128)(2,1)S(1)}, u32[]{:S(2)}, u32[]{:S(2)}) collective-permute-start(bf16[128,2048]{1,0:T(8,128)(2,1)S(1)} %fusion.4), channel_id=1, source_target_pairs={{0,0},{1,8},{2,4},{3,12},{4,1},{5,9},{6,5},{7,13},{8,2},{9,10},{10... | collective-permute-start | bytes 1572872 | tf_op jit(solution)/shard_map/ppermute | solution.py:223
Sparse Core Ops, SparseCore 0:
  50.3 44.2 reduce-scatter.1
  170.7 44.0 all-gather.1

commit v8 on v7

--- a/solution.py
+++ b/solution.py
@@ -24,6 +24,44 @@
             lax.ppermute(blocks[shift], axis, [(i, (i + shift) % count) for i in range(count)])
         )
     return jnp.stack(arrived)
+
+
+def line_reduce_scatter(chunk_of, axis, count, index):
+    right = None
+    left = None
+    for step in range(1, count):
+        dest_r = jnp.minimum(count - step + index, count - 1)
+        send_r = chunk_of(dest_r) if right is None else chunk_of(dest_r) + right
+        right = lax.ppermute(
+            send_r.astype(jnp.bfloat16), axis, [(i, i + 1) for i in range(step)]
+        ).astype(jnp.float32)
+        dest_l = jnp.maximum(index - (count - step), 0)
+        send_l = chunk_of(dest_l) if left is None else chunk_of(dest_l) + left
+        left = lax.ppermute(
+            send_l.astype(jnp.bfloat16), axis, [(i, i - 1) for i in range(count - step, count)]
+        ).astype(jnp.float32)
+    total = chunk_of(index)
+    if right is not None:
+        total = total + right + left
+    return total
+
+
+def line_gather_apply(block, apply, axis, count, index):
+    own = apply(block)
+    from_left = [own]
+    from_right = [own]
+    carry_r = block
+    carry_l = block
+    for step in range(1, count):
+        carry_r = lax.ppermute(carry_r, axis, [(i, i + 1) for i in range(step - 1, count - 1)])
+        carry_l = lax.ppermute(carry_l, axis, [(i, i - 1) for i in range(1, count - step + 1)])
+        from_left.append(apply(carry_r))
+        from_right.append(apply(carry_l))
+    origins = jnp.arange(count)
+    lower = jnp.take(jnp.stack(from_left), jnp.clip(index - origins, 0, count - 1), axis=0)
+    upper = jnp.take(jnp.stack(from_right), jnp.clip(origins - index, 0, count - 1), axis=0)
+    pick = (origins <= index).reshape((count,) + (1,) * own.ndim)
+    return jnp.where(pick, lower, upper)
 
 
 def exchange_sum(parts, axis, count, index):
@@ -138,13 +176,13 @@
         spread_cols = lax.dynamic_update_slice_in_dim(
             spread_cols, other_part, ((sub_index - shift) % sub_count) * part_width, 1
         )
-    query_sum = lax.psum_scatter(
-        jnp.dot(spread_cols, q_weight, preferred_element_type=jnp.float32).astype(jnp.bfloat16),
-        "req",
-        scatter_dimension=0,
-        tiled=True,
-    )
-    queries = lax.optimization_barrier(query_sum)
+    def query_chunk(owner):
+        rows = lax.dynamic_slice_in_dim(spread_cols, owner * local_rows, local_rows, 0)
+        product = jnp.dot(rows, q_weight, preferred_element_type=jnp.float32)
+        return product.astype(jnp.bfloat16).astype(jnp.float32)
+
+    query_sum = line_reduce_scatter(query_chunk, "req", req_count, req_index)
+    queries = lax.optimization_barrier(query_sum.astype(jnp.bfloat16))
     normalized = normalize_heads(queries, q_gain, head_dim)
     capacity = 2 * local_rows // req_count
     slot_total = req_count * capacity
@@ -192,11 +230,12 @@
         (((0,), (0,)), ((), ())),
         preferred_element_type=jnp.float32,
     ).astype(jnp.bfloat16)
-    partial_cols = jnp.dot(
-        lax.all_gather(attended, "req", axis=0, tiled=True),
-        out_weight,
-        preferred_element_type=jnp.float32,
-    ).astype(jnp.bfloat16)
+    def out_part(rows):
+        product = jnp.dot(rows, out_weight, preferred_element_type=jnp.float32)
+        return product.astype(jnp.bfloat16)
+
+    partial_cols = line_gather_apply(attended, out_part, "req", req_count, req_index)
+    partial_cols = partial_cols.reshape(req_count * local_rows, out_weight.shape[1])
     hs_count = lax.axis_size("head") * sub_count
     hs_index = lax.axis_index("head") * sub_count + sub_index
     head_count = lax.axis_size("head")

time: 274 us -> 262 us (0.956)
  waiting for transfers between devices: 184 us -> 133 us
  starting transfers between devices: 15.9 us -> 53.3 us
  between operations: 13.8 us -> 0.77 us
  matrix products: 19.3 us -> 26.1 us
  local copies, waits for them, and re-layouts: 10.5 us -> 15.7 us
  other arithmetic: 7.69 us -> 10.9 us
    ppermute x0 -> x12, waiting for transfers between devices: none -> 55.9 us  [the longest x3 24.7 us: line_reduce_scatter(): lax.ppermute(send_r.astype(jnp.bfloat16), axis, [(i, i + 1) for i in rang...]
    all_gather x1 -> x0, waiting for transfers between devices: 44.2 us -> none  [local(): lax.all_gather(attended, 'req', axis=0, tiled=True)]
    reduce_scatter x1 -> x0, waiting for transfers between devices: 43.1 us -> none  [local(): lax.psum_scatter(jnp.dot(spread_cols, q_weight, preferred_element_type=jn...]
    ppermute x0 -> x12, starting transfers between devices: none -> 33 us  [the longest x3 16.9 us: line_reduce_scatter(): lax.ppermute(send_r.astype(jnp.bfloat16), axis, [(i, i + 1) for i in rang...]
    ppermute x9, waiting for transfers between devices: 61.8 us -> 42.7 us  [shift_exchange(): lax.ppermute(blocks[shift], axis, [(i, (i + shift) % count) for i in rang...]
    dot_general x2 -> x14, matrix products: 17.6 us -> 25.2 us  [the longest x7 12.8 us: query_chunk(): product = jnp.dot(rows, q_weight, preferred_element_type=jnp.float32)]
    gather x0 -> x2, local copies, waits for them, and re-layouts: none -> 5.61 us  [the longest x1 3.61 us: line_gather_apply(): jnp.take(jnp.stack(from_left), jnp.clip(index - origins, 0, count - 1), a...]
    ppermute x9, starting transfers between devices: 13.1 us -> 17.6 us  [shift_exchange(): lax.ppermute(blocks[shift], axis, [(i, (i + shift) % count) for i in rang...]
  transfers between devices with their start and end apart: 15 -> 25, of which waited for: 12 -> 19; matrix products, arithmetic and copies ran while one was open for 1% -> 8% of each run, Pallas kernels for 0% -> 0%
where the time goes in v8:
time: 262 us; the launch traced here: 258 us
  waiting for transfers between devices  133 us (51%)
  starting transfers between devices  53.3 us (20%)
  matrix products  26.1 us (10%)
  Pallas kernels  18.2 us (7%)
  local copies, waits for them, and re-layouts  15.7 us (6%)
  other arithmetic  10.9 us (4%)
    ppermute x9, waiting for transfers between devices, shift_exchange(): lax.ppermute(blocks[shift], axis, [(i, (i + shift) % count) for i in rang...  42.7 us
    ppermute x3, waiting for transfers between devices, line_reduce_scatter(): lax.ppermute(send_r.astype(jnp.bfloat16), axis, [(i, i + 1) for i in rang...  24.7 us
    ppermute x3, waiting for transfers between devices, line_gather_apply(): lax.ppermute(carry_l, axis, [(i, i - 1) for i in range(1, count - step +...  21.4 us
    pallas_call x1, Pallas kernels, attend(): pl.pallas_call(kernel, grid=(kv_count,), in_specs=[pl.BlockSpec((rows, gr...  18.2 us
    ppermute x9, starting transfers between devices, shift_exchange(): lax.ppermute(blocks[shift], axis, [(i, (i + shift) % count) for i in rang...  17.6 us
    ppermute x3, starting transfers between devices, line_reduce_scatter(): lax.ppermute(send_r.astype(jnp.bfloat16), axis, [(i, i + 1) for i in rang...  16.9 us
    ppermute x1, waiting for transfers between devices, local(): arrived_blocks.append(lax.ppermute(chunk, ('req', 'head', 'sub'), pairs))  16.6 us
    ppermute x2, waiting for transfers between devices, exchange_sum(): lax.ppermute(outgoing, axis, [(i, (i + shift) % count) for i in range(cou...  16.1 us
  transfers between devices with their start and end apart: 25, of which 19 were waited for; matrix products, arithmetic and copies ran while one was open for 8% of the time, Pallas kernels for 0%

profile of v8, /device:TPU:6, one launch (start us, length us, event | category | flops | bytes accessed | tf_op | source)
XLA Modules:
  0.0 257.9 jit_solution(5765928196972978923)
XLA Ops:
  10.4 5.6 %collective-permute-done = bf16[128,1024]{1,0:T(8,128)(2,1)S(1)} collective-permute-done((bf16[128,1024]{1,0:T(8,128)(2,1)S(1)}, bf16[128,1024]{1,0:T(8,128)(2,1)S(1)}, u32[]{:S(2)}, u32[]{:S(2)}) %collective-permute-start) | collective-permute-done | bytes 262176 | tf_op jit(solution)/shard_map/ppermute | solution.py:24
  16.0 10.2 %collective-permute-done.1 = bf16[128,1024]{1,0:T(8,128)(2,1)S(1)} collective-permute-done((bf16[128,1024]{1,0:T(8,128)(2,1)S(1)}, bf16[128,1024]{1,0:T(8,128)(2,1)S(1)}, u32[]{:S(2)}, u32[]{:S(2)}) %collective-permute-start.1) | collective-permute-done | bytes 262176 | tf_op jit(solution)/shard_map/ppermute | solution.py:24
  30.0 4.8 %convolution_convert_fusion.11 = bf16[128,2048]{1,0:T(8,128)(2,1)S(1)} fusion(bf16[2048,2048]{1,0:T(8,128)(2,1)} %param.14, bf16[512,2048]{1,0:T(8,128)(2,1)S(1)} %constant_dynamic-update-slice_fusion, s32[]{:T(128)S(6)} %select_n.140), kind=kOutput, calls=%fused_computation.21 | convolution fusion | flops 1074003968 | bytes 9437188 | tf_op jit(solution)/shard_map/dot_general | solution.py:181
  34.8 8.0 %collective-permute-start.4 = (bf16[128,2048]{1,0:T(8,128)(2,1)S(1)}, bf16[128,2048]{1,0:T(8,128)(2,1)S(1)}, u32[]{:S(2)}, u32[]{:S(2)}) collective-permute-start(bf16[128,2048]{1,0:T(8,128)(2,1)S(1)} %convolution_convert_fusion.11), channel_id=1, source_target_pairs={{0,4},{1,5},{2,6},{3,7},{16,20},{17,21},{18,22},{19,23}} | collective-permute-start | bytes 1572872 | tf_op jit(solution)/shard_map/ppermute | solution.py:35
  44.8 9.4 %collective-permute-done.4 = bf16[128,2048]{1,0:T(8,128)(2,1)S(1)} collective-permute-done((bf16[128,2048]{1,0:T(8,128)(2,1)S(1)}, bf16[128,2048]{1,0:T(8,128)(2,1)S(1)}, u32[]{:S(2)}, u32[]{:S(2)}) %collective-permute-start.4) | collective-permute-done | bytes 524320 | tf_op jit(solution)/shard_map/ppermute | solution.py:35
  55.6 4.4 %collective-permute-start.5 = (bf16[128,2048]{1,0:T(8,128)(2,1)S(1)}, bf16[128,2048]{1,0:T(8,128)(2,1)S(1)}, u32[]{:S(2)}, u32[]{:S(2)}) collective-permute-start(bf16[128,2048]{1,0:T(8,128)(2,1)S(1)} %fusion.12), channel_id=1, source_target_pairs={{0,4},{4,8},{1,5},{5,9},{2,6},{6,10},{3,7},{7,11},{16,20},{20,24},... | collective-permute-start | bytes 1572872 | tf_op jit(solution)/shard_map/ppermute | solution.py:35
  62.0 8.6 %collective-permute-done.5 = bf16[128,2048]{1,0:T(8,128)(2,1)S(1)} collective-permute-done((bf16[128,2048]{1,0:T(8,128)(2,1)S(1)}, bf16[128,2048]{1,0:T(8,128)(2,1)S(1)}, u32[]{:S(2)}, u32[]{:S(2)}) %collective-permute-start.5) | collective-permute-done | bytes 524320 | tf_op jit(solution)/shard_map/ppermute | solution.py:35
  71.9 4.4 %collective-permute-start.6 = (bf16[128,2048]{1,0:T(8,128)(2,1)S(1)}, bf16[128,2048]{1,0:T(8,128)(2,1)S(1)}, u32[]{:S(2)}, u32[]{:S(2)}) collective-permute-start(bf16[128,2048]{1,0:T(8,128)(2,1)S(1)} %fusion.11), channel_id=1, source_target_pairs={{0,4},{4,8},{8,12},{1,5},{5,9},{9,13},{2,6},{6,10},{10,14},{3,7},{... | collective-permute-start | bytes 1572872 | tf_op jit(solution)/shard_map/ppermute | solution.py:35
  79.4 6.7 %collective-permute-done.6 = bf16[128,2048]{1,0:T(8,128)(2,1)S(1)} collective-permute-done((bf16[128,2048]{1,0:T(8,128)(2,1)S(1)}, bf16[128,2048]{1,0:T(8,128)(2,1)S(1)}, u32[]{:S(2)}, u32[]{:S(2)}) %collective-permute-start.6) | collective-permute-done | bytes 524320 | tf_op jit(solution)/shard_map/ppermute | solution.py:35
  86.0 5.5 %collective-permute-done.9 = bf16[128,2048]{1,0:T(8,128)(2,1)S(1)} collective-permute-done((bf16[128,2048]{1,0:T(8,128)(2,1)S(1)}, bf16[128,2048]{1,0:T(8,128)(2,1)S(1)}, u32[]{:S(2)}, u32[]{:S(2)}) %collective-permute-start.9) | collective-permute-done | bytes 524320 | tf_op jit(solution)/shard_map/ppermute | solution.py:40
  100.8 5.2 %collective-permute-done.10 = bf16[64,2048]{1,0:T(8,128)(2,1)S(1)} collective-permute-done((bf16[64,2048]{1,0:T(8,128)(2,1)S(1)}, bf16[64,2048]{1,0:T(8,128)(2,1)S(1)}, u32[]{:S(2)}, u32[]{:S(2)}) %collective-permute-start.10) | collective-permute-done | bytes 262176 | tf_op jit(solution)/shard_map/ppermute | solution.py:24
  106.0 7.6 %collective-permute-done.11 = bf16[64,2048]{1,0:T(8,128)(2,1)S(1)} collective-permute-done((bf16[64,2048]{1,0:T(8,128)(2,1)S(1)}, bf16[64,2048]{1,0:T(8,128)(2,1)S(1)}, u32[]{:S(2)}, u32[]{:S(2)}) %collective-permute-start.11) | collective-permute-done | bytes 262176 | tf_op jit(solution)/shard_map/ppermute | solution.py:24
  114.7 18.2 %shard_map.91 = bf16[256,2048]{1,0:T(8,128)(2,1)} custom-call(bf16[256,2048]{1,0:T(8,128)(2,1)} %bitcast.102, bf16[1664,256]{1,0:T(8,128)(2,1)} %pad.7.k_ref, bf16[1664,256]{1,0:T(8,128)(2,1)} %pad.8.v_ref), custom_call_target="tpu_custom_call" | custom-call | flops 3489660928 | bytes 3801088 | tf_op jit(solution)/shard_map/pallas_call | solution.py:120
  134.1 5.7 %collective-permute-start.13 = (bf16[64,2048]{1,0:T(8,128)(2,1)S(1)}, bf16[64,2048]{1,0:T(8,128)(2,1)S(1)}, u32[]{:S(2)}, u32[]{:S(2)}) collective-permute-start(bf16[64,2048]{1,0:T(8,128)(2,1)S(1)} %get-tuple-element.10), channel_id=1, source_target_pairs={{0,4},{4,8},{8,12},{12,0},{1,5},{5,9},{9,13},{13,1},{2,6},{6,10},{... | collective-permute-start | bytes 786440 | tf_op jit(solution)/shard_map/ppermute | solution.py:24
  142.3 4.3 %collective-permute-done.13 = bf16[64,2048]{1,0:T(8,128)(2,1)S(1)} collective-permute-done((bf16[64,2048]{1,0:T(8,128)(2,1)S(1)}, bf16[64,2048]{1,0:T(8,128)(2,1)S(1)}, u32[]{:S(2)}, u32[]{:S(2)}) %collective-permute-start.13) | collective-permute-done | bytes 262176 | tf_op jit(solution)/shard_map/ppermute | solution.py:24
  146.6 8.6 %collective-permute-done.14 = bf16[64,2048]{1,0:T(8,128)(2,1)S(1)} collective-permute-done((bf16[64,2048]{1,0:T(8,128)(2,1)S(1)}, bf16[64,2048]{1,0:T(8,128)(2,1)S(1)}, u32[]{:S(2)}, u32[]{:S(2)}) %collective-permute-start.14) | collective-permute-done | bytes 262176 | tf_op jit(solution)/shard_map/ppermute | solution.py:24
  157.1 8.1 %collective-permute-start.16 = (bf16[128,2048]{1,0:T(8,128)(2,1)S(1)}, bf16[128,2048]{1,0:T(8,128)(2,1)S(1)}, u32[]{:S(2)}, u32[]{:S(2)}) collective-permute-start(bf16[128,2048]{1,0:T(8,128)(2,1)S(1)} %convolution_convert_fusion.15), channel_id=1, source_target_pairs={{0,4},{4,8},{8,12},{1,5},{5,9},{9,13},{2,6},{6,10},{10,14},{3,7},{... | collective-permute-start | bytes 1572872 | tf_op jit(solution)/shard_map/ppermute | solution.py:56
  166.5 4.7 %fusion.16 = bf16[1,128,2048]{2,1,0:T(8,128)(2,1)S(1)} fusion(bf16[128,2048]{1,0:T(8,128)(2,1)S(1)} %convolution_convert_fusion.15, bf16[2048,2048]{1,0:T(8,128)(2,1)} %param.18), kind=kOutput, calls=%fused_computation.38 | convolution fusion | flops 1074003968 | bytes 9437184 | tf_op jit(solution)/shard_map/dot_general | solution.py:234
  171.2 4.4 %collective-permute-done.16 = bf16[128,2048]{1,0:T(8,128)(2,1)S(1)} collective-permute-done((bf16[128,2048]{1,0:T(8,128)(2,1)S(1)}, bf16[128,2048]{1,0:T(8,128)(2,1)S(1)}, u32[]{:S(2)}, u32[]{:S(2)}) %collective-permute-start.16) | collective-permute-done | bytes 524320 | tf_op jit(solution)/shard_map/ppermute | solution.py:56
  184.3 10.3 %collective-permute-done.20 = bf16[128,2048]{1,0:T(8,128)(2,1)S(1)} collective-permute-done((bf16[128,2048]{1,0:T(8,128)(2,1)S(1)}, bf16[128,2048]{1,0:T(8,128)(2,1)S(1)}, u32[]{:S(2)}, u32[]{:S(2)}) %collective-permute-start.20) | collective-permute-done | bytes 524320 | tf_op jit(solution)/shard_map/ppermute | solution.py:57
  198.5 9.0 %collective-permute-done.21 = bf16[128,2048]{1,0:T(8,128)(2,1)S(1)} collective-permute-done((bf16[128,2048]{1,0:T(8,128)(2,1)S(1)}, bf16[128,2048]{1,0:T(8,128)(2,1)S(1)}, u32[]{:S(2)}, u32[]{:S(2)}) %collective-permute-start.21) | collective-permute-done | bytes 524320 | tf_op jit(solution)/shard_map/ppermute | solution.py:57
  210.3 3.6 %gather_fusion.2 = bf16[4,128,2048]{2,1,0:T(8,128)(2,1)} fusion(bf16[4,128,2048]{2,1,0:T(8,128)(2,1)} %get-tuple-element.19, s32[1024]{0:T(1024)S(1)} %pad_clamp_fusion.1), kind=kCustom, calls=%fused_computation.1.clone | custom fusion | bytes 4194320 | tf_op jit(solution)/shard_map/jit(_take)/gather | solution.py:61
  223.9 13.4 %collective-permute-done.23 = bf16[128,2048]{1,0:T(8,128)(2,1)S(1)} collective-permute-done((bf16[128,2048]{1,0:T(8,128)(2,1)S(1)}, bf16[128,2048]{1,0:T(8,128)(2,1)S(1)}, u32[]{:S(2)}, u32[]{:S(2)}) %collective-permute-start.23) | collective-permute-done | bytes 524320 | tf_op jit(solution)/shard_map/ppermute | solution.py:71
  239.3 16.6 %collective-permute-done.24 = bf16[128,2048]{1,0:T(8,128)(2,1)S(1)} collective-permute-done((bf16[128,2048]{1,0:T(8,128)(2,1)S(1)}, bf16[128,2048]{1,0:T(8,128)(2,1)S(1)}, u32[]{:S(2)}, u32[]{:S(2)}) %collective-permute-start.24) | collective-permute-done | bytes 524320 | tf_op jit(solution)/shard_map/ppermute | solution.py:262
  (121 shorter events, 70.1 us)
Async XLA Ops:
  4.8 11.2 %collective-permute-start = (bf16[128,1024]{1,0:T(8,128)(2,1)S(1)}, bf16[128,1024]{1,0:T(8,128)(2,1)S(1)}, u32[]{:S(2)}, u32[]{:S(2)}) collective-permute-start(bf16[128,1024]{1,0:T(8,128)(2,1)S(1)} %get-tuple-element.18), channel_id=1, source_target_pairs={{0,4},{4,8},{8,12},{12,0},{1,5},{5,9},{9,13},{13,1},{2,6},{6,10},{... | collective-permute-start | bytes 786440 | tf_op jit(solution)/shard_map/ppermute | solution.py:24
  6.4 19.7 %collective-permute-start.1 = (bf16[128,1024]{1,0:T(8,128)(2,1)S(1)}, bf16[128,1024]{1,0:T(8,128)(2,1)S(1)}, u32[]{:S(2)}, u32[]{:S(2)}) collective-permute-start(bf16[128,1024]{1,0:T(8,128)(2,1)S(1)} %get-tuple-element.17), channel_id=1, source_target_pairs={{0,8},{4,12},{8,0},{12,4},{1,9},{5,13},{9,1},{13,5},{2,10},{6,14},... | collective-permute-start | bytes 786440 | tf_op jit(solution)/shard_map/ppermute | solution.py:24
  9.0 17.1 %collective-permute-start.2 = (bf16[128,1024]{1,0:T(8,128)(2,1)S(1)}, bf16[128,1024]{1,0:T(8,128)(2,1)S(1)}, u32[]{:S(2)}, u32[]{:S(2)}) collective-permute-start(bf16[128,1024]{1,0:T(8,128)(2,1)S(1)} %get-tuple-element.16), channel_id=1, source_target_pairs={{0,12},{4,0},{8,4},{12,8},{1,13},{5,1},{9,5},{13,9},{2,14},{6,2},{... | collective-permute-start | bytes 786440 | tf_op jit(solution)/shard_map/ppermute | solution.py:24
  34.8 19.5 %collective-permute-start.4 = (bf16[128,2048]{1,0:T(8,128)(2,1)S(1)}, bf16[128,2048]{1,0:T(8,128)(2,1)S(1)}, u32[]{:S(2)}, u32[]{:S(2)}) collective-permute-start(bf16[128,2048]{1,0:T(8,128)(2,1)S(1)} %convolution_convert_fusion.11), channel_id=1, source_target_pairs={{0,4},{1,5},{2,6},{3,7},{16,20},{17,21},{18,22},{19,23}} | collective-permute-start | bytes 1572872 | tf_op jit(solution)/shard_map/ppermute | solution.py:35
  44.1 15.9 %collective-permute-start.7 = (bf16[128,2048]{1,0:T(8,128)(2,1)S(1)}, bf16[128,2048]{1,0:T(8,128)(2,1)S(1)}, u32[]{:S(2)}, u32[]{:S(2)}) collective-permute-start(bf16[128,2048]{1,0:T(8,128)(2,1)S(1)} %convolution_convert_fusion.8), channel_id=1, source_target_pairs={{12,8},{13,9},{14,10},{15,11},{28,24},{29,25},{30,26},{31,27}} | collective-permute-start | bytes 1572872 | tf_op jit(solution)/shard_map/ppermute | solution.py:40
  55.6 15.0 %collective-permute-start.5 = (bf16[128,2048]{1,0:T(8,128)(2,1)S(1)}, bf16[128,2048]{1,0:T(8,128)(2,1)S(1)}, u32[]{:S(2)}, u32[]{:S(2)}) collective-permute-start(bf16[128,2048]{1,0:T(8,128)(2,1)S(1)} %fusion.12), channel_id=1, source_target_pairs={{0,4},{4,8},{1,5},{5,9},{2,6},{6,10},{3,7},{7,11},{16,20},{20,24},... | collective-permute-start | bytes 1572872 | tf_op jit(solution)/shard_map/ppermute | solution.py:35
  61.3 15.0 %collective-permute-start.8 = (bf16[128,2048]{1,0:T(8,128)(2,1)S(1)}, bf16[128,2048]{1,0:T(8,128)(2,1)S(1)}, u32[]{:S(2)}, u32[]{:S(2)}) collective-permute-start(bf16[128,2048]{1,0:T(8,128)(2,1)S(1)} %fusion.14), channel_id=1, source_target_pairs={{8,4},{12,8},{9,5},{13,9},{10,6},{14,10},{11,7},{15,11},{24,20},{2... | collective-permute-start | bytes 1572872 | tf_op jit(solution)/shard_map/ppermute | solution.py:40
  71.9 14.1 %collective-permute-start.6 = (bf16[128,2048]{1,0:T(8,128)(2,1)S(1)}, bf16[128,2048]{1,0:T(8,128)(2,1)S(1)}, u32[]{:S(2)}, u32[]{:S(2)}) collective-permute-start(bf16[128,2048]{1,0:T(8,128)(2,1)S(1)} %fusion.11), channel_id=1, source_target_pairs={{0,4},{4,8},{8,12},{1,5},{5,9},{9,13},{2,6},{6,10},{10,14},{3,7},{... | collective-permute-start | bytes 1572872 | tf_op jit(solution)/shard_map/ppermute | solution.py:35
  77.7 13.8 %collective-permute-start.9 = (bf16[128,2048]{1,0:T(8,128)(2,1)S(1)}, bf16[128,2048]{1,0:T(8,128)(2,1)S(1)}, u32[]{:S(2)}, u32[]{:S(2)}) collective-permute-start(bf16[128,2048]{1,0:T(8,128)(2,1)S(1)} %fusion.13), channel_id=1, source_target_pairs={{4,0},{8,4},{12,8},{5,1},{9,5},{13,9},{6,2},{10,6},{14,10},{7,3},{... | collective-permute-start | bytes 1572872 | tf_op jit(solution)/shard_map/ppermute | solution.py:40
  94.8 11.2 %collective-permute-start.10 = (bf16[64,2048]{1,0:T(8,128)(2,1)S(1)}, bf16[64,2048]{1,0:T(8,128)(2,1)S(1)}, u32[]{:S(2)}, u32[]{:S(2)}) collective-permute-start(bf16[64,2048]{1,0:T(8,128)(2,1)S(1)} %get-tuple-element.14), channel_id=1, source_target_pairs={{0,4},{4,8},{8,12},{12,0},{1,5},{5,9},{9,13},{13,1},{2,6},{6,10},{... | collective-permute-start | bytes 786440 | tf_op jit(solution)/shard_map/ppermute | solution.py:24
  95.4 18.1 %collective-permute-start.11 = (bf16[64,2048]{1,0:T(8,128)(2,1)S(1)}, bf16[64,2048]{1,0:T(8,128)(2,1)S(1)}, u32[]{:S(2)}, u32[]{:S(2)}) collective-permute-start(bf16[64,2048]{1,0:T(8,128)(2,1)S(1)} %get-tuple-element.13), channel_id=1, source_target_pairs={{0,8},{4,12},{8,0},{12,4},{1,9},{5,13},{9,1},{13,5},{2,10},{6,14},... | collective-permute-start | bytes 786440 | tf_op jit(solution)/shard_map/ppermute | solution.py:24
  95.4 18.1 %collective-permute-start.12 = (bf16[64,2048]{1,0:T(8,128)(2,1)S(1)}, bf16[64,2048]{1,0:T(8,128)(2,1)S(1)}, u32[]{:S(2)}, u32[]{:S(2)}) collective-permute-start(bf16[64,2048]{1,0:T(8,128)(2,1)S(1)} %get-tuple-element.12), channel_id=1, source_target_pairs={{0,12},{4,0},{8,4},{12,8},{1,13},{5,1},{9,5},{13,9},{2,14},{6,2},{... | collective-permute-start | bytes 786440 | tf_op jit(solution)/shard_map/ppermute | solution.py:24
  134.1 12.5 %collective-permute-start.13 = (bf16[64,2048]{1,0:T(8,128)(2,1)S(1)}, bf16[64,2048]{1,0:T(8,128)(2,1)S(1)}, u32[]{:S(2)}, u32[]{:S(2)}) collective-permute-start(bf16[64,2048]{1,0:T(8,128)(2,1)S(1)} %get-tuple-element.10), channel_id=1, source_target_pairs={{0,4},{4,8},{8,12},{12,0},{1,5},{5,9},{9,13},{13,1},{2,6},{6,10},{... | collective-permute-start | bytes 786440 | tf_op jit(solution)/shard_map/ppermute | solution.py:24
  139.8 15.3 %collective-permute-start.14 = (bf16[64,2048]{1,0:T(8,128)(2,1)S(1)}, bf16[64,2048]{1,0:T(8,128)(2,1)S(1)}, u32[]{:S(2)}, u32[]{:S(2)}) collective-permute-start(bf16[64,2048]{1,0:T(8,128)(2,1)S(1)} %get-tuple-element.9), channel_id=1, source_target_pairs={{0,8},{4,12},{8,0},{12,4},{1,9},{5,13},{9,1},{13,5},{2,10},{6,14},... | collective-permute-start | bytes 786440 | tf_op jit(solution)/shard_map/ppermute | solution.py:24
  140.0 16.4 %collective-permute-start.15 = (bf16[64,2048]{1,0:T(8,128)(2,1)S(1)}, bf16[64,2048]{1,0:T(8,128)(2,1)S(1)}, u32[]{:S(2)}, u32[]{:S(2)}) collective-permute-start(bf16[64,2048]{1,0:T(8,128)(2,1)S(1)} %get-tuple-element.8), channel_id=1, source_target_pairs={{0,12},{4,0},{8,4},{12,8},{1,13},{5,1},{9,5},{13,9},{2,14},{6,2},{... | collective-permute-start | bytes 786440 | tf_op jit(solution)/shard_map/ppermute | solution.py:24
  157.1 18.4 %collective-permute-start.16 = (bf16[128,2048]{1,0:T(8,128)(2,1)S(1)}, bf16[128,2048]{1,0:T(8,128)(2,1)S(1)}, u32[]{:S(2)}, u32[]{:S(2)}) collective-permute-start(bf16[128,2048]{1,0:T(8,128)(2,1)S(1)} %convolution_convert_fusion.15), channel_id=1, source_target_pairs={{0,4},{4,8},{8,12},{1,5},{5,9},{9,13},{2,6},{6,10},{10,14},{3,7},{... | collective-permute-start | bytes 1572872 | tf_op jit(solution)/shard_map/ppermute | solution.py:56
  165.2 14.5 %collective-permute-start.19 = (bf16[128,2048]{1,0:T(8,128)(2,1)S(1)}, bf16[128,2048]{1,0:T(8,128)(2,1)S(1)}, u32[]{:S(2)}, u32[]{:S(2)}) collective-permute-start(bf16[128,2048]{1,0:T(8,128)(2,1)S(1)} %convolution_convert_fusion.15), channel_id=1, source_target_pairs={{4,0},{8,4},{12,8},{5,1},{9,5},{13,9},{6,2},{10,6},{14,10},{7,3},{... | collective-permute-start | bytes 1572872 | tf_op jit(solution)/shard_map/ppermute | solution.py:57
  175.5 6.7 %collective-permute-start.17 = (bf16[128,2048]{1,0:T(8,128)(2,1)S(1)}, bf16[128,2048]{1,0:T(8,128)(2,1)S(1)}, u32[]{:S(2)}, u32[]{:S(2)}) collective-permute-start(bf16[128,2048]{1,0:T(8,128)(2,1)S(1)} %collective-permute-done.16), channel_id=1, source_target_pairs={{4,8},{8,12},{5,9},{9,13},{6,10},{10,14},{7,11},{11,15},{20,24},{2... | collective-permute-start | bytes 1572872 | tf_op jit(solution)/shard_map/ppermute | solution.py:56
  179.7 14.9 %collective-permute-start.20 = (bf16[128,2048]{1,0:T(8,128)(2,1)S(1)}, bf16[128,2048]{1,0:T(8,128)(2,1)S(1)}, u32[]{:S(2)}, u32[]{:S(2)}) collective-permute-start(bf16[128,2048]{1,0:T(8,128)(2,1)S(1)} %collective-permute-done.19), channel_id=1, source_target_pairs={{4,0},{8,4},{5,1},{9,5},{6,2},{10,6},{7,3},{11,7},{20,16},{24,20},... | collective-permute-start | bytes 1572872 | tf_op jit(solution)/shard_map/ppermute | solution.py:57
  182.3 14.9 %collective-permute-start.18 = (bf16[128,2048]{1,0:T(8,128)(2,1)S(1)}, bf16[128,2048]{1,0:T(8,128)(2,1)S(1)}, u32[]{:S(2)}, u32[]{:S(2)}) collective-permute-start(bf16[128,2048]{1,0:T(8,128)(2,1)S(1)} %collective-permute-done.17), channel_id=1, source_target_pairs={{8,12},{9,13},{10,14},{11,15},{24,28},{25,29},{26,30},{27,31}} | collective-permute-start | bytes 1572872 | tf_op jit(solution)/shard_map/ppermute | solution.py:56
  194.6 12.9 %collective-permute-start.21 = (bf16[128,2048]{1,0:T(8,128)(2,1)S(1)}, bf16[128,2048]{1,0:T(8,128)(2,1)S(1)}, u32[]{:S(2)}, u32[]{:S(2)}) collective-permute-start(bf16[128,2048]{1,0:T(8,128)(2,1)S(1)} %collective-permute-done.20), channel_id=1, source_target_pairs={{4,0},{5,1},{6,2},{7,3},{20,16},{21,17},{22,18},{23,19}} | collective-permute-start | bytes 1572872 | tf_op jit(solution)/shard_map/ppermute | solution.py:57
  218.7 2.9 %collective-permute-start.22 = (bf16[256,2048]{1,0:T(8,128)(2,1)S(1)}, bf16[256,2048]{1,0:T(8,128)(2,1)}, u32[]{:S(2)}, u32[]{:S(2)}) collective-permute-start(bf16[256,2048]{1,0:T(8,128)(2,1)S(1)} %dynamic-slice_bitcast_fusion), channel_id=1, source_target_pairs={{0,1},{1,0},{2,3},{3,2},{4,5},{5,4},{6,7},{7,6},{8,9},{9,8},{10,11... | collective-permute-start | bytes 3145736 | tf_op jit(solution)/shard_map/ppermute | solution.py:71
  223.2 14.0 %collective-permute-start.23 = (bf16[128,2048]{1,0:T(8,128)(2,1)S(1)}, bf16[128,2048]{1,0:T(8,128)(2,1)S(1)}, u32[]{:S(2)}, u32[]{:S(2)}) collective-permute-start(bf16[128,2048]{1,0:T(8,128)(2,1)S(1)} %dynamic-slice_bitcast_fusion.3), channel_id=1, source_target_pairs={{0,2},{2,0},{1,3},{3,1},{4,6},{6,4},{5,7},{7,5},{8,10},{10,8},{9,1... | collective-permute-start | bytes 1572872 | tf_op jit(solution)/shard_map/ppermute | solution.py:71
  237.4 18.5 %collective-permute-start.24 = (bf16[128,2048]{1,0:T(8,128)(2,1)S(1)}, bf16[128,2048]{1,0:T(8,128)(2,1)S(1)}, u32[]{:S(2)}, u32[]{:S(2)}) collective-permute-start(bf16[128,2048]{1,0:T(8,128)(2,1)S(1)} %fusion.31), channel_id=1, source_target_pairs={{0,0},{1,8},{2,4},{3,12},{4,1},{5,9},{6,5},{7,13},{8,2},{9,10},{10... | collective-permute-start | bytes 1572872 | tf_op jit(solution)/shard_map/ppermute | solution.py:262
  (12 other events, 193.5 us)

commit v9 on v8

--- a/solution.py
+++ b/solution.py
@@ -57,11 +57,12 @@
         carry_l = lax.ppermute(carry_l, axis, [(i, i - 1) for i in range(1, count - step + 1)])
         from_left.append(apply(carry_r))
         from_right.append(apply(carry_l))
-    origins = jnp.arange(count)
-    lower = jnp.take(jnp.stack(from_left), jnp.clip(index - origins, 0, count - 1), axis=0)
-    upper = jnp.take(jnp.stack(from_right), jnp.clip(origins - index, 0, count - 1), axis=0)
-    pick = (origins <= index).reshape((count,) + (1,) * own.ndim)
-    return jnp.where(pick, lower, upper)
+    placed = jnp.zeros((count,) + own.shape, own.dtype)
+    for step in range(count - 1, 0, -1):
+        placed = lax.dynamic_update_index_in_dim(placed, from_left[step], index - step, 0)
+    for step in range(count - 1, 0, -1):
+        placed = lax.dynamic_update_index_in_dim(placed, from_right[step], index + step, 0)
+    return lax.dynamic_update_index_in_dim(placed, own, index, 0)
 
 
 def exchange_sum(parts, axis, count, index):
@@ -159,11 +160,20 @@
     by_block = hidden_in.reshape(local_rows, req_count, sub_count, part_width)
     req_index = lax.axis_index("req")
     my_part = lax.dynamic_index_in_dim(by_block, sub_index, axis=2, keepdims=False)
-    shift_order = (req_index + jnp.arange(req_count)) % req_count
-    outgoing_parts = jnp.take(jnp.swapaxes(my_part, 0, 1), shift_order, axis=0)
-    arrived_parts = shift_exchange(outgoing_parts, "req", req_count)
-    source_order = (req_index - jnp.arange(req_count)) % req_count
-    spread_part = jnp.take(arrived_parts, source_order, axis=0)
+    spread_part = jnp.zeros((req_count, local_rows, part_width), my_part.dtype)
+    spread_part = lax.dynamic_update_index_in_dim(
+        spread_part, lax.dynamic_index_in_dim(my_part, req_index, 1, keepdims=False), req_index, 0
+    )
+    for shift in range(1, req_count):
+        outgoing_part = lax.dynamic_index_in_dim(
+            my_part, (req_index + shift) % req_count, 1, keepdims=False
+        )
+        arrived_part = lax.ppermute(
+            outgoing_part, "req", [(i, (i + shift) % req_count) for i in range(req_count)]
+        )
+        spread_part = lax.dynamic_update_index_in_dim(
+            spread_part, arrived_part, (req_index - shift) % req_count, 0
+        )
     spread_part = spread_part.reshape(req_count * local_rows, part_width)
     spread_cols = jnp.zeros((req_count * local_rows, block_width), spread_part.dtype)
     spread_cols = lax.dynamic_update_slice_in_dim(

time: 262 us -> 260 us (level)
  the two profiles are of different devices: /device:TPU:6 before, /device:TPU:26 now
where the time goes in v9:
time: 260 us; the launch traced here: 259 us
  waiting for transfers between devices  155 us (60%)
  starting transfers between devices  40.5 us (16%)
  matrix products  27.5 us (11%)
  Pallas kernels  18.2 us (7%)
  local copies, waits for them, and re-layouts  10.3 us (4%)
  other arithmetic  6.15 us (2%)
    ppermute x6, waiting for transfers between devices, shift_exchange(): lax.ppermute(blocks[shift], axis, [(i, (i + shift) % count) for i in rang...  37.9 us
    ppermute x3, waiting for transfers between devices, line_gather_apply(): lax.ppermute(carry_r, axis, [(i, i + 1) for i in range(step - 1, count -...  30.9 us
    ppermute x3, waiting for transfers between devices, local(): lax.ppermute(outgoing_part, 'req', [(i, (i + shift) % req_count) for i in...  21.6 us
    ppermute x3, waiting for transfers between devices, line_reduce_scatter(): lax.ppermute(send_l.astype(jnp.bfloat16), axis, [(i, i - 1) for i in rang...  20.5 us
    ppermute x1, waiting for transfers between devices, local(): arrived_blocks.append(lax.ppermute(chunk, ('req', 'head', 'sub'), pairs))  19.6 us
    pallas_call x1, Pallas kernels, attend(): pl.pallas_call(kernel, grid=(kv_count,), in_specs=[pl.BlockSpec((rows, gr...  18.2 us
    ppermute x2, waiting for transfers between devices, exchange_sum(): lax.ppermute(outgoing, axis, [(i, (i + shift) % count) for i in range(cou...  16.2 us
    dot_general x7, matrix products, out_part(): product = jnp.dot(rows, out_weight, preferred_element_type=jnp.float32)  13.8 us
  transfers between devices with their start and end apart: 25, of which 17 were waited for; matrix products, arithmetic and copies ran while one was open for 7% of the time, Pallas kernels for 0%

profile of v9, /device:TPU:26, one launch (start us, length us, event | category | flops | bytes accessed | tf_op | source)
XLA Modules:
  0.0 259.0 jit_solution(4720461623297550323)
XLA Ops:
  0.0 3.2 %copy.21 = bf16[128,8192]{0,1:T(8,128)(2,1)S(1)} copy(bf16[128,8192]{1,0:T(8,128)(2,1)} %param.9) | data formatting | bytes 4194304 | tf_op args[0]
  6.7 5.2 %collective-permute-done = bf16[128,1024]{1,0:T(8,128)(2,1)S(1)} collective-permute-done((bf16[128,1024]{1,0:T(8,128)(2,1)S(1)}, bf16[128,1024]{1,0:T(8,128)(2,1)S(1)}, u32[]{:S(2)}, u32[]{:S(2)}) %collective-permute-start) | collective-permute-done | bytes 262176 | tf_op jit(solution)/shard_map/ppermute | solution.py:171
  12.0 16.3 %collective-permute-done.1 = bf16[128,1024]{1,0:T(8,128)(2,1)S(1)} collective-permute-done((bf16[128,1024]{1,0:T(8,128)(2,1)S(1)}, bf16[128,1024]{1,0:T(8,128)(2,1)S(1)}, u32[]{:S(2)}, u32[]{:S(2)}) %collective-permute-start.1) | collective-permute-done | bytes 262176 | tf_op jit(solution)/shard_map/ppermute | solution.py:171
  31.3 4.8 %convolution_convert_fusion.11 = bf16[128,2048]{1,0:T(8,128)(2,1)S(1)} fusion(bf16[2048,2048]{1,0:T(8,128)(2,1)} %param.10, bf16[512,2048]{1,0:T(8,128)(2,1)S(1)} %constant_dynamic-update-slice_fusion, s32[]{:T(128)S(6)} %select_n.207), kind=kOutput, calls=%fused_computation.15 | convolution fusion | flops 1074003968 | bytes 9437188 | tf_op jit(solution)/shard_map/dot_general | solution.py:191
  41.7 9.7 %collective-permute-done.7 = bf16[128,2048]{1,0:T(8,128)(2,1)S(1)} collective-permute-done((bf16[128,2048]{1,0:T(8,128)(2,1)S(1)}, bf16[128,2048]{1,0:T(8,128)(2,1)S(1)}, u32[]{:S(2)}, u32[]{:S(2)}) %collective-permute-start.7) | collective-permute-done | bytes 524320 | tf_op jit(solution)/shard_map/ppermute | solution.py:40
  52.7 4.4 %collective-permute-start.8 = (bf16[128,2048]{1,0:T(8,128)(2,1)S(1)}, bf16[128,2048]{1,0:T(8,128)(2,1)S(1)}, u32[]{:S(2)}, u32[]{:S(2)}) collective-permute-start(bf16[128,2048]{1,0:T(8,128)(2,1)S(1)} %fusion.14), channel_id=1, source_target_pairs={{8,4},{12,8},{9,5},{13,9},{10,6},{14,10},{11,7},{15,11},{24,20},{2... | collective-permute-start | bytes 1572872 | tf_op jit(solution)/shard_map/ppermute | solution.py:40
  59.7 8.3 %collective-permute-done.8 = bf16[128,2048]{1,0:T(8,128)(2,1)S(1)} collective-permute-done((bf16[128,2048]{1,0:T(8,128)(2,1)S(1)}, bf16[128,2048]{1,0:T(8,128)(2,1)S(1)}, u32[]{:S(2)}, u32[]{:S(2)}) %collective-permute-start.8) | collective-permute-done | bytes 524320 | tf_op jit(solution)/shard_map/ppermute | solution.py:40
  69.3 5.8 %collective-permute-start.9 = (bf16[128,2048]{1,0:T(8,128)(2,1)S(1)}, bf16[128,2048]{1,0:T(8,128)(2,1)S(1)}, u32[]{:S(2)}, u32[]{:S(2)}) collective-permute-start(bf16[128,2048]{1,0:T(8,128)(2,1)S(1)} %fusion.13), channel_id=1, source_target_pairs={{4,0},{8,4},{12,8},{5,1},{9,5},{13,9},{6,2},{10,6},{14,10},{7,3},{... | collective-permute-start | bytes 1572872 | tf_op jit(solution)/shard_map/ppermute | solution.py:40
  75.3 7.1 %collective-permute-done.6 = bf16[128,2048]{1,0:T(8,128)(2,1)S(1)} collective-permute-done((bf16[128,2048]{1,0:T(8,128)(2,1)S(1)}, bf16[128,2048]{1,0:T(8,128)(2,1)S(1)}, u32[]{:S(2)}, u32[]{:S(2)}) %collective-permute-start.6) | collective-permute-done | bytes 524320 | tf_op jit(solution)/shard_map/ppermute | solution.py:35
  82.4 2.5 collective-permute-done.9
  88.2 4.6 %collective-permute-start.10 = (bf16[64,2048]{1,0:T(8,128)(2,1)S(1)}, bf16[64,2048]{1,0:T(8,128)(2,1)S(1)}, u32[]{:S(2)}, u32[]{:S(2)}) collective-permute-start(bf16[64,2048]{1,0:T(8,128)(2,1)S(1)} %get-tuple-element.16), channel_id=1, source_target_pairs={{0,4},{4,8},{8,12},{12,0},{1,5},{5,9},{9,13},{13,1},{2,6},{6,10},{... | collective-permute-start | bytes 786440 | tf_op jit(solution)/shard_map/ppermute | solution.py:24
  96.0 3.6 %collective-permute-done.10 = bf16[64,2048]{1,0:T(8,128)(2,1)S(1)} collective-permute-done((bf16[64,2048]{1,0:T(8,128)(2,1)S(1)}, bf16[64,2048]{1,0:T(8,128)(2,1)S(1)}, u32[]{:S(2)}, u32[]{:S(2)}) %collective-permute-start.10) | collective-permute-done | bytes 262176 | tf_op jit(solution)/shard_map/ppermute | solution.py:24
  99.6 13.4 %collective-permute-done.11 = bf16[64,2048]{1,0:T(8,128)(2,1)S(1)} collective-permute-done((bf16[64,2048]{1,0:T(8,128)(2,1)S(1)}, bf16[64,2048]{1,0:T(8,128)(2,1)S(1)}, u32[]{:S(2)}, u32[]{:S(2)}) %collective-permute-start.11) | collective-permute-done | bytes 262176 | tf_op jit(solution)/shard_map/ppermute | solution.py:24
  114.1 18.2 %shard_map.91 = bf16[256,2048]{1,0:T(8,128)(2,1)} custom-call(bf16[256,2048]{1,0:T(8,128)(2,1)} %bitcast.114, bf16[1664,256]{1,0:T(8,128)(2,1)} %pad.7.k_ref, bf16[1664,256]{1,0:T(8,128)(2,1)} %pad.8.v_ref), custom_call_target="tpu_custom_call" | custom-call | flops 3489660928 | bytes 3801088 | tf_op jit(solution)/shard_map/pallas_call | solution.py:121
  133.7 2.8 %collective-permute-start.14 = (bf16[64,2048]{1,0:T(8,128)(2,1)S(1)}, bf16[64,2048]{1,0:T(8,128)(2,1)S(1)}, u32[]{:S(2)}, u32[]{:S(2)}) collective-permute-start(bf16[64,2048]{1,0:T(8,128)(2,1)S(1)} %get-tuple-element.11), channel_id=1, source_target_pairs={{0,8},{4,12},{8,0},{12,4},{1,9},{5,13},{9,1},{13,5},{2,10},{6,14},... | collective-permute-start | bytes 786440 | tf_op jit(solution)/shard_map/ppermute | solution.py:24
  140.6 18.8 %collective-permute-done.14 = bf16[64,2048]{1,0:T(8,128)(2,1)S(1)} collective-permute-done((bf16[64,2048]{1,0:T(8,128)(2,1)S(1)}, bf16[64,2048]{1,0:T(8,128)(2,1)S(1)}, u32[]{:S(2)}, u32[]{:S(2)}) %collective-permute-start.14) | collective-permute-done | bytes 262176 | tf_op jit(solution)/shard_map/ppermute | solution.py:24
  161.3 4.6 %collective-permute-start.19 = (bf16[128,2048]{1,0:T(8,128)(2,1)S(1)}, bf16[128,2048]{1,0:T(8,128)(2,1)S(1)}, u32[]{:S(2)}, u32[]{:S(2)}) collective-permute-start(bf16[128,2048]{1,0:T(8,128)(2,1)S(1)} %convolution_convert_fusion.15), channel_id=1, source_target_pairs={{4,0},{8,4},{12,8},{5,1},{9,5},{13,9},{6,2},{10,6},{14,10},{7,3},{... | collective-permute-start | bytes 1572872 | tf_op jit(solution)/shard_map/ppermute | solution.py:57
  165.9 8.9 %collective-permute-done.16 = bf16[128,2048]{1,0:T(8,128)(2,1)S(1)} collective-permute-done((bf16[128,2048]{1,0:T(8,128)(2,1)S(1)}, bf16[128,2048]{1,0:T(8,128)(2,1)S(1)}, u32[]{:S(2)}, u32[]{:S(2)}) %collective-permute-start.16) | collective-permute-done | bytes 524320 | tf_op jit(solution)/shard_map/ppermute | solution.py:56
  177.5 11.0 %collective-permute-done.17 = bf16[128,2048]{1,0:T(8,128)(2,1)S(1)} collective-permute-done((bf16[128,2048]{1,0:T(8,128)(2,1)S(1)}, bf16[128,2048]{1,0:T(8,128)(2,1)S(1)}, u32[]{:S(2)}, u32[]{:S(2)}) %collective-permute-start.17) | collective-permute-done | bytes 524320 | tf_op jit(solution)/shard_map/ppermute | solution.py:56
  190.6 11.0 %collective-permute-done.18 = bf16[128,2048]{1,0:T(8,128)(2,1)} collective-permute-done((bf16[128,2048]{1,0:T(8,128)(2,1)S(1)}, bf16[128,2048]{1,0:T(8,128)(2,1)}, u32[]{:S(2)}, u32[]{:S(2)}) %collective-permute-start.18) | collective-permute-done | bytes 524320 | tf_op jit(solution)/shard_map/ppermute | solution.py:56
  201.9 5.0 %fusion.17 = bf16[4,128,2048]{2,1,0:T(8,128)(2,1)S(1)} fusion(bf16[4,128,2048]{2,1,0:T(8,128)(2,1)S(1)} %broadcast_in_dim.70, s32[]{:T(128)S(6)} %select_n.213, bf16[128,2048]{1,0:T(8,128)(2,1)} %collective-permute-done.18, bf16[2048,2048]{1,0:T(8,128)(2,1)} %param.14), kind=kOutput, calls=%fused_computation.33 | convolution fusion | flops 1074003968 | bytes 9437188 | tf_op jit(solution)/shard_map/dot_general | solution.py:244
  216.9 2.8 %collective-permute-done.22 = bf16[256,2048]{1,0:T(8,128)(2,1)} collective-permute-done((bf16[256,2048]{1,0:T(8,128)(2,1)S(1)}, bf16[256,2048]{1,0:T(8,128)(2,1)}, u32[]{:S(2)}, u32[]{:S(2)}) %collective-permute-start.22) | collective-permute-done | bytes 1048608 | tf_op jit(solution)/shard_map/ppermute | solution.py:72
  221.9 13.4 %collective-permute-done.23 = bf16[128,2048]{1,0:T(8,128)(2,1)S(1)} collective-permute-done((bf16[128,2048]{1,0:T(8,128)(2,1)S(1)}, bf16[128,2048]{1,0:T(8,128)(2,1)S(1)}, u32[]{:S(2)}, u32[]{:S(2)}) %collective-permute-start.23) | collective-permute-done | bytes 524320 | tf_op jit(solution)/shard_map/ppermute | solution.py:72
  237.4 19.6 %collective-permute-done.24 = bf16[128,2048]{1,0:T(8,128)(2,1)S(1)} collective-permute-done((bf16[128,2048]{1,0:T(8,128)(2,1)S(1)}, bf16[128,2048]{1,0:T(8,128)(2,1)S(1)}, u32[]{:S(2)}, u32[]{:S(2)}) %collective-permute-start.24) | collective-permute-done | bytes 524320 | tf_op jit(solution)/shard_map/ppermute | solution.py:272
  (116 shorter events, 53.3 us)
Async XLA Ops:
  3.5 8.5 %collective-permute-start = (bf16[128,1024]{1,0:T(8,128)(2,1)S(1)}, bf16[128,1024]{1,0:T(8,128)(2,1)S(1)}, u32[]{:S(2)}, u32[]{:S(2)}) collective-permute-start(bf16[128,1024]{1,0:T(8,128)(2,1)S(1)} %bitcast.117), channel_id=1, source_target_pairs={{0,4},{4,8},{8,12},{12,0},{1,5},{5,9},{9,13},{13,1},{2,6},{6,10},{... | collective-permute-start | bytes 786440 | tf_op jit(solution)/shard_map/ppermute | solution.py:171
  3.9 24.4 %collective-permute-start.1 = (bf16[128,1024]{1,0:T(8,128)(2,1)S(1)}, bf16[128,1024]{1,0:T(8,128)(2,1)S(1)}, u32[]{:S(2)}, u32[]{:S(2)}) collective-permute-start(bf16[128,1024]{1,0:T(8,128)(2,1)S(1)} %bitcast.116), channel_id=1, source_target_pairs={{0,8},{4,12},{8,0},{12,4},{1,9},{5,13},{9,1},{13,5},{2,10},{6,14},... | collective-permute-start | bytes 786440 | tf_op jit(solution)/shard_map/ppermute | solution.py:171
  5.8 22.5 %collective-permute-start.2 = (bf16[128,1024]{1,0:T(8,128)(2,1)S(1)}, bf16[128,1024]{1,0:T(8,128)(2,1)S(1)}, u32[]{:S(2)}, u32[]{:S(2)}) collective-permute-start(bf16[128,1024]{1,0:T(8,128)(2,1)S(1)} %bitcast.115), channel_id=1, source_target_pairs={{0,12},{4,0},{8,4},{12,8},{1,13},{5,1},{9,5},{13,9},{2,14},{6,2},{... | collective-permute-start | bytes 786440 | tf_op jit(solution)/shard_map/ppermute | solution.py:171
  36.1 3.6 %collective-permute-start.4 = (bf16[128,2048]{1,0:T(8,128)(2,1)S(1)}, bf16[128,2048]{1,0:T(8,128)(2,1)S(1)}, u32[]{:S(2)}, u32[]{:S(2)}) collective-permute-start(bf16[128,2048]{1,0:T(8,128)(2,1)S(1)} %convolution_convert_fusion.11), channel_id=1, source_target_pairs={{0,4},{1,5},{2,6},{3,7},{16,20},{17,21},{18,22},{19,23}} | collective-permute-start | bytes 1572872 | tf_op jit(solution)/shard_map/ppermute | solution.py:35
  38.3 13.0 %collective-permute-start.7 = (bf16[128,2048]{1,0:T(8,128)(2,1)S(1)}, bf16[128,2048]{1,0:T(8,128)(2,1)S(1)}, u32[]{:S(2)}, u32[]{:S(2)}) collective-permute-start(bf16[128,2048]{1,0:T(8,128)(2,1)S(1)} %convolution_convert_fusion.8), channel_id=1, source_target_pairs={{12,8},{13,9},{14,10},{15,11},{28,24},{29,25},{30,26},{31,27}} | collective-permute-start | bytes 1572872 | tf_op jit(solution)/shard_map/ppermute | solution.py:40
  41.0 16.1 %collective-permute-start.5 = (bf16[128,2048]{1,0:T(8,128)(2,1)S(1)}, bf16[128,2048]{1,0:T(8,128)(2,1)S(1)}, u32[]{:S(2)}, u32[]{:S(2)}) collective-permute-start(bf16[128,2048]{1,0:T(8,128)(2,1)S(1)} %fusion.12), channel_id=1, source_target_pairs={{0,4},{4,8},{1,5},{5,9},{2,6},{6,10},{3,7},{7,11},{16,20},{20,24},... | collective-permute-start | bytes 1572872 | tf_op jit(solution)/shard_map/ppermute | solution.py:35
  52.7 15.3 %collective-permute-start.8 = (bf16[128,2048]{1,0:T(8,128)(2,1)S(1)}, bf16[128,2048]{1,0:T(8,128)(2,1)S(1)}, u32[]{:S(2)}, u32[]{:S(2)}) collective-permute-start(bf16[128,2048]{1,0:T(8,128)(2,1)S(1)} %fusion.14), channel_id=1, source_target_pairs={{8,4},{12,8},{9,5},{13,9},{10,6},{14,10},{11,7},{15,11},{24,20},{2... | collective-permute-start | bytes 1572872 | tf_op jit(solution)/shard_map/ppermute | solution.py:40
  58.4 24.0 %collective-permute-start.6 = (bf16[128,2048]{1,0:T(8,128)(2,1)S(1)}, bf16[128,2048]{1,0:T(8,128)(2,1)S(1)}, u32[]{:S(2)}, u32[]{:S(2)}) collective-permute-start(bf16[128,2048]{1,0:T(8,128)(2,1)S(1)} %fusion.11), channel_id=1, source_target_pairs={{0,4},{4,8},{8,12},{1,5},{5,9},{9,13},{2,6},{6,10},{10,14},{3,7},{... | collective-permute-start | bytes 1572872 | tf_op jit(solution)/shard_map/ppermute | solution.py:35
  69.3 15.6 %collective-permute-start.9 = (bf16[128,2048]{1,0:T(8,128)(2,1)S(1)}, bf16[128,2048]{1,0:T(8,128)(2,1)S(1)}, u32[]{:S(2)}, u32[]{:S(2)}) collective-permute-start(bf16[128,2048]{1,0:T(8,128)(2,1)S(1)} %fusion.13), channel_id=1, source_target_pairs={{4,0},{8,4},{12,8},{5,1},{9,5},{13,9},{6,2},{10,6},{14,10},{7,3},{... | collective-permute-start | bytes 1572872 | tf_op jit(solution)/shard_map/ppermute | solution.py:40
  88.2 11.4 %collective-permute-start.10 = (bf16[64,2048]{1,0:T(8,128)(2,1)S(1)}, bf16[64,2048]{1,0:T(8,128)(2,1)S(1)}, u32[]{:S(2)}, u32[]{:S(2)}) collective-permute-start(bf16[64,2048]{1,0:T(8,128)(2,1)S(1)} %get-tuple-element.16), channel_id=1, source_target_pairs={{0,4},{4,8},{8,12},{12,0},{1,5},{5,9},{9,13},{13,1},{2,6},{6,10},{... | collective-permute-start | bytes 786440 | tf_op jit(solution)/shard_map/ppermute | solution.py:24
  92.8 20.2 %collective-permute-start.11 = (bf16[64,2048]{1,0:T(8,128)(2,1)S(1)}, bf16[64,2048]{1,0:T(8,128)(2,1)S(1)}, u32[]{:S(2)}, u32[]{:S(2)}) collective-permute-start(bf16[64,2048]{1,0:T(8,128)(2,1)S(1)} %get-tuple-element.15), channel_id=1, source_target_pairs={{0,8},{4,12},{8,0},{12,4},{1,9},{5,13},{9,1},{13,5},{2,10},{6,14},... | collective-permute-start | bytes 786440 | tf_op jit(solution)/shard_map/ppermute | solution.py:24
  92.8 20.2 %collective-permute-start.12 = (bf16[64,2048]{1,0:T(8,128)(2,1)S(1)}, bf16[64,2048]{1,0:T(8,128)(2,1)S(1)}, u32[]{:S(2)}, u32[]{:S(2)}) collective-permute-start(bf16[64,2048]{1,0:T(8,128)(2,1)S(1)} %get-tuple-element.14), channel_id=1, source_target_pairs={{0,12},{4,0},{8,4},{12,8},{1,13},{5,1},{9,5},{13,9},{2,14},{6,2},{... | collective-permute-start | bytes 786440 | tf_op jit(solution)/shard_map/ppermute | solution.py:24
  133.6 7.0 %collective-permute-start.13 = (bf16[64,2048]{1,0:T(8,128)(2,1)S(1)}, bf16[64,2048]{1,0:T(8,128)(2,1)S(1)}, u32[]{:S(2)}, u32[]{:S(2)}) collective-permute-start(bf16[64,2048]{1,0:T(8,128)(2,1)S(1)} %get-tuple-element.12), channel_id=1, source_target_pairs={{0,4},{4,8},{8,12},{12,0},{1,5},{5,9},{9,13},{13,1},{2,6},{6,10},{... | collective-permute-start | bytes 786440 | tf_op jit(solution)/shard_map/ppermute | solution.py:24
  133.7 25.7 %collective-permute-start.14 = (bf16[64,2048]{1,0:T(8,128)(2,1)S(1)}, bf16[64,2048]{1,0:T(8,128)(2,1)S(1)}, u32[]{:S(2)}, u32[]{:S(2)}) collective-permute-start(bf16[64,2048]{1,0:T(8,128)(2,1)S(1)} %get-tuple-element.11), channel_id=1, source_target_pairs={{0,8},{4,12},{8,0},{12,4},{1,9},{5,13},{9,1},{13,5},{2,10},{6,14},... | collective-permute-start | bytes 786440 | tf_op jit(solution)/shard_map/ppermute | solution.py:24
  136.5 22.9 %collective-permute-start.15 = (bf16[64,2048]{1,0:T(8,128)(2,1)S(1)}, bf16[64,2048]{1,0:T(8,128)(2,1)S(1)}, u32[]{:S(2)}, u32[]{:S(2)}) collective-permute-start(bf16[64,2048]{1,0:T(8,128)(2,1)S(1)} %get-tuple-element.10), channel_id=1, source_target_pairs={{0,12},{4,0},{8,4},{12,8},{1,13},{5,1},{9,5},{13,9},{2,14},{6,2},{... | collective-permute-start | bytes 786440 | tf_op jit(solution)/shard_map/ppermute | solution.py:24
  160.0 14.8 %collective-permute-start.16 = (bf16[128,2048]{1,0:T(8,128)(2,1)S(1)}, bf16[128,2048]{1,0:T(8,128)(2,1)S(1)}, u32[]{:S(2)}, u32[]{:S(2)}) collective-permute-start(bf16[128,2048]{1,0:T(8,128)(2,1)S(1)} %convolution_convert_fusion.15), channel_id=1, source_target_pairs={{0,4},{4,8},{8,12},{1,5},{5,9},{9,13},{2,6},{6,10},{10,14},{3,7},{... | collective-permute-start | bytes 1572872 | tf_op jit(solution)/shard_map/ppermute | solution.py:56
  161.3 14.8 %collective-permute-start.19 = (bf16[128,2048]{1,0:T(8,128)(2,1)S(1)}, bf16[128,2048]{1,0:T(8,128)(2,1)S(1)}, u32[]{:S(2)}, u32[]{:S(2)}) collective-permute-start(bf16[128,2048]{1,0:T(8,128)(2,1)S(1)} %convolution_convert_fusion.15), channel_id=1, source_target_pairs={{4,0},{8,4},{12,8},{5,1},{9,5},{13,9},{6,2},{10,6},{14,10},{7,3},{... | collective-permute-start | bytes 1572872 | tf_op jit(solution)/shard_map/ppermute | solution.py:57
  174.7 13.8 %collective-permute-start.17 = (bf16[128,2048]{1,0:T(8,128)(2,1)S(1)}, bf16[128,2048]{1,0:T(8,128)(2,1)S(1)}, u32[]{:S(2)}, u32[]{:S(2)}) collective-permute-start(bf16[128,2048]{1,0:T(8,128)(2,1)S(1)} %collective-permute-done.16), channel_id=1, source_target_pairs={{4,8},{8,12},{5,9},{9,13},{6,10},{10,14},{7,11},{11,15},{20,24},{2... | collective-permute-start | bytes 1572872 | tf_op jit(solution)/shard_map/ppermute | solution.py:56
  176.1 13.9 %collective-permute-start.20 = (bf16[128,2048]{1,0:T(8,128)(2,1)S(1)}, bf16[128,2048]{1,0:T(8,128)(2,1)}, u32[]{:S(2)}, u32[]{:S(2)}) collective-permute-start(bf16[128,2048]{1,0:T(8,128)(2,1)S(1)} %collective-permute-done.19), channel_id=1, source_target_pairs={{4,0},{8,4},{5,1},{9,5},{6,2},{10,6},{7,3},{11,7},{20,16},{24,20},... | collective-permute-start | bytes 1572872 | tf_op jit(solution)/shard_map/ppermute | solution.py:57
  188.6 13.0 %collective-permute-start.18 = (bf16[128,2048]{1,0:T(8,128)(2,1)S(1)}, bf16[128,2048]{1,0:T(8,128)(2,1)}, u32[]{:S(2)}, u32[]{:S(2)}) collective-permute-start(bf16[128,2048]{1,0:T(8,128)(2,1)S(1)} %collective-permute-done.17), channel_id=1, source_target_pairs={{8,12},{9,13},{10,14},{11,15},{24,28},{25,29},{26,30},{27,31}} | collective-permute-start | bytes 1572872 | tf_op jit(solution)/shard_map/ppermute | solution.py:56
  189.9 20.4 %collective-permute-start.21 = (bf16[128,2048]{1,0:T(8,128)(2,1)}, bf16[128,2048]{1,0:T(8,128)(2,1)S(1)}, u32[]{:S(2)}, u32[]{:S(2)}) collective-permute-start(bf16[128,2048]{1,0:T(8,128)(2,1)} %collective-permute-done.20), channel_id=1, source_target_pairs={{4,0},{5,1},{6,2},{7,3},{20,16},{21,17},{22,18},{23,19}} | collective-permute-start | bytes 1572872 | tf_op jit(solution)/shard_map/ppermute | solution.py:57
  216.8 2.9 %collective-permute-start.22 = (bf16[256,2048]{1,0:T(8,128)(2,1)S(1)}, bf16[256,2048]{1,0:T(8,128)(2,1)}, u32[]{:S(2)}, u32[]{:S(2)}) collective-permute-start(bf16[256,2048]{1,0:T(8,128)(2,1)S(1)} %dynamic-slice_bitcast_fusion), channel_id=1, source_target_pairs={{0,1},{1,0},{2,3},{3,2},{4,5},{5,4},{6,7},{7,6},{8,9},{9,8},{10,11... | collective-permute-start | bytes 3145736 | tf_op jit(solution)/shard_map/ppermute | solution.py:72
  221.3 14.0 %collective-permute-start.23 = (bf16[128,2048]{1,0:T(8,128)(2,1)S(1)}, bf16[128,2048]{1,0:T(8,128)(2,1)S(1)}, u32[]{:S(2)}, u32[]{:S(2)}) collective-permute-start(bf16[128,2048]{1,0:T(8,128)(2,1)S(1)} %dynamic-slice_bitcast_fusion.3), channel_id=1, source_target_pairs={{0,2},{2,0},{1,3},{3,1},{4,6},{6,4},{5,7},{7,5},{8,10},{10,8},{9,1... | collective-permute-start | bytes 1572872 | tf_op jit(solution)/shard_map/ppermute | solution.py:72
  235.5 21.5 %collective-permute-start.24 = (bf16[128,2048]{1,0:T(8,128)(2,1)S(1)}, bf16[128,2048]{1,0:T(8,128)(2,1)S(1)}, u32[]{:S(2)}, u32[]{:S(2)}) collective-permute-start(bf16[128,2048]{1,0:T(8,128)(2,1)S(1)} %fusion.34), channel_id=1, source_target_pairs={{0,0},{1,8},{2,4},{3,12},{4,1},{5,9},{6,5},{7,13},{8,2},{9,10},{10... | collective-permute-start | bytes 1572872 | tf_op jit(solution)/shard_map/ppermute | solution.py:272
  (15 other events, 192.7 us)

commit v10 on v9

--- a/solution.py
+++ b/solution.py
@@ -250,30 +250,33 @@
     hs_index = lax.axis_index("head") * sub_count + sub_index
     head_count = lax.axis_size("head")
     by_group = partial_cols.reshape(sub_count, -1, partial_cols.shape[1])
-    owner_sums = exchange_sum(by_group, "sub", sub_count, sub_index)
-    owner_sums = owner_sums.reshape(head_count, -1, partial_cols.shape[1])
-    owner_sums = exchange_sum(owner_sums, "head", head_count, lax.axis_index("head"))
+    sub_sums = exchange_sum(by_group, "sub", sub_count, sub_index)
     per_hs = req_count // hs_count
     out_block = partial_cols.shape[1]
-    owner_sums = owner_sums.reshape(per_hs, local_rows, out_block)
-    arrived_blocks = []
+    sub_sums = sub_sums.reshape(head_count, per_hs, local_rows, out_block)
+    head_index = lax.axis_index("head")
+    head_total = jnp.zeros((local_rows, per_hs * out_block), jnp.float32)
     for step in range(per_hs):
-        chunk = lax.dynamic_index_in_dim(
-            owner_sums, (req_index + step) % per_hs, axis=0, keepdims=False
-        )
-        pairs = []
-        for c in range(req_count):
-            for h in range(head_count):
-                for u in range(sub_count):
-                    j = u * head_count + h
-                    k = j * per_hs + (c + step) % per_hs
-                    src = c * hs_count + h * sub_count + u
-                    pairs.append((src, k * hs_count + c // per_hs))
-        arrived_blocks.append(lax.ppermute(chunk, ("req", "head", "sub"), pairs))
-    stacked = jnp.stack(arrived_blocks)
-    order = (req_index % per_hs - jnp.arange(per_hs)) % per_hs
-    head_total = jnp.take(stacked, order, axis=0)
-    head_total = jnp.transpose(head_total, (1, 0, 2)).reshape(local_rows, per_hs * out_block)
+        gathered = None
+        for turn in range(head_count):
+            group = (head_index + turn) % head_count
+            chunk = lax.dynamic_index_in_dim(sub_sums, group, 0, keepdims=False)
+            chunk = lax.dynamic_index_in_dim(
+                chunk, (req_index + step) % per_hs, 0, keepdims=False
+            )
+            pairs = []
+            for c in range(req_count):
+                for h in range(head_count):
+                    for u in range(sub_count):
+                        g = (h + turn) % head_count
+                        k = (u * head_count + g) * per_hs + (c + step) % per_hs
+                        src = c * hs_count + h * sub_count + u
+                        pairs.append((src, k * hs_count + c // per_hs))
+            got = lax.ppermute(chunk, ("req", "head", "sub"), pairs).astype(jnp.float32)
+            gathered = got if gathered is None else gathered + got
+        head_total = lax.dynamic_update_slice_in_dim(
+            head_total, gathered, ((req_index % per_hs - step) % per_hs) * out_block, 1
+        )
     head_total = head_total.astype(jnp.float32)
     out_width = head_total.shape[1]
     residual = lax.dynamic_slice_in_dim(hidden_in, hs_index * out_width, out_width, 1)

time: 260 us -> 253 us (0.973)
  the two profiles are of different devices: /device:TPU:26 before, /device:TPU:6 now
where the time goes in v10:
time: 253 us; the launch traced here: 251 us
  waiting for transfers between devices  135 us (53%)
  starting transfers between devices  53.3 us (21%)
  matrix products  27.5 us (11%)
  Pallas kernels  18.2 us (7%)
  local copies, waits for them, and re-layouts  10.2 us (4%)
  other arithmetic  6.09 us (2%)
    ppermute x2, waiting for transfers between devices, local(): got = lax.ppermute(chunk, ('req', 'head', 'sub'), pairs).astype(jnp.float32)  30.8 us
    ppermute x6, waiting for transfers between devices, shift_exchange(): lax.ppermute(blocks[shift], axis, [(i, (i + shift) % count) for i in rang...  27 us
    ppermute x3, waiting for transfers between devices, line_reduce_scatter(): lax.ppermute(send_r.astype(jnp.bfloat16), axis, [(i, i + 1) for i in rang...  24.7 us
    ppermute x3, waiting for transfers between devices, line_gather_apply(): lax.ppermute(carry_l, axis, [(i, i - 1) for i in range(1, count - step +...  18.4 us
    pallas_call x1, Pallas kernels, attend(): pl.pallas_call(kernel, grid=(kv_count,), in_specs=[pl.BlockSpec((rows, gr...  18.2 us
    ppermute x3, starting transfers between devices, line_reduce_scatter(): lax.ppermute(send_r.astype(jnp.bfloat16), axis, [(i, i + 1) for i in rang...  16.8 us
    ppermute x3, waiting for transfers between devices, local(): lax.ppermute(outgoing_part, 'req', [(i, (i + shift) % req_count) for i in...  14.9 us
    dot_general x7, matrix products, out_part(): product = jnp.dot(rows, out_weight, preferred_element_type=jnp.float32)  13.8 us
  transfers between devices with their start and end apart: 25, of which 19 were waited for; matrix products, arithmetic and copies ran while one was open for 7% of the time, Pallas kernels for 0%

profile of v10, /device:TPU:6, one launch (start us, length us, event | category | flops | bytes accessed | tf_op | source)
XLA Modules:
  0.0 250.9 jit_solution(14316718258849882017)
XLA Ops:
  9.9 4.8 %collective-permute-done = bf16[128,1024]{1,0:T(8,128)(2,1)S(1)} collective-permute-done((bf16[128,1024]{1,0:T(8,128)(2,1)S(1)}, bf16[128,1024]{1,0:T(8,128)(2,1)S(1)}, u32[]{:S(2)}, u32[]{:S(2)}) %collective-permute-start) | collective-permute-done | bytes 262176 | tf_op jit(solution)/shard_map/ppermute | solution.py:171
  14.7 10.1 %collective-permute-done.1 = bf16[128,1024]{1,0:T(8,128)(2,1)S(1)} collective-permute-done((bf16[128,1024]{1,0:T(8,128)(2,1)S(1)}, bf16[128,1024]{1,0:T(8,128)(2,1)S(1)}, u32[]{:S(2)}, u32[]{:S(2)}) %collective-permute-start.1) | collective-permute-done | bytes 262176 | tf_op jit(solution)/shard_map/ppermute | solution.py:171
  27.8 4.8 %convolution_convert_fusion.11 = bf16[128,2048]{1,0:T(8,128)(2,1)S(1)} fusion(bf16[2048,2048]{1,0:T(8,128)(2,1)} %param.10, bf16[512,2048]{1,0:T(8,128)(2,1)S(1)} %constant_dynamic-update-slice_fusion, s32[]{:T(128)S(6)} %select_n.205), kind=kOutput, calls=%fused_computation.15 | convolution fusion | flops 1074003968 | bytes 9437188 | tf_op jit(solution)/shard_map/dot_general | solution.py:191
  32.6 8.0 %collective-permute-start.4 = (bf16[128,2048]{1,0:T(8,128)(2,1)S(1)}, bf16[128,2048]{1,0:T(8,128)(2,1)S(1)}, u32[]{:S(2)}, u32[]{:S(2)}) collective-permute-start(bf16[128,2048]{1,0:T(8,128)(2,1)S(1)} %convolution_convert_fusion.11), channel_id=1, source_target_pairs={{0,4},{1,5},{2,6},{3,7},{16,20},{17,21},{18,22},{19,23}} | collective-permute-start | bytes 1572872 | tf_op jit(solution)/shard_map/ppermute | solution.py:35
  42.6 9.4 %collective-permute-done.4 = bf16[128,2048]{1,0:T(8,128)(2,1)S(1)} collective-permute-done((bf16[128,2048]{1,0:T(8,128)(2,1)S(1)}, bf16[128,2048]{1,0:T(8,128)(2,1)S(1)}, u32[]{:S(2)}, u32[]{:S(2)}) %collective-permute-start.4) | collective-permute-done | bytes 524320 | tf_op jit(solution)/shard_map/ppermute | solution.py:35
  53.3 4.4 %collective-permute-start.5 = (bf16[128,2048]{1,0:T(8,128)(2,1)S(1)}, bf16[128,2048]{1,0:T(8,128)(2,1)S(1)}, u32[]{:S(2)}, u32[]{:S(2)}) collective-permute-start(bf16[128,2048]{1,0:T(8,128)(2,1)S(1)} %fusion.12), channel_id=1, source_target_pairs={{0,4},{4,8},{1,5},{5,9},{2,6},{6,10},{3,7},{7,11},{16,20},{20,24},... | collective-permute-start | bytes 1572872 | tf_op jit(solution)/shard_map/ppermute | solution.py:35
  59.8 8.6 %collective-permute-done.5 = bf16[128,2048]{1,0:T(8,128)(2,1)S(1)} collective-permute-done((bf16[128,2048]{1,0:T(8,128)(2,1)S(1)}, bf16[128,2048]{1,0:T(8,128)(2,1)S(1)}, u32[]{:S(2)}, u32[]{:S(2)}) %collective-permute-start.5) | collective-permute-done | bytes 524320 | tf_op jit(solution)/shard_map/ppermute | solution.py:35
  69.7 4.4 %collective-permute-start.6 = (bf16[128,2048]{1,0:T(8,128)(2,1)S(1)}, bf16[128,2048]{1,0:T(8,128)(2,1)S(1)}, u32[]{:S(2)}, u32[]{:S(2)}) collective-permute-start(bf16[128,2048]{1,0:T(8,128)(2,1)S(1)} %fusion.11), channel_id=1, source_target_pairs={{0,4},{4,8},{8,12},{1,5},{5,9},{9,13},{2,6},{6,10},{10,14},{3,7},{... | collective-permute-start | bytes 1572872 | tf_op jit(solution)/shard_map/ppermute | solution.py:35
  77.1 6.7 %collective-permute-done.6 = bf16[128,2048]{1,0:T(8,128)(2,1)S(1)} collective-permute-done((bf16[128,2048]{1,0:T(8,128)(2,1)S(1)}, bf16[128,2048]{1,0:T(8,128)(2,1)S(1)}, u32[]{:S(2)}, u32[]{:S(2)}) %collective-permute-start.6) | collective-permute-done | bytes 524320 | tf_op jit(solution)/shard_map/ppermute | solution.py:35
  83.8 5.5 %collective-permute-done.9 = bf16[128,2048]{1,0:T(8,128)(2,1)S(1)} collective-permute-done((bf16[128,2048]{1,0:T(8,128)(2,1)S(1)}, bf16[128,2048]{1,0:T(8,128)(2,1)S(1)}, u32[]{:S(2)}, u32[]{:S(2)}) %collective-permute-start.9) | collective-permute-done | bytes 524320 | tf_op jit(solution)/shard_map/ppermute | solution.py:40
  98.5 5.2 %collective-permute-done.10 = bf16[64,2048]{1,0:T(8,128)(2,1)S(1)} collective-permute-done((bf16[64,2048]{1,0:T(8,128)(2,1)S(1)}, bf16[64,2048]{1,0:T(8,128)(2,1)S(1)}, u32[]{:S(2)}, u32[]{:S(2)}) %collective-permute-start.10) | collective-permute-done | bytes 262176 | tf_op jit(solution)/shard_map/ppermute | solution.py:24
  103.7 7.6 %collective-permute-done.11 = bf16[64,2048]{1,0:T(8,128)(2,1)S(1)} collective-permute-done((bf16[64,2048]{1,0:T(8,128)(2,1)S(1)}, bf16[64,2048]{1,0:T(8,128)(2,1)S(1)}, u32[]{:S(2)}, u32[]{:S(2)}) %collective-permute-start.11) | collective-permute-done | bytes 262176 | tf_op jit(solution)/shard_map/ppermute | solution.py:24
  112.4 18.2 %shard_map.91 = bf16[256,2048]{1,0:T(8,128)(2,1)} custom-call(bf16[256,2048]{1,0:T(8,128)(2,1)} %bitcast.112, bf16[1664,256]{1,0:T(8,128)(2,1)} %pad.7.k_ref, bf16[1664,256]{1,0:T(8,128)(2,1)} %pad.8.v_ref), custom_call_target="tpu_custom_call" | custom-call | flops 3489660928 | bytes 3801088 | tf_op jit(solution)/shard_map/pallas_call | solution.py:121
  131.9 5.7 %collective-permute-start.13 = (bf16[64,2048]{1,0:T(8,128)(2,1)S(1)}, bf16[64,2048]{1,0:T(8,128)(2,1)S(1)}, u32[]{:S(2)}, u32[]{:S(2)}) collective-permute-start(bf16[64,2048]{1,0:T(8,128)(2,1)S(1)} %get-tuple-element.14), channel_id=1, source_target_pairs={{0,4},{4,8},{8,12},{12,0},{1,5},{5,9},{9,13},{13,1},{2,6},{6,10},{... | collective-permute-start | bytes 786440 | tf_op jit(solution)/shard_map/ppermute | solution.py:24
  140.0 4.3 %collective-permute-done.13 = bf16[64,2048]{1,0:T(8,128)(2,1)S(1)} collective-permute-done((bf16[64,2048]{1,0:T(8,128)(2,1)S(1)}, bf16[64,2048]{1,0:T(8,128)(2,1)S(1)}, u32[]{:S(2)}, u32[]{:S(2)}) %collective-permute-start.13) | collective-permute-done | bytes 262176 | tf_op jit(solution)/shard_map/ppermute | solution.py:24
  144.3 8.6 %collective-permute-done.14 = bf16[64,2048]{1,0:T(8,128)(2,1)S(1)} collective-permute-done((bf16[64,2048]{1,0:T(8,128)(2,1)S(1)}, bf16[64,2048]{1,0:T(8,128)(2,1)S(1)}, u32[]{:S(2)}, u32[]{:S(2)}) %collective-permute-start.14) | collective-permute-done | bytes 262176 | tf_op jit(solution)/shard_map/ppermute | solution.py:24
  154.9 7.8 %collective-permute-start.16 = (bf16[128,2048]{1,0:T(8,128)(2,1)S(1)}, bf16[128,2048]{1,0:T(8,128)(2,1)S(1)}, u32[]{:S(2)}, u32[]{:S(2)}) collective-permute-start(bf16[128,2048]{1,0:T(8,128)(2,1)S(1)} %convolution_convert_fusion.15), channel_id=1, source_target_pairs={{0,4},{4,8},{8,12},{1,5},{5,9},{9,13},{2,6},{6,10},{10,14},{3,7},{... | collective-permute-start | bytes 1572872 | tf_op jit(solution)/shard_map/ppermute | solution.py:56
  164.0 9.0 %collective-permute-done.16 = bf16[128,2048]{1,0:T(8,128)(2,1)S(1)} collective-permute-done((bf16[128,2048]{1,0:T(8,128)(2,1)S(1)}, bf16[128,2048]{1,0:T(8,128)(2,1)S(1)}, u32[]{:S(2)}, u32[]{:S(2)}) %collective-permute-start.16) | collective-permute-done | bytes 524320 | tf_op jit(solution)/shard_map/ppermute | solution.py:56
  173.7 3.5 %collective-permute-done.19 = bf16[128,2048]{1,0:T(8,128)(2,1)S(1)} collective-permute-done((bf16[128,2048]{1,0:T(8,128)(2,1)S(1)}, bf16[128,2048]{1,0:T(8,128)(2,1)S(1)}, u32[]{:S(2)}, u32[]{:S(2)}) %collective-permute-start.19) | collective-permute-done | bytes 524320 | tf_op jit(solution)/shard_map/ppermute | solution.py:57
  179.9 11.6 %collective-permute-done.20 = bf16[128,2048]{1,0:T(8,128)(2,1)} collective-permute-done((bf16[128,2048]{1,0:T(8,128)(2,1)S(1)}, bf16[128,2048]{1,0:T(8,128)(2,1)}, u32[]{:S(2)}, u32[]{:S(2)}) %collective-permute-start.20) | collective-permute-done | bytes 524320 | tf_op jit(solution)/shard_map/ppermute | solution.py:57
  193.1 5.0 %fusion.17 = bf16[4,128,2048]{2,1,0:T(8,128)(2,1)S(1)} fusion(bf16[4,128,2048]{2,1,0:T(8,128)(2,1)S(1)} %broadcast_in_dim.65, s32[]{:T(128)S(6)} %select_n.211, bf16[128,2048]{1,0:T(8,128)(2,1)} %collective-permute-done.18, bf16[2048,2048]{1,0:T(8,128)(2,1)} %param.14), kind=kOutput, calls=%fused_computation.33 | convolution fusion | flops 1074003968 | bytes 9437188 | tf_op jit(solution)/shard_map/dot_general | solution.py:244
  201.6 3.4 %collective-permute-done.21 = bf16[128,2048]{1,0:T(8,128)(2,1)S(1)} collective-permute-done((bf16[128,2048]{1,0:T(8,128)(2,1)}, bf16[128,2048]{1,0:T(8,128)(2,1)S(1)}, u32[]{:S(2)}, u32[]{:S(2)}) %collective-permute-start.21) | collective-permute-done | bytes 524320 | tf_op jit(solution)/shard_map/ppermute | solution.py:57
  218.0 17.8 %collective-permute-done.23 = bf16[128,2048]{1,0:T(8,128)(2,1)S(1)} collective-permute-done((bf16[128,2048]{1,0:T(8,128)(2,1)S(1)}, bf16[128,2048]{1,0:T(8,128)(2,1)S(1)}, u32[]{:S(2)}, u32[]{:S(2)}) %collective-permute-start.23) | collective-permute-done | bytes 524320 | tf_op jit(solution)/shard_map/ppermute | solution.py:275
  235.8 13.0 %collective-permute-done.24 = bf16[128,2048]{1,0:T(8,128)(2,1)S(1)} collective-permute-done((bf16[128,2048]{1,0:T(8,128)(2,1)S(1)}, bf16[128,2048]{1,0:T(8,128)(2,1)S(1)}, u32[]{:S(2)}, u32[]{:S(2)}) %collective-permute-start.24) | collective-permute-done | bytes 524320 | tf_op jit(solution)/shard_map/ppermute | solution.py:275
  (115 shorter events, 62.8 us)
Async XLA Ops:
  3.5 11.2 %collective-permute-start = (bf16[128,1024]{1,0:T(8,128)(2,1)S(1)}, bf16[128,1024]{1,0:T(8,128)(2,1)S(1)}, u32[]{:S(2)}, u32[]{:S(2)}) collective-permute-start(bf16[128,1024]{1,0:T(8,128)(2,1)S(1)} %bitcast.115), channel_id=1, source_target_pairs={{0,4},{4,8},{8,12},{12,0},{1,5},{5,9},{9,13},{13,1},{2,6},{6,10},{... | collective-permute-start | bytes 786440 | tf_op jit(solution)/shard_map/ppermute | solution.py:171
  5.3 19.5 %collective-permute-start.1 = (bf16[128,1024]{1,0:T(8,128)(2,1)S(1)}, bf16[128,1024]{1,0:T(8,128)(2,1)S(1)}, u32[]{:S(2)}, u32[]{:S(2)}) collective-permute-start(bf16[128,1024]{1,0:T(8,128)(2,1)S(1)} %bitcast.114), channel_id=1, source_target_pairs={{0,8},{4,12},{8,0},{12,4},{1,9},{5,13},{9,1},{13,5},{2,10},{6,14},... | collective-permute-start | bytes 786440 | tf_op jit(solution)/shard_map/ppermute | solution.py:171
  8.1 16.8 %collective-permute-start.2 = (bf16[128,1024]{1,0:T(8,128)(2,1)S(1)}, bf16[128,1024]{1,0:T(8,128)(2,1)S(1)}, u32[]{:S(2)}, u32[]{:S(2)}) collective-permute-start(bf16[128,1024]{1,0:T(8,128)(2,1)S(1)} %bitcast.113), channel_id=1, source_target_pairs={{0,12},{4,0},{8,4},{12,8},{1,13},{5,1},{9,5},{13,9},{2,14},{6,2},{... | collective-permute-start | bytes 786440 | tf_op jit(solution)/shard_map/ppermute | solution.py:171
  32.6 19.4 %collective-permute-start.4 = (bf16[128,2048]{1,0:T(8,128)(2,1)S(1)}, bf16[128,2048]{1,0:T(8,128)(2,1)S(1)}, u32[]{:S(2)}, u32[]{:S(2)}) collective-permute-start(bf16[128,2048]{1,0:T(8,128)(2,1)S(1)} %convolution_convert_fusion.11), channel_id=1, source_target_pairs={{0,4},{1,5},{2,6},{3,7},{16,20},{17,21},{18,22},{19,23}} | collective-permute-start | bytes 1572872 | tf_op jit(solution)/shard_map/ppermute | solution.py:35
  41.9 15.9 %collective-permute-start.7 = (bf16[128,2048]{1,0:T(8,128)(2,1)S(1)}, bf16[128,2048]{1,0:T(8,128)(2,1)S(1)}, u32[]{:S(2)}, u32[]{:S(2)}) collective-permute-start(bf16[128,2048]{1,0:T(8,128)(2,1)S(1)} %convolution_convert_fusion.8), channel_id=1, source_target_pairs={{12,8},{13,9},{14,10},{15,11},{28,24},{29,25},{30,26},{31,27}} | collective-permute-start | bytes 1572872 | tf_op jit(solution)/shard_map/ppermute | solution.py:40
  53.3 15.0 %collective-permute-start.5 = (bf16[128,2048]{1,0:T(8,128)(2,1)S(1)}, bf16[128,2048]{1,0:T(8,128)(2,1)S(1)}, u32[]{:S(2)}, u32[]{:S(2)}) collective-permute-start(bf16[128,2048]{1,0:T(8,128)(2,1)S(1)} %fusion.12), channel_id=1, source_target_pairs={{0,4},{4,8},{1,5},{5,9},{2,6},{6,10},{3,7},{7,11},{16,20},{20,24},... | collective-permute-start | bytes 1572872 | tf_op jit(solution)/shard_map/ppermute | solution.py:35
  59.1 15.0 %collective-permute-start.8 = (bf16[128,2048]{1,0:T(8,128)(2,1)S(1)}, bf16[128,2048]{1,0:T(8,128)(2,1)S(1)}, u32[]{:S(2)}, u32[]{:S(2)}) collective-permute-start(bf16[128,2048]{1,0:T(8,128)(2,1)S(1)} %fusion.14), channel_id=1, source_target_pairs={{8,4},{12,8},{9,5},{13,9},{10,6},{14,10},{11,7},{15,11},{24,20},{2... | collective-permute-start | bytes 1572872 | tf_op jit(solution)/shard_map/ppermute | solution.py:40
  69.7 14.1 %collective-permute-start.6 = (bf16[128,2048]{1,0:T(8,128)(2,1)S(1)}, bf16[128,2048]{1,0:T(8,128)(2,1)S(1)}, u32[]{:S(2)}, u32[]{:S(2)}) collective-permute-start(bf16[128,2048]{1,0:T(8,128)(2,1)S(1)} %fusion.11), channel_id=1, source_target_pairs={{0,4},{4,8},{8,12},{1,5},{5,9},{9,13},{2,6},{6,10},{10,14},{3,7},{... | collective-permute-start | bytes 1572872 | tf_op jit(solution)/shard_map/ppermute | solution.py:35
  75.4 13.8 %collective-permute-start.9 = (bf16[128,2048]{1,0:T(8,128)(2,1)S(1)}, bf16[128,2048]{1,0:T(8,128)(2,1)S(1)}, u32[]{:S(2)}, u32[]{:S(2)}) collective-permute-start(bf16[128,2048]{1,0:T(8,128)(2,1)S(1)} %fusion.13), channel_id=1, source_target_pairs={{4,0},{8,4},{12,8},{5,1},{9,5},{13,9},{6,2},{10,6},{14,10},{7,3},{... | collective-permute-start | bytes 1572872 | tf_op jit(solution)/shard_map/ppermute | solution.py:40
  92.6 11.2 %collective-permute-start.10 = (bf16[64,2048]{1,0:T(8,128)(2,1)S(1)}, bf16[64,2048]{1,0:T(8,128)(2,1)S(1)}, u32[]{:S(2)}, u32[]{:S(2)}) collective-permute-start(bf16[64,2048]{1,0:T(8,128)(2,1)S(1)} %get-tuple-element.18), channel_id=1, source_target_pairs={{0,4},{4,8},{8,12},{12,0},{1,5},{5,9},{9,13},{13,1},{2,6},{6,10},{... | collective-permute-start | bytes 786440 | tf_op jit(solution)/shard_map/ppermute | solution.py:24
  93.2 18.1 %collective-permute-start.11 = (bf16[64,2048]{1,0:T(8,128)(2,1)S(1)}, bf16[64,2048]{1,0:T(8,128)(2,1)S(1)}, u32[]{:S(2)}, u32[]{:S(2)}) collective-permute-start(bf16[64,2048]{1,0:T(8,128)(2,1)S(1)} %get-tuple-element.17), channel_id=1, source_target_pairs={{0,8},{4,12},{8,0},{12,4},{1,9},{5,13},{9,1},{13,5},{2,10},{6,14},... | collective-permute-start | bytes 786440 | tf_op jit(solution)/shard_map/ppermute | solution.py:24
  93.2 18.1 %collective-permute-start.12 = (bf16[64,2048]{1,0:T(8,128)(2,1)S(1)}, bf16[64,2048]{1,0:T(8,128)(2,1)S(1)}, u32[]{:S(2)}, u32[]{:S(2)}) collective-permute-start(bf16[64,2048]{1,0:T(8,128)(2,1)S(1)} %get-tuple-element.16), channel_id=1, source_target_pairs={{0,12},{4,0},{8,4},{12,8},{1,13},{5,1},{9,5},{13,9},{2,14},{6,2},{... | collective-permute-start | bytes 786440 | tf_op jit(solution)/shard_map/ppermute | solution.py:24
  131.9 12.5 %collective-permute-start.13 = (bf16[64,2048]{1,0:T(8,128)(2,1)S(1)}, bf16[64,2048]{1,0:T(8,128)(2,1)S(1)}, u32[]{:S(2)}, u32[]{:S(2)}) collective-permute-start(bf16[64,2048]{1,0:T(8,128)(2,1)S(1)} %get-tuple-element.14), channel_id=1, source_target_pairs={{0,4},{4,8},{8,12},{12,0},{1,5},{5,9},{9,13},{13,1},{2,6},{6,10},{... | collective-permute-start | bytes 786440 | tf_op jit(solution)/shard_map/ppermute | solution.py:24
  137.6 15.3 %collective-permute-start.14 = (bf16[64,2048]{1,0:T(8,128)(2,1)S(1)}, bf16[64,2048]{1,0:T(8,128)(2,1)S(1)}, u32[]{:S(2)}, u32[]{:S(2)}) collective-permute-start(bf16[64,2048]{1,0:T(8,128)(2,1)S(1)} %get-tuple-element.13), channel_id=1, source_target_pairs={{0,8},{4,12},{8,0},{12,4},{1,9},{5,13},{9,1},{13,5},{2,10},{6,14},... | collective-permute-start | bytes 786440 | tf_op jit(solution)/shard_map/ppermute | solution.py:24
  137.8 16.4 %collective-permute-start.15 = (bf16[64,2048]{1,0:T(8,128)(2,1)S(1)}, bf16[64,2048]{1,0:T(8,128)(2,1)S(1)}, u32[]{:S(2)}, u32[]{:S(2)}) collective-permute-start(bf16[64,2048]{1,0:T(8,128)(2,1)S(1)} %get-tuple-element.12), channel_id=1, source_target_pairs={{0,12},{4,0},{8,4},{12,8},{1,13},{5,1},{9,5},{13,9},{2,14},{6,2},{... | collective-permute-start | bytes 786440 | tf_op jit(solution)/shard_map/ppermute | solution.py:24
  154.9 18.1 %collective-permute-start.16 = (bf16[128,2048]{1,0:T(8,128)(2,1)S(1)}, bf16[128,2048]{1,0:T(8,128)(2,1)S(1)}, u32[]{:S(2)}, u32[]{:S(2)}) collective-permute-start(bf16[128,2048]{1,0:T(8,128)(2,1)S(1)} %convolution_convert_fusion.15), channel_id=1, source_target_pairs={{0,4},{4,8},{8,12},{1,5},{5,9},{9,13},{2,6},{6,10},{10,14},{3,7},{... | collective-permute-start | bytes 1572872 | tf_op jit(solution)/shard_map/ppermute | solution.py:56
  162.7 14.5 %collective-permute-start.19 = (bf16[128,2048]{1,0:T(8,128)(2,1)S(1)}, bf16[128,2048]{1,0:T(8,128)(2,1)S(1)}, u32[]{:S(2)}, u32[]{:S(2)}) collective-permute-start(bf16[128,2048]{1,0:T(8,128)(2,1)S(1)} %convolution_convert_fusion.15), channel_id=1, source_target_pairs={{4,0},{8,4},{12,8},{5,1},{9,5},{13,9},{6,2},{10,6},{14,10},{7,3},{... | collective-permute-start | bytes 1572872 | tf_op jit(solution)/shard_map/ppermute | solution.py:57
  173.0 5.4 %collective-permute-start.17 = (bf16[128,2048]{1,0:T(8,128)(2,1)S(1)}, bf16[128,2048]{1,0:T(8,128)(2,1)S(1)}, u32[]{:S(2)}, u32[]{:S(2)}) collective-permute-start(bf16[128,2048]{1,0:T(8,128)(2,1)S(1)} %collective-permute-done.16), channel_id=1, source_target_pairs={{4,8},{8,12},{5,9},{9,13},{6,10},{10,14},{7,11},{11,15},{20,24},{2... | collective-permute-start | bytes 1572872 | tf_op jit(solution)/shard_map/ppermute | solution.py:56
  177.1 14.4 %collective-permute-start.20 = (bf16[128,2048]{1,0:T(8,128)(2,1)S(1)}, bf16[128,2048]{1,0:T(8,128)(2,1)}, u32[]{:S(2)}, u32[]{:S(2)}) collective-permute-start(bf16[128,2048]{1,0:T(8,128)(2,1)S(1)} %collective-permute-done.19), channel_id=1, source_target_pairs={{4,0},{8,4},{5,1},{9,5},{6,2},{10,6},{7,3},{11,7},{20,16},{24,20},... | collective-permute-start | bytes 1572872 | tf_op jit(solution)/shard_map/ppermute | solution.py:57
  178.5 14.4 %collective-permute-start.18 = (bf16[128,2048]{1,0:T(8,128)(2,1)S(1)}, bf16[128,2048]{1,0:T(8,128)(2,1)}, u32[]{:S(2)}, u32[]{:S(2)}) collective-permute-start(bf16[128,2048]{1,0:T(8,128)(2,1)S(1)} %collective-permute-done.17), channel_id=1, source_target_pairs={{8,12},{9,13},{10,14},{11,15},{24,28},{25,29},{26,30},{27,31}} | collective-permute-start | bytes 1572872 | tf_op jit(solution)/shard_map/ppermute | solution.py:56
  191.5 13.4 %collective-permute-start.21 = (bf16[128,2048]{1,0:T(8,128)(2,1)}, bf16[128,2048]{1,0:T(8,128)(2,1)S(1)}, u32[]{:S(2)}, u32[]{:S(2)}) collective-permute-start(bf16[128,2048]{1,0:T(8,128)(2,1)} %collective-permute-done.20), channel_id=1, source_target_pairs={{4,0},{5,1},{6,2},{7,3},{20,16},{21,17},{22,18},{23,19}} | collective-permute-start | bytes 1572872 | tf_op jit(solution)/shard_map/ppermute | solution.py:57
  211.4 2.9 %collective-permute-start.22 = (bf16[256,2048]{1,0:T(8,128)(2,1)S(1)}, bf16[256,2048]{1,0:T(8,128)(2,1)}, u32[]{:S(2)}, u32[]{:S(2)}) collective-permute-start(bf16[256,2048]{1,0:T(8,128)(2,1)S(1)} %dynamic-slice_bitcast_fusion), channel_id=1, source_target_pairs={{0,1},{1,0},{2,3},{3,2},{4,5},{5,4},{6,7},{7,6},{8,9},{9,8},{10,11... | collective-permute-start | bytes 3145736 | tf_op jit(solution)/shard_map/ppermute | solution.py:72
  215.9 19.8 %collective-permute-start.23 = (bf16[128,2048]{1,0:T(8,128)(2,1)S(1)}, bf16[128,2048]{1,0:T(8,128)(2,1)S(1)}, u32[]{:S(2)}, u32[]{:S(2)}) collective-permute-start(bf16[128,2048]{1,0:T(8,128)(2,1)S(1)} %get-tuple-element.9), channel_id=1, source_target_pairs={{0,0},{1,8},{2,4},{3,12},{4,1},{5,9},{6,5},{7,13},{8,2},{9,10},{10... | collective-permute-start | bytes 1572872 | tf_op jit(solution)/shard_map/ppermute | solution.py:275
  217.9 30.9 %collective-permute-start.24 = (bf16[128,2048]{1,0:T(8,128)(2,1)S(1)}, bf16[128,2048]{1,0:T(8,128)(2,1)S(1)}, u32[]{:S(2)}, u32[]{:S(2)}) collective-permute-start(bf16[128,2048]{1,0:T(8,128)(2,1)S(1)} %get-tuple-element.10), channel_id=1, source_target_pairs={{0,4},{1,12},{2,0},{3,8},{4,5},{5,13},{6,1},{7,9},{8,6},{9,14},{10... | collective-permute-start | bytes 1572872 | tf_op jit(solution)/shard_map/ppermute | solution.py:275
  (15 other events, 203.0 us)

commit v11 on v10

--- a/solution.py
+++ b/solution.py
@@ -26,43 +26,27 @@
     return jnp.stack(arrived)
 
 
-def line_reduce_scatter(chunk_of, axis, count, index):
-    right = None
-    left = None
-    for step in range(1, count):
-        dest_r = jnp.minimum(count - step + index, count - 1)
-        send_r = chunk_of(dest_r) if right is None else chunk_of(dest_r) + right
-        right = lax.ppermute(
-            send_r.astype(jnp.bfloat16), axis, [(i, i + 1) for i in range(step)]
-        ).astype(jnp.float32)
-        dest_l = jnp.maximum(index - (count - step), 0)
-        send_l = chunk_of(dest_l) if left is None else chunk_of(dest_l) + left
-        left = lax.ppermute(
-            send_l.astype(jnp.bfloat16), axis, [(i, i - 1) for i in range(count - step, count)]
-        ).astype(jnp.float32)
-    total = chunk_of(index)
-    if right is not None:
-        total = total + right + left
-    return total
-
-
-def line_gather_apply(block, apply, axis, count, index):
+def direct_reduce_scatter(chunk_of, axis, count, index):
+    total = None
+    for shift in range(1, count):
+        outgoing = chunk_of((index + shift) % count).astype(jnp.bfloat16)
+        incoming = lax.ppermute(outgoing, axis, [(i, (i + shift) % count) for i in range(count)])
+        incoming = incoming.astype(jnp.float32)
+        total = incoming if total is None else total + incoming
+    own = chunk_of(index)
+    return own if total is None else own + total
+
+
+def direct_gather_apply(block, apply, axis, count, index):
     own = apply(block)
-    from_left = [own]
-    from_right = [own]
-    carry_r = block
-    carry_l = block
-    for step in range(1, count):
-        carry_r = lax.ppermute(carry_r, axis, [(i, i + 1) for i in range(step - 1, count - 1)])
-        carry_l = lax.ppermute(carry_l, axis, [(i, i - 1) for i in range(1, count - step + 1)])
-        from_left.append(apply(carry_r))
-        from_right.append(apply(carry_l))
     placed = jnp.zeros((count,) + own.shape, own.dtype)
-    for step in range(count - 1, 0, -1):
-        placed = lax.dynamic_update_index_in_dim(placed, from_left[step], index - step, 0)
-    for step in range(count - 1, 0, -1):
-        placed = lax.dynamic_update_index_in_dim(placed, from_right[step], index + step, 0)
-    return lax.dynamic_update_index_in_dim(placed, own, index, 0)
+    placed = lax.dynamic_update_index_in_dim(placed, own, index, 0)
+    for shift in range(1, count):
+        incoming = lax.ppermute(block, axis, [(i, (i + shift) % count) for i in range(count)])
+        placed = lax.dynamic_update_index_in_dim(
+            placed, apply(incoming), (index - shift) % count, 0
+        )
+    return placed
 
 
 def exchange_sum(parts, axis, count, index):
@@ -191,7 +175,7 @@
         product = jnp.dot(rows, q_weight, preferred_element_type=jnp.float32)
         return product.astype(jnp.bfloat16).astype(jnp.float32)
 
-    query_sum = line_reduce_scatter(query_chunk, "req", req_count, req_index)
+    query_sum = direct_reduce_scatter(query_chunk, "req", req_count, req_index)
     queries = lax.optimization_barrier(query_sum.astype(jnp.bfloat16))
     normalized = normalize_heads(queries, q_gain, head_dim)
     capacity = 2 * local_rows // req_count
@@ -244,7 +228,7 @@
         product = jnp.dot(rows, out_weight, preferred_element_type=jnp.float32)
         return product.astype(jnp.bfloat16)
 
-    partial_cols = line_gather_apply(attended, out_part, "req", req_count, req_index)
+    partial_cols = direct_gather_apply(attended, out_part, "req", req_count, req_index)
     partial_cols = partial_cols.reshape(req_count * local_rows, out_weight.shape[1])
     hs_count = lax.axis_size("head") * sub_count
     hs_index = lax.axis_index("head") * sub_count + sub_index

time: 253 us -> 244 us (0.964)
  matrix products: 27.5 us -> 18.6 us
  starting transfers between devices: 53.3 us -> 59 us
  waiting for transfers between devices: 135 us -> 131 us
    ppermute x12 -> x6, starting transfers between devices: 33.5 us -> 18 us  [the longest x3 9.44 us: direct_reduce_scatter(): lax.ppermute(outgoing, axis, [(i, (i + shift) % count) for i in range(cou...]
    ppermute x6, starting transfers between devices: 12.1 us -> 22.8 us  [shift_exchange(): lax.ppermute(blocks[shift], axis, [(i, (i + shift) % count) for i in rang...]
    ppermute x2, starting transfers between devices: 1.98 us -> 12.3 us  [local(): got = lax.ppermute(chunk, ('req', 'head', 'sub'), pairs).astype(jnp.float32)]
    ppermute x2, waiting for transfers between devices: 30.8 us -> 25.4 us  [local(): got = lax.ppermute(chunk, ('req', 'head', 'sub'), pairs).astype(jnp.float32)]
    dot_general x7 -> x4, matrix products: 13.8 us -> 8.7 us  [out_part(): product = jnp.dot(rows, out_weight, preferred_element_type=jnp.float32)]
    dot_general x7 -> x4, matrix products: 12.8 us -> 8.96 us  [query_chunk(): product = jnp.dot(rows, q_weight, preferred_element_type=jnp.float32)]
    ppermute x6, waiting for transfers between devices: 27 us -> 30 us  [shift_exchange(): lax.ppermute(blocks[shift], axis, [(i, (i + shift) % count) for i in rang...]
    ppermute x12 -> x6, waiting for transfers between devices: 57.6 us -> 55.9 us  [the longest x3 29.7 us: direct_reduce_scatter(): lax.ppermute(outgoing, axis, [(i, (i + shift) % count) for i in range(cou...]
  transfers between devices with their start and end apart: 25 -> 19, of which waited for: 19 -> 14; matrix products, arithmetic and copies ran while one was open for 7% -> 6% of each run, Pallas kernels for 0% -> 0%
where the time goes in v11:
time: 244 us; the launch traced here: 242 us
  waiting for transfers between devices  131 us (54%)
  starting transfers between devices  59 us (24%)
  matrix products  18.6 us (8%)
  Pallas kernels  18.2 us (7%)
  local copies, waits for them, and re-layouts  9.25 us (4%)
  other arithmetic  6.13 us (3%)
    ppermute x6, waiting for transfers between devices, shift_exchange(): lax.ppermute(blocks[shift], axis, [(i, (i + shift) % count) for i in rang...  30 us
    ppermute x3, waiting for transfers between devices, direct_reduce_scatter(): lax.ppermute(outgoing, axis, [(i, (i + shift) % count) for i in range(cou...  29.7 us
    ppermute x3, waiting for transfers between devices, direct_gather_apply(): lax.ppermute(block, axis, [(i, (i + shift) % count) for i in range(count)])  26.2 us
    ppermute x2, waiting for transfers between devices, local(): got = lax.ppermute(chunk, ('req', 'head', 'sub'), pairs).astype(jnp.float32)  25.4 us
    ppermute x6, starting transfers between devices, shift_exchange(): lax.ppermute(blocks[shift], axis, [(i, (i + shift) % count) for i in rang...  22.8 us
    pallas_call x1, Pallas kernels, attend(): pl.pallas_call(kernel, grid=(kv_count,), in_specs=[pl.BlockSpec((rows, gr...  18.2 us
    ppermute x3, waiting for transfers between devices, local(): lax.ppermute(outgoing_part, 'req', [(i, (i + shift) % req_count) for i in...  14.9 us
    ppermute x2, starting transfers between devices, local(): got = lax.ppermute(chunk, ('req', 'head', 'sub'), pairs).astype(jnp.float32)  12.3 us
  transfers between devices with their start and end apart: 19, of which 14 were waited for; matrix products, arithmetic and copies ran while one was open for 6% of the time, Pallas kernels for 0%

profile of v11, /device:TPU:6, one launch (start us, length us, event | category | flops | bytes accessed | tf_op | source)
XLA Modules:
  0.0 242.4 jit_solution(15593735940933046716)
XLA Ops:
  0.0 3.2 %copy.21 = bf16[128,8192]{0,1:T(8,128)(2,1)S(1)} copy(bf16[128,8192]{1,0:T(8,128)(2,1)} %param.9) | data formatting | bytes 4194304 | tf_op args[0]
  5.3 2.7 %collective-permute-start.1 = (bf16[128,1024]{1,0:T(8,128)(2,1)S(1)}, bf16[128,1024]{1,0:T(8,128)(2,1)S(1)}, u32[]{:S(2)}, u32[]{:S(2)}) collective-permute-start(bf16[128,1024]{1,0:T(8,128)(2,1)S(1)} %bitcast.93), channel_id=1, source_target_pairs={{0,8},{4,12},{8,0},{12,4},{1,9},{5,13},{9,1},{13,5},{2,10},{6,14},... | collective-permute-start | bytes 786440 | tf_op jit(solution)/shard_map/ppermute | solution.py:155
  9.9 4.8 %collective-permute-done = bf16[128,1024]{1,0:T(8,128)(2,1)S(1)} collective-permute-done((bf16[128,1024]{1,0:T(8,128)(2,1)S(1)}, bf16[128,1024]{1,0:T(8,128)(2,1)S(1)}, u32[]{:S(2)}, u32[]{:S(2)}) %collective-permute-start) | collective-permute-done | bytes 262176 | tf_op jit(solution)/shard_map/ppermute | solution.py:155
  14.7 10.1 %collective-permute-done.1 = bf16[128,1024]{1,0:T(8,128)(2,1)S(1)} collective-permute-done((bf16[128,1024]{1,0:T(8,128)(2,1)S(1)}, bf16[128,1024]{1,0:T(8,128)(2,1)S(1)}, u32[]{:S(2)}, u32[]{:S(2)}) %collective-permute-start.1) | collective-permute-done | bytes 262176 | tf_op jit(solution)/shard_map/ppermute | solution.py:155
  27.8 4.8 %convolution_convert_fusion.7 = bf16[128,2048]{1,0:T(8,128)(2,1)S(1)} fusion(bf16[2048,2048]{1,0:T(8,128)(2,1)} %param.10, bf16[512,2048]{1,0:T(8,128)(2,1)S(1)} %constant_dynamic-update-slice_fusion, s32[]{:T(128)S(6)} %select_n.191), kind=kOutput, calls=%fused_computation.7 | convolution fusion | flops 1074003968 | bytes 9437188 | tf_op jit(solution)/shard_map/dot_general | solution.py:175
  32.6 6.1 %collective-permute-start.4 = (bf16[128,2048]{1,0:T(8,128)(2,1)S(1)}, bf16[128,2048]{1,0:T(8,128)(2,1)S(1)}, u32[]{:S(2)}, u32[]{:S(2)}) collective-permute-start(bf16[128,2048]{1,0:T(8,128)(2,1)S(1)} %convolution_convert_fusion.7), channel_id=1, source_target_pairs={{0,4},{4,8},{8,12},{12,0},{1,5},{5,9},{9,13},{13,1},{2,6},{6,10},{... | collective-permute-start | bytes 1572872 | tf_op jit(solution)/shard_map/ppermute | solution.py:33
  44.8 7.8 %collective-permute-done.4 = bf16[128,2048]{1,0:T(8,128)(2,1)S(1)} collective-permute-done((bf16[128,2048]{1,0:T(8,128)(2,1)S(1)}, bf16[128,2048]{1,0:T(8,128)(2,1)S(1)}, u32[]{:S(2)}, u32[]{:S(2)}) %collective-permute-start.4) | collective-permute-done | bytes 524320 | tf_op jit(solution)/shard_map/ppermute | solution.py:33
  52.6 22.0 %collective-permute-done.5 = bf16[128,2048]{1,0:T(8,128)(2,1)S(1)} collective-permute-done((bf16[128,2048]{1,0:T(8,128)(2,1)S(1)}, bf16[128,2048]{1,0:T(8,128)(2,1)S(1)}, u32[]{:S(2)}, u32[]{:S(2)}) %collective-permute-start.5) | collective-permute-done | bytes 524320 | tf_op jit(solution)/shard_map/ppermute | solution.py:33
  78.0 11.8 %collective-permute-start.7 = (bf16[64,2048]{1,0:T(8,128)(2,1)S(1)}, bf16[64,2048]{1,0:T(8,128)(2,1)S(1)}, u32[]{:S(2)}, u32[]{:S(2)}) collective-permute-start(bf16[64,2048]{1,0:T(8,128)(2,1)S(1)} %get-tuple-element.18), channel_id=1, source_target_pairs={{0,4},{4,8},{8,12},{12,0},{1,5},{5,9},{9,13},{13,1},{2,6},{6,10},{... | collective-permute-start | bytes 786440 | tf_op jit(solution)/shard_map/ppermute | solution.py:24
  94.3 3.5 %collective-permute-done.7 = bf16[64,2048]{1,0:T(8,128)(2,1)S(1)} collective-permute-done((bf16[64,2048]{1,0:T(8,128)(2,1)S(1)}, bf16[64,2048]{1,0:T(8,128)(2,1)S(1)}, u32[]{:S(2)}, u32[]{:S(2)}) %collective-permute-start.7) | collective-permute-done | bytes 262176 | tf_op jit(solution)/shard_map/ppermute | solution.py:24
  97.8 10.2 %collective-permute-done.8 = bf16[64,2048]{1,0:T(8,128)(2,1)S(1)} collective-permute-done((bf16[64,2048]{1,0:T(8,128)(2,1)S(1)}, bf16[64,2048]{1,0:T(8,128)(2,1)S(1)}, u32[]{:S(2)}, u32[]{:S(2)}) %collective-permute-start.8) | collective-permute-done | bytes 262176 | tf_op jit(solution)/shard_map/ppermute | solution.py:24
  109.1 18.2 %shard_map.91 = bf16[256,2048]{1,0:T(8,128)(2,1)} custom-call(bf16[256,2048]{1,0:T(8,128)(2,1)} %bitcast.91, bf16[1664,256]{1,0:T(8,128)(2,1)} %pad.7.k_ref, bf16[1664,256]{1,0:T(8,128)(2,1)} %pad.8.v_ref), custom_call_target="tpu_custom_call" | custom-call | flops 3489660928 | bytes 3801088 | tf_op jit(solution)/shard_map/pallas_call | solution.py:105
  128.5 6.2 %collective-permute-start.10 = (bf16[64,2048]{1,0:T(8,128)(2,1)S(1)}, bf16[64,2048]{1,0:T(8,128)(2,1)S(1)}, u32[]{:S(2)}, u32[]{:S(2)}) collective-permute-start(bf16[64,2048]{1,0:T(8,128)(2,1)S(1)} %get-tuple-element.14), channel_id=1, source_target_pairs={{0,4},{4,8},{8,12},{12,0},{1,5},{5,9},{9,13},{13,1},{2,6},{6,10},{... | collective-permute-start | bytes 786440 | tf_op jit(solution)/shard_map/ppermute | solution.py:24
  137.1 6.3 %collective-permute-done.10 = bf16[64,2048]{1,0:T(8,128)(2,1)S(1)} collective-permute-done((bf16[64,2048]{1,0:T(8,128)(2,1)S(1)}, bf16[64,2048]{1,0:T(8,128)(2,1)S(1)}, u32[]{:S(2)}, u32[]{:S(2)}) %collective-permute-start.10) | collective-permute-done | bytes 262176 | tf_op jit(solution)/shard_map/ppermute | solution.py:24
  143.4 10.0 %collective-permute-done.11 = bf16[64,2048]{1,0:T(8,128)(2,1)S(1)} collective-permute-done((bf16[64,2048]{1,0:T(8,128)(2,1)S(1)}, bf16[64,2048]{1,0:T(8,128)(2,1)S(1)}, u32[]{:S(2)}, u32[]{:S(2)}) %collective-permute-start.11) | collective-permute-done | bytes 262176 | tf_op jit(solution)/shard_map/ppermute | solution.py:24
  154.1 6.1 %collective-permute-start.13 = (bf16[128,2048]{1,0:T(8,128)(2,1)S(1)}, bf16[128,2048]{1,0:T(8,128)(2,1)S(1)}, u32[]{:S(2)}, u32[]{:S(2)}) collective-permute-start(bf16[128,2048]{1,0:T(8,128)(2,1)S(1)} %convolution_convert_fusion.9), channel_id=1, source_target_pairs={{0,4},{4,8},{8,12},{12,0},{1,5},{5,9},{9,13},{13,1},{2,6},{6,10},{... | collective-permute-start | bytes 1572872 | tf_op jit(solution)/shard_map/ppermute | solution.py:45
  162.9 4.8 %fusion.4 = bf16[4,128,2048]{2,1,0:T(8,128)(2,1)S(1)} fusion(bf16[4,128,2048]{2,1,0:T(8,128)(2,1)S(1)} %broadcast_in_dim.56, s32[]{:T(128)S(6)} %select_n.168, bf16[128,2048]{1,0:T(8,128)(2,1)S(1)} %convolution_convert_fusion.9, bf16[2048,2048]{1,0:T(8,128)(2,1)} %param.14), kind=kOutput, calls=%fused_computation.14 | convolution fusion | flops 1074003968 | bytes 9437188 | tf_op jit(solution)/shard_map/dot_general | solution.py:228
  167.7 6.2 %collective-permute-done.13 = bf16[128,2048]{1,0:T(8,128)(2,1)S(1)} collective-permute-done((bf16[128,2048]{1,0:T(8,128)(2,1)S(1)}, bf16[128,2048]{1,0:T(8,128)(2,1)S(1)}, u32[]{:S(2)}, u32[]{:S(2)}) %collective-permute-start.13) | collective-permute-done | bytes 524320 | tf_op jit(solution)/shard_map/ppermute | solution.py:45
  175.3 19.9 %collective-permute-done.14 = bf16[128,2048]{1,0:T(8,128)(2,1)S(1)} collective-permute-done((bf16[128,2048]{1,0:T(8,128)(2,1)S(1)}, bf16[128,2048]{1,0:T(8,128)(2,1)S(1)}, u32[]{:S(2)}, u32[]{:S(2)}) %collective-permute-start.14) | collective-permute-done | bytes 524320 | tf_op jit(solution)/shard_map/ppermute | solution.py:45
  198.0 2.8 %collective-permute-done.16 = bf16[256,2048]{1,0:T(8,128)(2,1)} collective-permute-done((bf16[256,2048]{1,0:T(8,128)(2,1)S(1)}, bf16[256,2048]{1,0:T(8,128)(2,1)}, u32[]{:S(2)}, u32[]{:S(2)}) %collective-permute-start.16) | collective-permute-done | bytes 1048608 | tf_op jit(solution)/shard_map/ppermute | solution.py:56
  202.5 12.3 %collective-permute-start.17 = (bf16[128,2048]{1,0:T(8,128)(2,1)S(1)}, bf16[128,2048]{1,0:T(8,128)(2,1)S(1)}, u32[]{:S(2)}, u32[]{:S(2)}) collective-permute-start(bf16[128,2048]{1,0:T(8,128)(2,1)S(1)} %get-tuple-element.9), channel_id=1, source_target_pairs={{0,0},{1,8},{2,4},{3,12},{4,1},{5,9},{6,5},{7,13},{8,2},{9,10},{10... | collective-permute-start | bytes 1572872 | tf_op jit(solution)/shard_map/ppermute | solution.py:259
  214.9 10.1 %collective-permute-done.17 = bf16[128,2048]{1,0:T(8,128)(2,1)S(1)} collective-permute-done((bf16[128,2048]{1,0:T(8,128)(2,1)S(1)}, bf16[128,2048]{1,0:T(8,128)(2,1)S(1)}, u32[]{:S(2)}, u32[]{:S(2)}) %collective-permute-start.17) | collective-permute-done | bytes 524320 | tf_op jit(solution)/shard_map/ppermute | solution.py:259
  225.0 15.3 %collective-permute-done.18 = bf16[128,2048]{1,0:T(8,128)(2,1)S(1)} collective-permute-done((bf16[128,2048]{1,0:T(8,128)(2,1)S(1)}, bf16[128,2048]{1,0:T(8,128)(2,1)S(1)}, u32[]{:S(2)}, u32[]{:S(2)}) %collective-permute-start.18) | collective-permute-done | bytes 524320 | tf_op jit(solution)/shard_map/ppermute | solution.py:259
  240.3 2.1 add_convert_fusion
  (89 shorter events, 34.6 us)
Async XLA Ops:
  0.0 44.8 %copy-start = (f32[128]{0:T(128)S(1)}, f32[128]{0:T(128)}, u32[]{:S(2)}) copy-start(f32[128]{0:T(128)} %param.11) | copy-start | bytes 1540
  3.5 11.2 %collective-permute-start = (bf16[128,1024]{1,0:T(8,128)(2,1)S(1)}, bf16[128,1024]{1,0:T(8,128)(2,1)S(1)}, u32[]{:S(2)}, u32[]{:S(2)}) collective-permute-start(bf16[128,1024]{1,0:T(8,128)(2,1)S(1)} %bitcast.94), channel_id=1, source_target_pairs={{0,4},{4,8},{8,12},{12,0},{1,5},{5,9},{9,13},{13,1},{2,6},{6,10},{... | collective-permute-start | bytes 786440 | tf_op jit(solution)/shard_map/ppermute | solution.py:155
  5.3 19.5 %collective-permute-start.1 = (bf16[128,1024]{1,0:T(8,128)(2,1)S(1)}, bf16[128,1024]{1,0:T(8,128)(2,1)S(1)}, u32[]{:S(2)}, u32[]{:S(2)}) collective-permute-start(bf16[128,1024]{1,0:T(8,128)(2,1)S(1)} %bitcast.93), channel_id=1, source_target_pairs={{0,8},{4,12},{8,0},{12,4},{1,9},{5,13},{9,1},{13,5},{2,10},{6,14},... | collective-permute-start | bytes 786440 | tf_op jit(solution)/shard_map/ppermute | solution.py:155
  7.9 17.1 %copy-start.3 = (s32[4]{0:T(128)S(1)}, s32[4]{0:T(128)}, u32[]{:S(2)}) copy-start(s32[4]{0:T(128)} %param.17) | copy-start | bytes 52
  7.9 17.1 %copy-start.4 = (s32[128]{0:T(128)S(1)}, s32[128]{0:T(128)}, u32[]{:S(2)}) copy-start(s32[128]{0:T(128)} %param.15) | copy-start | bytes 1540
  7.9 17.3 %copy-start.5 = (s32[128]{0:T(128)S(1)}, s32[128]{0:T(128)}, u32[]{:S(2)}) copy-start(s32[128]{0:T(128)} %param.16) | copy-start | bytes 1540
  8.1 16.8 %collective-permute-start.2 = (bf16[128,1024]{1,0:T(8,128)(2,1)S(1)}, bf16[128,1024]{1,0:T(8,128)(2,1)S(1)}, u32[]{:S(2)}, u32[]{:S(2)}) collective-permute-start(bf16[128,1024]{1,0:T(8,128)(2,1)S(1)} %bitcast.92), channel_id=1, source_target_pairs={{0,12},{4,0},{8,4},{12,8},{1,13},{5,1},{9,5},{13,9},{2,14},{6,2},{... | collective-permute-start | bytes 786440 | tf_op jit(solution)/shard_map/ppermute | solution.py:155
  24.9 2.7 %collective-permute-start.3 = (bf16[512,1024]{1,0:T(8,128)(2,1)S(1)}, bf16[512,1024]{1,0:T(8,128)(2,1)S(1)}, u32[]{:S(2)}, u32[]{:S(2)}) collective-permute-start(bf16[512,1024]{1,0:T(8,128)(2,1)S(1)} %bitcast.86), channel_id=1, source_target_pairs={{0,1},{1,0},{2,3},{3,2},{4,5},{5,4},{6,7},{7,6},{8,9},{9,8},{10,11... | collective-permute-start | bytes 3145736 | tf_op jit(solution)/shard_map/ppermute | solution.py:167
  32.6 20.0 %collective-permute-start.4 = (bf16[128,2048]{1,0:T(8,128)(2,1)S(1)}, bf16[128,2048]{1,0:T(8,128)(2,1)S(1)}, u32[]{:S(2)}, u32[]{:S(2)}) collective-permute-start(bf16[128,2048]{1,0:T(8,128)(2,1)S(1)} %convolution_convert_fusion.7), channel_id=1, source_target_pairs={{0,4},{4,8},{8,12},{12,0},{1,5},{5,9},{9,13},{13,1},{2,6},{6,10},{... | collective-permute-start | bytes 1572872 | tf_op jit(solution)/shard_map/ppermute | solution.py:33
  40.0 34.6 %collective-permute-start.5 = (bf16[128,2048]{1,0:T(8,128)(2,1)S(1)}, bf16[128,2048]{1,0:T(8,128)(2,1)S(1)}, u32[]{:S(2)}, u32[]{:S(2)}) collective-permute-start(bf16[128,2048]{1,0:T(8,128)(2,1)S(1)} %convolution_convert_fusion.6), channel_id=1, source_target_pairs={{0,8},{4,12},{8,0},{12,4},{1,9},{5,13},{9,1},{13,5},{2,10},{6,14},... | collective-permute-start | bytes 1572872 | tf_op jit(solution)/shard_map/ppermute | solution.py:33
  43.0 31.6 %collective-permute-start.6 = (bf16[128,2048]{1,0:T(8,128)(2,1)S(1)}, bf16[128,2048]{1,0:T(8,128)(2,1)S(1)}, u32[]{:S(2)}, u32[]{:S(2)}) collective-permute-start(bf16[128,2048]{1,0:T(8,128)(2,1)S(1)} %convolution_convert_fusion.5), channel_id=1, source_target_pairs={{0,12},{4,0},{8,4},{12,8},{1,13},{5,1},{9,5},{13,9},{2,14},{6,2},{... | collective-permute-start | bytes 1572872 | tf_op jit(solution)/shard_map/ppermute | solution.py:33
  77.3 14.9 %copy-start.1 = (bf16[1,1601,512]{2,1,0:T(8,128)(2,1)S(1)}, bf16[1,1601,512]{2,1,0:T(8,128)(2,1)}, u32[]{:S(2)}) copy-start(bf16[1,1601,512]{2,1,0:T(8,128)(2,1)} %param.13) | copy-start | bytes 4918276
  78.0 19.7 %collective-permute-start.7 = (bf16[64,2048]{1,0:T(8,128)(2,1)S(1)}, bf16[64,2048]{1,0:T(8,128)(2,1)S(1)}, u32[]{:S(2)}, u32[]{:S(2)}) collective-permute-start(bf16[64,2048]{1,0:T(8,128)(2,1)S(1)} %get-tuple-element.18), channel_id=1, source_target_pairs={{0,4},{4,8},{8,12},{12,0},{1,5},{5,9},{9,13},{13,1},{2,6},{6,10},{... | collective-permute-start | bytes 786440 | tf_op jit(solution)/shard_map/ppermute | solution.py:24
  89.8 18.1 %collective-permute-start.8 = (bf16[64,2048]{1,0:T(8,128)(2,1)S(1)}, bf16[64,2048]{1,0:T(8,128)(2,1)S(1)}, u32[]{:S(2)}, u32[]{:S(2)}) collective-permute-start(bf16[64,2048]{1,0:T(8,128)(2,1)S(1)} %get-tuple-element.17), channel_id=1, source_target_pairs={{0,8},{4,12},{8,0},{12,4},{1,9},{5,13},{9,1},{13,5},{2,10},{6,14},... | collective-permute-start | bytes 786440 | tf_op jit(solution)/shard_map/ppermute | solution.py:24
  91.0 16.9 %collective-permute-start.9 = (bf16[64,2048]{1,0:T(8,128)(2,1)S(1)}, bf16[64,2048]{1,0:T(8,128)(2,1)S(1)}, u32[]{:S(2)}, u32[]{:S(2)}) collective-permute-start(bf16[64,2048]{1,0:T(8,128)(2,1)S(1)} %get-tuple-element.16), channel_id=1, source_target_pairs={{0,12},{4,0},{8,4},{12,8},{1,13},{5,1},{9,5},{13,9},{2,14},{6,2},{... | collective-permute-start | bytes 786440 | tf_op jit(solution)/shard_map/ppermute | solution.py:24
  128.5 14.9 %collective-permute-start.10 = (bf16[64,2048]{1,0:T(8,128)(2,1)S(1)}, bf16[64,2048]{1,0:T(8,128)(2,1)S(1)}, u32[]{:S(2)}, u32[]{:S(2)}) collective-permute-start(bf16[64,2048]{1,0:T(8,128)(2,1)S(1)} %get-tuple-element.14), channel_id=1, source_target_pairs={{0,4},{4,8},{8,12},{12,0},{1,5},{5,9},{9,13},{13,1},{2,6},{6,10},{... | collective-permute-start | bytes 786440 | tf_op jit(solution)/shard_map/ppermute | solution.py:24
  134.6 18.8 %collective-permute-start.11 = (bf16[64,2048]{1,0:T(8,128)(2,1)S(1)}, bf16[64,2048]{1,0:T(8,128)(2,1)S(1)}, u32[]{:S(2)}, u32[]{:S(2)}) collective-permute-start(bf16[64,2048]{1,0:T(8,128)(2,1)S(1)} %get-tuple-element.13), channel_id=1, source_target_pairs={{0,8},{4,12},{8,0},{12,4},{1,9},{5,13},{9,1},{13,5},{2,10},{6,14},... | collective-permute-start | bytes 786440 | tf_op jit(solution)/shard_map/ppermute | solution.py:24
  136.7 16.8 %collective-permute-start.12 = (bf16[64,2048]{1,0:T(8,128)(2,1)S(1)}, bf16[64,2048]{1,0:T(8,128)(2,1)S(1)}, u32[]{:S(2)}, u32[]{:S(2)}) collective-permute-start(bf16[64,2048]{1,0:T(8,128)(2,1)S(1)} %get-tuple-element.12), channel_id=1, source_target_pairs={{0,12},{4,0},{8,4},{12,8},{1,13},{5,1},{9,5},{13,9},{2,14},{6,2},{... | collective-permute-start | bytes 786440 | tf_op jit(solution)/shard_map/ppermute | solution.py:24
  154.1 19.9 %collective-permute-start.13 = (bf16[128,2048]{1,0:T(8,128)(2,1)S(1)}, bf16[128,2048]{1,0:T(8,128)(2,1)S(1)}, u32[]{:S(2)}, u32[]{:S(2)}) collective-permute-start(bf16[128,2048]{1,0:T(8,128)(2,1)S(1)} %convolution_convert_fusion.9), channel_id=1, source_target_pairs={{0,4},{4,8},{8,12},{12,0},{1,5},{5,9},{9,13},{13,1},{2,6},{6,10},{... | collective-permute-start | bytes 1572872 | tf_op jit(solution)/shard_map/ppermute | solution.py:45
  160.2 35.0 %collective-permute-start.14 = (bf16[128,2048]{1,0:T(8,128)(2,1)S(1)}, bf16[128,2048]{1,0:T(8,128)(2,1)S(1)}, u32[]{:S(2)}, u32[]{:S(2)}) collective-permute-start(bf16[128,2048]{1,0:T(8,128)(2,1)S(1)} %convolution_convert_fusion.9), channel_id=1, source_target_pairs={{0,8},{4,12},{8,0},{12,4},{1,9},{5,13},{9,1},{13,5},{2,10},{6,14},... | collective-permute-start | bytes 1572872 | tf_op jit(solution)/shard_map/ppermute | solution.py:45
  161.6 34.9 %collective-permute-start.15 = (bf16[128,2048]{1,0:T(8,128)(2,1)S(1)}, bf16[128,2048]{1,0:T(8,128)(2,1)S(1)}, u32[]{:S(2)}, u32[]{:S(2)}) collective-permute-start(bf16[128,2048]{1,0:T(8,128)(2,1)S(1)} %convolution_convert_fusion.9), channel_id=1, source_target_pairs={{0,12},{4,0},{8,4},{12,8},{1,13},{5,1},{9,5},{13,9},{2,14},{6,2},{... | collective-permute-start | bytes 1572872 | tf_op jit(solution)/shard_map/ppermute | solution.py:45
  197.9 2.9 %collective-permute-start.16 = (bf16[256,2048]{1,0:T(8,128)(2,1)S(1)}, bf16[256,2048]{1,0:T(8,128)(2,1)}, u32[]{:S(2)}, u32[]{:S(2)}) collective-permute-start(bf16[256,2048]{1,0:T(8,128)(2,1)S(1)} %dynamic-slice_bitcast_fusion), channel_id=1, source_target_pairs={{0,1},{1,0},{2,3},{3,2},{4,5},{5,4},{6,7},{7,6},{8,9},{9,8},{10,11... | collective-permute-start | bytes 3145736 | tf_op jit(solution)/shard_map/ppermute | solution.py:56
  202.5 22.4 %collective-permute-start.17 = (bf16[128,2048]{1,0:T(8,128)(2,1)S(1)}, bf16[128,2048]{1,0:T(8,128)(2,1)S(1)}, u32[]{:S(2)}, u32[]{:S(2)}) collective-permute-start(bf16[128,2048]{1,0:T(8,128)(2,1)S(1)} %get-tuple-element.9), channel_id=1, source_target_pairs={{0,0},{1,8},{2,4},{3,12},{4,1},{5,9},{6,5},{7,13},{8,2},{9,10},{10... | collective-permute-start | bytes 1572872 | tf_op jit(solution)/shard_map/ppermute | solution.py:259
  214.8 25.5 %collective-permute-start.18 = (bf16[128,2048]{1,0:T(8,128)(2,1)S(1)}, bf16[128,2048]{1,0:T(8,128)(2,1)S(1)}, u32[]{:S(2)}, u32[]{:S(2)}) collective-permute-start(bf16[128,2048]{1,0:T(8,128)(2,1)S(1)} %get-tuple-element.10), channel_id=1, source_target_pairs={{0,4},{1,12},{2,0},{3,8},{4,5},{5,13},{6,1},{7,9},{8,6},{9,14},{10... | collective-permute-start | bytes 1572872 | tf_op jit(solution)/shard_map/ppermute | solution.py:259
  (5 other events, 59.3 us)

commit v12 on v11

--- a/solution.py
+++ b/solution.py
@@ -15,15 +15,6 @@
     per_head = queries.astype(jnp.float32).reshape(row_count, -1, head_dim)
     inv_rms = lax.rsqrt(jnp.mean(per_head * per_head, axis=2, keepdims=True) + 1e-05)
     return (per_head * inv_rms * q_gain).reshape(row_count, -1).astype(jnp.bfloat16)
-
-
-def shift_exchange(blocks, axis, count):
-    arrived = [blocks[0]]
-    for shift in range(1, count):
-        arrived.append(
-            lax.ppermute(blocks[shift], axis, [(i, (i + shift) % count) for i in range(count)])
-        )
-    return jnp.stack(arrived)
 
 
 def direct_reduce_scatter(chunk_of, axis, count, index):
@@ -208,16 +199,23 @@
         lax.dynamic_slice_in_dim(value_cache[0], kv_first * head_dim, kv_count * head_dim, 1),
         ((0, padded_tokens - token_count), (0, 0)),
     )
-    arrived = shift_exchange(outgoing, "req", req_count)
-    sources = arrived.shape[0]
-    slot_count = arrived.shape[1]
-    flat_rows = arrived.reshape(sources * slot_count, q_cols)
-    mixed_heads = attend(flat_rows, keys_here, values_here, kv_count, per_kv, head_dim, token_count)
-    replies = mixed_heads.reshape(sources, slot_count, q_cols)
-    returned = shift_exchange(
-        jnp.concatenate([replies[:1], replies[1:][::-1]]), "req", req_count
-    )
-    returned = jnp.concatenate([returned[:1], returned[1:][::-1]])
+    returned_blocks = []
+    for shift in range(req_count):
+        if shift == 0:
+            arrived_block = outgoing[0]
+        else:
+            arrived_block = lax.ppermute(
+                outgoing[shift], "req", [(i, (i + shift) % req_count) for i in range(req_count)]
+            )
+        mixed_block = attend(
+            arrived_block, keys_here, values_here, kv_count, per_kv, head_dim, token_count
+        )
+        if shift:
+            mixed_block = lax.ppermute(
+                mixed_block, "req", [(i, (i - shift) % req_count) for i in range(req_count)]
+            )
+        returned_blocks.append(mixed_block)
+    returned = jnp.stack(returned_blocks)
     attended = lax.dot_general(
         dispatch,
         returned.reshape(slot_total, q_cols),

time: 244 us -> 242 us (level)
  waiting for transfers between devices: 131 us -> 105 us
  Pallas kernels: 18.2 us -> 43.9 us
    ppermute x6, waiting for transfers between devices: 30 us -> 3.55 us  [the longest x3 3.54 us: local(): lax.ppermute(outgoing[shift], 'req', [(i, (i + shift) % req_count) for i...]
    pallas_call x1 -> x4, Pallas kernels: 18.2 us -> 43.9 us  [attend(): pl.pallas_call(kernel, grid=(kv_count,), in_specs=[pl.BlockSpec((rows, gr...]
    ppermute x3, starting transfers between devices: 8.58 us -> 3.87 us  [direct_gather_apply(): lax.ppermute(block, axis, [(i, (i + shift) % count) for i in range(count)])]
    ppermute x6, starting transfers between devices: 22.8 us -> 26.3 us  [the longest x3 14.1 us: local(): lax.ppermute(outgoing[shift], 'req', [(i, (i + shift) % req_count) for i...]
    unnamed x22 -> x28, local copies, waits for them, and re-layouts: 3.46 us -> 5.58 us
  transfers between devices with their start and end apart: 19 -> 19, of which waited for: 14 -> 11; matrix products, arithmetic and copies ran while one was open for 6% -> 6% of each run, Pallas kernels for 0% -> 18%
where the time goes in v12:
time: 242 us
  waiting for transfers between devices  105 us (43%)
  starting transfers between devices  56.8 us (23%)
  Pallas kernels  43.9 us (18%)
  matrix products  18.6 us (8%)
  local copies, waits for them, and re-layouts  10.8 us (4%)
  other arithmetic  5.88 us (2%)
    pallas_call x4, Pallas kernels, attend(): pl.pallas_call(kernel, grid=(kv_count,), in_specs=[pl.BlockSpec((rows, gr...  43.9 us
    ppermute x3, waiting for transfers between devices, direct_reduce_scatter(): lax.ppermute(outgoing, axis, [(i, (i + shift) % count) for i in range(cou...  29.7 us
    ppermute x3, waiting for transfers between devices, direct_gather_apply(): lax.ppermute(block, axis, [(i, (i + shift) % count) for i in range(count)])  27 us
    ppermute x2, waiting for transfers between devices, local(): got = lax.ppermute(chunk, ('req', 'head', 'sub'), pairs).astype(jnp.float32)  25.4 us
    ppermute x3, waiting for transfers between devices, local(): lax.ppermute(outgoing_part, 'req', [(i, (i + shift) % req_count) for i in...  14.9 us
    ppermute x3, starting transfers between devices, local(): lax.ppermute(outgoing[shift], 'req', [(i, (i + shift) % req_count) for i...  14.1 us
    ppermute x3, starting transfers between devices, local(): lax.ppermute(mixed_block, 'req', [(i, (i - shift) % req_count) for i in r...  12.2 us
    ppermute x2, starting transfers between devices, local(): got = lax.ppermute(chunk, ('req', 'head', 'sub'), pairs).astype(jnp.float32)  11.4 us
  transfers between devices with their start and end apart: 19, of which 11 were waited for; matrix products, arithmetic and copies ran while one was open for 6% of the time, Pallas kernels for 18%

profile of v12, /device:TPU:6, one launch (start us, length us, event | category | flops | bytes accessed | tf_op | source)
XLA Modules:
  0.0 241.8 jit_solution(14238812116996338807)
XLA Ops:
  0.0 3.2 %copy.21 = bf16[128,8192]{0,1:T(8,128)(2,1)S(1)} copy(bf16[128,8192]{1,0:T(8,128)(2,1)} %param.9) | data formatting | bytes 4194304 | tf_op args[0]
  5.3 2.7 %collective-permute-start.1 = (bf16[128,1024]{1,0:T(8,128)(2,1)S(1)}, bf16[128,1024]{1,0:T(8,128)(2,1)S(1)}, u32[]{:S(2)}, u32[]{:S(2)}) collective-permute-start(bf16[128,1024]{1,0:T(8,128)(2,1)S(1)} %bitcast.85), channel_id=1, source_target_pairs={{0,8},{4,12},{8,0},{12,4},{1,9},{5,13},{9,1},{13,5},{2,10},{6,14},... | collective-permute-start | bytes 786440 | tf_op jit(solution)/shard_map/ppermute | solution.py:146
  9.9 4.8 %collective-permute-done = bf16[128,1024]{1,0:T(8,128)(2,1)S(1)} collective-permute-done((bf16[128,1024]{1,0:T(8,128)(2,1)S(1)}, bf16[128,1024]{1,0:T(8,128)(2,1)S(1)}, u32[]{:S(2)}, u32[]{:S(2)}) %collective-permute-start) | collective-permute-done | bytes 262176 | tf_op jit(solution)/shard_map/ppermute | solution.py:146
  14.7 10.1 %collective-permute-done.1 = bf16[128,1024]{1,0:T(8,128)(2,1)S(1)} collective-permute-done((bf16[128,1024]{1,0:T(8,128)(2,1)S(1)}, bf16[128,1024]{1,0:T(8,128)(2,1)S(1)}, u32[]{:S(2)}, u32[]{:S(2)}) %collective-permute-start.1) | collective-permute-done | bytes 262176 | tf_op jit(solution)/shard_map/ppermute | solution.py:146
  27.8 4.8 %convolution_convert_fusion.7 = bf16[128,2048]{1,0:T(8,128)(2,1)S(1)} fusion(bf16[2048,2048]{1,0:T(8,128)(2,1)} %param.10, bf16[512,2048]{1,0:T(8,128)(2,1)S(1)} %constant_dynamic-update-slice_fusion, s32[]{:T(128)S(6)} %select_n.191), kind=kOutput, calls=%fused_computation.7 | convolution fusion | flops 1074003968 | bytes 9437188 | tf_op jit(solution)/shard_map/dot_general | solution.py:166
  32.6 6.1 %collective-permute-start.4 = (bf16[128,2048]{1,0:T(8,128)(2,1)S(1)}, bf16[128,2048]{1,0:T(8,128)(2,1)S(1)}, u32[]{:S(2)}, u32[]{:S(2)}) collective-permute-start(bf16[128,2048]{1,0:T(8,128)(2,1)S(1)} %convolution_convert_fusion.7), channel_id=1, source_target_pairs={{0,4},{4,8},{8,12},{12,0},{1,5},{5,9},{9,13},{13,1},{2,6},{6,10},{... | collective-permute-start | bytes 1572872 | tf_op jit(solution)/shard_map/ppermute | solution.py:24
  44.8 7.8 %collective-permute-done.4 = bf16[128,2048]{1,0:T(8,128)(2,1)S(1)} collective-permute-done((bf16[128,2048]{1,0:T(8,128)(2,1)S(1)}, bf16[128,2048]{1,0:T(8,128)(2,1)S(1)}, u32[]{:S(2)}, u32[]{:S(2)}) %collective-permute-start.4) | collective-permute-done | bytes 524320 | tf_op jit(solution)/shard_map/ppermute | solution.py:24
  52.6 22.0 %collective-permute-done.5 = bf16[128,2048]{1,0:T(8,128)(2,1)S(1)} collective-permute-done((bf16[128,2048]{1,0:T(8,128)(2,1)S(1)}, bf16[128,2048]{1,0:T(8,128)(2,1)S(1)}, u32[]{:S(2)}, u32[]{:S(2)}) %collective-permute-start.5) | collective-permute-done | bytes 524320 | tf_op jit(solution)/shard_map/ppermute | solution.py:24
  78.8 11.7 %collective-permute-start.7 = (bf16[64,2048]{1,0:T(8,128)(2,1)S(1)}, bf16[64,2048]{1,0:T(8,128)(2,1)S(1)}, u32[]{:S(2)}, u32[]{:S(2)}) collective-permute-start(bf16[64,2048]{1,0:T(8,128)(2,1)S(1)} %get-tuple-element.14), channel_id=1, source_target_pairs={{0,4},{4,8},{8,12},{12,0},{1,5},{5,9},{9,13},{13,1},{2,6},{6,10},{... | collective-permute-start | bytes 786440 | tf_op jit(solution)/shard_map/ppermute | solution.py:207
  94.9 3.5 %collective-permute-done.7.q_ref = bf16[64,2048]{1,0:T(8,128)(2,1)S(1)} collective-permute-done((bf16[64,2048]{1,0:T(8,128)(2,1)S(1)}, bf16[64,2048]{1,0:T(8,128)(2,1)S(1)}, u32[]{:S(2)}, u32[]{:S(2)}) %collective-permute-start.7) | collective-permute-done | bytes 262176 | tf_op jit(solution)/shard_map/ppermute | solution.py:207
  99.2 11.0 %shard_map.92 = bf16[64,2048]{1,0:T(8,128)(2,1)} custom-call(bf16[64,2048]{1,0:T(8,128)(2,1)} %copy-done.5, bf16[1664,256]{1,0:T(8,128)(2,1)} %pad.7.k_ref, bf16[1664,256]{1,0:T(8,128)(2,1)} %pad.8.v_ref), custom_call_target="tpu_custom_call" | custom-call | flops 872415232 | bytes 2228224 | tf_op jit(solution)/shard_map/pallas_call | solution.py:96
  111.6 11.0 %shard_map.93 = bf16[64,2048]{1,0:T(8,128)(2,1)} custom-call(bf16[64,2048]{1,0:T(8,128)(2,1)} %copy-done.4, bf16[1664,256]{1,0:T(8,128)(2,1)} %pad.7.k_ref, bf16[1664,256]{1,0:T(8,128)(2,1)} %pad.8.v_ref), custom_call_target="tpu_custom_call" | custom-call | flops 872415232 | bytes 2228224 | tf_op jit(solution)/shard_map/pallas_call | solution.py:96
  125.2 11.0 %shard_map.94 = bf16[64,2048]{1,0:T(8,128)(2,1)} custom-call(bf16[64,2048]{1,0:T(8,128)(2,1)} %copy-done.3, bf16[1664,256]{1,0:T(8,128)(2,1)} %pad.7.k_ref, bf16[1664,256]{1,0:T(8,128)(2,1)} %pad.8.v_ref), custom_call_target="tpu_custom_call" | custom-call | flops 872415232 | bytes 2228224 | tf_op jit(solution)/shard_map/pallas_call | solution.py:96
  136.2 9.6 %collective-permute-start.12 = (bf16[64,2048]{1,0:T(8,128)(2,1)}, bf16[64,2048]{1,0:T(8,128)(2,1)S(1)}, u32[]{:S(2)}, u32[]{:S(2)}) collective-permute-start(bf16[64,2048]{1,0:T(8,128)(2,1)} %shard_map.94), channel_id=1, source_target_pairs={{0,4},{4,8},{8,12},{12,0},{1,5},{5,9},{9,13},{13,1},{2,6},{6,10},{... | collective-permute-start | bytes 786440 | tf_op jit(solution)/shard_map/ppermute | solution.py:214
  145.7 11.0 %shard_map.91 = bf16[64,2048]{1,0:T(8,128)(2,1)} custom-call(bf16[64,2048]{1,0:T(8,128)(2,1)} %get-tuple-element.11.q_ref, bf16[1664,256]{1,0:T(8,128)(2,1)} %pad.7.k_ref, bf16[1664,256]{1,0:T(8,128)(2,1)} %pad.8.v_ref), custom_call_target="tpu_custom_call" | custom-call | flops 872415232 | bytes 2228224 | tf_op jit(solution)/shard_map/pallas_call | solution.py:96
  158.3 3.7 %collective-permute-start.15 = (bf16[128,2048]{1,0:T(8,128)(2,1)S(1)}, bf16[128,2048]{1,0:T(8,128)(2,1)S(1)}, u32[]{:S(2)}, u32[]{:S(2)}) collective-permute-start(bf16[128,2048]{1,0:T(8,128)(2,1)S(1)} %convolution_convert_fusion.9), channel_id=1, source_target_pairs={{0,12},{4,0},{8,4},{12,8},{1,13},{5,1},{9,5},{13,9},{2,14},{6,2},{... | collective-permute-start | bytes 1572872 | tf_op jit(solution)/shard_map/ppermute | solution.py:36
  162.3 4.8 %fusion.4 = bf16[4,128,2048]{2,1,0:T(8,128)(2,1)S(1)} fusion(bf16[4,128,2048]{2,1,0:T(8,128)(2,1)S(1)} %broadcast_in_dim.56, s32[]{:T(128)S(6)} %select_n.168, bf16[128,2048]{1,0:T(8,128)(2,1)S(1)} %convolution_convert_fusion.9, bf16[2048,2048]{1,0:T(8,128)(2,1)} %param.14), kind=kOutput, calls=%fused_computation.14 | convolution fusion | flops 1074003968 | bytes 9437188 | tf_op jit(solution)/shard_map/dot_general | solution.py:226
  167.2 7.8 %collective-permute-done.13 = bf16[128,2048]{1,0:T(8,128)(2,1)S(1)} collective-permute-done((bf16[128,2048]{1,0:T(8,128)(2,1)S(1)}, bf16[128,2048]{1,0:T(8,128)(2,1)S(1)}, u32[]{:S(2)}, u32[]{:S(2)}) %collective-permute-start.13) | collective-permute-done | bytes 524320 | tf_op jit(solution)/shard_map/ppermute | solution.py:36
  176.3 19.2 %collective-permute-done.14 = bf16[128,2048]{1,0:T(8,128)(2,1)S(1)} collective-permute-done((bf16[128,2048]{1,0:T(8,128)(2,1)S(1)}, bf16[128,2048]{1,0:T(8,128)(2,1)S(1)}, u32[]{:S(2)}, u32[]{:S(2)}) %collective-permute-start.14) | collective-permute-done | bytes 524320 | tf_op jit(solution)/shard_map/ppermute | solution.py:36
  198.3 2.8 %collective-permute-done.16 = bf16[256,2048]{1,0:T(8,128)(2,1)} collective-permute-done((bf16[256,2048]{1,0:T(8,128)(2,1)S(1)}, bf16[256,2048]{1,0:T(8,128)(2,1)}, u32[]{:S(2)}, u32[]{:S(2)}) %collective-permute-start.16) | collective-permute-done | bytes 1048608 | tf_op jit(solution)/shard_map/ppermute | solution.py:47
  202.8 11.4 %collective-permute-start.17 = (bf16[128,2048]{1,0:T(8,128)(2,1)S(1)}, bf16[128,2048]{1,0:T(8,128)(2,1)S(1)}, u32[]{:S(2)}, u32[]{:S(2)}) collective-permute-start(bf16[128,2048]{1,0:T(8,128)(2,1)S(1)} %get-tuple-element.9), channel_id=1, source_target_pairs={{0,0},{1,8},{2,4},{3,12},{4,1},{5,9},{6,5},{7,13},{8,2},{9,10},{10... | collective-permute-start | bytes 1572872 | tf_op jit(solution)/shard_map/ppermute | solution.py:257
  214.3 11.9 %collective-permute-done.17 = bf16[128,2048]{1,0:T(8,128)(2,1)S(1)} collective-permute-done((bf16[128,2048]{1,0:T(8,128)(2,1)S(1)}, bf16[128,2048]{1,0:T(8,128)(2,1)S(1)}, u32[]{:S(2)}, u32[]{:S(2)}) %collective-permute-start.17) | collective-permute-done | bytes 524320 | tf_op jit(solution)/shard_map/ppermute | solution.py:257
  226.1 13.5 %collective-permute-done.18 = bf16[128,2048]{1,0:T(8,128)(2,1)S(1)} collective-permute-done((bf16[128,2048]{1,0:T(8,128)(2,1)S(1)}, bf16[128,2048]{1,0:T(8,128)(2,1)S(1)}, u32[]{:S(2)}, u32[]{:S(2)}) %collective-permute-start.18) | collective-permute-done | bytes 524320 | tf_op jit(solution)/shard_map/ppermute | solution.py:257
  239.7 2.1 add_convert_fusion
  (94 shorter events, 33.8 us)
Async XLA Ops:
  0.0 44.8 %copy-start = (f32[128]{0:T(128)S(1)}, f32[128]{0:T(128)}, u32[]{:S(2)}) copy-start(f32[128]{0:T(128)} %param.11) | copy-start | bytes 1540
  3.5 11.2 %collective-permute-start = (bf16[128,1024]{1,0:T(8,128)(2,1)S(1)}, bf16[128,1024]{1,0:T(8,128)(2,1)S(1)}, u32[]{:S(2)}, u32[]{:S(2)}) collective-permute-start(bf16[128,1024]{1,0:T(8,128)(2,1)S(1)} %bitcast.86), channel_id=1, source_target_pairs={{0,4},{4,8},{8,12},{12,0},{1,5},{5,9},{9,13},{13,1},{2,6},{6,10},{... | collective-permute-start | bytes 786440 | tf_op jit(solution)/shard_map/ppermute | solution.py:146
  5.3 19.5 %collective-permute-start.1 = (bf16[128,1024]{1,0:T(8,128)(2,1)S(1)}, bf16[128,1024]{1,0:T(8,128)(2,1)S(1)}, u32[]{:S(2)}, u32[]{:S(2)}) collective-permute-start(bf16[128,1024]{1,0:T(8,128)(2,1)S(1)} %bitcast.85), channel_id=1, source_target_pairs={{0,8},{4,12},{8,0},{12,4},{1,9},{5,13},{9,1},{13,5},{2,10},{6,14},... | collective-permute-start | bytes 786440 | tf_op jit(solution)/shard_map/ppermute | solution.py:146
  7.9 17.1 %copy-start.6 = (s32[4]{0:T(128)S(1)}, s32[4]{0:T(128)}, u32[]{:S(2)}) copy-start(s32[4]{0:T(128)} %param.17) | copy-start | bytes 52
  7.9 17.1 %copy-start.7 = (s32[128]{0:T(128)S(1)}, s32[128]{0:T(128)}, u32[]{:S(2)}) copy-start(s32[128]{0:T(128)} %param.15) | copy-start | bytes 1540
  7.9 17.3 %copy-start.8 = (s32[128]{0:T(128)S(1)}, s32[128]{0:T(128)}, u32[]{:S(2)}) copy-start(s32[128]{0:T(128)} %param.16) | copy-start | bytes 1540
  8.1 16.8 %collective-permute-start.2 = (bf16[128,1024]{1,0:T(8,128)(2,1)S(1)}, bf16[128,1024]{1,0:T(8,128)(2,1)S(1)}, u32[]{:S(2)}, u32[]{:S(2)}) collective-permute-start(bf16[128,1024]{1,0:T(8,128)(2,1)S(1)} %bitcast.84), channel_id=1, source_target_pairs={{0,12},{4,0},{8,4},{12,8},{1,13},{5,1},{9,5},{13,9},{2,14},{6,2},{... | collective-permute-start | bytes 786440 | tf_op jit(solution)/shard_map/ppermute | solution.py:146
  24.9 2.7 %collective-permute-start.3 = (bf16[512,1024]{1,0:T(8,128)(2,1)S(1)}, bf16[512,1024]{1,0:T(8,128)(2,1)S(1)}, u32[]{:S(2)}, u32[]{:S(2)}) collective-permute-start(bf16[512,1024]{1,0:T(8,128)(2,1)S(1)} %bitcast.79), channel_id=1, source_target_pairs={{0,1},{1,0},{2,3},{3,2},{4,5},{5,4},{6,7},{7,6},{8,9},{9,8},{10,11... | collective-permute-start | bytes 3145736 | tf_op jit(solution)/shard_map/ppermute | solution.py:158
  32.6 20.0 %collective-permute-start.4 = (bf16[128,2048]{1,0:T(8,128)(2,1)S(1)}, bf16[128,2048]{1,0:T(8,128)(2,1)S(1)}, u32[]{:S(2)}, u32[]{:S(2)}) collective-permute-start(bf16[128,2048]{1,0:T(8,128)(2,1)S(1)} %convolution_convert_fusion.7), channel_id=1, source_target_pairs={{0,4},{4,8},{8,12},{12,0},{1,5},{5,9},{9,13},{13,1},{2,6},{6,10},{... | collective-permute-start | bytes 1572872 | tf_op jit(solution)/shard_map/ppermute | solution.py:24
  40.0 34.6 %collective-permute-start.5 = (bf16[128,2048]{1,0:T(8,128)(2,1)S(1)}, bf16[128,2048]{1,0:T(8,128)(2,1)S(1)}, u32[]{:S(2)}, u32[]{:S(2)}) collective-permute-start(bf16[128,2048]{1,0:T(8,128)(2,1)S(1)} %convolution_convert_fusion.6), channel_id=1, source_target_pairs={{0,8},{4,12},{8,0},{12,4},{1,9},{5,13},{9,1},{13,5},{2,10},{6,14},... | collective-permute-start | bytes 1572872 | tf_op jit(solution)/shard_map/ppermute | solution.py:24
  43.0 31.6 %collective-permute-start.6 = (bf16[128,2048]{1,0:T(8,128)(2,1)S(1)}, bf16[128,2048]{1,0:T(8,128)(2,1)S(1)}, u32[]{:S(2)}, u32[]{:S(2)}) collective-permute-start(bf16[128,2048]{1,0:T(8,128)(2,1)S(1)} %convolution_convert_fusion.5), channel_id=1, source_target_pairs={{0,12},{4,0},{8,4},{12,8},{1,13},{5,1},{9,5},{13,9},{2,14},{6,2},{... | collective-permute-start | bytes 1572872 | tf_op jit(solution)/shard_map/ppermute | solution.py:24
  77.3 15.5 %copy-start.1 = (bf16[1,1601,512]{2,1,0:T(8,128)(2,1)S(1)}, bf16[1,1601,512]{2,1,0:T(8,128)(2,1)}, u32[]{:S(2)}) copy-start(bf16[1,1601,512]{2,1,0:T(8,128)(2,1)} %param.13) | copy-start | bytes 4918276
  78.8 19.7 %collective-permute-start.7 = (bf16[64,2048]{1,0:T(8,128)(2,1)S(1)}, bf16[64,2048]{1,0:T(8,128)(2,1)S(1)}, u32[]{:S(2)}, u32[]{:S(2)}) collective-permute-start(bf16[64,2048]{1,0:T(8,128)(2,1)S(1)} %get-tuple-element.14), channel_id=1, source_target_pairs={{0,4},{4,8},{8,12},{12,0},{1,5},{5,9},{9,13},{13,1},{2,6},{6,10},{... | collective-permute-start | bytes 786440 | tf_op jit(solution)/shard_map/ppermute | solution.py:207
  90.5 20.5 %collective-permute-start.9 = (bf16[64,2048]{1,0:T(8,128)(2,1)S(1)}, bf16[64,2048]{1,0:T(8,128)(2,1)S(1)}, u32[]{:S(2)}, u32[]{:S(2)}) collective-permute-start(bf16[64,2048]{1,0:T(8,128)(2,1)S(1)} %get-tuple-element.13), channel_id=1, source_target_pairs={{0,8},{4,12},{8,0},{12,4},{1,9},{5,13},{9,1},{13,5},{2,10},{6,14},... | collective-permute-start | bytes 786440 | tf_op jit(solution)/shard_map/ppermute | solution.py:207
  91.7 32.8 %collective-permute-start.11 = (bf16[64,2048]{1,0:T(8,128)(2,1)S(1)}, bf16[64,2048]{1,0:T(8,128)(2,1)S(1)}, u32[]{:S(2)}, u32[]{:S(2)}) collective-permute-start(bf16[64,2048]{1,0:T(8,128)(2,1)S(1)} %get-tuple-element.12), channel_id=1, source_target_pairs={{0,12},{4,0},{8,4},{12,8},{1,13},{5,1},{9,5},{13,9},{2,14},{6,2},{... | collective-permute-start | bytes 786440 | tf_op jit(solution)/shard_map/ppermute | solution.py:207
  110.1 46.6 %collective-permute-start.8 = (bf16[64,2048]{1,0:T(8,128)(2,1)}, bf16[64,2048]{1,0:T(8,128)(2,1)S(1)}, u32[]{:S(2)}, u32[]{:S(2)}) collective-permute-start(bf16[64,2048]{1,0:T(8,128)(2,1)} %shard_map.92), channel_id=1, source_target_pairs={{0,12},{4,0},{8,4},{12,8},{1,13},{5,1},{9,5},{13,9},{2,14},{6,2},{... | collective-permute-start | bytes 786440 | tf_op jit(solution)/shard_map/ppermute | solution.py:214
  122.6 34.1 %collective-permute-start.10 = (bf16[64,2048]{1,0:T(8,128)(2,1)}, bf16[64,2048]{1,0:T(8,128)(2,1)S(1)}, u32[]{:S(2)}, u32[]{:S(2)}) collective-permute-start(bf16[64,2048]{1,0:T(8,128)(2,1)} %shard_map.93), channel_id=1, source_target_pairs={{0,8},{4,12},{8,0},{12,4},{1,9},{5,13},{9,1},{13,5},{2,10},{6,14},... | collective-permute-start | bytes 786440 | tf_op jit(solution)/shard_map/ppermute | solution.py:214
  136.2 20.6 %collective-permute-start.12 = (bf16[64,2048]{1,0:T(8,128)(2,1)}, bf16[64,2048]{1,0:T(8,128)(2,1)S(1)}, u32[]{:S(2)}, u32[]{:S(2)}) collective-permute-start(bf16[64,2048]{1,0:T(8,128)(2,1)} %shard_map.94), channel_id=1, source_target_pairs={{0,4},{4,8},{8,12},{12,0},{1,5},{5,9},{9,13},{13,1},{2,6},{6,10},{... | collective-permute-start | bytes 786440 | tf_op jit(solution)/shard_map/ppermute | solution.py:214
  158.2 16.8 %collective-permute-start.13 = (bf16[128,2048]{1,0:T(8,128)(2,1)S(1)}, bf16[128,2048]{1,0:T(8,128)(2,1)S(1)}, u32[]{:S(2)}, u32[]{:S(2)}) collective-permute-start(bf16[128,2048]{1,0:T(8,128)(2,1)S(1)} %convolution_convert_fusion.9), channel_id=1, source_target_pairs={{0,4},{4,8},{8,12},{12,0},{1,5},{5,9},{9,13},{13,1},{2,6},{6,10},{... | collective-permute-start | bytes 1572872 | tf_op jit(solution)/shard_map/ppermute | solution.py:36
  158.3 37.2 %collective-permute-start.14 = (bf16[128,2048]{1,0:T(8,128)(2,1)S(1)}, bf16[128,2048]{1,0:T(8,128)(2,1)S(1)}, u32[]{:S(2)}, u32[]{:S(2)}) collective-permute-start(bf16[128,2048]{1,0:T(8,128)(2,1)S(1)} %convolution_convert_fusion.9), channel_id=1, source_target_pairs={{0,8},{4,12},{8,0},{12,4},{1,9},{5,13},{9,1},{13,5},{2,10},{6,14},... | collective-permute-start | bytes 1572872 | tf_op jit(solution)/shard_map/ppermute | solution.py:36
  158.3 38.4 %collective-permute-start.15 = (bf16[128,2048]{1,0:T(8,128)(2,1)S(1)}, bf16[128,2048]{1,0:T(8,128)(2,1)S(1)}, u32[]{:S(2)}, u32[]{:S(2)}) collective-permute-start(bf16[128,2048]{1,0:T(8,128)(2,1)S(1)} %convolution_convert_fusion.9), channel_id=1, source_target_pairs={{0,12},{4,0},{8,4},{12,8},{1,13},{5,1},{9,5},{13,9},{2,14},{6,2},{... | collective-permute-start | bytes 1572872 | tf_op jit(solution)/shard_map/ppermute | solution.py:36
  198.2 2.9 %collective-permute-start.16 = (bf16[256,2048]{1,0:T(8,128)(2,1)S(1)}, bf16[256,2048]{1,0:T(8,128)(2,1)}, u32[]{:S(2)}, u32[]{:S(2)}) collective-permute-start(bf16[256,2048]{1,0:T(8,128)(2,1)S(1)} %dynamic-slice_bitcast_fusion), channel_id=1, source_target_pairs={{0,1},{1,0},{2,3},{3,2},{4,5},{5,4},{6,7},{7,6},{8,9},{9,8},{10,11... | collective-permute-start | bytes 3145736 | tf_op jit(solution)/shard_map/ppermute | solution.py:47
  202.8 23.3 %collective-permute-start.17 = (bf16[128,2048]{1,0:T(8,128)(2,1)S(1)}, bf16[128,2048]{1,0:T(8,128)(2,1)S(1)}, u32[]{:S(2)}, u32[]{:S(2)}) collective-permute-start(bf16[128,2048]{1,0:T(8,128)(2,1)S(1)} %get-tuple-element.9), channel_id=1, source_target_pairs={{0,0},{1,8},{2,4},{3,12},{4,1},{5,9},{6,5},{7,13},{8,2},{9,10},{10... | collective-permute-start | bytes 1572872 | tf_op jit(solution)/shard_map/ppermute | solution.py:257
  214.2 25.5 %collective-permute-start.18 = (bf16[128,2048]{1,0:T(8,128)(2,1)S(1)}, bf16[128,2048]{1,0:T(8,128)(2,1)S(1)}, u32[]{:S(2)}, u32[]{:S(2)}) collective-permute-start(bf16[128,2048]{1,0:T(8,128)(2,1)S(1)} %get-tuple-element.10), channel_id=1, source_target_pairs={{0,4},{1,12},{2,0},{3,8},{4,5},{5,13},{6,1},{7,9},{8,6},{9,14},{10... | collective-permute-start | bytes 1572872 | tf_op jit(solution)/shard_map/ppermute | solution.py:257
  (8 other events, 65.3 us)

commit v13 on v12

--- a/solution.py
+++ b/solution.py
@@ -15,6 +15,94 @@
     per_head = queries.astype(jnp.float32).reshape(row_count, -1, head_dim)
     inv_rms = lax.rsqrt(jnp.mean(per_head * per_head, axis=2, keepdims=True) + 1e-05)
     return (per_head * inv_rms * q_gain).reshape(row_count, -1).astype(jnp.bfloat16)
+
+
+def direct_reduce_scatter(chunk_of, axis, count, index):
+    total = None
+    for shift in range(1, count):
+        outgoing = chunk_of((index + shift) % count).astype(jnp.bfloat16)
+        incoming = lax.ppermute(outgoing, axis, [(i, (i + shift) % count) for i in range(count)])
+        incoming = incoming.astype(jnp.float32)
+        total = incoming if total is None else total + incoming
+    own = chunk_of(index)
+    return own if total is None else own + total
+
+
+def direct_gather_apply(block, apply, axis, count, index):
+    own = apply(block)
+    placed = jnp.zeros((count,) + own.shape, own.dtype)
+    placed = lax.dynamic_update_index_in_dim(placed, own, index, 0)
+    for shift in range(1, count):
+        incoming = lax.ppermute(block, axis, [(i, (i + shift) % count) for i in range(count)])
+        placed = lax.dynamic_update_index_in_dim(
+            placed, apply(incoming), (index - shift) % count, 0
+        )
+    return placed
+
+
+def exchange_sum(parts, axis, count, index):
+    total = lax.dynamic_index_in_dim(parts, index, axis=0, keepdims=False).astype(jnp.float32)
+    for shift in range(1, count):
+        outgoing = lax.dynamic_index_in_dim(parts, (index + shift) % count, axis=0, keepdims=False)
+        incoming = lax.ppermute(outgoing, axis, [(i, (i + shift) % count) for i in range(count)])
+        total = total + incoming.astype(jnp.float32)
+    return total.astype(jnp.bfloat16)
+
+
+def attend_kernel(q_ref, k_ref, v_ref, o_ref, *, head_dim, token_count):
+    padded_tokens = k_ref.shape[0]
+    split = (token_count // 128) * 128
+    scores = lax.dot_general(
+        q_ref[0], k_ref[...], (((1,), (1,)), ((), ())), preferred_element_type=jnp.float32
+    ) * (head_dim ** (-0.5))
+    pieces = [scores[:, :split]] if split else []
+    if split < padded_tokens:
+        tail = scores[:, split:]
+        valid = lax.broadcasted_iota(jnp.int32, tail.shape, 1) < token_count - split
+        pieces.append(jnp.where(valid, tail, -jnp.inf))
+    peak = jnp.max(pieces[0], axis=1, keepdims=True)
+    for piece in pieces[1:]:
+        peak = jnp.maximum(peak, jnp.max(piece, axis=1, keepdims=True))
+    weights = [jnp.exp(piece - peak) for piece in pieces]
+    total = sum(jnp.sum(w, axis=1, keepdims=True) for w in weights)
+    inverse = 1.0 / total
+    mixed = None
+    start = 0
+    for w in weights:
+        width = w.shape[1]
+        probs = (w * inverse).astype(jnp.bfloat16)
+        term = jnp.dot(probs, v_ref[start:start + width, :], preferred_element_type=jnp.float32)
+        mixed = term if mixed is None else mixed + term
+        start += width
+    o_ref[0] = mixed.astype(o_ref.dtype)
+
+
+def attend(rows_in, keys, values, kv_count, per_kv, head_dim, token_count):
+    rows, width = rows_in.shape
+    padded_tokens = keys.shape[0]
+    stacked = rows_in.reshape(rows, kv_count, per_kv, head_dim).transpose(1, 2, 0, 3)
+    stacked = stacked.reshape(kv_count, per_kv * rows, head_dim)
+    kernel = functools.partial(attend_kernel, head_dim=head_dim, token_count=token_count)
+    flops = 4 * rows * padded_tokens * head_dim * per_kv * kv_count
+    moved = 2 * (2 * rows * width + 2 * padded_tokens * head_dim * kv_count)
+    mixed = pl.pallas_call(
+        kernel,
+        grid=(kv_count,),
+        in_specs=[
+            pl.BlockSpec((1, per_kv * rows, head_dim), lambda k: (k, 0, 0)),
+            pl.BlockSpec((padded_tokens, head_dim), lambda k: (0, k)),
+            pl.BlockSpec((padded_tokens, head_dim), lambda k: (0, k)),
+        ],
+        out_specs=pl.BlockSpec((1, per_kv * rows, head_dim), lambda k: (k, 0, 0)),
+        out_shape=jax.ShapeDtypeStruct((kv_count, per_kv * rows, head_dim), jnp.bfloat16),
+        cost_estimate=pl.CostEstimate(
+            flops=flops,
+            transcendentals=rows * padded_tokens * per_kv * kv_count,
+            bytes_accessed=moved,
+        ),
+    )(stacked, keys, values)
+    mixed = mixed.reshape(kv_count, per_kv, rows, head_dim).transpose(2, 0, 1, 3)
+    return mixed.reshape(rows, width)
 
 
 def direct_reduce_scatter(chunk_of, axis, count, index):

time: 242 us -> 242 us (level)
  no operation moved by 1% of the time
where the time goes in v13:
time: 242 us
  waiting for transfers between devices  105 us (43%)
  starting transfers between devices  56.8 us (23%)
  Pallas kernels  43.9 us (18%)
  matrix products  18.6 us (8%)
  local copies, waits for them, and re-layouts  10.8 us (4%)
  other arithmetic  5.88 us (2%)
    pallas_call x4, Pallas kernels, attend(): pl.pallas_call(kernel, grid=(kv_count,), in_specs=[pl.BlockSpec((rows, gr...  43.9 us
    ppermute x3, waiting for transfers between devices, direct_reduce_scatter(): lax.ppermute(outgoing, axis, [(i, (i + shift) % count) for i in range(cou...  29.7 us
    ppermute x3, waiting for transfers between devices, direct_gather_apply(): lax.ppermute(block, axis, [(i, (i + shift) % count) for i in range(count)])  27 us
    ppermute x2, waiting for transfers between devices, local(): got = lax.ppermute(chunk, ('req', 'head', 'sub'), pairs).astype(jnp.float32)  25.4 us
    ppermute x3, waiting for transfers between devices, local(): lax.ppermute(outgoing_part, 'req', [(i, (i + shift) % req_count) for i in...  14.9 us
    ppermute x3, starting transfers between devices, local(): lax.ppermute(outgoing[shift], 'req', [(i, (i + shift) % req_count) for i...  14.1 us
    ppermute x3, starting transfers between devices, local(): lax.ppermute(mixed_block, 'req', [(i, (i - shift) % req_count) for i in r...  12.2 us
    ppermute x2, starting transfers between devices, local(): got = lax.ppermute(chunk, ('req', 'head', 'sub'), pairs).astype(jnp.float32)  11.4 us
  transfers between devices with their start and end apart: 19, of which 11 were waited for; matrix products, arithmetic and copies ran while one was open for 6% of the time, Pallas kernels for 18%

profile of v13, /device:TPU:6, one launch (start us, length us, event | category | flops | bytes accessed | tf_op | source)
XLA Modules:
  0.0 241.8 jit_solution(14238812116996338807)
XLA Ops:
  0.0 3.2 %copy.21 = bf16[128,8192]{0,1:T(8,128)(2,1)S(1)} copy(bf16[128,8192]{1,0:T(8,128)(2,1)} %param.9) | data formatting | bytes 4194304 | tf_op args[0]
  5.3 2.7 %collective-permute-start.1 = (bf16[128,1024]{1,0:T(8,128)(2,1)S(1)}, bf16[128,1024]{1,0:T(8,128)(2,1)S(1)}, u32[]{:S(2)}, u32[]{:S(2)}) collective-permute-start(bf16[128,1024]{1,0:T(8,128)(2,1)S(1)} %bitcast.85), channel_id=1, source_target_pairs={{0,8},{4,12},{8,0},{12,4},{1,9},{5,13},{9,1},{13,5},{2,10},{6,14},... | collective-permute-start | bytes 786440 | tf_op jit(solution)/shard_map/ppermute | solution.py:234
  9.9 4.8 %collective-permute-done = bf16[128,1024]{1,0:T(8,128)(2,1)S(1)} collective-permute-done((bf16[128,1024]{1,0:T(8,128)(2,1)S(1)}, bf16[128,1024]{1,0:T(8,128)(2,1)S(1)}, u32[]{:S(2)}, u32[]{:S(2)}) %collective-permute-start) | collective-permute-done | bytes 262176 | tf_op jit(solution)/shard_map/ppermute | solution.py:234
  14.7 10.1 %collective-permute-done.1 = bf16[128,1024]{1,0:T(8,128)(2,1)S(1)} collective-permute-done((bf16[128,1024]{1,0:T(8,128)(2,1)S(1)}, bf16[128,1024]{1,0:T(8,128)(2,1)S(1)}, u32[]{:S(2)}, u32[]{:S(2)}) %collective-permute-start.1) | collective-permute-done | bytes 262176 | tf_op jit(solution)/shard_map/ppermute | solution.py:234
  27.8 4.8 %convolution_convert_fusion.7 = bf16[128,2048]{1,0:T(8,128)(2,1)S(1)} fusion(bf16[2048,2048]{1,0:T(8,128)(2,1)} %param.10, bf16[512,2048]{1,0:T(8,128)(2,1)S(1)} %constant_dynamic-update-slice_fusion, s32[]{:T(128)S(6)} %select_n.191), kind=kOutput, calls=%fused_computation.7 | convolution fusion | flops 1074003968 | bytes 9437188 | tf_op jit(solution)/shard_map/dot_general | solution.py:254
  32.6 6.1 %collective-permute-start.4 = (bf16[128,2048]{1,0:T(8,128)(2,1)S(1)}, bf16[128,2048]{1,0:T(8,128)(2,1)S(1)}, u32[]{:S(2)}, u32[]{:S(2)}) collective-permute-start(bf16[128,2048]{1,0:T(8,128)(2,1)S(1)} %convolution_convert_fusion.7), channel_id=1, source_target_pairs={{0,4},{4,8},{8,12},{12,0},{1,5},{5,9},{9,13},{13,1},{2,6},{6,10},{... | collective-permute-start | bytes 1572872 | tf_op jit(solution)/shard_map/ppermute | solution.py:112
  44.8 7.8 %collective-permute-done.4 = bf16[128,2048]{1,0:T(8,128)(2,1)S(1)} collective-permute-done((bf16[128,2048]{1,0:T(8,128)(2,1)S(1)}, bf16[128,2048]{1,0:T(8,128)(2,1)S(1)}, u32[]{:S(2)}, u32[]{:S(2)}) %collective-permute-start.4) | collective-permute-done | bytes 524320 | tf_op jit(solution)/shard_map/ppermute | solution.py:112
  52.6 22.0 %collective-permute-done.5 = bf16[128,2048]{1,0:T(8,128)(2,1)S(1)} collective-permute-done((bf16[128,2048]{1,0:T(8,128)(2,1)S(1)}, bf16[128,2048]{1,0:T(8,128)(2,1)S(1)}, u32[]{:S(2)}, u32[]{:S(2)}) %collective-permute-start.5) | collective-permute-done | bytes 524320 | tf_op jit(solution)/shard_map/ppermute | solution.py:112
  78.8 11.7 %collective-permute-start.7 = (bf16[64,2048]{1,0:T(8,128)(2,1)S(1)}, bf16[64,2048]{1,0:T(8,128)(2,1)S(1)}, u32[]{:S(2)}, u32[]{:S(2)}) collective-permute-start(bf16[64,2048]{1,0:T(8,128)(2,1)S(1)} %get-tuple-element.14), channel_id=1, source_target_pairs={{0,4},{4,8},{8,12},{12,0},{1,5},{5,9},{9,13},{13,1},{2,6},{6,10},{... | collective-permute-start | bytes 786440 | tf_op jit(solution)/shard_map/ppermute | solution.py:295
  94.9 3.5 %collective-permute-done.7.q_ref = bf16[64,2048]{1,0:T(8,128)(2,1)S(1)} collective-permute-done((bf16[64,2048]{1,0:T(8,128)(2,1)S(1)}, bf16[64,2048]{1,0:T(8,128)(2,1)S(1)}, u32[]{:S(2)}, u32[]{:S(2)}) %collective-permute-start.7) | collective-permute-done | bytes 262176 | tf_op jit(solution)/shard_map/ppermute | solution.py:295
  99.2 11.0 %shard_map.92 = bf16[64,2048]{1,0:T(8,128)(2,1)} custom-call(bf16[64,2048]{1,0:T(8,128)(2,1)} %copy-done.5, bf16[1664,256]{1,0:T(8,128)(2,1)} %pad.7.k_ref, bf16[1664,256]{1,0:T(8,128)(2,1)} %pad.8.v_ref), custom_call_target="tpu_custom_call" | custom-call | flops 872415232 | bytes 2228224 | tf_op jit(solution)/shard_map/pallas_call | solution.py:184
  111.6 11.0 %shard_map.93 = bf16[64,2048]{1,0:T(8,128)(2,1)} custom-call(bf16[64,2048]{1,0:T(8,128)(2,1)} %copy-done.4, bf16[1664,256]{1,0:T(8,128)(2,1)} %pad.7.k_ref, bf16[1664,256]{1,0:T(8,128)(2,1)} %pad.8.v_ref), custom_call_target="tpu_custom_call" | custom-call | flops 872415232 | bytes 2228224 | tf_op jit(solution)/shard_map/pallas_call | solution.py:184
  125.2 11.0 %shard_map.94 = bf16[64,2048]{1,0:T(8,128)(2,1)} custom-call(bf16[64,2048]{1,0:T(8,128)(2,1)} %copy-done.3, bf16[1664,256]{1,0:T(8,128)(2,1)} %pad.7.k_ref, bf16[1664,256]{1,0:T(8,128)(2,1)} %pad.8.v_ref), custom_call_target="tpu_custom_call" | custom-call | flops 872415232 | bytes 2228224 | tf_op jit(solution)/shard_map/pallas_call | solution.py:184
  136.2 9.6 %collective-permute-start.12 = (bf16[64,2048]{1,0:T(8,128)(2,1)}, bf16[64,2048]{1,0:T(8,128)(2,1)S(1)}, u32[]{:S(2)}, u32[]{:S(2)}) collective-permute-start(bf16[64,2048]{1,0:T(8,128)(2,1)} %shard_map.94), channel_id=1, source_target_pairs={{0,4},{4,8},{8,12},{12,0},{1,5},{5,9},{9,13},{13,1},{2,6},{6,10},{... | collective-permute-start | bytes 786440 | tf_op jit(solution)/shard_map/ppermute | solution.py:302
  145.7 11.0 %shard_map.91 = bf16[64,2048]{1,0:T(8,128)(2,1)} custom-call(bf16[64,2048]{1,0:T(8,128)(2,1)} %get-tuple-element.11.q_ref, bf16[1664,256]{1,0:T(8,128)(2,1)} %pad.7.k_ref, bf16[1664,256]{1,0:T(8,128)(2,1)} %pad.8.v_ref), custom_call_target="tpu_custom_call" | custom-call | flops 872415232 | bytes 2228224 | tf_op jit(solution)/shard_map/pallas_call | solution.py:184
  158.3 3.7 %collective-permute-start.15 = (bf16[128,2048]{1,0:T(8,128)(2,1)S(1)}, bf16[128,2048]{1,0:T(8,128)(2,1)S(1)}, u32[]{:S(2)}, u32[]{:S(2)}) collective-permute-start(bf16[128,2048]{1,0:T(8,128)(2,1)S(1)} %convolution_convert_fusion.9), channel_id=1, source_target_pairs={{0,12},{4,0},{8,4},{12,8},{1,13},{5,1},{9,5},{13,9},{2,14},{6,2},{... | collective-permute-start | bytes 1572872 | tf_op jit(solution)/shard_map/ppermute | solution.py:124
  162.3 4.8 %fusion.4 = bf16[4,128,2048]{2,1,0:T(8,128)(2,1)S(1)} fusion(bf16[4,128,2048]{2,1,0:T(8,128)(2,1)S(1)} %broadcast_in_dim.56, s32[]{:T(128)S(6)} %select_n.168, bf16[128,2048]{1,0:T(8,128)(2,1)S(1)} %convolution_convert_fusion.9, bf16[2048,2048]{1,0:T(8,128)(2,1)} %param.14), kind=kOutput, calls=%fused_computation.14 | convolution fusion | flops 1074003968 | bytes 9437188 | tf_op jit(solution)/shard_map/dot_general | solution.py:314
  167.2 7.8 %collective-permute-done.13 = bf16[128,2048]{1,0:T(8,128)(2,1)S(1)} collective-permute-done((bf16[128,2048]{1,0:T(8,128)(2,1)S(1)}, bf16[128,2048]{1,0:T(8,128)(2,1)S(1)}, u32[]{:S(2)}, u32[]{:S(2)}) %collective-permute-start.13) | collective-permute-done | bytes 524320 | tf_op jit(solution)/shard_map/ppermute | solution.py:124
  176.3 19.2 %collective-permute-done.14 = bf16[128,2048]{1,0:T(8,128)(2,1)S(1)} collective-permute-done((bf16[128,2048]{1,0:T(8,128)(2,1)S(1)}, bf16[128,2048]{1,0:T(8,128)(2,1)S(1)}, u32[]{:S(2)}, u32[]{:S(2)}) %collective-permute-start.14) | collective-permute-done | bytes 524320 | tf_op jit(solution)/shard_map/ppermute | solution.py:124
  198.3 2.8 %collective-permute-done.16 = bf16[256,2048]{1,0:T(8,128)(2,1)} collective-permute-done((bf16[256,2048]{1,0:T(8,128)(2,1)S(1)}, bf16[256,2048]{1,0:T(8,128)(2,1)}, u32[]{:S(2)}, u32[]{:S(2)}) %collective-permute-start.16) | collective-permute-done | bytes 1048608 | tf_op jit(solution)/shard_map/ppermute | solution.py:135
  202.8 11.4 %collective-permute-start.17 = (bf16[128,2048]{1,0:T(8,128)(2,1)S(1)}, bf16[128,2048]{1,0:T(8,128)(2,1)S(1)}, u32[]{:S(2)}, u32[]{:S(2)}) collective-permute-start(bf16[128,2048]{1,0:T(8,128)(2,1)S(1)} %get-tuple-element.9), channel_id=1, source_target_pairs={{0,0},{1,8},{2,4},{3,12},{4,1},{5,9},{6,5},{7,13},{8,2},{9,10},{10... | collective-permute-start | bytes 1572872 | tf_op jit(solution)/shard_map/ppermute | solution.py:345
  214.3 11.9 %collective-permute-done.17 = bf16[128,2048]{1,0:T(8,128)(2,1)S(1)} collective-permute-done((bf16[128,2048]{1,0:T(8,128)(2,1)S(1)}, bf16[128,2048]{1,0:T(8,128)(2,1)S(1)}, u32[]{:S(2)}, u32[]{:S(2)}) %collective-permute-start.17) | collective-permute-done | bytes 524320 | tf_op jit(solution)/shard_map/ppermute | solution.py:345
  226.1 13.5 %collective-permute-done.18 = bf16[128,2048]{1,0:T(8,128)(2,1)S(1)} collective-permute-done((bf16[128,2048]{1,0:T(8,128)(2,1)S(1)}, bf16[128,2048]{1,0:T(8,128)(2,1)S(1)}, u32[]{:S(2)}, u32[]{:S(2)}) %collective-permute-start.18) | collective-permute-done | bytes 524320 | tf_op jit(solution)/shard_map/ppermute | solution.py:345
  239.7 2.1 add_convert_fusion
  (94 shorter events, 33.8 us)
Async XLA Ops:
  0.0 44.8 %copy-start = (f32[128]{0:T(128)S(1)}, f32[128]{0:T(128)}, u32[]{:S(2)}) copy-start(f32[128]{0:T(128)} %param.11) | copy-start | bytes 1540
  3.5 11.2 %collective-permute-start = (bf16[128,1024]{1,0:T(8,128)(2,1)S(1)}, bf16[128,1024]{1,0:T(8,128)(2,1)S(1)}, u32[]{:S(2)}, u32[]{:S(2)}) collective-permute-start(bf16[128,1024]{1,0:T(8,128)(2,1)S(1)} %bitcast.86), channel_id=1, source_target_pairs={{0,4},{4,8},{8,12},{12,0},{1,5},{5,9},{9,13},{13,1},{2,6},{6,10},{... | collective-permute-start | bytes 786440 | tf_op jit(solution)/shard_map/ppermute | solution.py:234
  5.3 19.5 %collective-permute-start.1 = (bf16[128,1024]{1,0:T(8,128)(2,1)S(1)}, bf16[128,1024]{1,0:T(8,128)(2,1)S(1)}, u32[]{:S(2)}, u32[]{:S(2)}) collective-permute-start(bf16[128,1024]{1,0:T(8,128)(2,1)S(1)} %bitcast.85), channel_id=1, source_target_pairs={{0,8},{4,12},{8,0},{12,4},{1,9},{5,13},{9,1},{13,5},{2,10},{6,14},... | collective-permute-start | bytes 786440 | tf_op jit(solution)/shard_map/ppermute | solution.py:234
  7.9 17.1 %copy-start.6 = (s32[4]{0:T(128)S(1)}, s32[4]{0:T(128)}, u32[]{:S(2)}) copy-start(s32[4]{0:T(128)} %param.17) | copy-start | bytes 52
  7.9 17.1 %copy-start.7 = (s32[128]{0:T(128)S(1)}, s32[128]{0:T(128)}, u32[]{:S(2)}) copy-start(s32[128]{0:T(128)} %param.15) | copy-start | bytes 1540
  7.9 17.3 %copy-start.8 = (s32[128]{0:T(128)S(1)}, s32[128]{0:T(128)}, u32[]{:S(2)}) copy-start(s32[128]{0:T(128)} %param.16) | copy-start | bytes 1540
  8.1 16.8 %collective-permute-start.2 = (bf16[128,1024]{1,0:T(8,128)(2,1)S(1)}, bf16[128,1024]{1,0:T(8,128)(2,1)S(1)}, u32[]{:S(2)}, u32[]{:S(2)}) collective-permute-start(bf16[128,1024]{1,0:T(8,128)(2,1)S(1)} %bitcast.84), channel_id=1, source_target_pairs={{0,12},{4,0},{8,4},{12,8},{1,13},{5,1},{9,5},{13,9},{2,14},{6,2},{... | collective-permute-start | bytes 786440 | tf_op jit(solution)/shard_map/ppermute | solution.py:234
  24.9 2.7 %collective-permute-start.3 = (bf16[512,1024]{1,0:T(8,128)(2,1)S(1)}, bf16[512,1024]{1,0:T(8,128)(2,1)S(1)}, u32[]{:S(2)}, u32[]{:S(2)}) collective-permute-start(bf16[512,1024]{1,0:T(8,128)(2,1)S(1)} %bitcast.79), channel_id=1, source_target_pairs={{0,1},{1,0},{2,3},{3,2},{4,5},{5,4},{6,7},{7,6},{8,9},{9,8},{10,11... | collective-permute-start | bytes 3145736 | tf_op jit(solution)/shard_map/ppermute | solution.py:246
  32.6 20.0 %collective-permute-start.4 = (bf16[128,2048]{1,0:T(8,128)(2,1)S(1)}, bf16[128,2048]{1,0:T(8,128)(2,1)S(1)}, u32[]{:S(2)}, u32[]{:S(2)}) collective-permute-start(bf16[128,2048]{1,0:T(8,128)(2,1)S(1)} %convolution_convert_fusion.7), channel_id=1, source_target_pairs={{0,4},{4,8},{8,12},{12,0},{1,5},{5,9},{9,13},{13,1},{2,6},{6,10},{... | collective-permute-start | bytes 1572872 | tf_op jit(solution)/shard_map/ppermute | solution.py:112
  40.0 34.6 %collective-permute-start.5 = (bf16[128,2048]{1,0:T(8,128)(2,1)S(1)}, bf16[128,2048]{1,0:T(8,128)(2,1)S(1)}, u32[]{:S(2)}, u32[]{:S(2)}) collective-permute-start(bf16[128,2048]{1,0:T(8,128)(2,1)S(1)} %convolution_convert_fusion.6), channel_id=1, source_target_pairs={{0,8},{4,12},{8,0},{12,4},{1,9},{5,13},{9,1},{13,5},{2,10},{6,14},... | collective-permute-start | bytes 1572872 | tf_op jit(solution)/shard_map/ppermute | solution.py:112
  43.0 31.6 %collective-permute-start.6 = (bf16[128,2048]{1,0:T(8,128)(2,1)S(1)}, bf16[128,2048]{1,0:T(8,128)(2,1)S(1)}, u32[]{:S(2)}, u32[]{:S(2)}) collective-permute-start(bf16[128,2048]{1,0:T(8,128)(2,1)S(1)} %convolution_convert_fusion.5), channel_id=1, source_target_pairs={{0,12},{4,0},{8,4},{12,8},{1,13},{5,1},{9,5},{13,9},{2,14},{6,2},{... | collective-permute-start | bytes 1572872 | tf_op jit(solution)/shard_map/ppermute | solution.py:112
  77.3 15.5 %copy-start.1 = (bf16[1,1601,512]{2,1,0:T(8,128)(2,1)S(1)}, bf16[1,1601,512]{2,1,0:T(8,128)(2,1)}, u32[]{:S(2)}) copy-start(bf16[1,1601,512]{2,1,0:T(8,128)(2,1)} %param.13) | copy-start | bytes 4918276
  78.8 19.7 %collective-permute-start.7 = (bf16[64,2048]{1,0:T(8,128)(2,1)S(1)}, bf16[64,2048]{1,0:T(8,128)(2,1)S(1)}, u32[]{:S(2)}, u32[]{:S(2)}) collective-permute-start(bf16[64,2048]{1,0:T(8,128)(2,1)S(1)} %get-tuple-element.14), channel_id=1, source_target_pairs={{0,4},{4,8},{8,12},{12,0},{1,5},{5,9},{9,13},{13,1},{2,6},{6,10},{... | collective-permute-start | bytes 786440 | tf_op jit(solution)/shard_map/ppermute | solution.py:295
  90.5 20.5 %collective-permute-start.9 = (bf16[64,2048]{1,0:T(8,128)(2,1)S(1)}, bf16[64,2048]{1,0:T(8,128)(2,1)S(1)}, u32[]{:S(2)}, u32[]{:S(2)}) collective-permute-start(bf16[64,2048]{1,0:T(8,128)(2,1)S(1)} %get-tuple-element.13), channel_id=1, source_target_pairs={{0,8},{4,12},{8,0},{12,4},{1,9},{5,13},{9,1},{13,5},{2,10},{6,14},... | collective-permute-start | bytes 786440 | tf_op jit(solution)/shard_map/ppermute | solution.py:295
  91.7 32.8 %collective-permute-start.11 = (bf16[64,2048]{1,0:T(8,128)(2,1)S(1)}, bf16[64,2048]{1,0:T(8,128)(2,1)S(1)}, u32[]{:S(2)}, u32[]{:S(2)}) collective-permute-start(bf16[64,2048]{1,0:T(8,128)(2,1)S(1)} %get-tuple-element.12), channel_id=1, source_target_pairs={{0,12},{4,0},{8,4},{12,8},{1,13},{5,1},{9,5},{13,9},{2,14},{6,2},{... | collective-permute-start | bytes 786440 | tf_op jit(solution)/shard_map/ppermute | solution.py:295
  110.1 46.6 %collective-permute-start.8 = (bf16[64,2048]{1,0:T(8,128)(2,1)}, bf16[64,2048]{1,0:T(8,128)(2,1)S(1)}, u32[]{:S(2)}, u32[]{:S(2)}) collective-permute-start(bf16[64,2048]{1,0:T(8,128)(2,1)} %shard_map.92), channel_id=1, source_target_pairs={{0,12},{4,0},{8,4},{12,8},{1,13},{5,1},{9,5},{13,9},{2,14},{6,2},{... | collective-permute-start | bytes 786440 | tf_op jit(solution)/shard_map/ppermute | solution.py:302
  122.6 34.1 %collective-permute-start.10 = (bf16[64,2048]{1,0:T(8,128)(2,1)}, bf16[64,2048]{1,0:T(8,128)(2,1)S(1)}, u32[]{:S(2)}, u32[]{:S(2)}) collective-permute-start(bf16[64,2048]{1,0:T(8,128)(2,1)} %shard_map.93), channel_id=1, source_target_pairs={{0,8},{4,12},{8,0},{12,4},{1,9},{5,13},{9,1},{13,5},{2,10},{6,14},... | collective-permute-start | bytes 786440 | tf_op jit(solution)/shard_map/ppermute | solution.py:302
  136.2 20.6 %collective-permute-start.12 = (bf16[64,2048]{1,0:T(8,128)(2,1)}, bf16[64,2048]{1,0:T(8,128)(2,1)S(1)}, u32[]{:S(2)}, u32[]{:S(2)}) collective-permute-start(bf16[64,2048]{1,0:T(8,128)(2,1)} %shard_map.94), channel_id=1, source_target_pairs={{0,4},{4,8},{8,12},{12,0},{1,5},{5,9},{9,13},{13,1},{2,6},{6,10},{... | collective-permute-start | bytes 786440 | tf_op jit(solution)/shard_map/ppermute | solution.py:302
  158.2 16.8 %collective-permute-start.13 = (bf16[128,2048]{1,0:T(8,128)(2,1)S(1)}, bf16[128,2048]{1,0:T(8,128)(2,1)S(1)}, u32[]{:S(2)}, u32[]{:S(2)}) collective-permute-start(bf16[128,2048]{1,0:T(8,128)(2,1)S(1)} %convolution_convert_fusion.9), channel_id=1, source_target_pairs={{0,4},{4,8},{8,12},{12,0},{1,5},{5,9},{9,13},{13,1},{2,6},{6,10},{... | collective-permute-start | bytes 1572872 | tf_op jit(solution)/shard_map/ppermute | solution.py:124
  158.3 37.2 %collective-permute-start.14 = (bf16[128,2048]{1,0:T(8,128)(2,1)S(1)}, bf16[128,2048]{1,0:T(8,128)(2,1)S(1)}, u32[]{:S(2)}, u32[]{:S(2)}) collective-permute-start(bf16[128,2048]{1,0:T(8,128)(2,1)S(1)} %convolution_convert_fusion.9), channel_id=1, source_target_pairs={{0,8},{4,12},{8,0},{12,4},{1,9},{5,13},{9,1},{13,5},{2,10},{6,14},... | collective-permute-start | bytes 1572872 | tf_op jit(solution)/shard_map/ppermute | solution.py:124
  158.3 38.4 %collective-permute-start.15 = (bf16[128,2048]{1,0:T(8,128)(2,1)S(1)}, bf16[128,2048]{1,0:T(8,128)(2,1)S(1)}, u32[]{:S(2)}, u32[]{:S(2)}) collective-permute-start(bf16[128,2048]{1,0:T(8,128)(2,1)S(1)} %convolution_convert_fusion.9), channel_id=1, source_target_pairs={{0,12},{4,0},{8,4},{12,8},{1,13},{5,1},{9,5},{13,9},{2,14},{6,2},{... | collective-permute-start | bytes 1572872 | tf_op jit(solution)/shard_map/ppermute | solution.py:124
  198.2 2.9 %collective-permute-start.16 = (bf16[256,2048]{1,0:T(8,128)(2,1)S(1)}, bf16[256,2048]{1,0:T(8,128)(2,1)}, u32[]{:S(2)}, u32[]{:S(2)}) collective-permute-start(bf16[256,2048]{1,0:T(8,128)(2,1)S(1)} %dynamic-slice_bitcast_fusion), channel_id=1, source_target_pairs={{0,1},{1,0},{2,3},{3,2},{4,5},{5,4},{6,7},{7,6},{8,9},{9,8},{10,11... | collective-permute-start | bytes 3145736 | tf_op jit(solution)/shard_map/ppermute | solution.py:135
  202.8 23.3 %collective-permute-start.17 = (bf16[128,2048]{1,0:T(8,128)(2,1)S(1)}, bf16[128,2048]{1,0:T(8,128)(2,1)S(1)}, u32[]{:S(2)}, u32[]{:S(2)}) collective-permute-start(bf16[128,2048]{1,0:T(8,128)(2,1)S(1)} %get-tuple-element.9), channel_id=1, source_target_pairs={{0,0},{1,8},{2,4},{3,12},{4,1},{5,9},{6,5},{7,13},{8,2},{9,10},{10... | collective-permute-start | bytes 1572872 | tf_op jit(solution)/shard_map/ppermute | solution.py:345
  214.2 25.5 %collective-permute-start.18 = (bf16[128,2048]{1,0:T(8,128)(2,1)S(1)}, bf16[128,2048]{1,0:T(8,128)(2,1)S(1)}, u32[]{:S(2)}, u32[]{:S(2)}) collective-permute-start(bf16[128,2048]{1,0:T(8,128)(2,1)S(1)} %get-tuple-element.10), channel_id=1, source_target_pairs={{0,4},{1,12},{2,0},{3,8},{4,5},{5,13},{6,1},{7,9},{8,6},{9,14},{10... | collective-permute-start | bytes 1572872 | tf_op jit(solution)/shard_map/ppermute | solution.py:345
  (8 other events, 65.3 us)

commit v14 on v12

--- a/solution.py
+++ b/solution.py
@@ -49,66 +49,60 @@
     return total.astype(jnp.bfloat16)
 
 
-def attend_kernel(q_ref, k_ref, v_ref, o_ref, *, per_kv, head_dim, token_count):
-    padded_tokens = k_ref.shape[0]
+def attend_kernel(q_ref, k_ref, v_ref, o_ref, *, head_dim, token_count):
+    padded_tokens = k_ref.shape[1]
     split = (token_count // 128) * 128
-    keys = k_ref[...]
-    rows = q_ref.shape[0]
-    score_scale = head_dim ** (-0.5)
-    for g in range(per_kv):
-        query = q_ref[:, g * head_dim:(g + 1) * head_dim]
-        scores = lax.dot_general(
-            query, keys, (((1,), (1,)), ((), ())), preferred_element_type=jnp.float32
-        ) * score_scale
-        pieces = [scores[:, :split]] if split else []
-        if split < padded_tokens:
-            tail = scores[:, split:]
-            valid = lax.broadcasted_iota(jnp.int32, tail.shape, 1) < token_count - split
-            pieces.append(jnp.where(valid, tail, -jnp.inf))
-        peak = jnp.max(pieces[0], axis=1, keepdims=True)
-        for piece in pieces[1:]:
-            peak = jnp.maximum(peak, jnp.max(piece, axis=1, keepdims=True))
-        weights = [jnp.exp(piece - peak) for piece in pieces]
-        total = sum(jnp.sum(w, axis=1, keepdims=True) for w in weights)
-        inverse = 1.0 / total
-        mixed = None
-        start = 0
-        for w in weights:
-            width = w.shape[1]
-            probs = (w * inverse).astype(jnp.bfloat16)
-            term = jnp.dot(
-                probs, v_ref[start:start + width, :], preferred_element_type=jnp.float32
-            )
-            mixed = term if mixed is None else mixed + term
-            start += width
-        o_ref[:, g * head_dim:(g + 1) * head_dim] = mixed.astype(o_ref.dtype)
+    scores = lax.dot_general(
+        q_ref[0], k_ref[0], (((1,), (1,)), ((), ())), preferred_element_type=jnp.float32
+    ) * (head_dim ** (-0.5))
+    pieces = [scores[:, :split]] if split else []
+    if split < padded_tokens:
+        tail = scores[:, split:]
+        valid = lax.broadcasted_iota(jnp.int32, tail.shape, 1) < token_count - split
+        pieces.append(jnp.where(valid, tail, -jnp.inf))
+    peak = jnp.max(pieces[0], axis=1, keepdims=True)
+    for piece in pieces[1:]:
+        peak = jnp.maximum(peak, jnp.max(piece, axis=1, keepdims=True))
+    weights = [jnp.exp(piece - peak) for piece in pieces]
+    total = sum(jnp.sum(w, axis=1, keepdims=True) for w in weights)
+    inverse = 1.0 / total
+    mixed = None
+    start = 0
+    for w in weights:
+        width = w.shape[1]
+        probs = (w * inverse).astype(jnp.bfloat16)
+        term = jnp.dot(probs, v_ref[0, start:start + width, :], preferred_element_type=jnp.float32)
+        mixed = term if mixed is None else mixed + term
+        start += width
+    o_ref[0] = mixed.astype(o_ref.dtype)
 
 
 def attend(rows_in, keys, values, kv_count, per_kv, head_dim, token_count):
     rows, width = rows_in.shape
-    padded_tokens = keys.shape[0]
-    group_width = per_kv * head_dim
-    kernel = functools.partial(
-        attend_kernel, per_kv=per_kv, head_dim=head_dim, token_count=token_count
-    )
+    padded_tokens = keys.shape[1]
+    stacked = rows_in.reshape(rows, kv_count, per_kv, head_dim).transpose(1, 2, 0, 3)
+    stacked = stacked.reshape(kv_count, per_kv * rows, head_dim)
+    kernel = functools.partial(attend_kernel, head_dim=head_dim, token_count=token_count)
     flops = 4 * rows * padded_tokens * head_dim * per_kv * kv_count
     moved = 2 * (2 * rows * width + 2 * padded_tokens * head_dim * kv_count)
-    return pl.pallas_call(
+    mixed = pl.pallas_call(
         kernel,
         grid=(kv_count,),
         in_specs=[
-            pl.BlockSpec((rows, group_width), lambda k: (0, k)),
-            pl.BlockSpec((padded_tokens, head_dim), lambda k: (0, k)),
-            pl.BlockSpec((padded_tokens, head_dim), lambda k: (0, k)),
+            pl.BlockSpec((1, per_kv * rows, head_dim), lambda k: (k, 0, 0)),
+            pl.BlockSpec((1, padded_tokens, head_dim), lambda k: (k, 0, 0)),
+            pl.BlockSpec((1, padded_tokens, head_dim), lambda k: (k, 0, 0)),
         ],
-        out_specs=pl.BlockSpec((rows, group_width), lambda k: (0, k)),
-        out_shape=jax.ShapeDtypeStruct((rows, width), jnp.bfloat16),
+        out_specs=pl.BlockSpec((1, per_kv * rows, head_dim), lambda k: (k, 0, 0)),
+        out_shape=jax.ShapeDtypeStruct((kv_count, per_kv * rows, head_dim), jnp.bfloat16),
         cost_estimate=pl.CostEstimate(
             flops=flops,
             transcendentals=rows * padded_tokens * per_kv * kv_count,
             bytes_accessed=moved,
         ),
-    )(rows_in, keys, values)
+    )(stacked, keys, values)
+    mixed = mixed.reshape(kv_count, per_kv, rows, head_dim).transpose(2, 0, 1, 3)
+    return mixed.reshape(rows, width)
 
 
 def local(
@@ -191,14 +185,13 @@
     kv_first = sub_index * heads_here // group_size
     token_count = key_cache.shape[1]
     padded_tokens = -(-token_count // 128) * 128
-    keys_here = jnp.pad(
-        lax.dynamic_slice_in_dim(key_cache[0], kv_first * head_dim, kv_count * head_dim, 1),
-        ((0, padded_tokens - token_count), (0, 0)),
-    )
-    values_here = jnp.pad(
-        lax.dynamic_slice_in_dim(value_cache[0], kv_first * head_dim, kv_count * head_dim, 1),
-        ((0, padded_tokens - token_count), (0, 0)),
-    )
+    def group_major(cache):
+        picked = lax.dynamic_slice_in_dim(cache[0], kv_first * head_dim, kv_count * head_dim, 1)
+        picked = jnp.pad(picked, ((0, padded_tokens - token_count), (0, 0)))
+        return picked.reshape(padded_tokens, kv_count, head_dim).transpose(1, 0, 2)
+
+    keys_here = group_major(key_cache)
+    values_here = group_major(value_cache)
     returned_blocks = []
     for shift in range(req_count):
         if shift == 0:

time: 242 us -> 234 us (0.967)
  Pallas kernels: 43.9 us -> 27.1 us
  local copies, waits for them, and re-layouts: 10.8 us -> 19.9 us
    pallas_call x4, Pallas kernels: 43.9 us -> 27.1 us  [attend(): pl.pallas_call(kernel, grid=(kv_count,), in_specs=[pl.BlockSpec((1, per_k...]
    reshape x0 -> x9, local copies, waits for them, and re-layouts: none -> 9.38 us  [the longest x4 4.49 us: attend(): mixed.reshape(kv_count, per_kv, rows, head_dim).transpose(2, 0, 1, 3)]
    unnamed x28 -> x30, local copies, waits for them, and re-layouts: 5.58 us -> 5.68 us
  transfers between devices with their start and end apart: 19 -> 19, of which waited for: 11 -> 11; matrix products, arithmetic and copies ran while one was open for 6% -> 11% of each run, Pallas kernels for 18% -> 12%
where the time goes in v14:
time: 234 us
  waiting for transfers between devices  103 us (44%)
  starting transfers between devices  59 us (25%)
  Pallas kernels  27.1 us (12%)
  local copies, waits for them, and re-layouts  19.9 us (9%)
  matrix products  18.6 us (8%)
  other arithmetic  4.93 us (2%)
    ppermute x3, waiting for transfers between devices, direct_reduce_scatter(): lax.ppermute(outgoing, axis, [(i, (i + shift) % count) for i in range(cou...  29.7 us
    pallas_call x4, Pallas kernels, attend(): pl.pallas_call(kernel, grid=(kv_count,), in_specs=[pl.BlockSpec((1, per_k...  27.1 us
    ppermute x3, waiting for transfers between devices, direct_gather_apply(): lax.ppermute(block, axis, [(i, (i + shift) % count) for i in range(count)])  27 us
    ppermute x2, waiting for transfers between devices, local(): got = lax.ppermute(chunk, ('req', 'head', 'sub'), pairs).astype(jnp.float32)  25.4 us
    ppermute x3, waiting for transfers between devices, local(): lax.ppermute(outgoing_part, 'req', [(i, (i + shift) % req_count) for i in...  14.9 us
    ppermute x3, starting transfers between devices, local(): lax.ppermute(mixed_block, 'req', [(i, (i - shift) % req_count) for i in r...  14.4 us
    ppermute x3, starting transfers between devices, local(): lax.ppermute(outgoing[shift], 'req', [(i, (i + shift) % req_count) for i...  14.1 us
    ppermute x2, starting transfers between devices, local(): got = lax.ppermute(chunk, ('req', 'head', 'sub'), pairs).astype(jnp.float32)  11.4 us
  transfers between devices with their start and end apart: 19, of which 11 were waited for; matrix products, arithmetic and copies ran while one was open for 11% of the time, Pallas kernels for 12%

profile of v14, /device:TPU:6, one launch (start us, length us, event | category | flops | bytes accessed | tf_op | source)
XLA Modules:
  0.0 233.5 jit_solution(12841377393398720493)
XLA Ops:
  0.0 3.2 %copy.61 = bf16[128,8192]{0,1:T(8,128)(2,1)S(1)} copy(bf16[128,8192]{1,0:T(8,128)(2,1)} %param.9) | data formatting | bytes 4194304 | tf_op args[0]
  5.3 2.7 %collective-permute-start.1 = (bf16[128,1024]{1,0:T(8,128)(2,1)S(1)}, bf16[128,1024]{1,0:T(8,128)(2,1)S(1)}, u32[]{:S(2)}, u32[]{:S(2)}) collective-permute-start(bf16[128,1024]{1,0:T(8,128)(2,1)S(1)} %bitcast.158), channel_id=1, source_target_pairs={{0,8},{4,12},{8,0},{12,4},{1,9},{5,13},{9,1},{13,5},{2,10},{6,14},... | collective-permute-start | bytes 786440 | tf_op jit(solution)/shard_map/ppermute | solution.py:140
  9.9 4.8 %collective-permute-done = bf16[128,1024]{1,0:T(8,128)(2,1)S(1)} collective-permute-done((bf16[128,1024]{1,0:T(8,128)(2,1)S(1)}, bf16[128,1024]{1,0:T(8,128)(2,1)S(1)}, u32[]{:S(2)}, u32[]{:S(2)}) %collective-permute-start) | collective-permute-done | bytes 262176 | tf_op jit(solution)/shard_map/ppermute | solution.py:140
  14.7 10.1 %collective-permute-done.1 = bf16[128,1024]{1,0:T(8,128)(2,1)S(1)} collective-permute-done((bf16[128,1024]{1,0:T(8,128)(2,1)S(1)}, bf16[128,1024]{1,0:T(8,128)(2,1)S(1)}, u32[]{:S(2)}, u32[]{:S(2)}) %collective-permute-start.1) | collective-permute-done | bytes 262176 | tf_op jit(solution)/shard_map/ppermute | solution.py:140
  27.8 4.8 %convolution_convert_fusion.7 = bf16[128,2048]{1,0:T(8,128)(2,1)S(1)} fusion(bf16[2048,2048]{1,0:T(8,128)(2,1)} %param.10, bf16[512,2048]{1,0:T(8,128)(2,1)S(1)} %constant_dynamic-update-slice_fusion, s32[]{:T(128)S(6)} %select_n.191), kind=kOutput, calls=%fused_computation.7 | convolution fusion | flops 1074003968 | bytes 9437188 | tf_op jit(solution)/shard_map/dot_general | solution.py:160
  32.6 6.1 %collective-permute-start.4 = (bf16[128,2048]{1,0:T(8,128)(2,1)S(1)}, bf16[128,2048]{1,0:T(8,128)(2,1)S(1)}, u32[]{:S(2)}, u32[]{:S(2)}) collective-permute-start(bf16[128,2048]{1,0:T(8,128)(2,1)S(1)} %convolution_convert_fusion.7), channel_id=1, source_target_pairs={{0,4},{4,8},{8,12},{12,0},{1,5},{5,9},{9,13},{13,1},{2,6},{6,10},{... | collective-permute-start | bytes 1572872 | tf_op jit(solution)/shard_map/ppermute | solution.py:24
  44.8 7.8 %collective-permute-done.4 = bf16[128,2048]{1,0:T(8,128)(2,1)S(1)} collective-permute-done((bf16[128,2048]{1,0:T(8,128)(2,1)S(1)}, bf16[128,2048]{1,0:T(8,128)(2,1)S(1)}, u32[]{:S(2)}, u32[]{:S(2)}) %collective-permute-start.4) | collective-permute-done | bytes 524320 | tf_op jit(solution)/shard_map/ppermute | solution.py:24
  52.6 22.0 %collective-permute-done.5 = bf16[128,2048]{1,0:T(8,128)(2,1)S(1)} collective-permute-done((bf16[128,2048]{1,0:T(8,128)(2,1)S(1)}, bf16[128,2048]{1,0:T(8,128)(2,1)S(1)}, u32[]{:S(2)}, u32[]{:S(2)}) %collective-permute-start.5) | collective-permute-done | bytes 524320 | tf_op jit(solution)/shard_map/ppermute | solution.py:24
  78.8 11.7 %collective-permute-start.7 = (bf16[64,2048]{1,0:T(8,128)(2,1)}, bf16[64,2048]{1,0:T(8,128)(2,1)}, u32[]{:S(2)}, u32[]{:S(2)}) collective-permute-start(bf16[64,2048]{1,0:T(8,128)(2,1)} %get-tuple-element.14), channel_id=1, source_target_pairs={{0,4},{4,8},{8,12},{12,0},{1,5},{5,9},{9,13},{13,1},{2,6},{6,10},{... | collective-permute-start | bytes 786440 | tf_op jit(solution)/shard_map/ppermute | solution.py:200
  100.6 6.8 %shard_map.92 = bf16[2,512,128]{2,1,0:T(8,128)(2,1)} custom-call(bf16[2,512,128]{2,1,0:T(8,128)(2,1)} %bitcast.167, bf16[2,1664,128]{2,1,0:T(8,128)(2,1)} %bitcast.149, bf16[2,1664,128]{2,1,0:T(8,128)(2,1)} %bitcast.153), custom_call_target="tpu_custom_call" | custom-call | flops 872415232 | bytes 2228224 | tf_op jit(solution)/shard_map/pallas_call | solution.py:88
  110.3 6.8 %shard_map.93 = bf16[2,512,128]{2,1,0:T(8,128)(2,1)} custom-call(bf16[2,512,128]{2,1,0:T(8,128)(2,1)} %bitcast.169, bf16[2,1664,128]{2,1,0:T(8,128)(2,1)} %bitcast.150, bf16[2,1664,128]{2,1,0:T(8,128)(2,1)} %bitcast.154), custom_call_target="tpu_custom_call" | custom-call | flops 872415232 | bytes 2228224 | tf_op jit(solution)/shard_map/pallas_call | solution.py:88
  118.3 1.9 collective-permute-start.10
  121.0 6.8 %shard_map.94 = bf16[2,512,128]{2,1,0:T(8,128)(2,1)} custom-call(bf16[2,512,128]{2,1,0:T(8,128)(2,1)} %bitcast.171, bf16[2,1664,128]{2,1,0:T(8,128)(2,1)} %bitcast.151, bf16[2,1664,128]{2,1,0:T(8,128)(2,1)} %bitcast.155), custom_call_target="tpu_custom_call" | custom-call | flops 872415232 | bytes 2228224 | tf_op jit(solution)/shard_map/pallas_call | solution.py:88
  129.0 11.6 %collective-permute-start.12 = (bf16[64,2048]{1,0:T(8,128)(2,1)S(1)}, bf16[64,2048]{1,0:T(8,128)(2,1)S(1)}, u32[]{:S(2)}, u32[]{:S(2)}) collective-permute-start(bf16[64,2048]{1,0:T(8,128)(2,1)S(1)} %bitcast.163), channel_id=1, source_target_pairs={{0,4},{4,8},{8,12},{12,0},{1,5},{5,9},{9,13},{13,1},{2,6},{6,10},{... | collective-permute-start | bytes 786440 | tf_op jit(solution)/shard_map/ppermute | solution.py:207
  141.4 6.8 %shard_map.91 = bf16[2,512,128]{2,1,0:T(8,128)(2,1)} custom-call(bf16[2,512,128]{2,1,0:T(8,128)(2,1)} %bitcast.165, bf16[2,1664,128]{2,1,0:T(8,128)(2,1)} %bitcast.152, bf16[2,1664,128]{2,1,0:T(8,128)(2,1)} %bitcast.156), custom_call_target="tpu_custom_call" | custom-call | flops 872415232 | bytes 2228224 | tf_op jit(solution)/shard_map/pallas_call | solution.py:88
  150.1 3.7 %collective-permute-start.15 = (bf16[128,2048]{1,0:T(8,128)(2,1)S(1)}, bf16[128,2048]{1,0:T(8,128)(2,1)S(1)}, u32[]{:S(2)}, u32[]{:S(2)}) collective-permute-start(bf16[128,2048]{1,0:T(8,128)(2,1)S(1)} %convolution_convert_fusion.9), channel_id=1, source_target_pairs={{0,12},{4,0},{8,4},{12,8},{1,13},{5,1},{9,5},{13,9},{2,14},{6,2},{... | collective-permute-start | bytes 1572872 | tf_op jit(solution)/shard_map/ppermute | solution.py:36
  154.1 4.8 %fusion.4 = bf16[4,128,2048]{2,1,0:T(8,128)(2,1)S(1)} fusion(bf16[4,128,2048]{2,1,0:T(8,128)(2,1)S(1)} %broadcast_in_dim.56, s32[]{:T(128)S(6)} %select_n.168, bf16[128,2048]{1,0:T(8,128)(2,1)S(1)} %convolution_convert_fusion.9, bf16[2048,2048]{1,0:T(8,128)(2,1)} %param.14), kind=kOutput, calls=%fused_computation.14 | convolution fusion | flops 1074003968 | bytes 9437188 | tf_op jit(solution)/shard_map/dot_general | solution.py:219
  158.9 7.8 %collective-permute-done.13 = bf16[128,2048]{1,0:T(8,128)(2,1)S(1)} collective-permute-done((bf16[128,2048]{1,0:T(8,128)(2,1)S(1)}, bf16[128,2048]{1,0:T(8,128)(2,1)S(1)}, u32[]{:S(2)}, u32[]{:S(2)}) %collective-permute-start.13) | collective-permute-done | bytes 524320 | tf_op jit(solution)/shard_map/ppermute | solution.py:36
  168.1 19.2 %collective-permute-done.14 = bf16[128,2048]{1,0:T(8,128)(2,1)S(1)} collective-permute-done((bf16[128,2048]{1,0:T(8,128)(2,1)S(1)}, bf16[128,2048]{1,0:T(8,128)(2,1)S(1)}, u32[]{:S(2)}, u32[]{:S(2)}) %collective-permute-start.14) | collective-permute-done | bytes 524320 | tf_op jit(solution)/shard_map/ppermute | solution.py:36
  190.1 2.8 %collective-permute-done.16 = bf16[256,2048]{1,0:T(8,128)(2,1)} collective-permute-done((bf16[256,2048]{1,0:T(8,128)(2,1)S(1)}, bf16[256,2048]{1,0:T(8,128)(2,1)}, u32[]{:S(2)}, u32[]{:S(2)}) %collective-permute-start.16) | collective-permute-done | bytes 1048608 | tf_op jit(solution)/shard_map/ppermute | solution.py:47
  194.6 11.4 %collective-permute-start.17 = (bf16[128,2048]{1,0:T(8,128)(2,1)S(1)}, bf16[128,2048]{1,0:T(8,128)(2,1)S(1)}, u32[]{:S(2)}, u32[]{:S(2)}) collective-permute-start(bf16[128,2048]{1,0:T(8,128)(2,1)S(1)} %get-tuple-element.9), channel_id=1, source_target_pairs={{0,0},{1,8},{2,4},{3,12},{4,1},{5,9},{6,5},{7,13},{8,2},{9,10},{10... | collective-permute-start | bytes 1572872 | tf_op jit(solution)/shard_map/ppermute | solution.py:250
  206.0 12.0 %collective-permute-done.17 = bf16[128,2048]{1,0:T(8,128)(2,1)S(1)} collective-permute-done((bf16[128,2048]{1,0:T(8,128)(2,1)S(1)}, bf16[128,2048]{1,0:T(8,128)(2,1)S(1)}, u32[]{:S(2)}, u32[]{:S(2)}) %collective-permute-start.17) | collective-permute-done | bytes 524320 | tf_op jit(solution)/shard_map/ppermute | solution.py:250
  218.0 13.5 %collective-permute-done.18 = bf16[128,2048]{1,0:T(8,128)(2,1)S(1)} collective-permute-done((bf16[128,2048]{1,0:T(8,128)(2,1)S(1)}, bf16[128,2048]{1,0:T(8,128)(2,1)S(1)}, u32[]{:S(2)}, u32[]{:S(2)}) %collective-permute-start.18) | collective-permute-done | bytes 524320 | tf_op jit(solution)/shard_map/ppermute | solution.py:250
  231.4 2.1 add_convert_fusion
  (108 shorter events, 41.9 us)
Async XLA Ops:
  0.0 44.8 %copy-start = (f32[128]{0:T(128)S(1)}, f32[128]{0:T(128)}, u32[]{:S(2)}) copy-start(f32[128]{0:T(128)} %param.11) | copy-start | bytes 1540
  3.5 11.2 %collective-permute-start = (bf16[128,1024]{1,0:T(8,128)(2,1)S(1)}, bf16[128,1024]{1,0:T(8,128)(2,1)S(1)}, u32[]{:S(2)}, u32[]{:S(2)}) collective-permute-start(bf16[128,1024]{1,0:T(8,128)(2,1)S(1)} %bitcast.159), channel_id=1, source_target_pairs={{0,4},{4,8},{8,12},{12,0},{1,5},{5,9},{9,13},{13,1},{2,6},{6,10},{... | collective-permute-start | bytes 786440 | tf_op jit(solution)/shard_map/ppermute | solution.py:140
  5.3 19.5 %collective-permute-start.1 = (bf16[128,1024]{1,0:T(8,128)(2,1)S(1)}, bf16[128,1024]{1,0:T(8,128)(2,1)S(1)}, u32[]{:S(2)}, u32[]{:S(2)}) collective-permute-start(bf16[128,1024]{1,0:T(8,128)(2,1)S(1)} %bitcast.158), channel_id=1, source_target_pairs={{0,8},{4,12},{8,0},{12,4},{1,9},{5,13},{9,1},{13,5},{2,10},{6,14},... | collective-permute-start | bytes 786440 | tf_op jit(solution)/shard_map/ppermute | solution.py:140
  7.9 17.1 %copy-start.3 = (s32[4]{0:T(128)S(1)}, s32[4]{0:T(128)}, u32[]{:S(2)}) copy-start(s32[4]{0:T(128)} %param.17) | copy-start | bytes 52
  7.9 17.1 %copy-start.4 = (s32[128]{0:T(128)S(1)}, s32[128]{0:T(128)}, u32[]{:S(2)}) copy-start(s32[128]{0:T(128)} %param.15) | copy-start | bytes 1540
  7.9 17.3 %copy-start.5 = (s32[128]{0:T(128)S(1)}, s32[128]{0:T(128)}, u32[]{:S(2)}) copy-start(s32[128]{0:T(128)} %param.16) | copy-start | bytes 1540
  8.1 16.8 %collective-permute-start.2 = (bf16[128,1024]{1,0:T(8,128)(2,1)S(1)}, bf16[128,1024]{1,0:T(8,128)(2,1)S(1)}, u32[]{:S(2)}, u32[]{:S(2)}) collective-permute-start(bf16[128,1024]{1,0:T(8,128)(2,1)S(1)} %bitcast.157), channel_id=1, source_target_pairs={{0,12},{4,0},{8,4},{12,8},{1,13},{5,1},{9,5},{13,9},{2,14},{6,2},{... | collective-permute-start | bytes 786440 | tf_op jit(solution)/shard_map/ppermute | solution.py:140
  24.9 2.7 %collective-permute-start.3 = (bf16[512,1024]{1,0:T(8,128)(2,1)S(1)}, bf16[512,1024]{1,0:T(8,128)(2,1)S(1)}, u32[]{:S(2)}, u32[]{:S(2)}) collective-permute-start(bf16[512,1024]{1,0:T(8,128)(2,1)S(1)} %bitcast.132), channel_id=1, source_target_pairs={{0,1},{1,0},{2,3},{3,2},{4,5},{5,4},{6,7},{7,6},{8,9},{9,8},{10,11... | collective-permute-start | bytes 3145736 | tf_op jit(solution)/shard_map/ppermute | solution.py:152
  32.6 20.0 %collective-permute-start.4 = (bf16[128,2048]{1,0:T(8,128)(2,1)S(1)}, bf16[128,2048]{1,0:T(8,128)(2,1)S(1)}, u32[]{:S(2)}, u32[]{:S(2)}) collective-permute-start(bf16[128,2048]{1,0:T(8,128)(2,1)S(1)} %convolution_convert_fusion.7), channel_id=1, source_target_pairs={{0,4},{4,8},{8,12},{12,0},{1,5},{5,9},{9,13},{13,1},{2,6},{6,10},{... | collective-permute-start | bytes 1572872 | tf_op jit(solution)/shard_map/ppermute | solution.py:24
  40.0 34.6 %collective-permute-start.5 = (bf16[128,2048]{1,0:T(8,128)(2,1)S(1)}, bf16[128,2048]{1,0:T(8,128)(2,1)S(1)}, u32[]{:S(2)}, u32[]{:S(2)}) collective-permute-start(bf16[128,2048]{1,0:T(8,128)(2,1)S(1)} %convolution_convert_fusion.6), channel_id=1, source_target_pairs={{0,8},{4,12},{8,0},{12,4},{1,9},{5,13},{9,1},{13,5},{2,10},{6,14},... | collective-permute-start | bytes 1572872 | tf_op jit(solution)/shard_map/ppermute | solution.py:24
  43.0 31.6 %collective-permute-start.6 = (bf16[128,2048]{1,0:T(8,128)(2,1)S(1)}, bf16[128,2048]{1,0:T(8,128)(2,1)S(1)}, u32[]{:S(2)}, u32[]{:S(2)}) collective-permute-start(bf16[128,2048]{1,0:T(8,128)(2,1)S(1)} %convolution_convert_fusion.5), channel_id=1, source_target_pairs={{0,12},{4,0},{8,4},{12,8},{1,13},{5,1},{9,5},{13,9},{2,14},{6,2},{... | collective-permute-start | bytes 1572872 | tf_op jit(solution)/shard_map/ppermute | solution.py:24
  77.3 15.6 %copy-start.1 = (bf16[1,1601,512]{2,1,0:T(8,128)(2,1)S(1)}, bf16[1,1601,512]{2,1,0:T(8,128)(2,1)}, u32[]{:S(2)}) copy-start(bf16[1,1601,512]{2,1,0:T(8,128)(2,1)} %param.13) | copy-start | bytes 4918276
  78.8 20.0 %collective-permute-start.7 = (bf16[64,2048]{1,0:T(8,128)(2,1)}, bf16[64,2048]{1,0:T(8,128)(2,1)}, u32[]{:S(2)}, u32[]{:S(2)}) collective-permute-start(bf16[64,2048]{1,0:T(8,128)(2,1)} %get-tuple-element.14), channel_id=1, source_target_pairs={{0,4},{4,8},{8,12},{12,0},{1,5},{5,9},{9,13},{13,1},{2,6},{6,10},{... | collective-permute-start | bytes 786440 | tf_op jit(solution)/shard_map/ppermute | solution.py:200
  90.5 18.9 %collective-permute-start.9 = (bf16[64,2048]{1,0:T(8,128)(2,1)}, bf16[64,2048]{1,0:T(8,128)(2,1)S(1)}, u32[]{:S(2)}, u32[]{:S(2)}) collective-permute-start(bf16[64,2048]{1,0:T(8,128)(2,1)} %get-tuple-element.13), channel_id=1, source_target_pairs={{0,8},{4,12},{8,0},{12,4},{1,9},{5,13},{9,1},{13,5},{2,10},{6,14},... | collective-permute-start | bytes 786440 | tf_op jit(solution)/shard_map/ppermute | solution.py:200
  91.8 28.4 %collective-permute-start.11 = (bf16[64,2048]{1,0:T(8,128)(2,1)}, bf16[64,2048]{1,0:T(8,128)(2,1)S(1)}, u32[]{:S(2)}, u32[]{:S(2)}) collective-permute-start(bf16[64,2048]{1,0:T(8,128)(2,1)} %get-tuple-element.12), channel_id=1, source_target_pairs={{0,12},{4,0},{8,4},{12,8},{1,13},{5,1},{9,5},{13,9},{2,14},{6,2},{... | collective-permute-start | bytes 786440 | tf_op jit(solution)/shard_map/ppermute | solution.py:200
  108.6 40.8 %collective-permute-start.8 = (bf16[64,2048]{1,0:T(8,128)(2,1)S(1)}, bf16[64,2048]{1,0:T(8,128)(2,1)S(1)}, u32[]{:S(2)}, u32[]{:S(2)}) collective-permute-start(bf16[64,2048]{1,0:T(8,128)(2,1)S(1)} %bitcast.160), channel_id=1, source_target_pairs={{0,12},{4,0},{8,4},{12,8},{1,13},{5,1},{9,5},{13,9},{2,14},{6,2},{... | collective-permute-start | bytes 786440 | tf_op jit(solution)/shard_map/ppermute | solution.py:207
  118.3 31.1 %collective-permute-start.10 = (bf16[64,2048]{1,0:T(8,128)(2,1)S(1)}, bf16[64,2048]{1,0:T(8,128)(2,1)S(1)}, u32[]{:S(2)}, u32[]{:S(2)}) collective-permute-start(bf16[64,2048]{1,0:T(8,128)(2,1)S(1)} %bitcast.161), channel_id=1, source_target_pairs={{0,8},{4,12},{8,0},{12,4},{1,9},{5,13},{9,1},{13,5},{2,10},{6,14},... | collective-permute-start | bytes 786440 | tf_op jit(solution)/shard_map/ppermute | solution.py:207
  129.0 20.5 %collective-permute-start.12 = (bf16[64,2048]{1,0:T(8,128)(2,1)S(1)}, bf16[64,2048]{1,0:T(8,128)(2,1)S(1)}, u32[]{:S(2)}, u32[]{:S(2)}) collective-permute-start(bf16[64,2048]{1,0:T(8,128)(2,1)S(1)} %bitcast.163), channel_id=1, source_target_pairs={{0,4},{4,8},{8,12},{12,0},{1,5},{5,9},{9,13},{13,1},{2,6},{6,10},{... | collective-permute-start | bytes 786440 | tf_op jit(solution)/shard_map/ppermute | solution.py:207
  150.0 16.8 %collective-permute-start.13 = (bf16[128,2048]{1,0:T(8,128)(2,1)S(1)}, bf16[128,2048]{1,0:T(8,128)(2,1)S(1)}, u32[]{:S(2)}, u32[]{:S(2)}) collective-permute-start(bf16[128,2048]{1,0:T(8,128)(2,1)S(1)} %convolution_convert_fusion.9), channel_id=1, source_target_pairs={{0,4},{4,8},{8,12},{12,0},{1,5},{5,9},{9,13},{13,1},{2,6},{6,10},{... | collective-permute-start | bytes 1572872 | tf_op jit(solution)/shard_map/ppermute | solution.py:36
  150.1 37.2 %collective-permute-start.14 = (bf16[128,2048]{1,0:T(8,128)(2,1)S(1)}, bf16[128,2048]{1,0:T(8,128)(2,1)S(1)}, u32[]{:S(2)}, u32[]{:S(2)}) collective-permute-start(bf16[128,2048]{1,0:T(8,128)(2,1)S(1)} %convolution_convert_fusion.9), channel_id=1, source_target_pairs={{0,8},{4,12},{8,0},{12,4},{1,9},{5,13},{9,1},{13,5},{2,10},{6,14},... | collective-permute-start | bytes 1572872 | tf_op jit(solution)/shard_map/ppermute | solution.py:36
  150.1 38.4 %collective-permute-start.15 = (bf16[128,2048]{1,0:T(8,128)(2,1)S(1)}, bf16[128,2048]{1,0:T(8,128)(2,1)S(1)}, u32[]{:S(2)}, u32[]{:S(2)}) collective-permute-start(bf16[128,2048]{1,0:T(8,128)(2,1)S(1)} %convolution_convert_fusion.9), channel_id=1, source_target_pairs={{0,12},{4,0},{8,4},{12,8},{1,13},{5,1},{9,5},{13,9},{2,14},{6,2},{... | collective-permute-start | bytes 1572872 | tf_op jit(solution)/shard_map/ppermute | solution.py:36
  190.0 2.9 %collective-permute-start.16 = (bf16[256,2048]{1,0:T(8,128)(2,1)S(1)}, bf16[256,2048]{1,0:T(8,128)(2,1)}, u32[]{:S(2)}, u32[]{:S(2)}) collective-permute-start(bf16[256,2048]{1,0:T(8,128)(2,1)S(1)} %dynamic-slice_bitcast_fusion), channel_id=1, source_target_pairs={{0,1},{1,0},{2,3},{3,2},{4,5},{5,4},{6,7},{7,6},{8,9},{9,8},{10,11... | collective-permute-start | bytes 3145736 | tf_op jit(solution)/shard_map/ppermute | solution.py:47
  194.6 23.4 %collective-permute-start.17 = (bf16[128,2048]{1,0:T(8,128)(2,1)S(1)}, bf16[128,2048]{1,0:T(8,128)(2,1)S(1)}, u32[]{:S(2)}, u32[]{:S(2)}) collective-permute-start(bf16[128,2048]{1,0:T(8,128)(2,1)S(1)} %get-tuple-element.9), channel_id=1, source_target_pairs={{0,0},{1,8},{2,4},{3,12},{4,1},{5,9},{6,5},{7,13},{8,2},{9,10},{10... | collective-permute-start | bytes 1572872 | tf_op jit(solution)/shard_map/ppermute | solution.py:250
  206.0 25.5 %collective-permute-start.18 = (bf16[128,2048]{1,0:T(8,128)(2,1)S(1)}, bf16[128,2048]{1,0:T(8,128)(2,1)S(1)}, u32[]{:S(2)}, u32[]{:S(2)}) collective-permute-start(bf16[128,2048]{1,0:T(8,128)(2,1)S(1)} %get-tuple-element.10), channel_id=1, source_target_pairs={{0,4},{1,12},{2,0},{3,8},{4,5},{5,13},{6,1},{7,9},{8,6},{9,14},{10... | collective-permute-start | bytes 1572872 | tf_op jit(solution)/shard_map/ppermute | solution.py:250
  (5 other events, 63.2 us)

commit v15 on v12

--- a/solution.py
+++ b/solution.py
@@ -50,10 +50,9 @@
 
 
 def attend_kernel(q_ref, k_ref, v_ref, o_ref, *, per_kv, head_dim, token_count):
-    padded_tokens = k_ref.shape[0]
+    padded_tokens = k_ref.shape[1]
     split = (token_count // 128) * 128
-    keys = k_ref[...]
-    rows = q_ref.shape[0]
+    keys = k_ref[0]
     score_scale = head_dim ** (-0.5)
     for g in range(per_kv):
         query = q_ref[:, g * head_dim:(g + 1) * head_dim]
@@ -77,7 +76,7 @@
             width = w.shape[1]
             probs = (w * inverse).astype(jnp.bfloat16)
             term = jnp.dot(
-                probs, v_ref[start:start + width, :], preferred_element_type=jnp.float32
+                probs, v_ref[0, start:start + width, :], preferred_element_type=jnp.float32
             )
             mixed = term if mixed is None else mixed + term
             start += width
@@ -86,7 +85,7 @@
 
 def attend(rows_in, keys, values, kv_count, per_kv, head_dim, token_count):
     rows, width = rows_in.shape
-    padded_tokens = keys.shape[0]
+    padded_tokens = keys.shape[1]
     group_width = per_kv * head_dim
     kernel = functools.partial(
         attend_kernel, per_kv=per_kv, head_dim=head_dim, token_count=token_count
@@ -98,8 +97,8 @@
         grid=(kv_count,),
         in_specs=[
             pl.BlockSpec((rows, group_width), lambda k: (0, k)),
-            pl.BlockSpec((padded_tokens, head_dim), lambda k: (0, k)),
-            pl.BlockSpec((padded_tokens, head_dim), lambda k: (0, k)),
+            pl.BlockSpec((1, padded_tokens, head_dim), lambda k: (k, 0, 0)),
+            pl.BlockSpec((1, padded_tokens, head_dim), lambda k: (k, 0, 0)),
         ],
         out_specs=pl.BlockSpec((rows, group_width), lambda k: (0, k)),
         out_shape=jax.ShapeDtypeStruct((rows, width), jnp.bfloat16),
@@ -191,14 +190,13 @@
     kv_first = sub_index * heads_here // group_size
     token_count = key_cache.shape[1]
     padded_tokens = -(-token_count // 128) * 128
-    keys_here = jnp.pad(
-        lax.dynamic_slice_in_dim(key_cache[0], kv_first * head_dim, kv_count * head_dim, 1),
-        ((0, padded_tokens - token_count), (0, 0)),
-    )
-    values_here = jnp.pad(
-        lax.dynamic_slice_in_dim(value_cache[0], kv_first * head_dim, kv_count * head_dim, 1),
-        ((0, padded_tokens - token_count), (0, 0)),
-    )
+    def group_major(cache):
+        picked = lax.dynamic_slice_in_dim(cache[0], kv_first * head_dim, kv_count * head_dim, 1)
+        picked = jnp.pad(picked, ((0, padded_tokens - token_count), (0, 0)))
+        return picked.reshape(padded_tokens, kv_count, head_dim).transpose(1, 0, 2)
+
+    keys_here = group_major(key_cache)
+    values_here = group_major(value_cache)
     returned_blocks = []
     for shift in range(req_count):
         if shift == 0:

time: 242 us -> 241 us (level)
    reshape x0 -> x2, local copies, waits for them, and re-layouts: none -> 2.53 us  [group_major(): return picked.reshape(padded_tokens, kv_count, head_dim).transpose(1, 0, 2)]
    unnamed x28 -> x22, local copies, waits for them, and re-layouts: 5.58 us -> 3.46 us
  transfers between devices with their start and end apart: 19 -> 19, of which waited for: 11 -> 11; matrix products, arithmetic and copies ran while one was open for 6% -> 7% of each run, Pallas kernels for 18% -> 18%
where the time goes in v15:
time: 241 us; the launch traced here: 240 us
  waiting for transfers between devices  103 us (43%)
  starting transfers between devices  57.6 us (24%)
  Pallas kernels  44 us (18%)
  matrix products  18.6 us (8%)
  local copies, waits for them, and re-layouts  10.7 us (4%)
  other arithmetic  5.88 us (2%)
    pallas_call x4, Pallas kernels, attend(): pl.pallas_call(kernel, grid=(kv_count,), in_specs=[pl.BlockSpec((rows, gr...  44 us
    ppermute x3, waiting for transfers between devices, direct_reduce_scatter(): lax.ppermute(outgoing, axis, [(i, (i + shift) % count) for i in range(cou...  29.7 us
    ppermute x3, waiting for transfers between devices, direct_gather_apply(): lax.ppermute(block, axis, [(i, (i + shift) % count) for i in range(count)])  27 us
    ppermute x2, waiting for transfers between devices, local(): got = lax.ppermute(chunk, ('req', 'head', 'sub'), pairs).astype(jnp.float32)  25.4 us
    ppermute x3, waiting for transfers between devices, local(): lax.ppermute(outgoing_part, 'req', [(i, (i + shift) % req_count) for i in...  14.9 us
    ppermute x3, starting transfers between devices, local(): lax.ppermute(outgoing[shift], 'req', [(i, (i + shift) % req_count) for i...  14.1 us
    ppermute x3, starting transfers between devices, local(): lax.ppermute(mixed_block, 'req', [(i, (i - shift) % req_count) for i in r...  12.9 us
    ppermute x2, starting transfers between devices, local(): got = lax.ppermute(chunk, ('req', 'head', 'sub'), pairs).astype(jnp.float32)  11.4 us
  transfers between devices with their start and end apart: 19, of which 11 were waited for; matrix products, arithmetic and copies ran while one was open for 7% of the time, Pallas kernels for 18%

profile of v15, /device:TPU:6, one launch (start us, length us, event | category | flops | bytes accessed | tf_op | source)
XLA Modules:
  0.0 240.5 jit_solution(12750107826888609459)
XLA Ops:
  0.0 3.2 %copy.33 = bf16[128,8192]{0,1:T(8,128)(2,1)S(1)} copy(bf16[128,8192]{1,0:T(8,128)(2,1)} %param.9) | data formatting | bytes 4194304 | tf_op args[0]
  5.3 2.7 %collective-permute-start.1 = (bf16[128,1024]{1,0:T(8,128)(2,1)S(1)}, bf16[128,1024]{1,0:T(8,128)(2,1)S(1)}, u32[]{:S(2)}, u32[]{:S(2)}) collective-permute-start(bf16[128,1024]{1,0:T(8,128)(2,1)S(1)} %bitcast.99), channel_id=1, source_target_pairs={{0,8},{4,12},{8,0},{12,4},{1,9},{5,13},{9,1},{13,5},{2,10},{6,14},... | collective-permute-start | bytes 786440 | tf_op jit(solution)/shard_map/ppermute | solution.py:145
  9.9 4.8 %collective-permute-done = bf16[128,1024]{1,0:T(8,128)(2,1)S(1)} collective-permute-done((bf16[128,1024]{1,0:T(8,128)(2,1)S(1)}, bf16[128,1024]{1,0:T(8,128)(2,1)S(1)}, u32[]{:S(2)}, u32[]{:S(2)}) %collective-permute-start) | collective-permute-done | bytes 262176 | tf_op jit(solution)/shard_map/ppermute | solution.py:145
  14.7 10.1 %collective-permute-done.1 = bf16[128,1024]{1,0:T(8,128)(2,1)S(1)} collective-permute-done((bf16[128,1024]{1,0:T(8,128)(2,1)S(1)}, bf16[128,1024]{1,0:T(8,128)(2,1)S(1)}, u32[]{:S(2)}, u32[]{:S(2)}) %collective-permute-start.1) | collective-permute-done | bytes 262176 | tf_op jit(solution)/shard_map/ppermute | solution.py:145
  27.8 4.8 %convolution_convert_fusion.7 = bf16[128,2048]{1,0:T(8,128)(2,1)S(1)} fusion(bf16[2048,2048]{1,0:T(8,128)(2,1)} %param.10, bf16[512,2048]{1,0:T(8,128)(2,1)S(1)} %constant_dynamic-update-slice_fusion, s32[]{:T(128)S(6)} %select_n.191), kind=kOutput, calls=%fused_computation.7 | convolution fusion | flops 1074003968 | bytes 9437188 | tf_op jit(solution)/shard_map/dot_general | solution.py:165
  32.6 6.1 %collective-permute-start.4 = (bf16[128,2048]{1,0:T(8,128)(2,1)S(1)}, bf16[128,2048]{1,0:T(8,128)(2,1)S(1)}, u32[]{:S(2)}, u32[]{:S(2)}) collective-permute-start(bf16[128,2048]{1,0:T(8,128)(2,1)S(1)} %convolution_convert_fusion.7), channel_id=1, source_target_pairs={{0,4},{4,8},{8,12},{12,0},{1,5},{5,9},{9,13},{13,1},{2,6},{6,10},{... | collective-permute-start | bytes 1572872 | tf_op jit(solution)/shard_map/ppermute | solution.py:24
  44.8 7.8 %collective-permute-done.4 = bf16[128,2048]{1,0:T(8,128)(2,1)S(1)} collective-permute-done((bf16[128,2048]{1,0:T(8,128)(2,1)S(1)}, bf16[128,2048]{1,0:T(8,128)(2,1)S(1)}, u32[]{:S(2)}, u32[]{:S(2)}) %collective-permute-start.4) | collective-permute-done | bytes 524320 | tf_op jit(solution)/shard_map/ppermute | solution.py:24
  52.6 22.0 %collective-permute-done.5 = bf16[128,2048]{1,0:T(8,128)(2,1)S(1)} collective-permute-done((bf16[128,2048]{1,0:T(8,128)(2,1)S(1)}, bf16[128,2048]{1,0:T(8,128)(2,1)S(1)}, u32[]{:S(2)}, u32[]{:S(2)}) %collective-permute-start.5) | collective-permute-done | bytes 524320 | tf_op jit(solution)/shard_map/ppermute | solution.py:24
  78.7 11.7 %collective-permute-start.7 = (bf16[64,2048]{1,0:T(8,128)(2,1)S(1)}, bf16[64,2048]{1,0:T(8,128)(2,1)}, u32[]{:S(2)}, u32[]{:S(2)}) collective-permute-start(bf16[64,2048]{1,0:T(8,128)(2,1)S(1)} %get-tuple-element.14), channel_id=1, source_target_pairs={{0,4},{4,8},{8,12},{12,0},{1,5},{5,9},{9,13},{13,1},{2,6},{6,10},{... | collective-permute-start | bytes 786440 | tf_op jit(solution)/shard_map/ppermute | solution.py:205
  98.5 11.0 %shard_map.92 = bf16[64,2048]{1,0:T(8,128)(2,1)} custom-call(bf16[64,2048]{1,0:T(8,128)(2,1)} %collective-permute-done.7.q_ref, bf16[2,1664,128]{2,1,0:T(8,128)(2,1)} %bitcast.90, bf16[2,1664,128]{2,1,0:T(8,128)(2,1)} %bitcast.94), custom_call_target="tpu_custom_call" | custom-call | flops 872415232 | bytes 2228224 | tf_op jit(solution)/shard_map/pallas_call | solution.py:95
  110.3 11.0 %shard_map.93 = bf16[64,2048]{1,0:T(8,128)(2,1)} custom-call(bf16[64,2048]{1,0:T(8,128)(2,1)} %collective-permute-done.9.q_ref, bf16[2,1664,128]{2,1,0:T(8,128)(2,1)} %bitcast.91, bf16[2,1664,128]{2,1,0:T(8,128)(2,1)} %bitcast.95), custom_call_target="tpu_custom_call" | custom-call | flops 872415232 | bytes 2228224 | tf_op jit(solution)/shard_map/pallas_call | solution.py:95
  121.3 1.8 collective-permute-start.10
  123.1 11.0 %shard_map.94 = bf16[64,2048]{1,0:T(8,128)(2,1)} custom-call(bf16[64,2048]{1,0:T(8,128)(2,1)} %collective-permute-done.11.q_ref, bf16[2,1664,128]{2,1,0:T(8,128)(2,1)} %bitcast.92, bf16[2,1664,128]{2,1,0:T(8,128)(2,1)} %bitcast.96), custom_call_target="tpu_custom_call" | custom-call | flops 872415232 | bytes 2228224 | tf_op jit(solution)/shard_map/pallas_call | solution.py:95
  134.2 10.3 %collective-permute-start.12 = (bf16[64,2048]{1,0:T(8,128)(2,1)}, bf16[64,2048]{1,0:T(8,128)(2,1)S(1)}, u32[]{:S(2)}, u32[]{:S(2)}) collective-permute-start(bf16[64,2048]{1,0:T(8,128)(2,1)} %shard_map.94), channel_id=1, source_target_pairs={{0,4},{4,8},{8,12},{12,0},{1,5},{5,9},{9,13},{13,1},{2,6},{6,10},{... | collective-permute-start | bytes 786440 | tf_op jit(solution)/shard_map/ppermute | solution.py:212
  144.4 11.0 %shard_map.91 = bf16[64,2048]{1,0:T(8,128)(2,1)} custom-call(bf16[64,2048]{1,0:T(8,128)(2,1)} %get-tuple-element.11.q_ref, bf16[2,1664,128]{2,1,0:T(8,128)(2,1)} %bitcast.93, bf16[2,1664,128]{2,1,0:T(8,128)(2,1)} %bitcast.97), custom_call_target="tpu_custom_call" | custom-call | flops 872415232 | bytes 2228224 | tf_op jit(solution)/shard_map/pallas_call | solution.py:95
  157.0 3.7 %collective-permute-start.15 = (bf16[128,2048]{1,0:T(8,128)(2,1)S(1)}, bf16[128,2048]{1,0:T(8,128)(2,1)S(1)}, u32[]{:S(2)}, u32[]{:S(2)}) collective-permute-start(bf16[128,2048]{1,0:T(8,128)(2,1)S(1)} %convolution_convert_fusion.9), channel_id=1, source_target_pairs={{0,12},{4,0},{8,4},{12,8},{1,13},{5,1},{9,5},{13,9},{2,14},{6,2},{... | collective-permute-start | bytes 1572872 | tf_op jit(solution)/shard_map/ppermute | solution.py:36
  161.0 4.8 %fusion.4 = bf16[4,128,2048]{2,1,0:T(8,128)(2,1)S(1)} fusion(bf16[4,128,2048]{2,1,0:T(8,128)(2,1)S(1)} %broadcast_in_dim.56, s32[]{:T(128)S(6)} %select_n.168, bf16[128,2048]{1,0:T(8,128)(2,1)S(1)} %convolution_convert_fusion.9, bf16[2048,2048]{1,0:T(8,128)(2,1)} %param.14), kind=kOutput, calls=%fused_computation.14 | convolution fusion | flops 1074003968 | bytes 9437188 | tf_op jit(solution)/shard_map/dot_general | solution.py:224
  165.9 7.8 %collective-permute-done.13 = bf16[128,2048]{1,0:T(8,128)(2,1)S(1)} collective-permute-done((bf16[128,2048]{1,0:T(8,128)(2,1)S(1)}, bf16[128,2048]{1,0:T(8,128)(2,1)S(1)}, u32[]{:S(2)}, u32[]{:S(2)}) %collective-permute-start.13) | collective-permute-done | bytes 524320 | tf_op jit(solution)/shard_map/ppermute | solution.py:36
  175.0 19.2 %collective-permute-done.14 = bf16[128,2048]{1,0:T(8,128)(2,1)S(1)} collective-permute-done((bf16[128,2048]{1,0:T(8,128)(2,1)S(1)}, bf16[128,2048]{1,0:T(8,128)(2,1)S(1)}, u32[]{:S(2)}, u32[]{:S(2)}) %collective-permute-start.14) | collective-permute-done | bytes 524320 | tf_op jit(solution)/shard_map/ppermute | solution.py:36
  197.0 2.8 %collective-permute-done.16 = bf16[256,2048]{1,0:T(8,128)(2,1)} collective-permute-done((bf16[256,2048]{1,0:T(8,128)(2,1)S(1)}, bf16[256,2048]{1,0:T(8,128)(2,1)}, u32[]{:S(2)}, u32[]{:S(2)}) %collective-permute-start.16) | collective-permute-done | bytes 1048608 | tf_op jit(solution)/shard_map/ppermute | solution.py:47
  201.5 11.4 %collective-permute-start.17 = (bf16[128,2048]{1,0:T(8,128)(2,1)S(1)}, bf16[128,2048]{1,0:T(8,128)(2,1)S(1)}, u32[]{:S(2)}, u32[]{:S(2)}) collective-permute-start(bf16[128,2048]{1,0:T(8,128)(2,1)S(1)} %get-tuple-element.9), channel_id=1, source_target_pairs={{0,0},{1,8},{2,4},{3,12},{4,1},{5,9},{6,5},{7,13},{8,2},{9,10},{10... | collective-permute-start | bytes 1572872 | tf_op jit(solution)/shard_map/ppermute | solution.py:255
  213.0 11.9 %collective-permute-done.17 = bf16[128,2048]{1,0:T(8,128)(2,1)S(1)} collective-permute-done((bf16[128,2048]{1,0:T(8,128)(2,1)S(1)}, bf16[128,2048]{1,0:T(8,128)(2,1)S(1)}, u32[]{:S(2)}, u32[]{:S(2)}) %collective-permute-start.17) | collective-permute-done | bytes 524320 | tf_op jit(solution)/shard_map/ppermute | solution.py:255
  224.9 13.5 %collective-permute-done.18 = bf16[128,2048]{1,0:T(8,128)(2,1)S(1)} collective-permute-done((bf16[128,2048]{1,0:T(8,128)(2,1)S(1)}, bf16[128,2048]{1,0:T(8,128)(2,1)S(1)}, u32[]{:S(2)}, u32[]{:S(2)}) %collective-permute-start.18) | collective-permute-done | bytes 524320 | tf_op jit(solution)/shard_map/ppermute | solution.py:255
  238.4 2.1 add_convert_fusion
  (92 shorter events, 33.5 us)
Async XLA Ops:
  0.0 44.8 %copy-start = (f32[128]{0:T(128)S(1)}, f32[128]{0:T(128)}, u32[]{:S(2)}) copy-start(f32[128]{0:T(128)} %param.11) | copy-start | bytes 1540
  3.5 11.2 %collective-permute-start = (bf16[128,1024]{1,0:T(8,128)(2,1)S(1)}, bf16[128,1024]{1,0:T(8,128)(2,1)S(1)}, u32[]{:S(2)}, u32[]{:S(2)}) collective-permute-start(bf16[128,1024]{1,0:T(8,128)(2,1)S(1)} %bitcast.100), channel_id=1, source_target_pairs={{0,4},{4,8},{8,12},{12,0},{1,5},{5,9},{9,13},{13,1},{2,6},{6,10},{... | collective-permute-start | bytes 786440 | tf_op jit(solution)/shard_map/ppermute | solution.py:145
  5.3 19.5 %collective-permute-start.1 = (bf16[128,1024]{1,0:T(8,128)(2,1)S(1)}, bf16[128,1024]{1,0:T(8,128)(2,1)S(1)}, u32[]{:S(2)}, u32[]{:S(2)}) collective-permute-start(bf16[128,1024]{1,0:T(8,128)(2,1)S(1)} %bitcast.99), channel_id=1, source_target_pairs={{0,8},{4,12},{8,0},{12,4},{1,9},{5,13},{9,1},{13,5},{2,10},{6,14},... | collective-permute-start | bytes 786440 | tf_op jit(solution)/shard_map/ppermute | solution.py:145
  7.9 17.1 %copy-start.3 = (s32[4]{0:T(128)S(1)}, s32[4]{0:T(128)}, u32[]{:S(2)}) copy-start(s32[4]{0:T(128)} %param.17) | copy-start | bytes 52
  7.9 17.1 %copy-start.4 = (s32[128]{0:T(128)S(1)}, s32[128]{0:T(128)}, u32[]{:S(2)}) copy-start(s32[128]{0:T(128)} %param.15) | copy-start | bytes 1540
  7.9 17.3 %copy-start.5 = (s32[128]{0:T(128)S(1)}, s32[128]{0:T(128)}, u32[]{:S(2)}) copy-start(s32[128]{0:T(128)} %param.16) | copy-start | bytes 1540
  8.1 16.8 %collective-permute-start.2 = (bf16[128,1024]{1,0:T(8,128)(2,1)S(1)}, bf16[128,1024]{1,0:T(8,128)(2,1)S(1)}, u32[]{:S(2)}, u32[]{:S(2)}) collective-permute-start(bf16[128,1024]{1,0:T(8,128)(2,1)S(1)} %bitcast.98), channel_id=1, source_target_pairs={{0,12},{4,0},{8,4},{12,8},{1,13},{5,1},{9,5},{13,9},{2,14},{6,2},{... | collective-permute-start | bytes 786440 | tf_op jit(solution)/shard_map/ppermute | solution.py:145
  24.9 2.7 %collective-permute-start.3 = (bf16[512,1024]{1,0:T(8,128)(2,1)S(1)}, bf16[512,1024]{1,0:T(8,128)(2,1)S(1)}, u32[]{:S(2)}, u32[]{:S(2)}) collective-permute-start(bf16[512,1024]{1,0:T(8,128)(2,1)S(1)} %bitcast.81), channel_id=1, source_target_pairs={{0,1},{1,0},{2,3},{3,2},{4,5},{5,4},{6,7},{7,6},{8,9},{9,8},{10,11... | collective-permute-start | bytes 3145736 | tf_op jit(solution)/shard_map/ppermute | solution.py:157
  32.6 20.0 %collective-permute-start.4 = (bf16[128,2048]{1,0:T(8,128)(2,1)S(1)}, bf16[128,2048]{1,0:T(8,128)(2,1)S(1)}, u32[]{:S(2)}, u32[]{:S(2)}) collective-permute-start(bf16[128,2048]{1,0:T(8,128)(2,1)S(1)} %convolution_convert_fusion.7), channel_id=1, source_target_pairs={{0,4},{4,8},{8,12},{12,0},{1,5},{5,9},{9,13},{13,1},{2,6},{6,10},{... | collective-permute-start | bytes 1572872 | tf_op jit(solution)/shard_map/ppermute | solution.py:24
  40.0 34.6 %collective-permute-start.5 = (bf16[128,2048]{1,0:T(8,128)(2,1)S(1)}, bf16[128,2048]{1,0:T(8,128)(2,1)S(1)}, u32[]{:S(2)}, u32[]{:S(2)}) collective-permute-start(bf16[128,2048]{1,0:T(8,128)(2,1)S(1)} %convolution_convert_fusion.6), channel_id=1, source_target_pairs={{0,8},{4,12},{8,0},{12,4},{1,9},{5,13},{9,1},{13,5},{2,10},{6,14},... | collective-permute-start | bytes 1572872 | tf_op jit(solution)/shard_map/ppermute | solution.py:24
  43.0 31.6 %collective-permute-start.6 = (bf16[128,2048]{1,0:T(8,128)(2,1)S(1)}, bf16[128,2048]{1,0:T(8,128)(2,1)S(1)}, u32[]{:S(2)}, u32[]{:S(2)}) collective-permute-start(bf16[128,2048]{1,0:T(8,128)(2,1)S(1)} %convolution_convert_fusion.5), channel_id=1, source_target_pairs={{0,12},{4,0},{8,4},{12,8},{1,13},{5,1},{9,5},{13,9},{2,14},{6,2},{... | collective-permute-start | bytes 1572872 | tf_op jit(solution)/shard_map/ppermute | solution.py:24
  77.3 15.5 %copy-start.1 = (bf16[1,1601,512]{2,1,0:T(8,128)(2,1)S(1)}, bf16[1,1601,512]{2,1,0:T(8,128)(2,1)}, u32[]{:S(2)}) copy-start(bf16[1,1601,512]{2,1,0:T(8,128)(2,1)} %param.13) | copy-start | bytes 4918276
  78.7 19.8 %collective-permute-start.7 = (bf16[64,2048]{1,0:T(8,128)(2,1)S(1)}, bf16[64,2048]{1,0:T(8,128)(2,1)}, u32[]{:S(2)}, u32[]{:S(2)}) collective-permute-start(bf16[64,2048]{1,0:T(8,128)(2,1)S(1)} %get-tuple-element.14), channel_id=1, source_target_pairs={{0,4},{4,8},{8,12},{12,0},{1,5},{5,9},{9,13},{13,1},{2,6},{6,10},{... | collective-permute-start | bytes 786440 | tf_op jit(solution)/shard_map/ppermute | solution.py:205
  90.4 19.9 %collective-permute-start.9 = (bf16[64,2048]{1,0:T(8,128)(2,1)S(1)}, bf16[64,2048]{1,0:T(8,128)(2,1)}, u32[]{:S(2)}, u32[]{:S(2)}) collective-permute-start(bf16[64,2048]{1,0:T(8,128)(2,1)S(1)} %get-tuple-element.13), channel_id=1, source_target_pairs={{0,8},{4,12},{8,0},{12,4},{1,9},{5,13},{9,1},{13,5},{2,10},{6,14},... | collective-permute-start | bytes 786440 | tf_op jit(solution)/shard_map/ppermute | solution.py:205
  91.7 31.4 %collective-permute-start.11 = (bf16[64,2048]{1,0:T(8,128)(2,1)S(1)}, bf16[64,2048]{1,0:T(8,128)(2,1)}, u32[]{:S(2)}, u32[]{:S(2)}) collective-permute-start(bf16[64,2048]{1,0:T(8,128)(2,1)S(1)} %get-tuple-element.12), channel_id=1, source_target_pairs={{0,12},{4,0},{8,4},{12,8},{1,13},{5,1},{9,5},{13,9},{2,14},{6,2},{... | collective-permute-start | bytes 786440 | tf_op jit(solution)/shard_map/ppermute | solution.py:205
  109.5 45.9 %collective-permute-start.8 = (bf16[64,2048]{1,0:T(8,128)(2,1)}, bf16[64,2048]{1,0:T(8,128)(2,1)S(1)}, u32[]{:S(2)}, u32[]{:S(2)}) collective-permute-start(bf16[64,2048]{1,0:T(8,128)(2,1)} %shard_map.92), channel_id=1, source_target_pairs={{0,12},{4,0},{8,4},{12,8},{1,13},{5,1},{9,5},{13,9},{2,14},{6,2},{... | collective-permute-start | bytes 786440 | tf_op jit(solution)/shard_map/ppermute | solution.py:212
  121.3 34.1 %collective-permute-start.10 = (bf16[64,2048]{1,0:T(8,128)(2,1)}, bf16[64,2048]{1,0:T(8,128)(2,1)S(1)}, u32[]{:S(2)}, u32[]{:S(2)}) collective-permute-start(bf16[64,2048]{1,0:T(8,128)(2,1)} %shard_map.93), channel_id=1, source_target_pairs={{0,8},{4,12},{8,0},{12,4},{1,9},{5,13},{9,1},{13,5},{2,10},{6,14},... | collective-permute-start | bytes 786440 | tf_op jit(solution)/shard_map/ppermute | solution.py:212
  134.2 21.3 %collective-permute-start.12 = (bf16[64,2048]{1,0:T(8,128)(2,1)}, bf16[64,2048]{1,0:T(8,128)(2,1)S(1)}, u32[]{:S(2)}, u32[]{:S(2)}) collective-permute-start(bf16[64,2048]{1,0:T(8,128)(2,1)} %shard_map.94), channel_id=1, source_target_pairs={{0,4},{4,8},{8,12},{12,0},{1,5},{5,9},{9,13},{13,1},{2,6},{6,10},{... | collective-permute-start | bytes 786440 | tf_op jit(solution)/shard_map/ppermute | solution.py:212
  156.9 16.8 %collective-permute-start.13 = (bf16[128,2048]{1,0:T(8,128)(2,1)S(1)}, bf16[128,2048]{1,0:T(8,128)(2,1)S(1)}, u32[]{:S(2)}, u32[]{:S(2)}) collective-permute-start(bf16[128,2048]{1,0:T(8,128)(2,1)S(1)} %convolution_convert_fusion.9), channel_id=1, source_target_pairs={{0,4},{4,8},{8,12},{12,0},{1,5},{5,9},{9,13},{13,1},{2,6},{6,10},{... | collective-permute-start | bytes 1572872 | tf_op jit(solution)/shard_map/ppermute | solution.py:36
  157.0 37.2 %collective-permute-start.14 = (bf16[128,2048]{1,0:T(8,128)(2,1)S(1)}, bf16[128,2048]{1,0:T(8,128)(2,1)S(1)}, u32[]{:S(2)}, u32[]{:S(2)}) collective-permute-start(bf16[128,2048]{1,0:T(8,128)(2,1)S(1)} %convolution_convert_fusion.9), channel_id=1, source_target_pairs={{0,8},{4,12},{8,0},{12,4},{1,9},{5,13},{9,1},{13,5},{2,10},{6,14},... | collective-permute-start | bytes 1572872 | tf_op jit(solution)/shard_map/ppermute | solution.py:36
  157.0 38.4 %collective-permute-start.15 = (bf16[128,2048]{1,0:T(8,128)(2,1)S(1)}, bf16[128,2048]{1,0:T(8,128)(2,1)S(1)}, u32[]{:S(2)}, u32[]{:S(2)}) collective-permute-start(bf16[128,2048]{1,0:T(8,128)(2,1)S(1)} %convolution_convert_fusion.9), channel_id=1, source_target_pairs={{0,12},{4,0},{8,4},{12,8},{1,13},{5,1},{9,5},{13,9},{2,14},{6,2},{... | collective-permute-start | bytes 1572872 | tf_op jit(solution)/shard_map/ppermute | solution.py:36
  196.9 2.9 %collective-permute-start.16 = (bf16[256,2048]{1,0:T(8,128)(2,1)S(1)}, bf16[256,2048]{1,0:T(8,128)(2,1)}, u32[]{:S(2)}, u32[]{:S(2)}) collective-permute-start(bf16[256,2048]{1,0:T(8,128)(2,1)S(1)} %dynamic-slice_bitcast_fusion), channel_id=1, source_target_pairs={{0,1},{1,0},{2,3},{3,2},{4,5},{5,4},{6,7},{7,6},{8,9},{9,8},{10,11... | collective-permute-start | bytes 3145736 | tf_op jit(solution)/shard_map/ppermute | solution.py:47
  201.5 23.4 %collective-permute-start.17 = (bf16[128,2048]{1,0:T(8,128)(2,1)S(1)}, bf16[128,2048]{1,0:T(8,128)(2,1)S(1)}, u32[]{:S(2)}, u32[]{:S(2)}) collective-permute-start(bf16[128,2048]{1,0:T(8,128)(2,1)S(1)} %get-tuple-element.9), channel_id=1, source_target_pairs={{0,0},{1,8},{2,4},{3,12},{4,1},{5,9},{6,5},{7,13},{8,2},{9,10},{10... | collective-permute-start | bytes 1572872 | tf_op jit(solution)/shard_map/ppermute | solution.py:255
  212.9 25.5 %collective-permute-start.18 = (bf16[128,2048]{1,0:T(8,128)(2,1)S(1)}, bf16[128,2048]{1,0:T(8,128)(2,1)S(1)}, u32[]{:S(2)}, u32[]{:S(2)}) collective-permute-start(bf16[128,2048]{1,0:T(8,128)(2,1)S(1)} %get-tuple-element.10), channel_id=1, source_target_pairs={{0,4},{1,12},{2,0},{3,8},{4,5},{5,13},{6,1},{7,9},{8,6},{9,14},{10... | collective-permute-start | bytes 1572872 | tf_op jit(solution)/shard_map/ppermute | solution.py:255
  (5 other events, 63.1 us)

commit v16 on v14

--- a/solution.py
+++ b/solution.py
@@ -50,11 +50,11 @@
 
 
 def attend_kernel(q_ref, k_ref, v_ref, o_ref, *, head_dim, token_count):
-    padded_tokens = k_ref.shape[1]
+    padded_tokens = k_ref.shape[2]
     split = (token_count // 128) * 128
-    scores = lax.dot_general(
-        q_ref[0], k_ref[0], (((1,), (1,)), ((), ())), preferred_element_type=jnp.float32
-    ) * (head_dim ** (-0.5))
+    scores = jnp.dot(q_ref[0], k_ref[0], preferred_element_type=jnp.float32) * (
+        head_dim ** (-0.5)
+    )
     pieces = [scores[:, :split]] if split else []
     if split < padded_tokens:
         tail = scores[:, split:]
@@ -77,32 +77,28 @@
     o_ref[0] = mixed.astype(o_ref.dtype)
 
 
-def attend(rows_in, keys, values, kv_count, per_kv, head_dim, token_count):
-    rows, width = rows_in.shape
-    padded_tokens = keys.shape[1]
-    stacked = rows_in.reshape(rows, kv_count, per_kv, head_dim).transpose(1, 2, 0, 3)
-    stacked = stacked.reshape(kv_count, per_kv * rows, head_dim)
+def attend(stacked, keys_t, values, token_count):
+    kv_count, stacked_rows, head_dim = stacked.shape
+    padded_tokens = keys_t.shape[2]
     kernel = functools.partial(attend_kernel, head_dim=head_dim, token_count=token_count)
-    flops = 4 * rows * padded_tokens * head_dim * per_kv * kv_count
-    moved = 2 * (2 * rows * width + 2 * padded_tokens * head_dim * kv_count)
-    mixed = pl.pallas_call(
+    flops = 4 * stacked_rows * padded_tokens * head_dim * kv_count
+    moved = 2 * (2 * stacked_rows * head_dim * kv_count + 2 * padded_tokens * head_dim * kv_count)
+    return pl.pallas_call(
         kernel,
         grid=(kv_count,),
         in_specs=[
-            pl.BlockSpec((1, per_kv * rows, head_dim), lambda k: (k, 0, 0)),
-            pl.BlockSpec((1, padded_tokens, head_dim), lambda k: (k, 0, 0)),
+            pl.BlockSpec((1, stacked_rows, head_dim), lambda k: (k, 0, 0)),
+            pl.BlockSpec((1, head_dim, padded_tokens), lambda k: (k, 0, 0)),
             pl.BlockSpec((1, padded_tokens, head_dim), lambda k: (k, 0, 0)),
         ],
-        out_specs=pl.BlockSpec((1, per_kv * rows, head_dim), lambda k: (k, 0, 0)),
-        out_shape=jax.ShapeDtypeStruct((kv_count, per_kv * rows, head_dim), jnp.bfloat16),
+        out_specs=pl.BlockSpec((1, stacked_rows, head_dim), lambda k: (k, 0, 0)),
+        out_shape=jax.ShapeDtypeStruct((kv_count, stacked_rows, head_dim), jnp.bfloat16),
         cost_estimate=pl.CostEstimate(
             flops=flops,
-            transcendentals=rows * padded_tokens * per_kv * kv_count,
+            transcendentals=stacked_rows * padded_tokens * kv_count,
             bytes_accessed=moved,
         ),
-    )(stacked, keys, values)
-    mixed = mixed.reshape(kv_count, per_kv, rows, head_dim).transpose(2, 0, 1, 3)
-    return mixed.reshape(rows, width)
+    )(stacked, keys_t, values)
 
 
 def local(
@@ -179,9 +175,12 @@
     outgoing = jnp.dot(dispatch, normalized, preferred_element_type=jnp.float32).astype(
         jnp.bfloat16
     )
-    outgoing = outgoing.reshape(req_count, capacity, q_cols)
     kv_count = max(1, heads_here // group_size)
     per_kv = heads_here // kv_count
+    outgoing = outgoing.reshape(req_count, capacity, kv_count, per_kv, head_dim)
+    outgoing = outgoing.transpose(0, 2, 3, 1, 4).reshape(
+        req_count, kv_count, per_kv * capacity, head_dim
+    )
     kv_first = sub_index * heads_here // group_size
     token_count = key_cache.shape[1]
     padded_tokens = -(-token_count // 128) * 128
@@ -190,7 +189,7 @@
         picked = jnp.pad(picked, ((0, padded_tokens - token_count), (0, 0)))
         return picked.reshape(padded_tokens, kv_count, head_dim).transpose(1, 0, 2)
 
-    keys_here = group_major(key_cache)
+    keys_here = group_major(key_cache).transpose(0, 2, 1)
     values_here = group_major(value_cache)
     returned_blocks = []
     for shift in range(req_count):
@@ -200,15 +199,16 @@
             arrived_block = lax.ppermute(
                 outgoing[shift], "req", [(i, (i + shift) % req_count) for i in range(req_count)]
             )
-        mixed_block = attend(
-            arrived_block, keys_here, values_here, kv_count, per_kv, head_dim, token_count
-        )
+        mixed_block = attend(arrived_block, keys_here, values_here, token_count)
         if shift:
             mixed_block = lax.ppermute(
                 mixed_block, "req", [(i, (i - shift) % req_count) for i in range(req_count)]
             )
         returned_blocks.append(mixed_block)
-    returned = jnp.stack(returned_blocks)
+    returned = jnp.stack(returned_blocks).reshape(
+        req_count, kv_count, per_kv, capacity, head_dim
+    )
+    returned = returned.transpose(0, 3, 1, 2, 4)
     attended = lax.dot_general(
         dispatch,
         returned.reshape(slot_total, q_cols),

time: 234 us -> 245 us (1.047)
  starting transfers between devices: 59 us -> 64.9 us
  local copies, waits for them, and re-layouts: 19.9 us -> 24.5 us
    ppermute x3, starting transfers between devices: 14.4 us -> 21.2 us  [local(): lax.ppermute(mixed_block, 'req', [(i, (i - shift) % req_count) for i in r...]
    reshape x7 -> x2, local copies, waits for them, and re-layouts: 6.85 us -> 1.55 us  [the longest x1 1.28 us: local(): returned.reshape(slot_total, q_cols)]
    dynamic_slice x4, local copies, waits for them, and re-layouts: 0.53 us -> 3.81 us  [local(): lax.dynamic_index_in_dim(my_part, (req_index + shift) % req_count, 1, kee...]
    unnamed x30 -> x26, local copies, waits for them, and re-layouts: 5.68 us -> 7.49 us
  transfers between devices with their start and end apart: 19 -> 19, of which waited for: 11 -> 12; matrix products, arithmetic and copies ran while one was open for 11% -> 9% of each run, Pallas kernels for 12% -> 11%
where the time goes in v16:
time: 245 us
  waiting for transfers between devices  102 us (42%)
  starting transfers between devices  64.9 us (26%)
  Pallas kernels  27 us (11%)
  local copies, waits for them, and re-layouts  24.5 us (10%)
  matrix products  19.9 us (8%)
  other arithmetic  5.25 us (2%)
    ppermute x3, waiting for transfers between devices, direct_reduce_scatter(): lax.ppermute(outgoing, axis, [(i, (i + shift) % count) for i in range(cou...  30.6 us
    ppermute x3, waiting for transfers between devices, direct_gather_apply(): lax.ppermute(block, axis, [(i, (i + shift) % count) for i in range(count)])  27 us
    pallas_call x4, Pallas kernels, attend(): pl.pallas_call(kernel, grid=(kv_count,), in_specs=[pl.BlockSpec((1, stack...  27 us
    ppermute x2, waiting for transfers between devices, local(): got = lax.ppermute(chunk, ('req', 'head', 'sub'), pairs).astype(jnp.float32)  25.6 us
    ppermute x3, starting transfers between devices, local(): lax.ppermute(mixed_block, 'req', [(i, (i - shift) % req_count) for i in r...  21.2 us
    ppermute x3, starting transfers between devices, local(): lax.ppermute(outgoing[shift], 'req', [(i, (i + shift) % req_count) for i...  14.1 us
    ppermute x3, waiting for transfers between devices, local(): lax.ppermute(outgoing_part, 'req', [(i, (i + shift) % req_count) for i in...  12.9 us
    ppermute x2, starting transfers between devices, local(): got = lax.ppermute(chunk, ('req', 'head', 'sub'), pairs).astype(jnp.float32)  11.4 us
  transfers between devices with their start and end apart: 19, of which 12 were waited for; matrix products, arithmetic and copies ran while one was open for 9% of the time, Pallas kernels for 11%

profile of v16, /device:TPU:6, one launch (start us, length us, event | category | flops | bytes accessed | tf_op | source)
XLA Modules:
  0.0 244.6 jit_solution(3372697089460210843)
XLA Ops:
  0.0 4.2 %copy.46 = bf16[128,8192]{0,1:T(8,128)(2,1)} copy(bf16[128,8192]{1,0:T(8,128)(2,1)} %param.9) | data formatting | bytes 4194304 | tf_op args[0]
  8.7 2.6 %collective-permute-start.1 = (bf16[128,1024]{1,0:T(8,128)(2,1)}, bf16[128,1024]{1,0:T(8,128)(2,1)S(1)}, u32[]{:S(2)}, u32[]{:S(2)}) collective-permute-start(bf16[128,1024]{1,0:T(8,128)(2,1)} %bitcast.4), channel_id=1, source_target_pairs={{0,8},{4,12},{8,0},{12,4},{1,9},{5,13},{9,1},{13,5},{2,10},{6,14},... | collective-permute-start | bytes 786440 | tf_op jit(solution)/shard_map/ppermute | solution.py:136
  13.9 3.8 %collective-permute-done = bf16[128,1024]{1,0:T(8,128)(2,1)} collective-permute-done((bf16[128,1024]{1,0:T(8,128)(2,1)}, bf16[128,1024]{1,0:T(8,128)(2,1)}, u32[]{:S(2)}, u32[]{:S(2)}) %collective-permute-start) | collective-permute-done | bytes 262176 | tf_op jit(solution)/shard_map/ppermute | solution.py:136
  18.7 9.1 %collective-permute-done.1 = bf16[128,1024]{1,0:T(8,128)(2,1)S(1)} collective-permute-done((bf16[128,1024]{1,0:T(8,128)(2,1)}, bf16[128,1024]{1,0:T(8,128)(2,1)S(1)}, u32[]{:S(2)}, u32[]{:S(2)}) %collective-permute-start.1) | collective-permute-done | bytes 262176 | tf_op jit(solution)/shard_map/ppermute | solution.py:136
  32.2 4.8 %convolution_convert_fusion.7 = bf16[128,2048]{1,0:T(8,128)(2,1)S(1)} fusion(bf16[2048,2048]{1,0:T(8,128)(2,1)} %param.10, bf16[512,2048]{1,0:T(8,128)(2,1)S(1)} %constant_dynamic-update-slice_fusion, s32[]{:T(128)S(6)} %select_n.191), kind=kOutput, calls=%fused_computation.7 | convolution fusion | flops 1074003968 | bytes 9437188 | tf_op jit(solution)/shard_map/dot_general | solution.py:156
  37.0 6.1 %collective-permute-start.4 = (bf16[128,2048]{1,0:T(8,128)(2,1)S(1)}, bf16[128,2048]{1,0:T(8,128)(2,1)S(1)}, u32[]{:S(2)}, u32[]{:S(2)}) collective-permute-start(bf16[128,2048]{1,0:T(8,128)(2,1)S(1)} %convolution_convert_fusion.7), channel_id=1, source_target_pairs={{0,4},{4,8},{8,12},{12,0},{1,5},{5,9},{9,13},{13,1},{2,6},{6,10},{... | collective-permute-start | bytes 1572872 | tf_op jit(solution)/shard_map/ppermute | solution.py:24
  48.5 8.6 %collective-permute-done.4 = bf16[128,2048]{1,0:T(8,128)(2,1)S(1)} collective-permute-done((bf16[128,2048]{1,0:T(8,128)(2,1)S(1)}, bf16[128,2048]{1,0:T(8,128)(2,1)S(1)}, u32[]{:S(2)}, u32[]{:S(2)}) %collective-permute-start.4) | collective-permute-done | bytes 524320 | tf_op jit(solution)/shard_map/ppermute | solution.py:24
  57.1 22.0 %collective-permute-done.5 = bf16[128,2048]{1,0:T(8,128)(2,1)S(1)} collective-permute-done((bf16[128,2048]{1,0:T(8,128)(2,1)S(1)}, bf16[128,2048]{1,0:T(8,128)(2,1)S(1)}, u32[]{:S(2)}, u32[]{:S(2)}) %collective-permute-start.5) | collective-permute-done | bytes 524320 | tf_op jit(solution)/shard_map/ppermute | solution.py:24
  83.9 11.7 %collective-permute-start.7 = (bf16[2,512,128]{2,1,0:T(8,128)(2,1)}, bf16[2,512,128]{2,1,0:T(8,128)(2,1)}, u32[]{:S(2)}, u32[]{:S(2)}) collective-permute-start(bf16[2,512,128]{2,1,0:T(8,128)(2,1)} %bitcast.19), channel_id=1, source_target_pairs={{0,4},{4,8},{8,12},{12,0},{1,5},{5,9},{9,13},{13,1},{2,6},{6,10},{... | collective-permute-start | bytes 786440 | tf_op jit(solution)/shard_map/ppermute | solution.py:199
  103.9 6.7 %shard_map.92 = bf16[2,512,128]{2,1,0:T(8,128)(2,1)} custom-call(bf16[2,512,128]{2,1,0:T(8,128)(2,1)} %collective-permute-done.7.q_ref, bf16[2,128,1664]{2,1,0:T(8,128)(2,1)} %bitcast.105, bf16[2,1664,128]{2,1,0:T(8,128)(2,1)} %bitcast.109), custom_call_target="tpu_custom_call" | custom-call | flops 872415232 | bytes 2228224 | tf_op jit(solution)/shard_map/pallas_call | solution.py:86
  114.0 6.7 %shard_map.93 = bf16[2,512,128]{2,1,0:T(8,128)(2,1)} custom-call(bf16[2,512,128]{2,1,0:T(8,128)(2,1)} %collective-permute-done.9.q_ref, bf16[2,128,1664]{2,1,0:T(8,128)(2,1)} %bitcast.106, bf16[2,1664,128]{2,1,0:T(8,128)(2,1)} %bitcast.110), custom_call_target="tpu_custom_call" | custom-call | flops 872415232 | bytes 2228224 | tf_op jit(solution)/shard_map/pallas_call | solution.py:86
  120.8 6.8 %shard_map.94 = bf16[2,512,128]{2,1,0:T(8,128)(2,1)} custom-call(bf16[2,512,128]{2,1,0:T(8,128)(2,1)} %collective-permute-done.11.q_ref, bf16[2,128,1664]{2,1,0:T(8,128)(2,1)} %bitcast.107, bf16[2,1664,128]{2,1,0:T(8,128)(2,1)} %bitcast.111), custom_call_target="tpu_custom_call" | custom-call | flops 872415232 | bytes 2228224 | tf_op jit(solution)/shard_map/pallas_call | solution.py:86
  127.6 19.4 %collective-permute-start.12 = (bf16[2,512,128]{2,1,0:T(8,128)(2,1)}, bf16[2,512,128]{2,1,0:T(8,128)(2,1)S(1)}, u32[]{:S(2)}, u32[]{:S(2)}) collective-permute-start(bf16[2,512,128]{2,1,0:T(8,128)(2,1)} %shard_map.94), channel_id=1, source_target_pairs={{0,4},{4,8},{8,12},{12,0},{1,5},{5,9},{9,13},{13,1},{2,6},{6,10},{... | collective-permute-start | bytes 786440 | tf_op jit(solution)/shard_map/ppermute | solution.py:204
  146.9 6.7 %shard_map.91 = bf16[2,512,128]{2,1,0:T(8,128)(2,1)} custom-call(bf16[2,512,128]{2,1,0:T(8,128)(2,1)} %bitcast.117, bf16[2,128,1664]{2,1,0:T(8,128)(2,1)} %bitcast.108, bf16[2,1664,128]{2,1,0:T(8,128)(2,1)} %bitcast.112), custom_call_target="tpu_custom_call" | custom-call | flops 872415232 | bytes 2228224 | tf_op jit(solution)/shard_map/pallas_call | solution.py:86
  158.5 3.7 %collective-permute-start.15 = (bf16[128,2048]{1,0:T(8,128)(2,1)S(1)}, bf16[128,2048]{1,0:T(8,128)(2,1)S(1)}, u32[]{:S(2)}, u32[]{:S(2)}) collective-permute-start(bf16[128,2048]{1,0:T(8,128)(2,1)S(1)} %convolution_convert_fusion.9), channel_id=1, source_target_pairs={{0,12},{4,0},{8,4},{12,8},{1,13},{5,1},{9,5},{13,9},{2,14},{6,2},{... | collective-permute-start | bytes 1572872 | tf_op jit(solution)/shard_map/ppermute | solution.py:36
  162.5 4.8 %fusion.4 = bf16[4,128,2048]{2,1,0:T(8,128)(2,1)S(1)} fusion(bf16[4,128,2048]{2,1,0:T(8,128)(2,1)S(1)} %broadcast_in_dim.56, s32[]{:T(128)S(6)} %select_n.168, bf16[128,2048]{1,0:T(8,128)(2,1)S(1)} %convolution_convert_fusion.9, bf16[2048,2048]{1,0:T(8,128)(2,1)} %param.14), kind=kOutput, calls=%fused_computation.14 | convolution fusion | flops 1074003968 | bytes 9437188 | tf_op jit(solution)/shard_map/dot_general | solution.py:219
  167.3 7.8 %collective-permute-done.13 = bf16[128,2048]{1,0:T(8,128)(2,1)S(1)} collective-permute-done((bf16[128,2048]{1,0:T(8,128)(2,1)S(1)}, bf16[128,2048]{1,0:T(8,128)(2,1)S(1)}, u32[]{:S(2)}, u32[]{:S(2)}) %collective-permute-start.13) | collective-permute-done | bytes 524320 | tf_op jit(solution)/shard_map/ppermute | solution.py:36
  176.5 19.2 %collective-permute-done.14 = bf16[128,2048]{1,0:T(8,128)(2,1)S(1)} collective-permute-done((bf16[128,2048]{1,0:T(8,128)(2,1)S(1)}, bf16[128,2048]{1,0:T(8,128)(2,1)S(1)}, u32[]{:S(2)}, u32[]{:S(2)}) %collective-permute-start.14) | collective-permute-done | bytes 524320 | tf_op jit(solution)/shard_map/ppermute | solution.py:36
  199.8 2.8 %collective-permute-done.16 = bf16[256,2048]{1,0:T(8,128)(2,1)} collective-permute-done((bf16[256,2048]{1,0:T(8,128)(2,1)S(1)}, bf16[256,2048]{1,0:T(8,128)(2,1)}, u32[]{:S(2)}, u32[]{:S(2)}) %collective-permute-start.16) | collective-permute-done | bytes 1048608 | tf_op jit(solution)/shard_map/ppermute | solution.py:47
  202.6 1.9 fusion.11
  205.4 11.4 %collective-permute-start.17 = (bf16[128,2048]{1,0:T(8,128)(2,1)}, bf16[128,2048]{1,0:T(8,128)(2,1)S(1)}, u32[]{:S(2)}, u32[]{:S(2)}) collective-permute-start(bf16[128,2048]{1,0:T(8,128)(2,1)} %get-tuple-element.9), channel_id=1, source_target_pairs={{0,0},{1,8},{2,4},{3,12},{4,1},{5,9},{6,5},{7,13},{8,2},{9,10},{10... | collective-permute-start | bytes 1572872 | tf_op jit(solution)/shard_map/ppermute | solution.py:250
  216.9 12.2 %collective-permute-done.17 = bf16[128,2048]{1,0:T(8,128)(2,1)S(1)} collective-permute-done((bf16[128,2048]{1,0:T(8,128)(2,1)}, bf16[128,2048]{1,0:T(8,128)(2,1)S(1)}, u32[]{:S(2)}, u32[]{:S(2)}) %collective-permute-start.17) | collective-permute-done | bytes 524320 | tf_op jit(solution)/shard_map/ppermute | solution.py:250
  229.1 13.3 %collective-permute-done.18 = bf16[128,2048]{1,0:T(8,128)(2,1)S(1)} collective-permute-done((bf16[128,2048]{1,0:T(8,128)(2,1)S(1)}, bf16[128,2048]{1,0:T(8,128)(2,1)S(1)}, u32[]{:S(2)}, u32[]{:S(2)}) %collective-permute-start.18) | collective-permute-done | bytes 524320 | tf_op jit(solution)/shard_map/ppermute | solution.py:250
  242.5 2.1 add_convert_fusion
  (101 shorter events, 45.5 us)
Async XLA Ops:
  0.0 95.6 %copy-start = (bf16[1,1601,512]{2,1,0:T(8,128)(2,1)S(1)}, bf16[1,1601,512]{2,1,0:T(8,128)(2,1)}, u32[]{:S(2)}) copy-start(bf16[1,1601,512]{2,1,0:T(8,128)(2,1)} %param.13) | copy-start | bytes 4918276
  6.3 11.4 %collective-permute-start = (bf16[128,1024]{1,0:T(8,128)(2,1)}, bf16[128,1024]{1,0:T(8,128)(2,1)}, u32[]{:S(2)}, u32[]{:S(2)}) collective-permute-start(bf16[128,1024]{1,0:T(8,128)(2,1)} %bitcast.2), channel_id=1, source_target_pairs={{0,4},{4,8},{8,12},{12,0},{1,5},{5,9},{9,13},{13,1},{2,6},{6,10},{... | collective-permute-start | bytes 786440 | tf_op jit(solution)/shard_map/ppermute | solution.py:136
  8.7 19.0 %collective-permute-start.1 = (bf16[128,1024]{1,0:T(8,128)(2,1)}, bf16[128,1024]{1,0:T(8,128)(2,1)S(1)}, u32[]{:S(2)}, u32[]{:S(2)}) collective-permute-start(bf16[128,1024]{1,0:T(8,128)(2,1)} %bitcast.4), channel_id=1, source_target_pairs={{0,8},{4,12},{8,0},{12,4},{1,9},{5,13},{9,1},{13,5},{2,10},{6,14},... | collective-permute-start | bytes 786440 | tf_op jit(solution)/shard_map/ppermute | solution.py:136
  11.3 16.6 %copy-start.4 = (s32[4]{0:T(128)S(1)}, s32[4]{0:T(128)}, u32[]{:S(2)}) copy-start(s32[4]{0:T(128)} %param.17) | copy-start | bytes 52
  11.3 16.6 %copy-start.5 = (s32[128]{0:T(128)S(1)}, s32[128]{0:T(128)}, u32[]{:S(2)}) copy-start(s32[128]{0:T(128)} %param.15) | copy-start | bytes 1540
  11.3 16.8 %copy-start.6 = (s32[128]{0:T(128)S(1)}, s32[128]{0:T(128)}, u32[]{:S(2)}) copy-start(s32[128]{0:T(128)} %param.16) | copy-start | bytes 1540
  12.2 15.6 %collective-permute-start.2 = (bf16[128,1024]{1,0:T(8,128)(2,1)}, bf16[128,1024]{1,0:T(8,128)(2,1)S(1)}, u32[]{:S(2)}, u32[]{:S(2)}) collective-permute-start(bf16[128,1024]{1,0:T(8,128)(2,1)} %bitcast.6), channel_id=1, source_target_pairs={{0,12},{4,0},{8,4},{12,8},{1,13},{5,1},{9,5},{13,9},{2,14},{6,2},{... | collective-permute-start | bytes 786440 | tf_op jit(solution)/shard_map/ppermute | solution.py:136
  27.8 2.9 %collective-permute-start.3 = (bf16[512,1024]{1,0:T(8,128)(2,1)S(1)}, bf16[512,1024]{1,0:T(8,128)(2,1)}, u32[]{:S(2)}, u32[]{:S(2)}) collective-permute-start(bf16[512,1024]{1,0:T(8,128)(2,1)S(1)} %bitcast.97), channel_id=1, source_target_pairs={{0,1},{1,0},{2,3},{3,2},{4,5},{5,4},{6,7},{7,6},{8,9},{9,8},{10,11... | collective-permute-start | bytes 3145736 | tf_op jit(solution)/shard_map/ppermute | solution.py:148
  37.0 20.1 %collective-permute-start.4 = (bf16[128,2048]{1,0:T(8,128)(2,1)S(1)}, bf16[128,2048]{1,0:T(8,128)(2,1)S(1)}, u32[]{:S(2)}, u32[]{:S(2)}) collective-permute-start(bf16[128,2048]{1,0:T(8,128)(2,1)S(1)} %convolution_convert_fusion.7), channel_id=1, source_target_pairs={{0,4},{4,8},{8,12},{12,0},{1,5},{5,9},{9,13},{13,1},{2,6},{6,10},{... | collective-permute-start | bytes 1572872 | tf_op jit(solution)/shard_map/ppermute | solution.py:24
  44.5 34.6 %collective-permute-start.5 = (bf16[128,2048]{1,0:T(8,128)(2,1)S(1)}, bf16[128,2048]{1,0:T(8,128)(2,1)S(1)}, u32[]{:S(2)}, u32[]{:S(2)}) collective-permute-start(bf16[128,2048]{1,0:T(8,128)(2,1)S(1)} %convolution_convert_fusion.6), channel_id=1, source_target_pairs={{0,8},{4,12},{8,0},{12,4},{1,9},{5,13},{9,1},{13,5},{2,10},{6,14},... | collective-permute-start | bytes 1572872 | tf_op jit(solution)/shard_map/ppermute | solution.py:24
  47.5 31.5 %collective-permute-start.6 = (bf16[128,2048]{1,0:T(8,128)(2,1)S(1)}, bf16[128,2048]{1,0:T(8,128)(2,1)S(1)}, u32[]{:S(2)}, u32[]{:S(2)}) collective-permute-start(bf16[128,2048]{1,0:T(8,128)(2,1)S(1)} %convolution_convert_fusion.5), channel_id=1, source_target_pairs={{0,12},{4,0},{8,4},{12,8},{1,13},{5,1},{9,5},{13,9},{2,14},{6,2},{... | collective-permute-start | bytes 1572872 | tf_op jit(solution)/shard_map/ppermute | solution.py:24
  82.9 15.2 %copy-start.2 = (bf16[1,1601,512]{2,1,0:T(8,128)(2,1)S(1)}, bf16[1,1601,512]{2,1,0:T(8,128)(2,1)}, u32[]{:S(2)}) copy-start(bf16[1,1601,512]{2,1,0:T(8,128)(2,1)} %param.12) | copy-start | bytes 4918276
  83.9 20.0 %collective-permute-start.7 = (bf16[2,512,128]{2,1,0:T(8,128)(2,1)}, bf16[2,512,128]{2,1,0:T(8,128)(2,1)}, u32[]{:S(2)}, u32[]{:S(2)}) collective-permute-start(bf16[2,512,128]{2,1,0:T(8,128)(2,1)} %bitcast.19), channel_id=1, source_target_pairs={{0,4},{4,8},{8,12},{12,0},{1,5},{5,9},{9,13},{13,1},{2,6},{6,10},{... | collective-permute-start | bytes 786440 | tf_op jit(solution)/shard_map/ppermute | solution.py:199
  95.7 18.4 %collective-permute-start.9 = (bf16[2,512,128]{2,1,0:T(8,128)(2,1)}, bf16[2,512,128]{2,1,0:T(8,128)(2,1)}, u32[]{:S(2)}, u32[]{:S(2)}) collective-permute-start(bf16[2,512,128]{2,1,0:T(8,128)(2,1)} %bitcast.22), channel_id=1, source_target_pairs={{0,8},{4,12},{8,0},{12,4},{1,9},{5,13},{9,1},{13,5},{2,10},{6,14},... | collective-permute-start | bytes 786440 | tf_op jit(solution)/shard_map/ppermute | solution.py:199
  97.0 23.8 %collective-permute-start.11 = (bf16[2,512,128]{2,1,0:T(8,128)(2,1)}, bf16[2,512,128]{2,1,0:T(8,128)(2,1)}, u32[]{:S(2)}, u32[]{:S(2)}) collective-permute-start(bf16[2,512,128]{2,1,0:T(8,128)(2,1)} %bitcast.24), channel_id=1, source_target_pairs={{0,12},{4,0},{8,4},{12,8},{1,13},{5,1},{9,5},{13,9},{2,14},{6,2},{... | collective-permute-start | bytes 786440 | tf_op jit(solution)/shard_map/ppermute | solution.py:199
  110.6 44.2 %collective-permute-start.8 = (bf16[2,512,128]{2,1,0:T(8,128)(2,1)}, bf16[2,512,128]{2,1,0:T(8,128)(2,1)S(1)}, u32[]{:S(2)}, u32[]{:S(2)}) collective-permute-start(bf16[2,512,128]{2,1,0:T(8,128)(2,1)} %shard_map.92), channel_id=1, source_target_pairs={{0,12},{4,0},{8,4},{12,8},{1,13},{5,1},{9,5},{13,9},{2,14},{6,2},{... | collective-permute-start | bytes 786440 | tf_op jit(solution)/shard_map/ppermute | solution.py:204
  120.8 34.2 %collective-permute-start.10 = (bf16[2,512,128]{2,1,0:T(8,128)(2,1)}, bf16[2,512,128]{2,1,0:T(8,128)(2,1)S(1)}, u32[]{:S(2)}, u32[]{:S(2)}) collective-permute-start(bf16[2,512,128]{2,1,0:T(8,128)(2,1)} %shard_map.93), channel_id=1, source_target_pairs={{0,8},{4,12},{8,0},{12,4},{1,9},{5,13},{9,1},{13,5},{2,10},{6,14},... | collective-permute-start | bytes 786440 | tf_op jit(solution)/shard_map/ppermute | solution.py:204
  127.6 27.6 %collective-permute-start.12 = (bf16[2,512,128]{2,1,0:T(8,128)(2,1)}, bf16[2,512,128]{2,1,0:T(8,128)(2,1)S(1)}, u32[]{:S(2)}, u32[]{:S(2)}) collective-permute-start(bf16[2,512,128]{2,1,0:T(8,128)(2,1)} %shard_map.94), channel_id=1, source_target_pairs={{0,4},{4,8},{8,12},{12,0},{1,5},{5,9},{9,13},{13,1},{2,6},{6,10},{... | collective-permute-start | bytes 786440 | tf_op jit(solution)/shard_map/ppermute | solution.py:204
  158.4 16.8 %collective-permute-start.13 = (bf16[128,2048]{1,0:T(8,128)(2,1)S(1)}, bf16[128,2048]{1,0:T(8,128)(2,1)S(1)}, u32[]{:S(2)}, u32[]{:S(2)}) collective-permute-start(bf16[128,2048]{1,0:T(8,128)(2,1)S(1)} %convolution_convert_fusion.9), channel_id=1, source_target_pairs={{0,4},{4,8},{8,12},{12,0},{1,5},{5,9},{9,13},{13,1},{2,6},{6,10},{... | collective-permute-start | bytes 1572872 | tf_op jit(solution)/shard_map/ppermute | solution.py:36
  158.4 37.2 %collective-permute-start.14 = (bf16[128,2048]{1,0:T(8,128)(2,1)S(1)}, bf16[128,2048]{1,0:T(8,128)(2,1)S(1)}, u32[]{:S(2)}, u32[]{:S(2)}) collective-permute-start(bf16[128,2048]{1,0:T(8,128)(2,1)S(1)} %convolution_convert_fusion.9), channel_id=1, source_target_pairs={{0,8},{4,12},{8,0},{12,4},{1,9},{5,13},{9,1},{13,5},{2,10},{6,14},... | collective-permute-start | bytes 1572872 | tf_op jit(solution)/shard_map/ppermute | solution.py:36
  158.5 38.5 %collective-permute-start.15 = (bf16[128,2048]{1,0:T(8,128)(2,1)S(1)}, bf16[128,2048]{1,0:T(8,128)(2,1)S(1)}, u32[]{:S(2)}, u32[]{:S(2)}) collective-permute-start(bf16[128,2048]{1,0:T(8,128)(2,1)S(1)} %convolution_convert_fusion.9), channel_id=1, source_target_pairs={{0,12},{4,0},{8,4},{12,8},{1,13},{5,1},{9,5},{13,9},{2,14},{6,2},{... | collective-permute-start | bytes 1572872 | tf_op jit(solution)/shard_map/ppermute | solution.py:36
  199.7 2.9 %collective-permute-start.16 = (bf16[256,2048]{1,0:T(8,128)(2,1)S(1)}, bf16[256,2048]{1,0:T(8,128)(2,1)}, u32[]{:S(2)}, u32[]{:S(2)}) collective-permute-start(bf16[256,2048]{1,0:T(8,128)(2,1)S(1)} %dynamic-slice_bitcast_fusion), channel_id=1, source_target_pairs={{0,1},{1,0},{2,3},{3,2},{4,5},{5,4},{6,7},{7,6},{8,9},{9,8},{10,11... | collective-permute-start | bytes 3145736 | tf_op jit(solution)/shard_map/ppermute | solution.py:47
  205.4 23.7 %collective-permute-start.17 = (bf16[128,2048]{1,0:T(8,128)(2,1)}, bf16[128,2048]{1,0:T(8,128)(2,1)S(1)}, u32[]{:S(2)}, u32[]{:S(2)}) collective-permute-start(bf16[128,2048]{1,0:T(8,128)(2,1)} %get-tuple-element.9), channel_id=1, source_target_pairs={{0,0},{1,8},{2,4},{3,12},{4,1},{5,9},{6,5},{7,13},{8,2},{9,10},{10... | collective-permute-start | bytes 1572872 | tf_op jit(solution)/shard_map/ppermute | solution.py:250
  216.8 25.7 %collective-permute-start.18 = (bf16[128,2048]{1,0:T(8,128)(2,1)S(1)}, bf16[128,2048]{1,0:T(8,128)(2,1)S(1)}, u32[]{:S(2)}, u32[]{:S(2)}) collective-permute-start(bf16[128,2048]{1,0:T(8,128)(2,1)S(1)} %get-tuple-element.10), channel_id=1, source_target_pairs={{0,4},{1,12},{2,0},{3,8},{4,5},{5,13},{6,1},{7,9},{8,6},{9,14},{10... | collective-permute-start | bytes 1572872 | tf_op jit(solution)/shard_map/ppermute | solution.py:250
  (6 other events, 54.4 us)

commit v17 on v14

--- a/solution.py
+++ b/solution.py
@@ -192,21 +192,26 @@
 
     keys_here = group_major(key_cache)
     values_here = group_major(value_cache)
-    returned_blocks = []
-    for shift in range(req_count):
-        if shift == 0:
-            arrived_block = outgoing[0]
-        else:
-            arrived_block = lax.ppermute(
-                outgoing[shift], "req", [(i, (i + shift) % req_count) for i in range(req_count)]
-            )
+    arrived_blocks = [outgoing[0]] + [
+        lax.ppermute(
+            outgoing[shift], "req", [(i, (i + shift) % req_count) for i in range(req_count)]
+        )
+        for shift in range(1, req_count)
+    ]
+    returned_blocks = [
+        attend(outgoing[0], keys_here, values_here, kv_count, per_kv, head_dim, token_count)
+    ]
+    if req_count > 1:
+        returned_blocks[0], arrived_blocks[1] = lax.optimization_barrier(
+            (returned_blocks[0], arrived_blocks[1])
+        )
+    for shift in range(1, req_count):
         mixed_block = attend(
-            arrived_block, keys_here, values_here, kv_count, per_kv, head_dim, token_count
-        )
-        if shift:
-            mixed_block = lax.ppermute(
-                mixed_block, "req", [(i, (i - shift) % req_count) for i in range(req_count)]
-            )
+            arrived_blocks[shift], keys_here, values_here, kv_count, per_kv, head_dim, token_count
+        )
+        mixed_block = lax.ppermute(
+            mixed_block, "req", [(i, (i - shift) % req_count) for i in range(req_count)]
+        )
         returned_blocks.append(mixed_block)
     returned = jnp.stack(returned_blocks)
     attended = lax.dot_general(

time: 234 us -> 231 us (0.987)
  starting transfers between devices: 59 us -> 47.7 us
  waiting for transfers between devices: 103 us -> 112 us
    ppermute x3, starting transfers between devices: 14.4 us -> 3 us  [local(): lax.ppermute(mixed_block, 'req', [(i, (i - shift) % req_count) for i in r...]
    ppermute x3, waiting for transfers between devices: 0.01 us -> 9.53 us  [local(): lax.ppermute(mixed_block, 'req', [(i, (i - shift) % req_count) for i in r...]
where the time goes in v17:
time: 231 us
  waiting for transfers between devices  112 us (48%)
  starting transfers between devices  47.7 us (21%)
  Pallas kernels  27.1 us (12%)
  local copies, waits for them, and re-layouts  19.8 us (9%)
  matrix products  18.6 us (8%)
  other arithmetic  4.93 us (2%)
    ppermute x3, waiting for transfers between devices, direct_reduce_scatter(): lax.ppermute(outgoing, axis, [(i, (i + shift) % count) for i in range(cou...  29.7 us
    ppermute x3, waiting for transfers between devices, direct_gather_apply(): lax.ppermute(block, axis, [(i, (i + shift) % count) for i in range(count)])  28 us
    pallas_call x4, Pallas kernels, attend(): pl.pallas_call(kernel, grid=(kv_count,), in_specs=[pl.BlockSpec((1, per_k...  27.1 us
    ppermute x2, waiting for transfers between devices, local(): got = lax.ppermute(chunk, ('req', 'head', 'sub'), pairs).astype(jnp.float32)  25.4 us
    ppermute x3, waiting for transfers between devices, local(): lax.ppermute(outgoing_part, 'req', [(i, (i + shift) % req_count) for i in...  14.9 us
    ppermute x3, starting transfers between devices, local(): lax.ppermute(outgoing[shift], 'req', [(i, (i + shift) % req_count) for i...  14.1 us
    ppermute x2, starting transfers between devices, local(): got = lax.ppermute(chunk, ('req', 'head', 'sub'), pairs).astype(jnp.float32)  11.5 us
    ppermute x3, waiting for transfers between devices, local(): lax.ppermute(mixed_block, 'req', [(i, (i - shift) % req_count) for i in r...  9.53 us
  transfers between devices with their start and end apart: 19, of which 11 were waited for; matrix products, arithmetic and copies ran while one was open for 11% of the time, Pallas kernels for 12%

profile of v17, /device:TPU:6, one launch (start us, length us, event | category | flops | bytes accessed | tf_op | source)
XLA Modules:
  0.0 230.9 jit_solution(12694580749077892935)
XLA Ops:
  0.0 3.2 %copy.61 = bf16[128,8192]{0,1:T(8,128)(2,1)S(1)} copy(bf16[128,8192]{1,0:T(8,128)(2,1)} %param.9) | data formatting | bytes 4194304 | tf_op args[0]
  5.3 2.7 %collective-permute-start.1 = (bf16[128,1024]{1,0:T(8,128)(2,1)S(1)}, bf16[128,1024]{1,0:T(8,128)(2,1)S(1)}, u32[]{:S(2)}, u32[]{:S(2)}) collective-permute-start(bf16[128,1024]{1,0:T(8,128)(2,1)S(1)} %bitcast.161), channel_id=1, source_target_pairs={{0,8},{4,12},{8,0},{12,4},{1,9},{5,13},{9,1},{13,5},{2,10},{6,14},... | collective-permute-start | bytes 786440 | tf_op jit(solution)/shard_map/ppermute | solution.py:140
  9.9 4.8 %collective-permute-done = bf16[128,1024]{1,0:T(8,128)(2,1)S(1)} collective-permute-done((bf16[128,1024]{1,0:T(8,128)(2,1)S(1)}, bf16[128,1024]{1,0:T(8,128)(2,1)S(1)}, u32[]{:S(2)}, u32[]{:S(2)}) %collective-permute-start) | collective-permute-done | bytes 262176 | tf_op jit(solution)/shard_map/ppermute | solution.py:140
  14.7 10.1 %collective-permute-done.1 = bf16[128,1024]{1,0:T(8,128)(2,1)S(1)} collective-permute-done((bf16[128,1024]{1,0:T(8,128)(2,1)S(1)}, bf16[128,1024]{1,0:T(8,128)(2,1)S(1)}, u32[]{:S(2)}, u32[]{:S(2)}) %collective-permute-start.1) | collective-permute-done | bytes 262176 | tf_op jit(solution)/shard_map/ppermute | solution.py:140
  27.8 4.8 %convolution_convert_fusion.7 = bf16[128,2048]{1,0:T(8,128)(2,1)S(1)} fusion(bf16[2048,2048]{1,0:T(8,128)(2,1)} %param.10, bf16[512,2048]{1,0:T(8,128)(2,1)S(1)} %constant_dynamic-update-slice_fusion, s32[]{:T(128)S(6)} %select_n.191), kind=kOutput, calls=%fused_computation.7 | convolution fusion | flops 1074003968 | bytes 9437188 | tf_op jit(solution)/shard_map/dot_general | solution.py:160
  32.6 6.1 %collective-permute-start.4 = (bf16[128,2048]{1,0:T(8,128)(2,1)S(1)}, bf16[128,2048]{1,0:T(8,128)(2,1)S(1)}, u32[]{:S(2)}, u32[]{:S(2)}) collective-permute-start(bf16[128,2048]{1,0:T(8,128)(2,1)S(1)} %convolution_convert_fusion.7), channel_id=1, source_target_pairs={{0,4},{4,8},{8,12},{12,0},{1,5},{5,9},{9,13},{13,1},{2,6},{6,10},{... | collective-permute-start | bytes 1572872 | tf_op jit(solution)/shard_map/ppermute | solution.py:24
  44.8 7.8 %collective-permute-done.4 = bf16[128,2048]{1,0:T(8,128)(2,1)S(1)} collective-permute-done((bf16[128,2048]{1,0:T(8,128)(2,1)S(1)}, bf16[128,2048]{1,0:T(8,128)(2,1)S(1)}, u32[]{:S(2)}, u32[]{:S(2)}) %collective-permute-start.4) | collective-permute-done | bytes 524320 | tf_op jit(solution)/shard_map/ppermute | solution.py:24
  52.6 22.0 %collective-permute-done.5 = bf16[128,2048]{1,0:T(8,128)(2,1)S(1)} collective-permute-done((bf16[128,2048]{1,0:T(8,128)(2,1)S(1)}, bf16[128,2048]{1,0:T(8,128)(2,1)S(1)}, u32[]{:S(2)}, u32[]{:S(2)}) %collective-permute-start.5) | collective-permute-done | bytes 524320 | tf_op jit(solution)/shard_map/ppermute | solution.py:24
  78.8 11.7 %collective-permute-start.7 = (bf16[64,2048]{1,0:T(8,128)(2,1)}, bf16[64,2048]{1,0:T(8,128)(2,1)}, u32[]{:S(2)}, u32[]{:S(2)}) collective-permute-start(bf16[64,2048]{1,0:T(8,128)(2,1)} %get-tuple-element.15), channel_id=1, source_target_pairs={{0,4},{4,8},{8,12},{12,0},{1,5},{5,9},{9,13},{13,1},{2,6},{6,10},{... | collective-permute-start | bytes 786440 | tf_op jit(solution)/shard_map/ppermute | solution.py:196
  97.9 6.8 %shard_map.91 = bf16[2,512,128]{2,1,0:T(8,128)(2,1)} custom-call(bf16[2,512,128]{2,1,0:T(8,128)(2,1)} %bitcast.170, bf16[2,1664,128]{2,1,0:T(8,128)(2,1)} %bitcast.152, bf16[2,1664,128]{2,1,0:T(8,128)(2,1)} %bitcast.156), custom_call_target="tpu_custom_call" | custom-call | flops 872415232 | bytes 2228224 | tf_op jit(solution)/shard_map/pallas_call | solution.py:88
  107.6 6.8 %shard_map.92 = bf16[2,512,128]{2,1,0:T(8,128)(2,1)} custom-call(bf16[2,512,128]{2,1,0:T(8,128)(2,1)} %bitcast.172, bf16[2,1664,128]{2,1,0:T(8,128)(2,1)} %bitcast.153, bf16[2,1664,128]{2,1,0:T(8,128)(2,1)} %bitcast.157), custom_call_target="tpu_custom_call" | custom-call | flops 872415232 | bytes 2228224 | tf_op jit(solution)/shard_map/pallas_call | solution.py:88
  115.6 2.3 collective-permute-start.8
  118.7 6.8 %shard_map.93 = bf16[2,512,128]{2,1,0:T(8,128)(2,1)} custom-call(bf16[2,512,128]{2,1,0:T(8,128)(2,1)} %bitcast.174, bf16[2,1664,128]{2,1,0:T(8,128)(2,1)} %bitcast.154, bf16[2,1664,128]{2,1,0:T(8,128)(2,1)} %bitcast.158), custom_call_target="tpu_custom_call" | custom-call | flops 872415232 | bytes 2228224 | tf_op jit(solution)/shard_map/pallas_call | solution.py:88
  128.0 6.8 %shard_map.94 = bf16[2,512,128]{2,1,0:T(8,128)(2,1)} custom-call(bf16[2,512,128]{2,1,0:T(8,128)(2,1)} %bitcast.168, bf16[2,1664,128]{2,1,0:T(8,128)(2,1)} %bitcast.155, bf16[2,1664,128]{2,1,0:T(8,128)(2,1)} %bitcast.159), custom_call_target="tpu_custom_call" | custom-call | flops 872415232 | bytes 2228224 | tf_op jit(solution)/shard_map/pallas_call | solution.py:88
  136.2 9.5 %collective-permute-done.10 = bf16[64,2048]{1,0:T(8,128)(2,1)S(1)} collective-permute-done((bf16[64,2048]{1,0:T(8,128)(2,1)S(1)}, bf16[64,2048]{1,0:T(8,128)(2,1)S(1)}, u32[]{:S(2)}, u32[]{:S(2)}) %collective-permute-start.10) | collective-permute-done | bytes 262176 | tf_op jit(solution)/shard_map/ppermute | solution.py:212
  147.4 2.7 %collective-permute-start.15 = (bf16[128,2048]{1,0:T(8,128)(2,1)S(1)}, bf16[128,2048]{1,0:T(8,128)(2,1)S(1)}, u32[]{:S(2)}, u32[]{:S(2)}) collective-permute-start(bf16[128,2048]{1,0:T(8,128)(2,1)S(1)} %convolution_convert_fusion.9), channel_id=1, source_target_pairs={{0,12},{4,0},{8,4},{12,8},{1,13},{5,1},{9,5},{13,9},{2,14},{6,2},{... | collective-permute-start | bytes 1572872 | tf_op jit(solution)/shard_map/ppermute | solution.py:36
  150.4 4.8 %fusion.4 = bf16[4,128,2048]{2,1,0:T(8,128)(2,1)S(1)} fusion(bf16[4,128,2048]{2,1,0:T(8,128)(2,1)S(1)} %broadcast_in_dim.56, s32[]{:T(128)S(6)} %select_n.168, bf16[128,2048]{1,0:T(8,128)(2,1)S(1)} %convolution_convert_fusion.9, bf16[2048,2048]{1,0:T(8,128)(2,1)} %param.14), kind=kOutput, calls=%fused_computation.14 | convolution fusion | flops 1074003968 | bytes 9437188 | tf_op jit(solution)/shard_map/dot_general | solution.py:224
  155.2 7.8 %collective-permute-done.13 = bf16[128,2048]{1,0:T(8,128)(2,1)S(1)} collective-permute-done((bf16[128,2048]{1,0:T(8,128)(2,1)S(1)}, bf16[128,2048]{1,0:T(8,128)(2,1)S(1)}, u32[]{:S(2)}, u32[]{:S(2)}) %collective-permute-start.13) | collective-permute-done | bytes 524320 | tf_op jit(solution)/shard_map/ppermute | solution.py:36
  164.3 20.2 %collective-permute-done.14 = bf16[128,2048]{1,0:T(8,128)(2,1)S(1)} collective-permute-done((bf16[128,2048]{1,0:T(8,128)(2,1)S(1)}, bf16[128,2048]{1,0:T(8,128)(2,1)S(1)}, u32[]{:S(2)}, u32[]{:S(2)}) %collective-permute-start.14) | collective-permute-done | bytes 524320 | tf_op jit(solution)/shard_map/ppermute | solution.py:36
  187.4 2.8 %collective-permute-done.16 = bf16[256,2048]{1,0:T(8,128)(2,1)} collective-permute-done((bf16[256,2048]{1,0:T(8,128)(2,1)S(1)}, bf16[256,2048]{1,0:T(8,128)(2,1)}, u32[]{:S(2)}, u32[]{:S(2)}) %collective-permute-start.16) | collective-permute-done | bytes 1048608 | tf_op jit(solution)/shard_map/ppermute | solution.py:47
  191.9 11.5 %collective-permute-start.17 = (bf16[128,2048]{1,0:T(8,128)(2,1)S(1)}, bf16[128,2048]{1,0:T(8,128)(2,1)S(1)}, u32[]{:S(2)}, u32[]{:S(2)}) collective-permute-start(bf16[128,2048]{1,0:T(8,128)(2,1)S(1)} %get-tuple-element.13), channel_id=1, source_target_pairs={{0,0},{1,8},{2,4},{3,12},{4,1},{5,9},{6,5},{7,13},{8,2},{9,10},{10... | collective-permute-start | bytes 1572872 | tf_op jit(solution)/shard_map/ppermute | solution.py:255
  203.4 12.1 %collective-permute-done.17 = bf16[128,2048]{1,0:T(8,128)(2,1)S(1)} collective-permute-done((bf16[128,2048]{1,0:T(8,128)(2,1)S(1)}, bf16[128,2048]{1,0:T(8,128)(2,1)S(1)}, u32[]{:S(2)}, u32[]{:S(2)}) %collective-permute-start.17) | collective-permute-done | bytes 524320 | tf_op jit(solution)/shard_map/ppermute | solution.py:255
  215.5 13.3 %collective-permute-done.18 = bf16[128,2048]{1,0:T(8,128)(2,1)S(1)} collective-permute-done((bf16[128,2048]{1,0:T(8,128)(2,1)S(1)}, bf16[128,2048]{1,0:T(8,128)(2,1)S(1)}, u32[]{:S(2)}, u32[]{:S(2)}) %collective-permute-start.18) | collective-permute-done | bytes 524320 | tf_op jit(solution)/shard_map/ppermute | solution.py:255
  228.8 2.1 add_convert_fusion
  (108 shorter events, 40.9 us)
Async XLA Ops:
  0.0 44.8 %copy-start = (f32[128]{0:T(128)S(1)}, f32[128]{0:T(128)}, u32[]{:S(2)}) copy-start(f32[128]{0:T(128)} %param.11) | copy-start | bytes 1540
  3.5 11.2 %collective-permute-start = (bf16[128,1024]{1,0:T(8,128)(2,1)S(1)}, bf16[128,1024]{1,0:T(8,128)(2,1)S(1)}, u32[]{:S(2)}, u32[]{:S(2)}) collective-permute-start(bf16[128,1024]{1,0:T(8,128)(2,1)S(1)} %bitcast.162), channel_id=1, source_target_pairs={{0,4},{4,8},{8,12},{12,0},{1,5},{5,9},{9,13},{13,1},{2,6},{6,10},{... | collective-permute-start | bytes 786440 | tf_op jit(solution)/shard_map/ppermute | solution.py:140
  5.3 19.5 %collective-permute-start.1 = (bf16[128,1024]{1,0:T(8,128)(2,1)S(1)}, bf16[128,1024]{1,0:T(8,128)(2,1)S(1)}, u32[]{:S(2)}, u32[]{:S(2)}) collective-permute-start(bf16[128,1024]{1,0:T(8,128)(2,1)S(1)} %bitcast.161), channel_id=1, source_target_pairs={{0,8},{4,12},{8,0},{12,4},{1,9},{5,13},{9,1},{13,5},{2,10},{6,14},... | collective-permute-start | bytes 786440 | tf_op jit(solution)/shard_map/ppermute | solution.py:140
  7.9 17.1 %copy-start.3 = (s32[4]{0:T(128)S(1)}, s32[4]{0:T(128)}, u32[]{:S(2)}) copy-start(s32[4]{0:T(128)} %param.17) | copy-start | bytes 52
  7.9 17.1 %copy-start.4 = (s32[128]{0:T(128)S(1)}, s32[128]{0:T(128)}, u32[]{:S(2)}) copy-start(s32[128]{0:T(128)} %param.15) | copy-start | bytes 1540
  7.9 17.3 %copy-start.5 = (s32[128]{0:T(128)S(1)}, s32[128]{0:T(128)}, u32[]{:S(2)}) copy-start(s32[128]{0:T(128)} %param.16) | copy-start | bytes 1540
  8.1 16.8 %collective-permute-start.2 = (bf16[128,1024]{1,0:T(8,128)(2,1)S(1)}, bf16[128,1024]{1,0:T(8,128)(2,1)S(1)}, u32[]{:S(2)}, u32[]{:S(2)}) collective-permute-start(bf16[128,1024]{1,0:T(8,128)(2,1)S(1)} %bitcast.160), channel_id=1, source_target_pairs={{0,12},{4,0},{8,4},{12,8},{1,13},{5,1},{9,5},{13,9},{2,14},{6,2},{... | collective-permute-start | bytes 786440 | tf_op jit(solution)/shard_map/ppermute | solution.py:140
  24.9 2.7 %collective-permute-start.3 = (bf16[512,1024]{1,0:T(8,128)(2,1)S(1)}, bf16[512,1024]{1,0:T(8,128)(2,1)S(1)}, u32[]{:S(2)}, u32[]{:S(2)}) collective-permute-start(bf16[512,1024]{1,0:T(8,128)(2,1)S(1)} %bitcast.134), channel_id=1, source_target_pairs={{0,1},{1,0},{2,3},{3,2},{4,5},{5,4},{6,7},{7,6},{8,9},{9,8},{10,11... | collective-permute-start | bytes 3145736 | tf_op jit(solution)/shard_map/ppermute | solution.py:152
  32.6 20.0 %collective-permute-start.4 = (bf16[128,2048]{1,0:T(8,128)(2,1)S(1)}, bf16[128,2048]{1,0:T(8,128)(2,1)S(1)}, u32[]{:S(2)}, u32[]{:S(2)}) collective-permute-start(bf16[128,2048]{1,0:T(8,128)(2,1)S(1)} %convolution_convert_fusion.7), channel_id=1, source_target_pairs={{0,4},{4,8},{8,12},{12,0},{1,5},{5,9},{9,13},{13,1},{2,6},{6,10},{... | collective-permute-start | bytes 1572872 | tf_op jit(solution)/shard_map/ppermute | solution.py:24
  40.0 34.6 %collective-permute-start.5 = (bf16[128,2048]{1,0:T(8,128)(2,1)S(1)}, bf16[128,2048]{1,0:T(8,128)(2,1)S(1)}, u32[]{:S(2)}, u32[]{:S(2)}) collective-permute-start(bf16[128,2048]{1,0:T(8,128)(2,1)S(1)} %convolution_convert_fusion.6), channel_id=1, source_target_pairs={{0,8},{4,12},{8,0},{12,4},{1,9},{5,13},{9,1},{13,5},{2,10},{6,14},... | collective-permute-start | bytes 1572872 | tf_op jit(solution)/shard_map/ppermute | solution.py:24
  43.0 31.6 %collective-permute-start.6 = (bf16[128,2048]{1,0:T(8,128)(2,1)S(1)}, bf16[128,2048]{1,0:T(8,128)(2,1)S(1)}, u32[]{:S(2)}, u32[]{:S(2)}) collective-permute-start(bf16[128,2048]{1,0:T(8,128)(2,1)S(1)} %convolution_convert_fusion.5), channel_id=1, source_target_pairs={{0,12},{4,0},{8,4},{12,8},{1,13},{5,1},{9,5},{13,9},{2,14},{6,2},{... | collective-permute-start | bytes 1572872 | tf_op jit(solution)/shard_map/ppermute | solution.py:24
  77.3 15.6 %copy-start.1 = (bf16[1,1601,512]{2,1,0:T(8,128)(2,1)S(1)}, bf16[1,1601,512]{2,1,0:T(8,128)(2,1)}, u32[]{:S(2)}) copy-start(bf16[1,1601,512]{2,1,0:T(8,128)(2,1)} %param.13) | copy-start | bytes 4918276
  78.8 27.0 %collective-permute-start.7 = (bf16[64,2048]{1,0:T(8,128)(2,1)}, bf16[64,2048]{1,0:T(8,128)(2,1)}, u32[]{:S(2)}, u32[]{:S(2)}) collective-permute-start(bf16[64,2048]{1,0:T(8,128)(2,1)} %get-tuple-element.15), channel_id=1, source_target_pairs={{0,4},{4,8},{8,12},{12,0},{1,5},{5,9},{9,13},{13,1},{2,6},{6,10},{... | collective-permute-start | bytes 786440 | tf_op jit(solution)/shard_map/ppermute | solution.py:196
  90.5 27.4 %collective-permute-start.9 = (bf16[64,2048]{1,0:T(8,128)(2,1)}, bf16[64,2048]{1,0:T(8,128)(2,1)S(1)}, u32[]{:S(2)}, u32[]{:S(2)}) collective-permute-start(bf16[64,2048]{1,0:T(8,128)(2,1)} %get-tuple-element.17), channel_id=1, source_target_pairs={{0,8},{4,12},{8,0},{12,4},{1,9},{5,13},{9,1},{13,5},{2,10},{6,14},... | collective-permute-start | bytes 786440 | tf_op jit(solution)/shard_map/ppermute | solution.py:196
  91.8 35.4 %collective-permute-start.11 = (bf16[64,2048]{1,0:T(8,128)(2,1)}, bf16[64,2048]{1,0:T(8,128)(2,1)S(1)}, u32[]{:S(2)}, u32[]{:S(2)}) collective-permute-start(bf16[64,2048]{1,0:T(8,128)(2,1)} %get-tuple-element.16), channel_id=1, source_target_pairs={{0,12},{4,0},{8,4},{12,8},{1,13},{5,1},{9,5},{13,9},{2,14},{6,2},{... | collective-permute-start | bytes 786440 | tf_op jit(solution)/shard_map/ppermute | solution.py:196
  115.6 20.6 %collective-permute-start.8 = (bf16[64,2048]{1,0:T(8,128)(2,1)S(1)}, bf16[64,2048]{1,0:T(8,128)(2,1)S(1)}, u32[]{:S(2)}, u32[]{:S(2)}) collective-permute-start(bf16[64,2048]{1,0:T(8,128)(2,1)S(1)} %bitcast.163), channel_id=1, source_target_pairs={{0,12},{4,0},{8,4},{12,8},{1,13},{5,1},{9,5},{13,9},{2,14},{6,2},{... | collective-permute-start | bytes 786440 | tf_op jit(solution)/shard_map/ppermute | solution.py:212
  126.7 19.0 %collective-permute-start.10 = (bf16[64,2048]{1,0:T(8,128)(2,1)S(1)}, bf16[64,2048]{1,0:T(8,128)(2,1)S(1)}, u32[]{:S(2)}, u32[]{:S(2)}) collective-permute-start(bf16[64,2048]{1,0:T(8,128)(2,1)S(1)} %bitcast.165), channel_id=1, source_target_pairs={{0,8},{4,12},{8,0},{12,4},{1,9},{5,13},{9,1},{13,5},{2,10},{6,14},... | collective-permute-start | bytes 786440 | tf_op jit(solution)/shard_map/ppermute | solution.py:212
  135.9 9.8 %collective-permute-start.12 = (bf16[64,2048]{1,0:T(8,128)(2,1)S(1)}, bf16[64,2048]{1,0:T(8,128)(2,1)S(1)}, u32[]{:S(2)}, u32[]{:S(2)}) collective-permute-start(bf16[64,2048]{1,0:T(8,128)(2,1)S(1)} %bitcast.167), channel_id=1, source_target_pairs={{0,4},{4,8},{8,12},{12,0},{1,5},{5,9},{9,13},{13,1},{2,6},{6,10},{... | collective-permute-start | bytes 786440 | tf_op jit(solution)/shard_map/ppermute | solution.py:212
  146.3 16.8 %collective-permute-start.13 = (bf16[128,2048]{1,0:T(8,128)(2,1)S(1)}, bf16[128,2048]{1,0:T(8,128)(2,1)S(1)}, u32[]{:S(2)}, u32[]{:S(2)}) collective-permute-start(bf16[128,2048]{1,0:T(8,128)(2,1)S(1)} %convolution_convert_fusion.9), channel_id=1, source_target_pairs={{0,4},{4,8},{8,12},{12,0},{1,5},{5,9},{9,13},{13,1},{2,6},{6,10},{... | collective-permute-start | bytes 1572872 | tf_op jit(solution)/shard_map/ppermute | solution.py:36
  146.3 38.2 %collective-permute-start.14 = (bf16[128,2048]{1,0:T(8,128)(2,1)S(1)}, bf16[128,2048]{1,0:T(8,128)(2,1)S(1)}, u32[]{:S(2)}, u32[]{:S(2)}) collective-permute-start(bf16[128,2048]{1,0:T(8,128)(2,1)S(1)} %convolution_convert_fusion.9), channel_id=1, source_target_pairs={{0,8},{4,12},{8,0},{12,4},{1,9},{5,13},{9,1},{13,5},{2,10},{6,14},... | collective-permute-start | bytes 1572872 | tf_op jit(solution)/shard_map/ppermute | solution.py:36
  147.4 38.4 %collective-permute-start.15 = (bf16[128,2048]{1,0:T(8,128)(2,1)S(1)}, bf16[128,2048]{1,0:T(8,128)(2,1)S(1)}, u32[]{:S(2)}, u32[]{:S(2)}) collective-permute-start(bf16[128,2048]{1,0:T(8,128)(2,1)S(1)} %convolution_convert_fusion.9), channel_id=1, source_target_pairs={{0,12},{4,0},{8,4},{12,8},{1,13},{5,1},{9,5},{13,9},{2,14},{6,2},{... | collective-permute-start | bytes 1572872 | tf_op jit(solution)/shard_map/ppermute | solution.py:36
  187.3 2.9 %collective-permute-start.16 = (bf16[256,2048]{1,0:T(8,128)(2,1)S(1)}, bf16[256,2048]{1,0:T(8,128)(2,1)}, u32[]{:S(2)}, u32[]{:S(2)}) collective-permute-start(bf16[256,2048]{1,0:T(8,128)(2,1)S(1)} %dynamic-slice_bitcast_fusion), channel_id=1, source_target_pairs={{0,1},{1,0},{2,3},{3,2},{4,5},{5,4},{6,7},{7,6},{8,9},{9,8},{10,11... | collective-permute-start | bytes 3145736 | tf_op jit(solution)/shard_map/ppermute | solution.py:47
  191.9 23.7 %collective-permute-start.17 = (bf16[128,2048]{1,0:T(8,128)(2,1)S(1)}, bf16[128,2048]{1,0:T(8,128)(2,1)S(1)}, u32[]{:S(2)}, u32[]{:S(2)}) collective-permute-start(bf16[128,2048]{1,0:T(8,128)(2,1)S(1)} %get-tuple-element.13), channel_id=1, source_target_pairs={{0,0},{1,8},{2,4},{3,12},{4,1},{5,9},{6,5},{7,13},{8,2},{9,10},{10... | collective-permute-start | bytes 1572872 | tf_op jit(solution)/shard_map/ppermute | solution.py:255
  203.3 25.5 %collective-permute-start.18 = (bf16[128,2048]{1,0:T(8,128)(2,1)S(1)}, bf16[128,2048]{1,0:T(8,128)(2,1)S(1)}, u32[]{:S(2)}, u32[]{:S(2)}) collective-permute-start(bf16[128,2048]{1,0:T(8,128)(2,1)S(1)} %get-tuple-element.14), channel_id=1, source_target_pairs={{0,4},{1,12},{2,0},{3,8},{4,5},{5,13},{6,1},{7,9},{8,6},{9,14},{10... | collective-permute-start | bytes 1572872 | tf_op jit(solution)/shard_map/ppermute | solution.py:255
  (5 other events, 63.1 us)

commit v18 on v17

--- a/solution.py
+++ b/solution.py
@@ -77,32 +77,28 @@
     o_ref[0] = mixed.astype(o_ref.dtype)
 
 
-def attend(rows_in, keys, values, kv_count, per_kv, head_dim, token_count):
-    rows, width = rows_in.shape
+def attend(stacked, keys, values, token_count):
+    kv_count, stacked_rows, head_dim = stacked.shape
     padded_tokens = keys.shape[1]
-    stacked = rows_in.reshape(rows, kv_count, per_kv, head_dim).transpose(1, 2, 0, 3)
-    stacked = stacked.reshape(kv_count, per_kv * rows, head_dim)
     kernel = functools.partial(attend_kernel, head_dim=head_dim, token_count=token_count)
-    flops = 4 * rows * padded_tokens * head_dim * per_kv * kv_count
-    moved = 2 * (2 * rows * width + 2 * padded_tokens * head_dim * kv_count)
-    mixed = pl.pallas_call(
+    flops = 4 * stacked_rows * padded_tokens * head_dim * kv_count
+    moved = 2 * (2 * stacked_rows * head_dim * kv_count + 2 * padded_tokens * head_dim * kv_count)
+    return pl.pallas_call(
         kernel,
         grid=(kv_count,),
         in_specs=[
-            pl.BlockSpec((1, per_kv * rows, head_dim), lambda k: (k, 0, 0)),
+            pl.BlockSpec((1, stacked_rows, head_dim), lambda k: (k, 0, 0)),
             pl.BlockSpec((1, padded_tokens, head_dim), lambda k: (k, 0, 0)),
             pl.BlockSpec((1, padded_tokens, head_dim), lambda k: (k, 0, 0)),
         ],
-        out_specs=pl.BlockSpec((1, per_kv * rows, head_dim), lambda k: (k, 0, 0)),
-        out_shape=jax.ShapeDtypeStruct((kv_count, per_kv * rows, head_dim), jnp.bfloat16),
+        out_specs=pl.BlockSpec((1, stacked_rows, head_dim), lambda k: (k, 0, 0)),
+        out_shape=jax.ShapeDtypeStruct((kv_count, stacked_rows, head_dim), jnp.bfloat16),
         cost_estimate=pl.CostEstimate(
             flops=flops,
-            transcendentals=rows * padded_tokens * per_kv * kv_count,
+            transcendentals=stacked_rows * padded_tokens * kv_count,
             bytes_accessed=moved,
         ),
     )(stacked, keys, values)
-    mixed = mixed.reshape(kv_count, per_kv, rows, head_dim).transpose(2, 0, 1, 3)
-    return mixed.reshape(rows, width)
 
 
 def local(
@@ -179,9 +175,12 @@
     outgoing = jnp.dot(dispatch, normalized, preferred_element_type=jnp.float32).astype(
         jnp.bfloat16
     )
-    outgoing = outgoing.reshape(req_count, capacity, q_cols)
     kv_count = max(1, heads_here // group_size)
     per_kv = heads_here // kv_count
+    outgoing = outgoing.reshape(req_count, capacity, kv_count, per_kv, head_dim)
+    outgoing = outgoing.transpose(0, 2, 3, 1, 4).reshape(
+        req_count, kv_count, per_kv * capacity, head_dim
+    )
     kv_first = sub_index * heads_here // group_size
     token_count = key_cache.shape[1]
     padded_tokens = -(-token_count // 128) * 128
@@ -199,21 +198,22 @@
         for shift in range(1, req_count)
     ]
     returned_blocks = [
-        attend(outgoing[0], keys_here, values_here, kv_count, per_kv, head_dim, token_count)
+        attend(outgoing[0], keys_here, values_here, token_count)
     ]
     if req_count > 1:
         returned_blocks[0], arrived_blocks[1] = lax.optimization_barrier(
             (returned_blocks[0], arrived_blocks[1])
         )
     for shift in range(1, req_count):
-        mixed_block = attend(
-            arrived_blocks[shift], keys_here, values_here, kv_count, per_kv, head_dim, token_count
-        )
+        mixed_block = attend(arrived_blocks[shift], keys_here, values_here, token_count)
         mixed_block = lax.ppermute(
             mixed_block, "req", [(i, (i - shift) % req_count) for i in range(req_count)]
         )
         returned_blocks.append(mixed_block)
-    returned = jnp.stack(returned_blocks)
+    returned = jnp.stack(returned_blocks).reshape(
+        req_count, kv_count, per_kv, capacity, head_dim
+    )
+    returned = returned.transpose(0, 3, 1, 2, 4)
     attended = lax.dot_general(
         dispatch,
         returned.reshape(slot_total, q_cols),

time: 231 us -> 225 us (0.974)
  local copies, waits for them, and re-layouts: 19.8 us -> 12.4 us
  starting transfers between devices: 47.7 us -> 51.2 us
  waiting for transfers between devices: 112 us -> 109 us
    reshape x7 -> x2, local copies, waits for them, and re-layouts: 6.81 us -> 0.77 us  [the longest x1 0.49 us: local(): returned.reshape(slot_total, q_cols)]
    ppermute x3, starting transfers between devices: 3 us -> 6.27 us  [local(): lax.ppermute(mixed_block, 'req', [(i, (i - shift) % req_count) for i in r...]
    unnamed x30 -> x25, local copies, waits for them, and re-layouts: 4.84 us -> 3.7 us
  transfers between devices with their start and end apart: 19 -> 19, of which waited for: 11 -> 11; matrix products, arithmetic and copies ran while one was open for 11% -> 7% of each run, Pallas kernels for 12% -> 12%
where the time goes in v18:
time: 225 us; the launch traced here: 224 us
  waiting for transfers between devices  109 us (48%)
  starting transfers between devices  51.2 us (23%)
  Pallas kernels  27.1 us (12%)
  matrix products  18.6 us (8%)
  local copies, waits for them, and re-layouts  12.4 us (6%)
  other arithmetic  4.93 us (2%)
    ppermute x3, waiting for transfers between devices, direct_reduce_scatter(): lax.ppermute(outgoing, axis, [(i, (i + shift) % count) for i in range(cou...  29.7 us
    pallas_call x4, Pallas kernels, attend(): pl.pallas_call(kernel, grid=(kv_count,), in_specs=[pl.BlockSpec((1, stack...  27.1 us
    ppermute x3, waiting for transfers between devices, direct_gather_apply(): lax.ppermute(block, axis, [(i, (i + shift) % count) for i in range(count)])  26.4 us
    ppermute x2, waiting for transfers between devices, local(): got = lax.ppermute(chunk, ('req', 'head', 'sub'), pairs).astype(jnp.float32)  25.4 us
    ppermute x3, waiting for transfers between devices, local(): lax.ppermute(outgoing_part, 'req', [(i, (i + shift) % req_count) for i in...  14.9 us
    ppermute x3, starting transfers between devices, local(): lax.ppermute(outgoing[shift], 'req', [(i, (i + shift) % req_count) for i...  14.1 us
    ppermute x2, starting transfers between devices, local(): got = lax.ppermute(chunk, ('req', 'head', 'sub'), pairs).astype(jnp.float32)  11.7 us
    ppermute x3, starting transfers between devices, direct_reduce_scatter(): lax.ppermute(outgoing, axis, [(i, (i + shift) % count) for i in range(cou...  9.44 us
  transfers between devices with their start and end apart: 19, of which 11 were waited for; matrix products, arithmetic and copies ran while one was open for 7% of the time, Pallas kernels for 12%

profile of v18, /device:TPU:6, one launch (start us, length us, event | category | flops | bytes accessed | tf_op | source)
XLA Modules:
  0.0 223.9 jit_solution(1404718904603317291)
XLA Ops:
  0.0 3.2 %copy.49 = bf16[128,8192]{0,1:T(8,128)(2,1)S(1)} copy(bf16[128,8192]{1,0:T(8,128)(2,1)} %param.9) | data formatting | bytes 4194304 | tf_op args[0]
  5.3 2.7 %collective-permute-start.1 = (bf16[128,1024]{1,0:T(8,128)(2,1)S(1)}, bf16[128,1024]{1,0:T(8,128)(2,1)S(1)}, u32[]{:S(2)}, u32[]{:S(2)}) collective-permute-start(bf16[128,1024]{1,0:T(8,128)(2,1)S(1)} %bitcast.114), channel_id=1, source_target_pairs={{0,8},{4,12},{8,0},{12,4},{1,9},{5,13},{9,1},{13,5},{2,10},{6,14},... | collective-permute-start | bytes 786440 | tf_op jit(solution)/shard_map/ppermute | solution.py:136
  9.9 4.8 %collective-permute-done = bf16[128,1024]{1,0:T(8,128)(2,1)S(1)} collective-permute-done((bf16[128,1024]{1,0:T(8,128)(2,1)S(1)}, bf16[128,1024]{1,0:T(8,128)(2,1)S(1)}, u32[]{:S(2)}, u32[]{:S(2)}) %collective-permute-start) | collective-permute-done | bytes 262176 | tf_op jit(solution)/shard_map/ppermute | solution.py:136
  14.7 10.1 %collective-permute-done.1 = bf16[128,1024]{1,0:T(8,128)(2,1)S(1)} collective-permute-done((bf16[128,1024]{1,0:T(8,128)(2,1)S(1)}, bf16[128,1024]{1,0:T(8,128)(2,1)S(1)}, u32[]{:S(2)}, u32[]{:S(2)}) %collective-permute-start.1) | collective-permute-done | bytes 262176 | tf_op jit(solution)/shard_map/ppermute | solution.py:136
  27.8 4.8 %convolution_convert_fusion.7 = bf16[128,2048]{1,0:T(8,128)(2,1)S(1)} fusion(bf16[2048,2048]{1,0:T(8,128)(2,1)} %param.10, bf16[512,2048]{1,0:T(8,128)(2,1)S(1)} %constant_dynamic-update-slice_fusion, s32[]{:T(128)S(6)} %select_n.191), kind=kOutput, calls=%fused_computation.7 | convolution fusion | flops 1074003968 | bytes 9437188 | tf_op jit(solution)/shard_map/dot_general | solution.py:156
  32.6 6.1 %collective-permute-start.4 = (bf16[128,2048]{1,0:T(8,128)(2,1)S(1)}, bf16[128,2048]{1,0:T(8,128)(2,1)S(1)}, u32[]{:S(2)}, u32[]{:S(2)}) collective-permute-start(bf16[128,2048]{1,0:T(8,128)(2,1)S(1)} %convolution_convert_fusion.7), channel_id=1, source_target_pairs={{0,4},{4,8},{8,12},{12,0},{1,5},{5,9},{9,13},{13,1},{2,6},{6,10},{... | collective-permute-start | bytes 1572872 | tf_op jit(solution)/shard_map/ppermute | solution.py:24
  44.8 7.8 %collective-permute-done.4 = bf16[128,2048]{1,0:T(8,128)(2,1)S(1)} collective-permute-done((bf16[128,2048]{1,0:T(8,128)(2,1)S(1)}, bf16[128,2048]{1,0:T(8,128)(2,1)S(1)}, u32[]{:S(2)}, u32[]{:S(2)}) %collective-permute-start.4) | collective-permute-done | bytes 524320 | tf_op jit(solution)/shard_map/ppermute | solution.py:24
  52.6 22.0 %collective-permute-done.5 = bf16[128,2048]{1,0:T(8,128)(2,1)S(1)} collective-permute-done((bf16[128,2048]{1,0:T(8,128)(2,1)S(1)}, bf16[128,2048]{1,0:T(8,128)(2,1)S(1)}, u32[]{:S(2)}, u32[]{:S(2)}) %collective-permute-start.5) | collective-permute-done | bytes 524320 | tf_op jit(solution)/shard_map/ppermute | solution.py:24
  79.2 11.7 %collective-permute-start.7 = (bf16[2,512,128]{2,1,0:T(8,128)(2,1)S(1)}, bf16[2,512,128]{2,1,0:T(8,128)(2,1)}, u32[]{:S(2)}, u32[]{:S(2)}) collective-permute-start(bf16[2,512,128]{2,1,0:T(8,128)(2,1)S(1)} %bitcast.123), channel_id=1, source_target_pairs={{0,4},{4,8},{8,12},{12,0},{1,5},{5,9},{9,13},{13,1},{2,6},{6,10},{... | collective-permute-start | bytes 786440 | tf_op jit(solution)/shard_map/ppermute | solution.py:195
  97.5 6.8 %shard_map.91 = bf16[2,512,128]{2,1,0:T(8,128)(2,1)} custom-call(bf16[2,512,128]{2,1,0:T(8,128)(2,1)} %bitcast.122, bf16[2,1664,128]{2,1,0:T(8,128)(2,1)} %bitcast.105, bf16[2,1664,128]{2,1,0:T(8,128)(2,1)} %bitcast.109), custom_call_target="tpu_custom_call" | custom-call | flops 872415232 | bytes 2228224 | tf_op jit(solution)/shard_map/pallas_call | solution.py:86
  104.3 6.8 %shard_map.92 = bf16[2,512,128]{2,1,0:T(8,128)(2,1)} custom-call(bf16[2,512,128]{2,1,0:T(8,128)(2,1)} %collective-permute-done.7.q_ref, bf16[2,1664,128]{2,1,0:T(8,128)(2,1)} %bitcast.106, bf16[2,1664,128]{2,1,0:T(8,128)(2,1)} %bitcast.110), custom_call_target="tpu_custom_call" | custom-call | flops 872415232 | bytes 2228224 | tf_op jit(solution)/shard_map/pallas_call | solution.py:86
  113.1 6.8 %shard_map.93 = bf16[2,512,128]{2,1,0:T(8,128)(2,1)} custom-call(bf16[2,512,128]{2,1,0:T(8,128)(2,1)} %collective-permute-done.9.q_ref, bf16[2,1664,128]{2,1,0:T(8,128)(2,1)} %bitcast.107, bf16[2,1664,128]{2,1,0:T(8,128)(2,1)} %bitcast.111), custom_call_target="tpu_custom_call" | custom-call | flops 872415232 | bytes 2228224 | tf_op jit(solution)/shard_map/pallas_call | solution.py:86
  120.2 6.8 %shard_map.94 = bf16[2,512,128]{2,1,0:T(8,128)(2,1)} custom-call(bf16[2,512,128]{2,1,0:T(8,128)(2,1)} %collective-permute-done.11.q_ref, bf16[2,1664,128]{2,1,0:T(8,128)(2,1)} %bitcast.108, bf16[2,1664,128]{2,1,0:T(8,128)(2,1)} %bitcast.112), custom_call_target="tpu_custom_call" | custom-call | flops 872415232 | bytes 2228224 | tf_op jit(solution)/shard_map/pallas_call | solution.py:86
  127.0 3.9 %collective-permute-start.12 = (bf16[2,512,128]{2,1,0:T(8,128)(2,1)}, bf16[2,512,128]{2,1,0:T(8,128)(2,1)S(1)}, u32[]{:S(2)}, u32[]{:S(2)}) collective-permute-start(bf16[2,512,128]{2,1,0:T(8,128)(2,1)} %shard_map.94), channel_id=1, source_target_pairs={{0,4},{4,8},{8,12},{12,0},{1,5},{5,9},{9,13},{13,1},{2,6},{6,10},{... | collective-permute-start | bytes 786440 | tf_op jit(solution)/shard_map/ppermute | solution.py:209
  131.2 8.1 %collective-permute-done.10 = bf16[2,512,128]{2,1,0:T(8,128)(2,1)S(1)} collective-permute-done((bf16[2,512,128]{2,1,0:T(8,128)(2,1)}, bf16[2,512,128]{2,1,0:T(8,128)(2,1)S(1)}, u32[]{:S(2)}, u32[]{:S(2)}) %collective-permute-start.10) | collective-permute-done | bytes 262176 | tf_op jit(solution)/shard_map/ppermute | solution.py:209
  142.3 2.3 %collective-permute-start.15 = (bf16[128,2048]{1,0:T(8,128)(2,1)S(1)}, bf16[128,2048]{1,0:T(8,128)(2,1)S(1)}, u32[]{:S(2)}, u32[]{:S(2)}) collective-permute-start(bf16[128,2048]{1,0:T(8,128)(2,1)S(1)} %convolution_convert_fusion.9), channel_id=1, source_target_pairs={{0,12},{4,0},{8,4},{12,8},{1,13},{5,1},{9,5},{13,9},{2,14},{6,2},{... | collective-permute-start | bytes 1572872 | tf_op jit(solution)/shard_map/ppermute | solution.py:36
  144.8 4.8 %fusion.4 = bf16[4,128,2048]{2,1,0:T(8,128)(2,1)S(1)} fusion(bf16[4,128,2048]{2,1,0:T(8,128)(2,1)S(1)} %broadcast_in_dim.56, s32[]{:T(128)S(6)} %select_n.168, bf16[128,2048]{1,0:T(8,128)(2,1)S(1)} %convolution_convert_fusion.9, bf16[2048,2048]{1,0:T(8,128)(2,1)} %param.14), kind=kOutput, calls=%fused_computation.14 | convolution fusion | flops 1074003968 | bytes 9437188 | tf_op jit(solution)/shard_map/dot_general | solution.py:224
  149.6 7.8 %collective-permute-done.13 = bf16[128,2048]{1,0:T(8,128)(2,1)S(1)} collective-permute-done((bf16[128,2048]{1,0:T(8,128)(2,1)S(1)}, bf16[128,2048]{1,0:T(8,128)(2,1)S(1)}, u32[]{:S(2)}, u32[]{:S(2)}) %collective-permute-start.13) | collective-permute-done | bytes 524320 | tf_op jit(solution)/shard_map/ppermute | solution.py:36
  158.8 18.5 %collective-permute-done.14 = bf16[128,2048]{1,0:T(8,128)(2,1)S(1)} collective-permute-done((bf16[128,2048]{1,0:T(8,128)(2,1)S(1)}, bf16[128,2048]{1,0:T(8,128)(2,1)S(1)}, u32[]{:S(2)}, u32[]{:S(2)}) %collective-permute-start.14) | collective-permute-done | bytes 524320 | tf_op jit(solution)/shard_map/ppermute | solution.py:36
  180.2 2.8 %collective-permute-done.16 = bf16[256,2048]{1,0:T(8,128)(2,1)} collective-permute-done((bf16[256,2048]{1,0:T(8,128)(2,1)S(1)}, bf16[256,2048]{1,0:T(8,128)(2,1)}, u32[]{:S(2)}, u32[]{:S(2)}) %collective-permute-start.16) | collective-permute-done | bytes 1048608 | tf_op jit(solution)/shard_map/ppermute | solution.py:47
  184.7 11.6 %collective-permute-start.17 = (bf16[128,2048]{1,0:T(8,128)(2,1)S(1)}, bf16[128,2048]{1,0:T(8,128)(2,1)S(1)}, u32[]{:S(2)}, u32[]{:S(2)}) collective-permute-start(bf16[128,2048]{1,0:T(8,128)(2,1)S(1)} %get-tuple-element.13), channel_id=1, source_target_pairs={{0,0},{1,8},{2,4},{3,12},{4,1},{5,9},{6,5},{7,13},{8,2},{9,10},{10... | collective-permute-start | bytes 1572872 | tf_op jit(solution)/shard_map/ppermute | solution.py:255
  196.4 10.6 %collective-permute-done.17 = bf16[128,2048]{1,0:T(8,128)(2,1)S(1)} collective-permute-done((bf16[128,2048]{1,0:T(8,128)(2,1)S(1)}, bf16[128,2048]{1,0:T(8,128)(2,1)S(1)}, u32[]{:S(2)}, u32[]{:S(2)}) %collective-permute-start.17) | collective-permute-done | bytes 524320 | tf_op jit(solution)/shard_map/ppermute | solution.py:255
  207.0 14.8 %collective-permute-done.18 = bf16[128,2048]{1,0:T(8,128)(2,1)S(1)} collective-permute-done((bf16[128,2048]{1,0:T(8,128)(2,1)S(1)}, bf16[128,2048]{1,0:T(8,128)(2,1)S(1)}, u32[]{:S(2)}, u32[]{:S(2)}) %collective-permute-start.18) | collective-permute-done | bytes 524320 | tf_op jit(solution)/shard_map/ppermute | solution.py:255
  221.8 2.1 add_convert_fusion
  (101 shorter events, 35.6 us)
Async XLA Ops:
  0.0 44.8 %copy-start = (f32[128]{0:T(128)S(1)}, f32[128]{0:T(128)}, u32[]{:S(2)}) copy-start(f32[128]{0:T(128)} %param.11) | copy-start | bytes 1540
  3.5 11.2 %collective-permute-start = (bf16[128,1024]{1,0:T(8,128)(2,1)S(1)}, bf16[128,1024]{1,0:T(8,128)(2,1)S(1)}, u32[]{:S(2)}, u32[]{:S(2)}) collective-permute-start(bf16[128,1024]{1,0:T(8,128)(2,1)S(1)} %bitcast.115), channel_id=1, source_target_pairs={{0,4},{4,8},{8,12},{12,0},{1,5},{5,9},{9,13},{13,1},{2,6},{6,10},{... | collective-permute-start | bytes 786440 | tf_op jit(solution)/shard_map/ppermute | solution.py:136
  5.3 19.5 %collective-permute-start.1 = (bf16[128,1024]{1,0:T(8,128)(2,1)S(1)}, bf16[128,1024]{1,0:T(8,128)(2,1)S(1)}, u32[]{:S(2)}, u32[]{:S(2)}) collective-permute-start(bf16[128,1024]{1,0:T(8,128)(2,1)S(1)} %bitcast.114), channel_id=1, source_target_pairs={{0,8},{4,12},{8,0},{12,4},{1,9},{5,13},{9,1},{13,5},{2,10},{6,14},... | collective-permute-start | bytes 786440 | tf_op jit(solution)/shard_map/ppermute | solution.py:136
  7.9 17.1 %copy-start.4 = (s32[4]{0:T(128)S(1)}, s32[4]{0:T(128)}, u32[]{:S(2)}) copy-start(s32[4]{0:T(128)} %param.17) | copy-start | bytes 52
  7.9 17.1 %copy-start.5 = (s32[128]{0:T(128)S(1)}, s32[128]{0:T(128)}, u32[]{:S(2)}) copy-start(s32[128]{0:T(128)} %param.15) | copy-start | bytes 1540
  7.9 17.3 %copy-start.6 = (s32[128]{0:T(128)S(1)}, s32[128]{0:T(128)}, u32[]{:S(2)}) copy-start(s32[128]{0:T(128)} %param.16) | copy-start | bytes 1540
  8.1 16.8 %collective-permute-start.2 = (bf16[128,1024]{1,0:T(8,128)(2,1)S(1)}, bf16[128,1024]{1,0:T(8,128)(2,1)S(1)}, u32[]{:S(2)}, u32[]{:S(2)}) collective-permute-start(bf16[128,1024]{1,0:T(8,128)(2,1)S(1)} %bitcast.113), channel_id=1, source_target_pairs={{0,12},{4,0},{8,4},{12,8},{1,13},{5,1},{9,5},{13,9},{2,14},{6,2},{... | collective-permute-start | bytes 786440 | tf_op jit(solution)/shard_map/ppermute | solution.py:136
  24.9 2.7 %collective-permute-start.3 = (bf16[512,1024]{1,0:T(8,128)(2,1)S(1)}, bf16[512,1024]{1,0:T(8,128)(2,1)S(1)}, u32[]{:S(2)}, u32[]{:S(2)}) collective-permute-start(bf16[512,1024]{1,0:T(8,128)(2,1)S(1)} %bitcast.95), channel_id=1, source_target_pairs={{0,1},{1,0},{2,3},{3,2},{4,5},{5,4},{6,7},{7,6},{8,9},{9,8},{10,11... | collective-permute-start | bytes 3145736 | tf_op jit(solution)/shard_map/ppermute | solution.py:148
  32.6 20.0 %collective-permute-start.4 = (bf16[128,2048]{1,0:T(8,128)(2,1)S(1)}, bf16[128,2048]{1,0:T(8,128)(2,1)S(1)}, u32[]{:S(2)}, u32[]{:S(2)}) collective-permute-start(bf16[128,2048]{1,0:T(8,128)(2,1)S(1)} %convolution_convert_fusion.7), channel_id=1, source_target_pairs={{0,4},{4,8},{8,12},{12,0},{1,5},{5,9},{9,13},{13,1},{2,6},{6,10},{... | collective-permute-start | bytes 1572872 | tf_op jit(solution)/shard_map/ppermute | solution.py:24
  40.0 34.6 %collective-permute-start.5 = (bf16[128,2048]{1,0:T(8,128)(2,1)S(1)}, bf16[128,2048]{1,0:T(8,128)(2,1)S(1)}, u32[]{:S(2)}, u32[]{:S(2)}) collective-permute-start(bf16[128,2048]{1,0:T(8,128)(2,1)S(1)} %convolution_convert_fusion.6), channel_id=1, source_target_pairs={{0,8},{4,12},{8,0},{12,4},{1,9},{5,13},{9,1},{13,5},{2,10},{6,14},... | collective-permute-start | bytes 1572872 | tf_op jit(solution)/shard_map/ppermute | solution.py:24
  43.0 31.6 %collective-permute-start.6 = (bf16[128,2048]{1,0:T(8,128)(2,1)S(1)}, bf16[128,2048]{1,0:T(8,128)(2,1)S(1)}, u32[]{:S(2)}, u32[]{:S(2)}) collective-permute-start(bf16[128,2048]{1,0:T(8,128)(2,1)S(1)} %convolution_convert_fusion.5), channel_id=1, source_target_pairs={{0,12},{4,0},{8,4},{12,8},{1,13},{5,1},{9,5},{13,9},{2,14},{6,2},{... | collective-permute-start | bytes 1572872 | tf_op jit(solution)/shard_map/ppermute | solution.py:24
  78.1 15.2 %copy-start.1 = (bf16[1,1601,512]{2,1,0:T(8,128)(2,1)S(1)}, bf16[1,1601,512]{2,1,0:T(8,128)(2,1)}, u32[]{:S(2)}) copy-start(bf16[1,1601,512]{2,1,0:T(8,128)(2,1)} %param.13) | copy-start | bytes 4918276
  79.2 25.0 %collective-permute-start.7 = (bf16[2,512,128]{2,1,0:T(8,128)(2,1)S(1)}, bf16[2,512,128]{2,1,0:T(8,128)(2,1)}, u32[]{:S(2)}, u32[]{:S(2)}) collective-permute-start(bf16[2,512,128]{2,1,0:T(8,128)(2,1)S(1)} %bitcast.123), channel_id=1, source_target_pairs={{0,4},{4,8},{8,12},{12,0},{1,5},{5,9},{9,13},{13,1},{2,6},{6,10},{... | collective-permute-start | bytes 786440 | tf_op jit(solution)/shard_map/ppermute | solution.py:195
  90.9 22.1 %collective-permute-start.9 = (bf16[2,512,128]{2,1,0:T(8,128)(2,1)S(1)}, bf16[2,512,128]{2,1,0:T(8,128)(2,1)}, u32[]{:S(2)}, u32[]{:S(2)}) collective-permute-start(bf16[2,512,128]{2,1,0:T(8,128)(2,1)S(1)} %bitcast.121), channel_id=1, source_target_pairs={{0,8},{4,12},{8,0},{12,4},{1,9},{5,13},{9,1},{13,5},{2,10},{6,14},... | collective-permute-start | bytes 786440 | tf_op jit(solution)/shard_map/ppermute | solution.py:195
  92.2 28.0 %collective-permute-start.11 = (bf16[2,512,128]{2,1,0:T(8,128)(2,1)S(1)}, bf16[2,512,128]{2,1,0:T(8,128)(2,1)}, u32[]{:S(2)}, u32[]{:S(2)}) collective-permute-start(bf16[2,512,128]{2,1,0:T(8,128)(2,1)S(1)} %bitcast.120), channel_id=1, source_target_pairs={{0,12},{4,0},{8,4},{12,8},{1,13},{5,1},{9,5},{13,9},{2,14},{6,2},{... | collective-permute-start | bytes 786440 | tf_op jit(solution)/shard_map/ppermute | solution.py:195
  111.0 20.0 %collective-permute-start.8 = (bf16[2,512,128]{2,1,0:T(8,128)(2,1)}, bf16[2,512,128]{2,1,0:T(8,128)(2,1)S(1)}, u32[]{:S(2)}, u32[]{:S(2)}) collective-permute-start(bf16[2,512,128]{2,1,0:T(8,128)(2,1)} %shard_map.92), channel_id=1, source_target_pairs={{0,12},{4,0},{8,4},{12,8},{1,13},{5,1},{9,5},{13,9},{2,14},{6,2},{... | collective-permute-start | bytes 786440 | tf_op jit(solution)/shard_map/ppermute | solution.py:209
  119.8 19.5 %collective-permute-start.10 = (bf16[2,512,128]{2,1,0:T(8,128)(2,1)}, bf16[2,512,128]{2,1,0:T(8,128)(2,1)S(1)}, u32[]{:S(2)}, u32[]{:S(2)}) collective-permute-start(bf16[2,512,128]{2,1,0:T(8,128)(2,1)} %shard_map.93), channel_id=1, source_target_pairs={{0,8},{4,12},{8,0},{12,4},{1,9},{5,13},{9,1},{13,5},{2,10},{6,14},... | collective-permute-start | bytes 786440 | tf_op jit(solution)/shard_map/ppermute | solution.py:209
  127.0 12.5 %collective-permute-start.12 = (bf16[2,512,128]{2,1,0:T(8,128)(2,1)}, bf16[2,512,128]{2,1,0:T(8,128)(2,1)S(1)}, u32[]{:S(2)}, u32[]{:S(2)}) collective-permute-start(bf16[2,512,128]{2,1,0:T(8,128)(2,1)} %shard_map.94), channel_id=1, source_target_pairs={{0,4},{4,8},{8,12},{12,0},{1,5},{5,9},{9,13},{13,1},{2,6},{6,10},{... | collective-permute-start | bytes 786440 | tf_op jit(solution)/shard_map/ppermute | solution.py:209
  140.7 16.8 %collective-permute-start.13 = (bf16[128,2048]{1,0:T(8,128)(2,1)S(1)}, bf16[128,2048]{1,0:T(8,128)(2,1)S(1)}, u32[]{:S(2)}, u32[]{:S(2)}) collective-permute-start(bf16[128,2048]{1,0:T(8,128)(2,1)S(1)} %convolution_convert_fusion.9), channel_id=1, source_target_pairs={{0,4},{4,8},{8,12},{12,0},{1,5},{5,9},{9,13},{13,1},{2,6},{6,10},{... | collective-permute-start | bytes 1572872 | tf_op jit(solution)/shard_map/ppermute | solution.py:36
  140.7 36.6 %collective-permute-start.14 = (bf16[128,2048]{1,0:T(8,128)(2,1)S(1)}, bf16[128,2048]{1,0:T(8,128)(2,1)S(1)}, u32[]{:S(2)}, u32[]{:S(2)}) collective-permute-start(bf16[128,2048]{1,0:T(8,128)(2,1)S(1)} %convolution_convert_fusion.9), channel_id=1, source_target_pairs={{0,8},{4,12},{8,0},{12,4},{1,9},{5,13},{9,1},{13,5},{2,10},{6,14},... | collective-permute-start | bytes 1572872 | tf_op jit(solution)/shard_map/ppermute | solution.py:36
  142.3 36.4 %collective-permute-start.15 = (bf16[128,2048]{1,0:T(8,128)(2,1)S(1)}, bf16[128,2048]{1,0:T(8,128)(2,1)S(1)}, u32[]{:S(2)}, u32[]{:S(2)}) collective-permute-start(bf16[128,2048]{1,0:T(8,128)(2,1)S(1)} %convolution_convert_fusion.9), channel_id=1, source_target_pairs={{0,12},{4,0},{8,4},{12,8},{1,13},{5,1},{9,5},{13,9},{2,14},{6,2},{... | collective-permute-start | bytes 1572872 | tf_op jit(solution)/shard_map/ppermute | solution.py:36
  180.1 2.9 %collective-permute-start.16 = (bf16[256,2048]{1,0:T(8,128)(2,1)S(1)}, bf16[256,2048]{1,0:T(8,128)(2,1)}, u32[]{:S(2)}, u32[]{:S(2)}) collective-permute-start(bf16[256,2048]{1,0:T(8,128)(2,1)S(1)} %dynamic-slice_bitcast_fusion), channel_id=1, source_target_pairs={{0,1},{1,0},{2,3},{3,2},{4,5},{5,4},{6,7},{7,6},{8,9},{9,8},{10,11... | collective-permute-start | bytes 3145736 | tf_op jit(solution)/shard_map/ppermute | solution.py:47
  184.7 22.3 %collective-permute-start.17 = (bf16[128,2048]{1,0:T(8,128)(2,1)S(1)}, bf16[128,2048]{1,0:T(8,128)(2,1)S(1)}, u32[]{:S(2)}, u32[]{:S(2)}) collective-permute-start(bf16[128,2048]{1,0:T(8,128)(2,1)S(1)} %get-tuple-element.13), channel_id=1, source_target_pairs={{0,0},{1,8},{2,4},{3,12},{4,1},{5,9},{6,5},{7,13},{8,2},{9,10},{10... | collective-permute-start | bytes 1572872 | tf_op jit(solution)/shard_map/ppermute | solution.py:255
  196.3 25.5 %collective-permute-start.18 = (bf16[128,2048]{1,0:T(8,128)(2,1)S(1)}, bf16[128,2048]{1,0:T(8,128)(2,1)S(1)}, u32[]{:S(2)}, u32[]{:S(2)}) collective-permute-start(bf16[128,2048]{1,0:T(8,128)(2,1)S(1)} %get-tuple-element.14), channel_id=1, source_target_pairs={{0,4},{1,12},{2,0},{3,8},{4,5},{5,13},{6,1},{7,9},{8,6},{9,14},{10... | collective-permute-start | bytes 1572872 | tf_op jit(solution)/shard_map/ppermute | solution.py:255
  (6 other events, 73.8 us)

commit v19 on v18

--- a/solution.py
+++ b/solution.py
@@ -121,36 +121,34 @@
     sub_count = lax.axis_size("sub")
     sub_index = lax.axis_index("sub")
     block_width = hidden_in.shape[1] // req_count
-    part_width = block_width // sub_count
-    by_block = hidden_in.reshape(local_rows, req_count, sub_count, part_width)
+    half_rows = local_rows // sub_count
     req_index = lax.axis_index("req")
-    my_part = lax.dynamic_index_in_dim(by_block, sub_index, axis=2, keepdims=False)
-    spread_part = jnp.zeros((req_count, local_rows, part_width), my_part.dtype)
-    spread_part = lax.dynamic_update_index_in_dim(
-        spread_part, lax.dynamic_index_in_dim(my_part, req_index, 1, keepdims=False), req_index, 0
-    )
+    my_rows = lax.dynamic_slice_in_dim(hidden_in, sub_index * half_rows, half_rows, 0)
+
+    def my_block(dest):
+        return lax.dynamic_slice_in_dim(my_rows, dest * block_width, block_width, 1)
+
+    spread_part = jnp.zeros((req_count, half_rows, block_width), hidden_in.dtype)
+    spread_part = lax.dynamic_update_index_in_dim(spread_part, my_block(req_index), req_index, 0)
     for shift in range(1, req_count):
-        outgoing_part = lax.dynamic_index_in_dim(
-            my_part, (req_index + shift) % req_count, 1, keepdims=False
-        )
         arrived_part = lax.ppermute(
-            outgoing_part, "req", [(i, (i + shift) % req_count) for i in range(req_count)]
+            my_block((req_index + shift) % req_count),
+            "req",
+            [(i, (i + shift) % req_count) for i in range(req_count)],
         )
         spread_part = lax.dynamic_update_index_in_dim(
             spread_part, arrived_part, (req_index - shift) % req_count, 0
         )
-    spread_part = spread_part.reshape(req_count * local_rows, part_width)
-    spread_cols = jnp.zeros((req_count * local_rows, block_width), spread_part.dtype)
-    spread_cols = lax.dynamic_update_slice_in_dim(
-        spread_cols, spread_part, sub_index * part_width, 1
-    )
+    spread_cols = jnp.zeros((req_count, sub_count, half_rows, block_width), hidden_in.dtype)
+    spread_cols = lax.dynamic_update_index_in_dim(spread_cols, spread_part, sub_index, 1)
     for shift in range(1, sub_count):
         other_part = lax.ppermute(
             spread_part, "sub", [(i, (i + shift) % sub_count) for i in range(sub_count)]
         )
-        spread_cols = lax.dynamic_update_slice_in_dim(
-            spread_cols, other_part, ((sub_index - shift) % sub_count) * part_width, 1
-        )
+        spread_cols = lax.dynamic_update_index_in_dim(
+            spread_cols, other_part, (sub_index - shift) % sub_count, 1
+        )
+    spread_cols = spread_cols.reshape(req_count * local_rows, block_width)
     def query_chunk(owner):
         rows = lax.dynamic_slice_in_dim(spread_cols, owner * local_rows, local_rows, 0)
         product = jnp.dot(rows, q_weight, preferred_element_type=jnp.float32)

time: 225 us -> 223 us (level)
    unnamed x25 -> x24, local copies, waits for them, and re-layouts: 3.7 us -> 0.47 us
  transfers between devices with their start and end apart: 19 -> 19, of which waited for: 11 -> 11; matrix products, arithmetic and copies ran while one was open for 7% -> 8% of each run, Pallas kernels for 12% -> 12%
where the time goes in v19:
time: 223 us; the launch traced here: 222 us
  waiting for transfers between devices  109 us (49%)
  starting transfers between devices  51 us (23%)
  Pallas kernels  27.1 us (12%)
  matrix products  18.6 us (8%)
  local copies, waits for them, and re-layouts  11.2 us (5%)
  other arithmetic  4.93 us (2%)
    ppermute x3, waiting for transfers between devices, direct_reduce_scatter(): lax.ppermute(outgoing, axis, [(i, (i + shift) % count) for i in range(cou...  29.7 us
    pallas_call x4, Pallas kernels, attend(): pl.pallas_call(kernel, grid=(kv_count,), in_specs=[pl.BlockSpec((1, stack...  27.1 us
    ppermute x3, waiting for transfers between devices, direct_gather_apply(): lax.ppermute(block, axis, [(i, (i + shift) % count) for i in range(count)])  26.4 us
    ppermute x2, waiting for transfers between devices, local(): got = lax.ppermute(chunk, ('req', 'head', 'sub'), pairs).astype(jnp.float32)  25.4 us
    ppermute x3, waiting for transfers between devices, local(): lax.ppermute(my_block((req_index + shift) % req_count), 'req', [(i, (i +...  14.5 us
    ppermute x3, starting transfers between devices, local(): lax.ppermute(outgoing[shift], 'req', [(i, (i + shift) % req_count) for i...  14.1 us
    ppermute x2, starting transfers between devices, local(): got = lax.ppermute(chunk, ('req', 'head', 'sub'), pairs).astype(jnp.float32)  11.7 us
    ppermute x3, starting transfers between devices, direct_reduce_scatter(): lax.ppermute(outgoing, axis, [(i, (i + shift) % count) for i in range(cou...  9.44 us
  transfers between devices with their start and end apart: 19, of which 11 were waited for; matrix products, arithmetic and copies ran while one was open for 8% of the time, Pallas kernels for 12%

profile of v19, /device:TPU:6, one launch (start us, length us, event | category | flops | bytes accessed | tf_op | source)
XLA Modules:
  0.0 222.0 jit_solution(8221263115306170144)
XLA Ops:
  3.3 2.6 %collective-permute-start.1 = (bf16[64,2048]{1,0:T(8,128)(2,1)S(1)}, bf16[64,2048]{1,0:T(8,128)(2,1)S(1)}, u32[]{:S(2)}, u32[]{:S(2)}) collective-permute-start(bf16[64,2048]{1,0:T(8,128)(2,1)S(1)} %get-tuple-element.11), channel_id=1, source_target_pairs={{0,8},{4,12},{8,0},{12,4},{1,9},{5,13},{9,1},{13,5},{2,10},{6,14},... | collective-permute-start | bytes 786440 | tf_op jit(solution)/shard_map/ppermute | solution.py:134
  8.5 4.4 %collective-permute-done = bf16[64,2048]{1,0:T(8,128)(2,1)S(1)} collective-permute-done((bf16[64,2048]{1,0:T(8,128)(2,1)S(1)}, bf16[64,2048]{1,0:T(8,128)(2,1)S(1)}, u32[]{:S(2)}, u32[]{:S(2)}) %collective-permute-start) | collective-permute-done | bytes 262176 | tf_op jit(solution)/shard_map/ppermute | solution.py:134
  12.8 10.1 %collective-permute-done.1 = bf16[64,2048]{1,0:T(8,128)(2,1)S(1)} collective-permute-done((bf16[64,2048]{1,0:T(8,128)(2,1)S(1)}, bf16[64,2048]{1,0:T(8,128)(2,1)S(1)}, u32[]{:S(2)}, u32[]{:S(2)}) %collective-permute-start.1) | collective-permute-done | bytes 262176 | tf_op jit(solution)/shard_map/ppermute | solution.py:134
  25.9 4.8 %convolution_convert_fusion.7 = bf16[128,2048]{1,0:T(8,128)(2,1)S(1)} fusion(bf16[2048,2048]{1,0:T(8,128)(2,1)} %param.10, bf16[512,2048]{1,0:T(8,128)(2,1)S(1)} %bitcast.95, s32[]{:T(128)S(6)} %select_n.193), kind=kOutput, calls=%fused_computation.7 | convolution fusion | flops 1074003968 | bytes 9437188 | tf_op jit(solution)/shard_map/dot_general | solution.py:154
  30.7 6.1 %collective-permute-start.4 = (bf16[128,2048]{1,0:T(8,128)(2,1)S(1)}, bf16[128,2048]{1,0:T(8,128)(2,1)S(1)}, u32[]{:S(2)}, u32[]{:S(2)}) collective-permute-start(bf16[128,2048]{1,0:T(8,128)(2,1)S(1)} %convolution_convert_fusion.7), channel_id=1, source_target_pairs={{0,4},{4,8},{8,12},{12,0},{1,5},{5,9},{9,13},{13,1},{2,6},{6,10},{... | collective-permute-start | bytes 1572872 | tf_op jit(solution)/shard_map/ppermute | solution.py:24
  43.0 7.7 %collective-permute-done.4 = bf16[128,2048]{1,0:T(8,128)(2,1)S(1)} collective-permute-done((bf16[128,2048]{1,0:T(8,128)(2,1)S(1)}, bf16[128,2048]{1,0:T(8,128)(2,1)S(1)}, u32[]{:S(2)}, u32[]{:S(2)}) %collective-permute-start.4) | collective-permute-done | bytes 524320 | tf_op jit(solution)/shard_map/ppermute | solution.py:24
  50.7 22.0 %collective-permute-done.5 = bf16[128,2048]{1,0:T(8,128)(2,1)S(1)} collective-permute-done((bf16[128,2048]{1,0:T(8,128)(2,1)S(1)}, bf16[128,2048]{1,0:T(8,128)(2,1)S(1)}, u32[]{:S(2)}, u32[]{:S(2)}) %collective-permute-start.5) | collective-permute-done | bytes 524320 | tf_op jit(solution)/shard_map/ppermute | solution.py:24
  77.4 11.7 %collective-permute-start.7 = (bf16[2,512,128]{2,1,0:T(8,128)(2,1)S(1)}, bf16[2,512,128]{2,1,0:T(8,128)(2,1)}, u32[]{:S(2)}, u32[]{:S(2)}) collective-permute-start(bf16[2,512,128]{2,1,0:T(8,128)(2,1)S(1)} %bitcast.123), channel_id=1, source_target_pairs={{0,4},{4,8},{8,12},{12,0},{1,5},{5,9},{9,13},{13,1},{2,6},{6,10},{... | collective-permute-start | bytes 786440 | tf_op jit(solution)/shard_map/ppermute | solution.py:193
  95.6 6.8 %shard_map.91 = bf16[2,512,128]{2,1,0:T(8,128)(2,1)} custom-call(bf16[2,512,128]{2,1,0:T(8,128)(2,1)} %bitcast.122, bf16[2,1664,128]{2,1,0:T(8,128)(2,1)} %bitcast.108, bf16[2,1664,128]{2,1,0:T(8,128)(2,1)} %bitcast.112), custom_call_target="tpu_custom_call" | custom-call | flops 872415232 | bytes 2228224 | tf_op jit(solution)/shard_map/pallas_call | solution.py:86
  102.4 6.8 %shard_map.92 = bf16[2,512,128]{2,1,0:T(8,128)(2,1)} custom-call(bf16[2,512,128]{2,1,0:T(8,128)(2,1)} %collective-permute-done.7.q_ref, bf16[2,1664,128]{2,1,0:T(8,128)(2,1)} %bitcast.109, bf16[2,1664,128]{2,1,0:T(8,128)(2,1)} %bitcast.113), custom_call_target="tpu_custom_call" | custom-call | flops 872415232 | bytes 2228224 | tf_op jit(solution)/shard_map/pallas_call | solution.py:86
  109.2 2.0 collective-permute-start.8
  111.2 6.8 %shard_map.93 = bf16[2,512,128]{2,1,0:T(8,128)(2,1)} custom-call(bf16[2,512,128]{2,1,0:T(8,128)(2,1)} %collective-permute-done.9.q_ref, bf16[2,1664,128]{2,1,0:T(8,128)(2,1)} %bitcast.110, bf16[2,1664,128]{2,1,0:T(8,128)(2,1)} %bitcast.114), custom_call_target="tpu_custom_call" | custom-call | flops 872415232 | bytes 2228224 | tf_op jit(solution)/shard_map/pallas_call | solution.py:86
  118.3 6.8 %shard_map.94 = bf16[2,512,128]{2,1,0:T(8,128)(2,1)} custom-call(bf16[2,512,128]{2,1,0:T(8,128)(2,1)} %collective-permute-done.11.q_ref, bf16[2,1664,128]{2,1,0:T(8,128)(2,1)} %bitcast.111, bf16[2,1664,128]{2,1,0:T(8,128)(2,1)} %bitcast.115), custom_call_target="tpu_custom_call" | custom-call | flops 872415232 | bytes 2228224 | tf_op jit(solution)/shard_map/pallas_call | solution.py:86
  125.1 3.9 %collective-permute-start.12 = (bf16[2,512,128]{2,1,0:T(8,128)(2,1)}, bf16[2,512,128]{2,1,0:T(8,128)(2,1)S(1)}, u32[]{:S(2)}, u32[]{:S(2)}) collective-permute-start(bf16[2,512,128]{2,1,0:T(8,128)(2,1)} %shard_map.94), channel_id=1, source_target_pairs={{0,4},{4,8},{8,12},{12,0},{1,5},{5,9},{9,13},{13,1},{2,6},{6,10},{... | collective-permute-start | bytes 786440 | tf_op jit(solution)/shard_map/ppermute | solution.py:207
  129.4 8.1 %collective-permute-done.10 = bf16[2,512,128]{2,1,0:T(8,128)(2,1)S(1)} collective-permute-done((bf16[2,512,128]{2,1,0:T(8,128)(2,1)}, bf16[2,512,128]{2,1,0:T(8,128)(2,1)S(1)}, u32[]{:S(2)}, u32[]{:S(2)}) %collective-permute-start.10) | collective-permute-done | bytes 262176 | tf_op jit(solution)/shard_map/ppermute | solution.py:207
  140.4 2.3 %collective-permute-start.15 = (bf16[128,2048]{1,0:T(8,128)(2,1)S(1)}, bf16[128,2048]{1,0:T(8,128)(2,1)S(1)}, u32[]{:S(2)}, u32[]{:S(2)}) collective-permute-start(bf16[128,2048]{1,0:T(8,128)(2,1)S(1)} %convolution_convert_fusion.9), channel_id=1, source_target_pairs={{0,12},{4,0},{8,4},{12,8},{1,13},{5,1},{9,5},{13,9},{2,14},{6,2},{... | collective-permute-start | bytes 1572872 | tf_op jit(solution)/shard_map/ppermute | solution.py:36
  142.9 4.8 %fusion.4 = bf16[4,128,2048]{2,1,0:T(8,128)(2,1)S(1)} fusion(bf16[4,128,2048]{2,1,0:T(8,128)(2,1)S(1)} %broadcast_in_dim.63, s32[]{:T(128)S(6)} %select_n.173, bf16[128,2048]{1,0:T(8,128)(2,1)S(1)} %convolution_convert_fusion.9, bf16[2048,2048]{1,0:T(8,128)(2,1)} %param.14), kind=kOutput, calls=%fused_computation.14 | convolution fusion | flops 1074003968 | bytes 9437188 | tf_op jit(solution)/shard_map/dot_general | solution.py:222
  147.8 7.8 %collective-permute-done.13 = bf16[128,2048]{1,0:T(8,128)(2,1)S(1)} collective-permute-done((bf16[128,2048]{1,0:T(8,128)(2,1)S(1)}, bf16[128,2048]{1,0:T(8,128)(2,1)S(1)}, u32[]{:S(2)}, u32[]{:S(2)}) %collective-permute-start.13) | collective-permute-done | bytes 524320 | tf_op jit(solution)/shard_map/ppermute | solution.py:36
  156.9 18.6 %collective-permute-done.14 = bf16[128,2048]{1,0:T(8,128)(2,1)S(1)} collective-permute-done((bf16[128,2048]{1,0:T(8,128)(2,1)S(1)}, bf16[128,2048]{1,0:T(8,128)(2,1)S(1)}, u32[]{:S(2)}, u32[]{:S(2)}) %collective-permute-start.14) | collective-permute-done | bytes 524320 | tf_op jit(solution)/shard_map/ppermute | solution.py:36
  178.3 2.8 %collective-permute-done.16 = bf16[256,2048]{1,0:T(8,128)(2,1)} collective-permute-done((bf16[256,2048]{1,0:T(8,128)(2,1)S(1)}, bf16[256,2048]{1,0:T(8,128)(2,1)}, u32[]{:S(2)}, u32[]{:S(2)}) %collective-permute-start.16) | collective-permute-done | bytes 1048608 | tf_op jit(solution)/shard_map/ppermute | solution.py:47
  182.8 11.6 %collective-permute-start.17 = (bf16[128,2048]{1,0:T(8,128)(2,1)S(1)}, bf16[128,2048]{1,0:T(8,128)(2,1)S(1)}, u32[]{:S(2)}, u32[]{:S(2)}) collective-permute-start(bf16[128,2048]{1,0:T(8,128)(2,1)S(1)} %get-tuple-element.12), channel_id=1, source_target_pairs={{0,0},{1,8},{2,4},{3,12},{4,1},{5,9},{6,5},{7,13},{8,2},{9,10},{10... | collective-permute-start | bytes 1572872 | tf_op jit(solution)/shard_map/ppermute | solution.py:253
  194.5 10.6 %collective-permute-done.17 = bf16[128,2048]{1,0:T(8,128)(2,1)S(1)} collective-permute-done((bf16[128,2048]{1,0:T(8,128)(2,1)S(1)}, bf16[128,2048]{1,0:T(8,128)(2,1)S(1)}, u32[]{:S(2)}, u32[]{:S(2)}) %collective-permute-start.17) | collective-permute-done | bytes 524320 | tf_op jit(solution)/shard_map/ppermute | solution.py:253
  205.1 14.8 %collective-permute-done.18 = bf16[128,2048]{1,0:T(8,128)(2,1)S(1)} collective-permute-done((bf16[128,2048]{1,0:T(8,128)(2,1)S(1)}, bf16[128,2048]{1,0:T(8,128)(2,1)S(1)}, u32[]{:S(2)}, u32[]{:S(2)}) %collective-permute-start.18) | collective-permute-done | bytes 524320 | tf_op jit(solution)/shard_map/ppermute | solution.py:253
  219.9 2.1 add_convert_fusion
  (96 shorter events, 35.6 us)
Async XLA Ops:
  0.0 42.9 %copy-start = (f32[128]{0:T(128)S(1)}, f32[128]{0:T(128)}, u32[]{:S(2)}) copy-start(f32[128]{0:T(128)} %param.11) | copy-start | bytes 1540
  0.0 23.1 %copy-start.4 = (s32[4]{0:T(128)S(1)}, s32[4]{0:T(128)}, u32[]{:S(2)}) copy-start(s32[4]{0:T(128)} %param.17) | copy-start | bytes 52
  0.0 23.1 %copy-start.5 = (s32[128]{0:T(128)S(1)}, s32[128]{0:T(128)}, u32[]{:S(2)}) copy-start(s32[128]{0:T(128)} %param.15) | copy-start | bytes 1540
  0.0 23.3 %copy-start.6 = (s32[128]{0:T(128)S(1)}, s32[128]{0:T(128)}, u32[]{:S(2)}) copy-start(s32[128]{0:T(128)} %param.16) | copy-start | bytes 1540
  1.6 11.2 %collective-permute-start = (bf16[64,2048]{1,0:T(8,128)(2,1)S(1)}, bf16[64,2048]{1,0:T(8,128)(2,1)S(1)}, u32[]{:S(2)}, u32[]{:S(2)}) collective-permute-start(bf16[64,2048]{1,0:T(8,128)(2,1)S(1)} %get-tuple-element.10), channel_id=1, source_target_pairs={{0,4},{4,8},{8,12},{12,0},{1,5},{5,9},{9,13},{13,1},{2,6},{6,10},{... | collective-permute-start | bytes 786440 | tf_op jit(solution)/shard_map/ppermute | solution.py:134
  3.3 19.7 %collective-permute-start.1 = (bf16[64,2048]{1,0:T(8,128)(2,1)S(1)}, bf16[64,2048]{1,0:T(8,128)(2,1)S(1)}, u32[]{:S(2)}, u32[]{:S(2)}) collective-permute-start(bf16[64,2048]{1,0:T(8,128)(2,1)S(1)} %get-tuple-element.11), channel_id=1, source_target_pairs={{0,8},{4,12},{8,0},{12,4},{1,9},{5,13},{9,1},{13,5},{2,10},{6,14},... | collective-permute-start | bytes 786440 | tf_op jit(solution)/shard_map/ppermute | solution.py:134
  5.9 17.1 %collective-permute-start.2 = (bf16[64,2048]{1,0:T(8,128)(2,1)S(1)}, bf16[64,2048]{1,0:T(8,128)(2,1)S(1)}, u32[]{:S(2)}, u32[]{:S(2)}) collective-permute-start(bf16[64,2048]{1,0:T(8,128)(2,1)S(1)} %get-tuple-element.9), channel_id=1, source_target_pairs={{0,12},{4,0},{8,4},{12,8},{1,13},{5,1},{9,5},{13,9},{2,14},{6,2},{... | collective-permute-start | bytes 786440 | tf_op jit(solution)/shard_map/ppermute | solution.py:134
  23.0 2.7 %collective-permute-start.3 = (bf16[4,64,2048]{2,1,0:T(8,128)(2,1)S(1)}, bf16[4,64,2048]{2,1,0:T(8,128)(2,1)S(1)}, u32[]{:S(2)}, u32[]{:S(2)}) collective-permute-start(bf16[4,64,2048]{2,1,0:T(8,128)(2,1)S(1)} %bitcast_dynamic-update-slice_fusion.2), channel_id=1, source_target_pairs={{0,1},{1,0},{2,3},{3,2},{4,5},{5,4},{6,7},{7,6},{8,9},{9,8},{10,11... | collective-permute-start | bytes 3145736 | tf_op jit(solution)/shard_map/ppermute | solution.py:145
  30.7 20.0 %collective-permute-start.4 = (bf16[128,2048]{1,0:T(8,128)(2,1)S(1)}, bf16[128,2048]{1,0:T(8,128)(2,1)S(1)}, u32[]{:S(2)}, u32[]{:S(2)}) collective-permute-start(bf16[128,2048]{1,0:T(8,128)(2,1)S(1)} %convolution_convert_fusion.7), channel_id=1, source_target_pairs={{0,4},{4,8},{8,12},{12,0},{1,5},{5,9},{9,13},{13,1},{2,6},{6,10},{... | collective-permute-start | bytes 1572872 | tf_op jit(solution)/shard_map/ppermute | solution.py:24
  38.1 34.6 %collective-permute-start.5 = (bf16[128,2048]{1,0:T(8,128)(2,1)S(1)}, bf16[128,2048]{1,0:T(8,128)(2,1)S(1)}, u32[]{:S(2)}, u32[]{:S(2)}) collective-permute-start(bf16[128,2048]{1,0:T(8,128)(2,1)S(1)} %convolution_convert_fusion.6), channel_id=1, source_target_pairs={{0,8},{4,12},{8,0},{12,4},{1,9},{5,13},{9,1},{13,5},{2,10},{6,14},... | collective-permute-start | bytes 1572872 | tf_op jit(solution)/shard_map/ppermute | solution.py:24
  41.1 31.6 %collective-permute-start.6 = (bf16[128,2048]{1,0:T(8,128)(2,1)S(1)}, bf16[128,2048]{1,0:T(8,128)(2,1)S(1)}, u32[]{:S(2)}, u32[]{:S(2)}) collective-permute-start(bf16[128,2048]{1,0:T(8,128)(2,1)S(1)} %convolution_convert_fusion.5), channel_id=1, source_target_pairs={{0,12},{4,0},{8,4},{12,8},{1,13},{5,1},{9,5},{13,9},{2,14},{6,2},{... | collective-permute-start | bytes 1572872 | tf_op jit(solution)/shard_map/ppermute | solution.py:24
  76.3 15.1 %copy-start.1 = (bf16[1,1601,512]{2,1,0:T(8,128)(2,1)S(1)}, bf16[1,1601,512]{2,1,0:T(8,128)(2,1)}, u32[]{:S(2)}) copy-start(bf16[1,1601,512]{2,1,0:T(8,128)(2,1)} %param.13) | copy-start | bytes 4918276
  77.4 25.0 %collective-permute-start.7 = (bf16[2,512,128]{2,1,0:T(8,128)(2,1)S(1)}, bf16[2,512,128]{2,1,0:T(8,128)(2,1)}, u32[]{:S(2)}, u32[]{:S(2)}) collective-permute-start(bf16[2,512,128]{2,1,0:T(8,128)(2,1)S(1)} %bitcast.123), channel_id=1, source_target_pairs={{0,4},{4,8},{8,12},{12,0},{1,5},{5,9},{9,13},{13,1},{2,6},{6,10},{... | collective-permute-start | bytes 786440 | tf_op jit(solution)/shard_map/ppermute | solution.py:193
  89.1 22.1 %collective-permute-start.9 = (bf16[2,512,128]{2,1,0:T(8,128)(2,1)S(1)}, bf16[2,512,128]{2,1,0:T(8,128)(2,1)}, u32[]{:S(2)}, u32[]{:S(2)}) collective-permute-start(bf16[2,512,128]{2,1,0:T(8,128)(2,1)S(1)} %bitcast.121), channel_id=1, source_target_pairs={{0,8},{4,12},{8,0},{12,4},{1,9},{5,13},{9,1},{13,5},{2,10},{6,14},... | collective-permute-start | bytes 786440 | tf_op jit(solution)/shard_map/ppermute | solution.py:193
  90.3 28.0 %collective-permute-start.11 = (bf16[2,512,128]{2,1,0:T(8,128)(2,1)S(1)}, bf16[2,512,128]{2,1,0:T(8,128)(2,1)}, u32[]{:S(2)}, u32[]{:S(2)}) collective-permute-start(bf16[2,512,128]{2,1,0:T(8,128)(2,1)S(1)} %bitcast.120), channel_id=1, source_target_pairs={{0,12},{4,0},{8,4},{12,8},{1,13},{5,1},{9,5},{13,9},{2,14},{6,2},{... | collective-permute-start | bytes 786440 | tf_op jit(solution)/shard_map/ppermute | solution.py:193
  109.2 20.0 %collective-permute-start.8 = (bf16[2,512,128]{2,1,0:T(8,128)(2,1)}, bf16[2,512,128]{2,1,0:T(8,128)(2,1)S(1)}, u32[]{:S(2)}, u32[]{:S(2)}) collective-permute-start(bf16[2,512,128]{2,1,0:T(8,128)(2,1)} %shard_map.92), channel_id=1, source_target_pairs={{0,12},{4,0},{8,4},{12,8},{1,13},{5,1},{9,5},{13,9},{2,14},{6,2},{... | collective-permute-start | bytes 786440 | tf_op jit(solution)/shard_map/ppermute | solution.py:207
  118.0 19.5 %collective-permute-start.10 = (bf16[2,512,128]{2,1,0:T(8,128)(2,1)}, bf16[2,512,128]{2,1,0:T(8,128)(2,1)S(1)}, u32[]{:S(2)}, u32[]{:S(2)}) collective-permute-start(bf16[2,512,128]{2,1,0:T(8,128)(2,1)} %shard_map.93), channel_id=1, source_target_pairs={{0,8},{4,12},{8,0},{12,4},{1,9},{5,13},{9,1},{13,5},{2,10},{6,14},... | collective-permute-start | bytes 786440 | tf_op jit(solution)/shard_map/ppermute | solution.py:207
  125.1 12.5 %collective-permute-start.12 = (bf16[2,512,128]{2,1,0:T(8,128)(2,1)}, bf16[2,512,128]{2,1,0:T(8,128)(2,1)S(1)}, u32[]{:S(2)}, u32[]{:S(2)}) collective-permute-start(bf16[2,512,128]{2,1,0:T(8,128)(2,1)} %shard_map.94), channel_id=1, source_target_pairs={{0,4},{4,8},{8,12},{12,0},{1,5},{5,9},{9,13},{13,1},{2,6},{6,10},{... | collective-permute-start | bytes 786440 | tf_op jit(solution)/shard_map/ppermute | solution.py:207
  138.8 16.8 %collective-permute-start.13 = (bf16[128,2048]{1,0:T(8,128)(2,1)S(1)}, bf16[128,2048]{1,0:T(8,128)(2,1)S(1)}, u32[]{:S(2)}, u32[]{:S(2)}) collective-permute-start(bf16[128,2048]{1,0:T(8,128)(2,1)S(1)} %convolution_convert_fusion.9), channel_id=1, source_target_pairs={{0,4},{4,8},{8,12},{12,0},{1,5},{5,9},{9,13},{13,1},{2,6},{6,10},{... | collective-permute-start | bytes 1572872 | tf_op jit(solution)/shard_map/ppermute | solution.py:36
  138.9 36.6 %collective-permute-start.14 = (bf16[128,2048]{1,0:T(8,128)(2,1)S(1)}, bf16[128,2048]{1,0:T(8,128)(2,1)S(1)}, u32[]{:S(2)}, u32[]{:S(2)}) collective-permute-start(bf16[128,2048]{1,0:T(8,128)(2,1)S(1)} %convolution_convert_fusion.9), channel_id=1, source_target_pairs={{0,8},{4,12},{8,0},{12,4},{1,9},{5,13},{9,1},{13,5},{2,10},{6,14},... | collective-permute-start | bytes 1572872 | tf_op jit(solution)/shard_map/ppermute | solution.py:36
  140.4 36.4 %collective-permute-start.15 = (bf16[128,2048]{1,0:T(8,128)(2,1)S(1)}, bf16[128,2048]{1,0:T(8,128)(2,1)S(1)}, u32[]{:S(2)}, u32[]{:S(2)}) collective-permute-start(bf16[128,2048]{1,0:T(8,128)(2,1)S(1)} %convolution_convert_fusion.9), channel_id=1, source_target_pairs={{0,12},{4,0},{8,4},{12,8},{1,13},{5,1},{9,5},{13,9},{2,14},{6,2},{... | collective-permute-start | bytes 1572872 | tf_op jit(solution)/shard_map/ppermute | solution.py:36
  178.2 2.9 %collective-permute-start.16 = (bf16[256,2048]{1,0:T(8,128)(2,1)S(1)}, bf16[256,2048]{1,0:T(8,128)(2,1)}, u32[]{:S(2)}, u32[]{:S(2)}) collective-permute-start(bf16[256,2048]{1,0:T(8,128)(2,1)S(1)} %dynamic-slice_bitcast_fusion), channel_id=1, source_target_pairs={{0,1},{1,0},{2,3},{3,2},{4,5},{5,4},{6,7},{7,6},{8,9},{9,8},{10,11... | collective-permute-start | bytes 3145736 | tf_op jit(solution)/shard_map/ppermute | solution.py:47
  182.8 22.3 %collective-permute-start.17 = (bf16[128,2048]{1,0:T(8,128)(2,1)S(1)}, bf16[128,2048]{1,0:T(8,128)(2,1)S(1)}, u32[]{:S(2)}, u32[]{:S(2)}) collective-permute-start(bf16[128,2048]{1,0:T(8,128)(2,1)S(1)} %get-tuple-element.12), channel_id=1, source_target_pairs={{0,0},{1,8},{2,4},{3,12},{4,1},{5,9},{6,5},{7,13},{8,2},{9,10},{10... | collective-permute-start | bytes 1572872 | tf_op jit(solution)/shard_map/ppermute | solution.py:253
  194.4 25.5 %collective-permute-start.18 = (bf16[128,2048]{1,0:T(8,128)(2,1)S(1)}, bf16[128,2048]{1,0:T(8,128)(2,1)S(1)}, u32[]{:S(2)}, u32[]{:S(2)}) collective-permute-start(bf16[128,2048]{1,0:T(8,128)(2,1)S(1)} %get-tuple-element.13), channel_id=1, source_target_pairs={{0,4},{1,12},{2,0},{3,8},{4,5},{5,13},{6,1},{7,9},{8,6},{9,14},{10... | collective-permute-start | bytes 1572872 | tf_op jit(solution)/shard_map/ppermute | solution.py:253
  (6 other events, 73.8 us)

commit v20 on v19

--- a/solution.py
+++ b/solution.py
@@ -15,17 +15,6 @@
     per_head = queries.astype(jnp.float32).reshape(row_count, -1, head_dim)
     inv_rms = lax.rsqrt(jnp.mean(per_head * per_head, axis=2, keepdims=True) + 1e-05)
     return (per_head * inv_rms * q_gain).reshape(row_count, -1).astype(jnp.bfloat16)
-
-
-def direct_reduce_scatter(chunk_of, axis, count, index):
-    total = None
-    for shift in range(1, count):
-        outgoing = chunk_of((index + shift) % count).astype(jnp.bfloat16)
-        incoming = lax.ppermute(outgoing, axis, [(i, (i + shift) % count) for i in range(count)])
-        incoming = incoming.astype(jnp.float32)
-        total = incoming if total is None else total + incoming
-    own = chunk_of(index)
-    return own if total is None else own + total
 
 
 def direct_gather_apply(block, apply, axis, count, index):
@@ -128,33 +117,41 @@
     def my_block(dest):
         return lax.dynamic_slice_in_dim(my_rows, dest * block_width, block_width, 1)
 
-    spread_part = jnp.zeros((req_count, half_rows, block_width), hidden_in.dtype)
-    spread_part = lax.dynamic_update_index_in_dim(spread_part, my_block(req_index), req_index, 0)
+    arrived = [my_block(req_index)]
     for shift in range(1, req_count):
-        arrived_part = lax.ppermute(
-            my_block((req_index + shift) % req_count),
+        arrived.append(
+            lax.ppermute(
+                my_block((req_index + shift) % req_count),
+                "req",
+                [(i, (i + shift) % req_count) for i in range(req_count)],
+            )
+        )
+
+    def source_rows(h):
+        whole = jnp.zeros((sub_count, half_rows, block_width), hidden_in.dtype)
+        whole = lax.dynamic_update_index_in_dim(whole, arrived[h], sub_index, 0)
+        for shift in range(1, sub_count):
+            other = lax.ppermute(
+                arrived[h], "sub", [(i, (i + shift) % sub_count) for i in range(sub_count)]
+            )
+            whole = lax.dynamic_update_index_in_dim(
+                whole, other, (sub_index - shift) % sub_count, 0
+            )
+        return whole.reshape(local_rows, block_width)
+
+    def query_chunk(shift):
+        rows = source_rows((req_count - shift) % req_count)
+        product = jnp.dot(rows, q_weight, preferred_element_type=jnp.float32)
+        return product.astype(jnp.bfloat16).astype(jnp.float32)
+
+    query_sum = query_chunk(0)
+    for shift in range(1, req_count):
+        incoming = lax.ppermute(
+            query_chunk(shift).astype(jnp.bfloat16),
             "req",
             [(i, (i + shift) % req_count) for i in range(req_count)],
         )
-        spread_part = lax.dynamic_update_index_in_dim(
-            spread_part, arrived_part, (req_index - shift) % req_count, 0
-        )
-    spread_cols = jnp.zeros((req_count, sub_count, half_rows, block_width), hidden_in.dtype)
-    spread_cols = lax.dynamic_update_index_in_dim(spread_cols, spread_part, sub_index, 1)
-    for shift in range(1, sub_count):
-        other_part = lax.ppermute(
-            spread_part, "sub", [(i, (i + shift) % sub_count) for i in range(sub_count)]
-        )
-        spread_cols = lax.dynamic_update_index_in_dim(
-            spread_cols, other_part, (sub_index - shift) % sub_count, 1
-        )
-    spread_cols = spread_cols.reshape(req_count * local_rows, block_width)
-    def query_chunk(owner):
-        rows = lax.dynamic_slice_in_dim(spread_cols, owner * local_rows, local_rows, 0)
-        product = jnp.dot(rows, q_weight, preferred_element_type=jnp.float32)
-        return product.astype(jnp.bfloat16).astype(jnp.float32)
-
-    query_sum = direct_reduce_scatter(query_chunk, "req", req_count, req_index)
+        query_sum = query_sum + incoming.astype(jnp.float32)
     queries = lax.optimization_barrier(query_sum.astype(jnp.bfloat16))
     normalized = normalize_heads(queries, q_gain, head_dim)
     capacity = 2 * local_rows // req_count

time: 223 us -> 227 us (1.018)
  waiting for transfers between devices: 109 us -> 103 us
  starting transfers between devices: 51 us -> 56.6 us
  matrix products: 18.6 us -> 22.8 us
    ppermute x3, starting transfers between devices: 6.26 us -> 11.7 us  [local(): lax.ppermute(mixed_block, 'req', [(i, (i - shift) % req_count) for i in r...]
    dot_general x4, matrix products: 8.96 us -> 13.2 us  [query_chunk(): product = jnp.dot(rows, q_weight, preferred_element_type=jnp.float32)]
    ppermute x3, waiting for transfers between devices: 8.07 us -> 4.79 us  [local(): lax.ppermute(mixed_block, 'req', [(i, (i - shift) % req_count) for i in r...]
    ppermute x4 -> x7, starting transfers between devices: 9.51 us -> 8.7 us  [the longest x3 8.12 us: local(): lax.ppermute(query_chunk(shift).astype(jnp.bfloat16), 'req', [(i, (i + sh...]
    ppermute x4 -> x7, waiting for transfers between devices: 31.5 us -> 31.2 us  [the longest x3 30.4 us: local(): lax.ppermute(query_chunk(shift).astype(jnp.bfloat16), 'req', [(i, (i + sh...]
  transfers between devices with their start and end apart: 19 -> 22, of which waited for: 11 -> 12; matrix products, arithmetic and copies ran while one was open for 8% -> 10% of each run, Pallas kernels for 12% -> 12%
where the time goes in v20:
time: 227 us
  waiting for transfers between devices  103 us (45%)
  starting transfers between devices  56.6 us (25%)
  Pallas kernels  27.1 us (12%)
  matrix products  22.8 us (10%)
  local copies, waits for them, and re-layouts  11.6 us (5%)
  other arithmetic  4.94 us (2%)
    ppermute x3, waiting for transfers between devices, local(): lax.ppermute(query_chunk(shift).astype(jnp.bfloat16), 'req', [(i, (i + sh...  30.4 us
    pallas_call x4, Pallas kernels, attend(): pl.pallas_call(kernel, grid=(kv_count,), in_specs=[pl.BlockSpec((1, stack...  27.1 us
    ppermute x3, waiting for transfers between devices, direct_gather_apply(): lax.ppermute(block, axis, [(i, (i + shift) % count) for i in range(count)])  25.8 us
    ppermute x2, waiting for transfers between devices, local(): got = lax.ppermute(chunk, ('req', 'head', 'sub'), pairs).astype(jnp.float32)  25.4 us
    ppermute x3, starting transfers between devices, local(): lax.ppermute(outgoing[shift], 'req', [(i, (i + shift) % req_count) for i...  13.6 us
    dot_general x4, matrix products, query_chunk(): product = jnp.dot(rows, q_weight, preferred_element_type=jnp.float32)  13.2 us
    ppermute x3, waiting for transfers between devices, local(): lax.ppermute(my_block((req_index + shift) % req_count), 'req', [(i, (i +...  13 us
    ppermute x2, starting transfers between devices, local(): got = lax.ppermute(chunk, ('req', 'head', 'sub'), pairs).astype(jnp.float32)  12.4 us
  transfers between devices with their start and end apart: 22, of which 12 were waited for; matrix products, arithmetic and copies ran while one was open for 10% of the time, Pallas kernels for 12%

profile of v20, /device:TPU:6, one launch (start us, length us, event | category | flops | bytes accessed | tf_op | source)
XLA Modules:
  0.0 226.6 jit_solution(7832356662383400510)
XLA Ops:
  9.9 3.0 %collective-permute-done.7 = bf16[64,2048]{1,0:T(8,128)(2,1)S(1)} collective-permute-done((bf16[64,2048]{1,0:T(8,128)(2,1)S(1)}, bf16[64,2048]{1,0:T(8,128)(2,1)S(1)}, u32[]{:S(2)}, u32[]{:S(2)}) %collective-permute-start.7) | collective-permute-done | bytes 262176 | tf_op jit(solution)/shard_map/ppermute | solution.py:123
  12.9 10.0 %collective-permute-done.4 = bf16[64,2048]{1,0:T(8,128)(2,1)S(1)} collective-permute-done((bf16[64,2048]{1,0:T(8,128)(2,1)S(1)}, bf16[64,2048]{1,0:T(8,128)(2,1)S(1)}, u32[]{:S(2)}, u32[]{:S(2)}) %collective-permute-start.4) | collective-permute-done | bytes 262176 | tf_op jit(solution)/shard_map/ppermute | solution.py:123
  24.6 4.8 %convolution_convert_fusion.6 = bf16[128,2048]{1,0:T(8,128)(2,1)S(1)} fusion(bf16[128,2048]{1,0:T(8,128)(2,1)S(1)} %bitcast.110, bf16[2048,2048]{1,0:T(8,128)(2,1)} %param.10), kind=kOutput, calls=%fused_computation.6 | convolution fusion | flops 1074003968 | bytes 9437184 | tf_op jit(solution)/shard_map/dot_general | solution.py:144
  29.4 3.7 %collective-permute-start.6 = (bf16[128,2048]{1,0:T(8,128)(2,1)S(1)}, bf16[128,2048]{1,0:T(8,128)(2,1)S(1)}, u32[]{:S(2)}, u32[]{:S(2)}) collective-permute-start(bf16[128,2048]{1,0:T(8,128)(2,1)S(1)} %convolution_convert_fusion.6), channel_id=1, source_target_pairs={{0,8},{4,12},{8,0},{12,4},{1,9},{5,13},{9,1},{13,5},{2,10},{6,14},... | collective-permute-start | bytes 1572872 | tf_op jit(solution)/shard_map/ppermute | solution.py:149
  34.5 4.4 %collective-permute-start.9 = (bf16[128,2048]{1,0:T(8,128)(2,1)S(1)}, bf16[128,2048]{1,0:T(8,128)(2,1)S(1)}, u32[]{:S(2)}, u32[]{:S(2)}) collective-permute-start(bf16[128,2048]{1,0:T(8,128)(2,1)S(1)} %convolution_convert_fusion.5), channel_id=1, source_target_pairs={{0,12},{4,0},{8,4},{12,8},{1,13},{5,1},{9,5},{13,9},{2,14},{6,2},{... | collective-permute-start | bytes 1572872 | tf_op jit(solution)/shard_map/ppermute | solution.py:149
  41.0 16.2 %collective-permute-done.6 = bf16[128,2048]{1,0:T(8,128)(2,1)S(1)} collective-permute-done((bf16[128,2048]{1,0:T(8,128)(2,1)S(1)}, bf16[128,2048]{1,0:T(8,128)(2,1)S(1)}, u32[]{:S(2)}, u32[]{:S(2)}) %collective-permute-start.6) | collective-permute-done | bytes 524320 | tf_op jit(solution)/shard_map/ppermute | solution.py:149
  58.5 13.0 %collective-permute-done.3 = bf16[128,2048]{1,0:T(8,128)(2,1)S(1)} collective-permute-done((bf16[128,2048]{1,0:T(8,128)(2,1)}, bf16[128,2048]{1,0:T(8,128)(2,1)S(1)}, u32[]{:S(2)}, u32[]{:S(2)}) %collective-permute-start.3) | collective-permute-done | bytes 524320 | tf_op jit(solution)/shard_map/ppermute | solution.py:149
  71.5 5.0 %fusion.4 = bf16[128,2048]{1,0:T(8,128)(2,1)S(1)} fusion(bf16[128,2048]{1,0:T(8,128)(2,1)S(1)} %bitcast.112, bf16[2048,2048]{1,0:T(8,128)(2,1)} %param.10, bf16[128,2048]{1,0:T(8,128)(2,1)S(1)} %collective-permute-done.9, bf16[128,2048]{1,0:T(8,128)(2,1)S(1)} %collective-permute-done.6, bf16[128,2048]{1,0:T(8,128)(2,1)S(1)} %collective-permute-done.3), kind=kOutput, calls=%fused_computation.13 | convolution fusion | flops 1076101120 | bytes 11010048 | tf_op jit(solution)/shard_map/dot_general | solution.py:144
  79.5 8.9 %collective-permute-start.10 = (bf16[2,512,128]{2,1,0:T(8,128)(2,1)S(1)}, bf16[2,512,128]{2,1,0:T(8,128)(2,1)}, u32[]{:S(2)}, u32[]{:S(2)}) collective-permute-start(bf16[2,512,128]{2,1,0:T(8,128)(2,1)S(1)} %bitcast.132), channel_id=1, source_target_pairs={{0,4},{4,8},{8,12},{12,0},{1,5},{5,9},{9,13},{13,1},{2,6},{6,10},{... | collective-permute-start | bytes 786440 | tf_op jit(solution)/shard_map/ppermute | solution.py:190
  90.2 2.9 %collective-permute-start.14 = (bf16[2,512,128]{2,1,0:T(8,128)(2,1)S(1)}, bf16[2,512,128]{2,1,0:T(8,128)(2,1)}, u32[]{:S(2)}, u32[]{:S(2)}) collective-permute-start(bf16[2,512,128]{2,1,0:T(8,128)(2,1)S(1)} %bitcast.129), channel_id=1, source_target_pairs={{0,12},{4,0},{8,4},{12,8},{1,13},{5,1},{9,5},{13,9},{2,14},{6,2},{... | collective-permute-start | bytes 786440 | tf_op jit(solution)/shard_map/ppermute | solution.py:190
  97.3 6.8 %shard_map.91 = bf16[2,512,128]{2,1,0:T(8,128)(2,1)} custom-call(bf16[2,512,128]{2,1,0:T(8,128)(2,1)} %bitcast.131, bf16[2,1664,128]{2,1,0:T(8,128)(2,1)} %bitcast.117, bf16[2,1664,128]{2,1,0:T(8,128)(2,1)} %bitcast.121), custom_call_target="tpu_custom_call" | custom-call | flops 872415232 | bytes 2228224 | tf_op jit(solution)/shard_map/pallas_call | solution.py:75
  104.1 6.8 %shard_map.92 = bf16[2,512,128]{2,1,0:T(8,128)(2,1)} custom-call(bf16[2,512,128]{2,1,0:T(8,128)(2,1)} %collective-permute-done.10.q_ref, bf16[2,1664,128]{2,1,0:T(8,128)(2,1)} %bitcast.118, bf16[2,1664,128]{2,1,0:T(8,128)(2,1)} %bitcast.122), custom_call_target="tpu_custom_call" | custom-call | flops 872415232 | bytes 2228224 | tf_op jit(solution)/shard_map/pallas_call | solution.py:75
  110.8 6.8 %shard_map.93 = bf16[2,512,128]{2,1,0:T(8,128)(2,1)} custom-call(bf16[2,512,128]{2,1,0:T(8,128)(2,1)} %collective-permute-done.12.q_ref, bf16[2,1664,128]{2,1,0:T(8,128)(2,1)} %bitcast.119, bf16[2,1664,128]{2,1,0:T(8,128)(2,1)} %bitcast.123), custom_call_target="tpu_custom_call" | custom-call | flops 872415232 | bytes 2228224 | tf_op jit(solution)/shard_map/pallas_call | solution.py:75
  117.6 6.7 %collective-permute-start.13 = (bf16[2,512,128]{2,1,0:T(8,128)(2,1)}, bf16[2,512,128]{2,1,0:T(8,128)(2,1)S(1)}, u32[]{:S(2)}, u32[]{:S(2)}) collective-permute-start(bf16[2,512,128]{2,1,0:T(8,128)(2,1)} %shard_map.93), channel_id=1, source_target_pairs={{0,8},{4,12},{8,0},{12,4},{1,9},{5,13},{9,1},{13,5},{2,10},{6,14},... | collective-permute-start | bytes 786440 | tf_op jit(solution)/shard_map/ppermute | solution.py:204
  124.3 6.8 %shard_map.94 = bf16[2,512,128]{2,1,0:T(8,128)(2,1)} custom-call(bf16[2,512,128]{2,1,0:T(8,128)(2,1)} %collective-permute-done.14.q_ref, bf16[2,1664,128]{2,1,0:T(8,128)(2,1)} %bitcast.120, bf16[2,1664,128]{2,1,0:T(8,128)(2,1)} %bitcast.124), custom_call_target="tpu_custom_call" | custom-call | flops 872415232 | bytes 2228224 | tf_op jit(solution)/shard_map/pallas_call | solution.py:75
  131.1 5.0 %collective-permute-start.15 = (bf16[2,512,128]{2,1,0:T(8,128)(2,1)}, bf16[2,512,128]{2,1,0:T(8,128)(2,1)S(1)}, u32[]{:S(2)}, u32[]{:S(2)}) collective-permute-start(bf16[2,512,128]{2,1,0:T(8,128)(2,1)} %shard_map.94), channel_id=1, source_target_pairs={{0,4},{4,8},{8,12},{12,0},{1,5},{5,9},{9,13},{13,1},{2,6},{6,10},{... | collective-permute-start | bytes 786440 | tf_op jit(solution)/shard_map/ppermute | solution.py:204
  136.6 4.8 %collective-permute-done.15 = bf16[2,512,128]{2,1,0:T(8,128)(2,1)S(1)} collective-permute-done((bf16[2,512,128]{2,1,0:T(8,128)(2,1)}, bf16[2,512,128]{2,1,0:T(8,128)(2,1)S(1)}, u32[]{:S(2)}, u32[]{:S(2)}) %collective-permute-start.15) | collective-permute-done | bytes 262176 | tf_op jit(solution)/shard_map/ppermute | solution.py:204
  147.5 4.8 %fusion.6 = bf16[4,128,2048]{2,1,0:T(8,128)(2,1)S(1)} fusion(bf16[4,128,2048]{2,1,0:T(8,128)(2,1)S(1)} %broadcast_in_dim.62, s32[]{:T(128)S(6)} %select_n.170, bf16[128,2048]{1,0:T(8,128)(2,1)S(1)} %convolution_convert_fusion.9, bf16[2048,2048]{1,0:T(8,128)(2,1)} %param.14), kind=kOutput, calls=%fused_computation.16 | convolution fusion | flops 1074003968 | bytes 9437188 | tf_op jit(solution)/shard_map/dot_general | solution.py:219
  152.3 7.0 %collective-permute-done.16 = bf16[128,2048]{1,0:T(8,128)(2,1)S(1)} collective-permute-done((bf16[128,2048]{1,0:T(8,128)(2,1)S(1)}, bf16[128,2048]{1,0:T(8,128)(2,1)S(1)}, u32[]{:S(2)}, u32[]{:S(2)}) %collective-permute-start.16) | collective-permute-done | bytes 524320 | tf_op jit(solution)/shard_map/ppermute | solution.py:25
  160.7 18.7 %collective-permute-done.17 = bf16[128,2048]{1,0:T(8,128)(2,1)S(1)} collective-permute-done((bf16[128,2048]{1,0:T(8,128)(2,1)S(1)}, bf16[128,2048]{1,0:T(8,128)(2,1)S(1)}, u32[]{:S(2)}, u32[]{:S(2)}) %collective-permute-start.17) | collective-permute-done | bytes 524320 | tf_op jit(solution)/shard_map/ppermute | solution.py:25
  182.2 2.8 %collective-permute-done.19 = bf16[256,2048]{1,0:T(8,128)(2,1)} collective-permute-done((bf16[256,2048]{1,0:T(8,128)(2,1)S(1)}, bf16[256,2048]{1,0:T(8,128)(2,1)}, u32[]{:S(2)}, u32[]{:S(2)}) %collective-permute-start.19) | collective-permute-done | bytes 1048608 | tf_op jit(solution)/shard_map/ppermute | solution.py:36
  186.7 12.3 %collective-permute-start.20 = (bf16[128,2048]{1,0:T(8,128)(2,1)S(1)}, bf16[128,2048]{1,0:T(8,128)(2,1)S(1)}, u32[]{:S(2)}, u32[]{:S(2)}) collective-permute-start(bf16[128,2048]{1,0:T(8,128)(2,1)S(1)} %get-tuple-element.14), channel_id=1, source_target_pairs={{0,0},{1,8},{2,4},{3,12},{4,1},{5,9},{6,5},{7,13},{8,2},{9,10},{10... | collective-permute-start | bytes 1572872 | tf_op jit(solution)/shard_map/ppermute | solution.py:250
  199.1 11.6 %collective-permute-done.20 = bf16[128,2048]{1,0:T(8,128)(2,1)S(1)} collective-permute-done((bf16[128,2048]{1,0:T(8,128)(2,1)S(1)}, bf16[128,2048]{1,0:T(8,128)(2,1)S(1)}, u32[]{:S(2)}, u32[]{:S(2)}) %collective-permute-start.20) | collective-permute-done | bytes 524320 | tf_op jit(solution)/shard_map/ppermute | solution.py:250
  210.7 13.8 %collective-permute-done.21 = bf16[128,2048]{1,0:T(8,128)(2,1)S(1)} collective-permute-done((bf16[128,2048]{1,0:T(8,128)(2,1)S(1)}, bf16[128,2048]{1,0:T(8,128)(2,1)S(1)}, u32[]{:S(2)}, u32[]{:S(2)}) %collective-permute-start.21) | collective-permute-done | bytes 524320 | tf_op jit(solution)/shard_map/ppermute | solution.py:250
  (105 shorter events, 39.6 us)
Async XLA Ops:
  1.7 11.2 %collective-permute-start.7 = (bf16[64,2048]{1,0:T(8,128)(2,1)S(1)}, bf16[64,2048]{1,0:T(8,128)(2,1)S(1)}, u32[]{:S(2)}, u32[]{:S(2)}) collective-permute-start(bf16[64,2048]{1,0:T(8,128)(2,1)S(1)} %get-tuple-element.12), channel_id=1, source_target_pairs={{0,4},{4,8},{8,12},{12,0},{1,5},{5,9},{9,13},{13,1},{2,6},{6,10},{... | collective-permute-start | bytes 786440 | tf_op jit(solution)/shard_map/ppermute | solution.py:123
  3.3 19.7 %collective-permute-start.4 = (bf16[64,2048]{1,0:T(8,128)(2,1)S(1)}, bf16[64,2048]{1,0:T(8,128)(2,1)S(1)}, u32[]{:S(2)}, u32[]{:S(2)}) collective-permute-start(bf16[64,2048]{1,0:T(8,128)(2,1)S(1)} %get-tuple-element.13), channel_id=1, source_target_pairs={{0,8},{4,12},{8,0},{12,4},{1,9},{5,13},{9,1},{13,5},{2,10},{6,14},... | collective-permute-start | bytes 786440 | tf_op jit(solution)/shard_map/ppermute | solution.py:123
  5.9 17.2 %collective-permute-start.1 = (bf16[64,2048]{1,0:T(8,128)(2,1)S(1)}, bf16[64,2048]{1,0:T(8,128)(2,1)S(1)}, u32[]{:S(2)}, u32[]{:S(2)}) collective-permute-start(bf16[64,2048]{1,0:T(8,128)(2,1)S(1)} %get-tuple-element.11), channel_id=1, source_target_pairs={{0,12},{4,0},{8,4},{12,8},{1,13},{5,1},{9,5},{13,9},{2,14},{6,2},{... | collective-permute-start | bytes 786440 | tf_op jit(solution)/shard_map/ppermute | solution.py:123
  9.1 31.9 %collective-permute-start = (bf16[64,2048]{1,0:T(8,128)(2,1)}, bf16[64,2048]{1,0:T(8,128)(2,1)S(1)}, u32[]{:S(2)}, u32[]{:S(2)}) collective-permute-start(bf16[64,2048]{1,0:T(8,128)(2,1)} %get-tuple-element.10), channel_id=1, source_target_pairs={{0,1},{1,0},{2,3},{3,2},{4,5},{5,4},{6,7},{7,6},{8,9},{9,8},{10,11... | collective-permute-start | bytes 786440 | tf_op jit(solution)/shard_map/ppermute | solution.py:134
  12.9 11.7 %collective-permute-start.8 = (bf16[64,2048]{1,0:T(8,128)(2,1)S(1)}, bf16[64,2048]{1,0:T(8,128)(2,1)S(1)}, u32[]{:S(2)}, u32[]{:S(2)}) collective-permute-start(bf16[64,2048]{1,0:T(8,128)(2,1)S(1)} %collective-permute-done.7), channel_id=1, source_target_pairs={{0,1},{1,0},{2,3},{3,2},{4,5},{5,4},{6,7},{7,6},{8,9},{9,8},{10,11... | collective-permute-start | bytes 786440 | tf_op jit(solution)/shard_map/ppermute | solution.py:134
  23.0 1.5 collective-permute-start.5
  23.1 15.8 %collective-permute-start.2 = (bf16[64,2048]{1,0:T(8,128)(2,1)S(1)}, bf16[64,2048]{1,0:T(8,128)(2,1)S(1)}, u32[]{:S(2)}, u32[]{:S(2)}) collective-permute-start(bf16[64,2048]{1,0:T(8,128)(2,1)S(1)} %collective-permute-done.1), channel_id=1, source_target_pairs={{0,1},{1,0},{2,3},{3,2},{4,5},{5,4},{6,7},{7,6},{8,9},{9,8},{10,11... | collective-permute-start | bytes 786440 | tf_op jit(solution)/shard_map/ppermute | solution.py:134
  29.4 27.8 %collective-permute-start.6 = (bf16[128,2048]{1,0:T(8,128)(2,1)S(1)}, bf16[128,2048]{1,0:T(8,128)(2,1)S(1)}, u32[]{:S(2)}, u32[]{:S(2)}) collective-permute-start(bf16[128,2048]{1,0:T(8,128)(2,1)S(1)} %convolution_convert_fusion.6), channel_id=1, source_target_pairs={{0,8},{4,12},{8,0},{12,4},{1,9},{5,13},{9,1},{13,5},{2,10},{6,14},... | collective-permute-start | bytes 1572872 | tf_op jit(solution)/shard_map/ppermute | solution.py:149
  34.5 24.0 %collective-permute-start.9 = (bf16[128,2048]{1,0:T(8,128)(2,1)S(1)}, bf16[128,2048]{1,0:T(8,128)(2,1)S(1)}, u32[]{:S(2)}, u32[]{:S(2)}) collective-permute-start(bf16[128,2048]{1,0:T(8,128)(2,1)S(1)} %convolution_convert_fusion.5), channel_id=1, source_target_pairs={{0,12},{4,0},{8,4},{12,8},{1,13},{5,1},{9,5},{13,9},{2,14},{6,2},{... | collective-permute-start | bytes 1572872 | tf_op jit(solution)/shard_map/ppermute | solution.py:149
  41.0 30.5 %collective-permute-start.3 = (bf16[128,2048]{1,0:T(8,128)(2,1)}, bf16[128,2048]{1,0:T(8,128)(2,1)S(1)}, u32[]{:S(2)}, u32[]{:S(2)}) collective-permute-start(bf16[128,2048]{1,0:T(8,128)(2,1)} %convolution_convert_fusion.7), channel_id=1, source_target_pairs={{0,4},{4,8},{8,12},{12,0},{1,5},{5,9},{9,13},{13,1},{2,6},{6,10},{... | collective-permute-start | bytes 1572872 | tf_op jit(solution)/shard_map/ppermute | solution.py:149
  78.4 14.7 %copy-start.1 = (bf16[1,1601,512]{2,1,0:T(8,128)(2,1)S(1)}, bf16[1,1601,512]{2,1,0:T(8,128)(2,1)}, u32[]{:S(2)}) copy-start(bf16[1,1601,512]{2,1,0:T(8,128)(2,1)} %param.13) | copy-start | bytes 4918276
  79.5 24.5 %collective-permute-start.10 = (bf16[2,512,128]{2,1,0:T(8,128)(2,1)S(1)}, bf16[2,512,128]{2,1,0:T(8,128)(2,1)}, u32[]{:S(2)}, u32[]{:S(2)}) collective-permute-start(bf16[2,512,128]{2,1,0:T(8,128)(2,1)S(1)} %bitcast.132), channel_id=1, source_target_pairs={{0,4},{4,8},{8,12},{12,0},{1,5},{5,9},{9,13},{13,1},{2,6},{6,10},{... | collective-permute-start | bytes 786440 | tf_op jit(solution)/shard_map/ppermute | solution.py:190
  88.4 22.5 %collective-permute-start.12 = (bf16[2,512,128]{2,1,0:T(8,128)(2,1)S(1)}, bf16[2,512,128]{2,1,0:T(8,128)(2,1)}, u32[]{:S(2)}, u32[]{:S(2)}) collective-permute-start(bf16[2,512,128]{2,1,0:T(8,128)(2,1)S(1)} %bitcast.130), channel_id=1, source_target_pairs={{0,8},{4,12},{8,0},{12,4},{1,9},{5,13},{9,1},{13,5},{2,10},{6,14},... | collective-permute-start | bytes 786440 | tf_op jit(solution)/shard_map/ppermute | solution.py:190
  90.2 34.1 %collective-permute-start.14 = (bf16[2,512,128]{2,1,0:T(8,128)(2,1)S(1)}, bf16[2,512,128]{2,1,0:T(8,128)(2,1)}, u32[]{:S(2)}, u32[]{:S(2)}) collective-permute-start(bf16[2,512,128]{2,1,0:T(8,128)(2,1)S(1)} %bitcast.129), channel_id=1, source_target_pairs={{0,12},{4,0},{8,4},{12,8},{1,13},{5,1},{9,5},{13,9},{2,14},{6,2},{... | collective-permute-start | bytes 786440 | tf_op jit(solution)/shard_map/ppermute | solution.py:190
  110.8 25.4 %collective-permute-start.11 = (bf16[2,512,128]{2,1,0:T(8,128)(2,1)}, bf16[2,512,128]{2,1,0:T(8,128)(2,1)S(1)}, u32[]{:S(2)}, u32[]{:S(2)}) collective-permute-start(bf16[2,512,128]{2,1,0:T(8,128)(2,1)} %shard_map.92), channel_id=1, source_target_pairs={{0,12},{4,0},{8,4},{12,8},{1,13},{5,1},{9,5},{13,9},{2,14},{6,2},{... | collective-permute-start | bytes 786440 | tf_op jit(solution)/shard_map/ppermute | solution.py:204
  117.6 18.4 %copy-start.3 = (bf16[2,512,128]{2,1,0:T(8,128)(2,1)S(1)}, bf16[2,512,128]{2,1,0:T(8,128)(2,1)}, u32[]{:S(2)}) copy-start(bf16[2,512,128]{2,1,0:T(8,128)(2,1)} %shard_map.91) | copy-start | bytes 786436
  117.6 18.8 %collective-permute-start.13 = (bf16[2,512,128]{2,1,0:T(8,128)(2,1)}, bf16[2,512,128]{2,1,0:T(8,128)(2,1)S(1)}, u32[]{:S(2)}, u32[]{:S(2)}) collective-permute-start(bf16[2,512,128]{2,1,0:T(8,128)(2,1)} %shard_map.93), channel_id=1, source_target_pairs={{0,8},{4,12},{8,0},{12,4},{1,9},{5,13},{9,1},{13,5},{2,10},{6,14},... | collective-permute-start | bytes 786440 | tf_op jit(solution)/shard_map/ppermute | solution.py:204
  131.1 10.3 %collective-permute-start.15 = (bf16[2,512,128]{2,1,0:T(8,128)(2,1)}, bf16[2,512,128]{2,1,0:T(8,128)(2,1)S(1)}, u32[]{:S(2)}, u32[]{:S(2)}) collective-permute-start(bf16[2,512,128]{2,1,0:T(8,128)(2,1)} %shard_map.94), channel_id=1, source_target_pairs={{0,4},{4,8},{8,12},{12,0},{1,5},{5,9},{9,13},{13,1},{2,6},{6,10},{... | collective-permute-start | bytes 786440 | tf_op jit(solution)/shard_map/ppermute | solution.py:204
  142.6 16.8 %collective-permute-start.16 = (bf16[128,2048]{1,0:T(8,128)(2,1)S(1)}, bf16[128,2048]{1,0:T(8,128)(2,1)S(1)}, u32[]{:S(2)}, u32[]{:S(2)}) collective-permute-start(bf16[128,2048]{1,0:T(8,128)(2,1)S(1)} %convolution_convert_fusion.9), channel_id=1, source_target_pairs={{0,4},{4,8},{8,12},{12,0},{1,5},{5,9},{9,13},{13,1},{2,6},{6,10},{... | collective-permute-start | bytes 1572872 | tf_op jit(solution)/shard_map/ppermute | solution.py:25
  144.6 34.8 %collective-permute-start.17 = (bf16[128,2048]{1,0:T(8,128)(2,1)S(1)}, bf16[128,2048]{1,0:T(8,128)(2,1)S(1)}, u32[]{:S(2)}, u32[]{:S(2)}) collective-permute-start(bf16[128,2048]{1,0:T(8,128)(2,1)S(1)} %convolution_convert_fusion.9), channel_id=1, source_target_pairs={{0,8},{4,12},{8,0},{12,4},{1,9},{5,13},{9,1},{13,5},{2,10},{6,14},... | collective-permute-start | bytes 1572872 | tf_op jit(solution)/shard_map/ppermute | solution.py:25
  145.7 35.0 %collective-permute-start.18 = (bf16[128,2048]{1,0:T(8,128)(2,1)S(1)}, bf16[128,2048]{1,0:T(8,128)(2,1)S(1)}, u32[]{:S(2)}, u32[]{:S(2)}) collective-permute-start(bf16[128,2048]{1,0:T(8,128)(2,1)S(1)} %convolution_convert_fusion.9), channel_id=1, source_target_pairs={{0,12},{4,0},{8,4},{12,8},{1,13},{5,1},{9,5},{13,9},{2,14},{6,2},{... | collective-permute-start | bytes 1572872 | tf_op jit(solution)/shard_map/ppermute | solution.py:25
  182.1 2.9 %collective-permute-start.19 = (bf16[256,2048]{1,0:T(8,128)(2,1)S(1)}, bf16[256,2048]{1,0:T(8,128)(2,1)}, u32[]{:S(2)}, u32[]{:S(2)}) collective-permute-start(bf16[256,2048]{1,0:T(8,128)(2,1)S(1)} %dynamic-slice_bitcast_fusion), channel_id=1, source_target_pairs={{0,1},{1,0},{2,3},{3,2},{4,5},{5,4},{6,7},{7,6},{8,9},{9,8},{10,11... | collective-permute-start | bytes 3145736 | tf_op jit(solution)/shard_map/ppermute | solution.py:36
  186.7 24.0 %collective-permute-start.20 = (bf16[128,2048]{1,0:T(8,128)(2,1)S(1)}, bf16[128,2048]{1,0:T(8,128)(2,1)S(1)}, u32[]{:S(2)}, u32[]{:S(2)}) collective-permute-start(bf16[128,2048]{1,0:T(8,128)(2,1)S(1)} %get-tuple-element.14), channel_id=1, source_target_pairs={{0,0},{1,8},{2,4},{3,12},{4,1},{5,9},{6,5},{7,13},{8,2},{9,10},{10... | collective-permute-start | bytes 1572872 | tf_op jit(solution)/shard_map/ppermute | solution.py:250
  199.0 25.5 %collective-permute-start.21 = (bf16[128,2048]{1,0:T(8,128)(2,1)S(1)}, bf16[128,2048]{1,0:T(8,128)(2,1)S(1)}, u32[]{:S(2)}, u32[]{:S(2)}) collective-permute-start(bf16[128,2048]{1,0:T(8,128)(2,1)S(1)} %get-tuple-element.15), channel_id=1, source_target_pairs={{0,4},{1,12},{2,0},{3,8},{4,5},{5,13},{6,1},{7,9},{8,6},{9,14},{10... | collective-permute-start | bytes 1572872 | tf_op jit(solution)/shard_map/ppermute | solution.py:250
  (9 other events, 93.2 us)

commit v21 on v19

--- a/solution.py
+++ b/solution.py
@@ -228,32 +228,28 @@
     hs_index = lax.axis_index("head") * sub_count + sub_index
     head_count = lax.axis_size("head")
     by_group = partial_cols.reshape(sub_count, -1, partial_cols.shape[1])
-    sub_sums = exchange_sum(by_group, "sub", sub_count, sub_index)
+    owner_sums = exchange_sum(by_group, "sub", sub_count, sub_index)
+    owner_sums = owner_sums.reshape(head_count, -1, partial_cols.shape[1])
+    owner_sums = exchange_sum(owner_sums, "head", head_count, lax.axis_index("head"))
     per_hs = req_count // hs_count
     out_block = partial_cols.shape[1]
-    sub_sums = sub_sums.reshape(head_count, per_hs, local_rows, out_block)
-    head_index = lax.axis_index("head")
+    owner_sums = owner_sums.reshape(per_hs, local_rows, out_block)
     head_total = jnp.zeros((local_rows, per_hs * out_block), jnp.float32)
     for step in range(per_hs):
-        gathered = None
-        for turn in range(head_count):
-            group = (head_index + turn) % head_count
-            chunk = lax.dynamic_index_in_dim(sub_sums, group, 0, keepdims=False)
-            chunk = lax.dynamic_index_in_dim(
-                chunk, (req_index + step) % per_hs, 0, keepdims=False
-            )
-            pairs = []
-            for c in range(req_count):
-                for h in range(head_count):
-                    for u in range(sub_count):
-                        g = (h + turn) % head_count
-                        k = (u * head_count + g) * per_hs + (c + step) % per_hs
-                        src = c * hs_count + h * sub_count + u
-                        pairs.append((src, k * hs_count + c // per_hs))
-            got = lax.ppermute(chunk, ("req", "head", "sub"), pairs).astype(jnp.float32)
-            gathered = got if gathered is None else gathered + got
+        chunk = lax.dynamic_index_in_dim(
+            owner_sums, (req_index + step) % per_hs, axis=0, keepdims=False
+        )
+        pairs = []
+        for c in range(req_count):
+            for h in range(head_count):
+                for u in range(sub_count):
+                    j = u * head_count + h
+                    k = j * per_hs + (c + step) % per_hs
+                    src = c * hs_count + h * sub_count + u
+                    pairs.append((src, k * hs_count + c // per_hs))
+        got = lax.ppermute(chunk, ("req", "head", "sub"), pairs).astype(jnp.float32)
         head_total = lax.dynamic_update_slice_in_dim(
-            head_total, gathered, ((req_index % per_hs - step) % per_hs) * out_block, 1
+            head_total, got, ((req_index % per_hs - step) % per_hs) * out_block, 1
         )
     head_total = head_total.astype(jnp.float32)
     out_width = head_total.shape[1]

time: 223 us -> 229 us (1.027)
  the two profiles are of different devices: /device:TPU:6 before, /device:TPU:26 now
where the time goes in v21:
time: 229 us
  waiting for transfers between devices  150 us (66%)
  Pallas kernels  27.2 us (12%)
  matrix products  18.6 us (8%)
  starting transfers between devices  15.4 us (7%)
  local copies, waits for them, and re-layouts  12 us (5%)
  other arithmetic  4.99 us (2%)
    ppermute x3, waiting for transfers between devices, direct_reduce_scatter(): lax.ppermute(outgoing, axis, [(i, (i + shift) % count) for i in range(cou...  41 us
    ppermute x3, waiting for transfers between devices, direct_gather_apply(): lax.ppermute(block, axis, [(i, (i + shift) % count) for i in range(count)])  37.7 us
    pallas_call x4, Pallas kernels, attend(): pl.pallas_call(kernel, grid=(kv_count,), in_specs=[pl.BlockSpec((1, stack...  27.2 us
    ppermute x3, waiting for transfers between devices, local(): lax.ppermute(my_block((req_index + shift) % req_count), 'req', [(i, (i +...  21.1 us
    ppermute x1, waiting for transfers between devices, local(): got = lax.ppermute(chunk, ('req', 'head', 'sub'), pairs).astype(jnp.float32)  19.6 us
    ppermute x2, waiting for transfers between devices, exchange_sum(): lax.ppermute(outgoing, axis, [(i, (i + shift) % count) for i in range(cou...  16.2 us
    ppermute x3, waiting for transfers between devices, local(): lax.ppermute(mixed_block, 'req', [(i, (i - shift) % req_count) for i in r...  9.11 us
    dot_general x4, matrix products, query_chunk(): product = jnp.dot(rows, q_weight, preferred_element_type=jnp.float32)  8.94 us
  transfers between devices with their start and end apart: 19, of which 13 were waited for; matrix products, arithmetic and copies ran while one was open for 7% of the time, Pallas kernels for 12%

profile of v21, /device:TPU:26, one launch (start us, length us, event | category | flops | bytes accessed | tf_op | source)
XLA Modules:
  0.0 228.8 jit_solution(14111817087835510103)
XLA Ops:
  1.9 1.7 collective-permute-start.1
  5.3 4.8 %collective-permute-done = bf16[64,2048]{1,0:T(8,128)(2,1)S(1)} collective-permute-done((bf16[64,2048]{1,0:T(8,128)(2,1)S(1)}, bf16[64,2048]{1,0:T(8,128)(2,1)S(1)}, u32[]{:S(2)}, u32[]{:S(2)}) %collective-permute-start) | collective-permute-done | bytes 262176 | tf_op jit(solution)/shard_map/ppermute | solution.py:134
  10.1 16.3 %collective-permute-done.1 = bf16[64,2048]{1,0:T(8,128)(2,1)S(1)} collective-permute-done((bf16[64,2048]{1,0:T(8,128)(2,1)S(1)}, bf16[64,2048]{1,0:T(8,128)(2,1)S(1)}, u32[]{:S(2)}, u32[]{:S(2)}) %collective-permute-start.1) | collective-permute-done | bytes 262176 | tf_op jit(solution)/shard_map/ppermute | solution.py:134
  27.5 1.8 collective-permute-done.3
  29.4 4.8 %convolution_convert_fusion.7 = bf16[128,2048]{1,0:T(8,128)(2,1)S(1)} fusion(bf16[2048,2048]{1,0:T(8,128)(2,1)} %param.10, bf16[512,2048]{1,0:T(8,128)(2,1)S(1)} %bitcast.96, s32[]{:T(128)S(6)} %select_n.186), kind=kOutput, calls=%fused_computation.7 | convolution fusion | flops 1074003968 | bytes 9437188 | tf_op jit(solution)/shard_map/dot_general | solution.py:154
  40.5 8.5 %collective-permute-done.4 = bf16[128,2048]{1,0:T(8,128)(2,1)S(1)} collective-permute-done((bf16[128,2048]{1,0:T(8,128)(2,1)S(1)}, bf16[128,2048]{1,0:T(8,128)(2,1)S(1)}, u32[]{:S(2)}, u32[]{:S(2)}) %collective-permute-start.4) | collective-permute-done | bytes 524320 | tf_op jit(solution)/shard_map/ppermute | solution.py:24
  49.0 32.5 %collective-permute-done.5 = bf16[128,2048]{1,0:T(8,128)(2,1)S(1)} collective-permute-done((bf16[128,2048]{1,0:T(8,128)(2,1)S(1)}, bf16[128,2048]{1,0:T(8,128)(2,1)S(1)}, u32[]{:S(2)}, u32[]{:S(2)}) %collective-permute-start.5) | collective-permute-done | bytes 524320 | tf_op jit(solution)/shard_map/ppermute | solution.py:24
  87.8 2.0 collective-permute-start.11
  94.0 6.8 %shard_map.91 = bf16[2,512,128]{2,1,0:T(8,128)(2,1)} custom-call(bf16[2,512,128]{2,1,0:T(8,128)(2,1)} %bitcast.124, bf16[2,1664,128]{2,1,0:T(8,128)(2,1)} %bitcast.110, bf16[2,1664,128]{2,1,0:T(8,128)(2,1)} %bitcast.114), custom_call_target="tpu_custom_call" | custom-call | flops 872415232 | bytes 2228224 | tf_op jit(solution)/shard_map/pallas_call | solution.py:86
  100.8 6.8 %shard_map.92 = bf16[2,512,128]{2,1,0:T(8,128)(2,1)} custom-call(bf16[2,512,128]{2,1,0:T(8,128)(2,1)} %collective-permute-done.7.q_ref, bf16[2,1664,128]{2,1,0:T(8,128)(2,1)} %bitcast.111, bf16[2,1664,128]{2,1,0:T(8,128)(2,1)} %bitcast.115), custom_call_target="tpu_custom_call" | custom-call | flops 872415232 | bytes 2228224 | tf_op jit(solution)/shard_map/pallas_call | solution.py:86
  107.6 3.7 %collective-permute-done.9.q_ref = bf16[2,512,128]{2,1,0:T(8,128)(2,1)} collective-permute-done((bf16[2,512,128]{2,1,0:T(8,128)(2,1)S(1)}, bf16[2,512,128]{2,1,0:T(8,128)(2,1)}, u32[]{:S(2)}, u32[]{:S(2)}) %collective-permute-start.9) | collective-permute-done | bytes 262176 | tf_op jit(solution)/shard_map/ppermute | solution.py:193
  111.3 6.8 %shard_map.93 = bf16[2,512,128]{2,1,0:T(8,128)(2,1)} custom-call(bf16[2,512,128]{2,1,0:T(8,128)(2,1)} %collective-permute-done.9.q_ref, bf16[2,1664,128]{2,1,0:T(8,128)(2,1)} %bitcast.112, bf16[2,1664,128]{2,1,0:T(8,128)(2,1)} %bitcast.116), custom_call_target="tpu_custom_call" | custom-call | flops 872415232 | bytes 2228224 | tf_op jit(solution)/shard_map/pallas_call | solution.py:86
  118.0 6.8 %shard_map.94 = bf16[2,512,128]{2,1,0:T(8,128)(2,1)} custom-call(bf16[2,512,128]{2,1,0:T(8,128)(2,1)} %collective-permute-done.11.q_ref, bf16[2,1664,128]{2,1,0:T(8,128)(2,1)} %bitcast.113, bf16[2,1664,128]{2,1,0:T(8,128)(2,1)} %bitcast.117), custom_call_target="tpu_custom_call" | custom-call | flops 872415232 | bytes 2228224 | tf_op jit(solution)/shard_map/pallas_call | solution.py:86
  125.7 3.8 %collective-permute-done.10 = bf16[2,512,128]{2,1,0:T(8,128)(2,1)S(1)} collective-permute-done((bf16[2,512,128]{2,1,0:T(8,128)(2,1)}, bf16[2,512,128]{2,1,0:T(8,128)(2,1)S(1)}, u32[]{:S(2)}, u32[]{:S(2)}) %collective-permute-start.10) | collective-permute-done | bytes 262176 | tf_op jit(solution)/shard_map/ppermute | solution.py:207
  129.7 5.3 %collective-permute-done.12 = bf16[2,512,128]{2,1,0:T(8,128)(2,1)S(1)} collective-permute-done((bf16[2,512,128]{2,1,0:T(8,128)(2,1)}, bf16[2,512,128]{2,1,0:T(8,128)(2,1)S(1)}, u32[]{:S(2)}, u32[]{:S(2)}) %collective-permute-start.12) | collective-permute-done | bytes 262176 | tf_op jit(solution)/shard_map/ppermute | solution.py:207
  136.2 2.9 %collective-permute-start.13 = (bf16[128,2048]{1,0:T(8,128)(2,1)S(1)}, bf16[128,2048]{1,0:T(8,128)(2,1)S(1)}, u32[]{:S(2)}, u32[]{:S(2)}) collective-permute-start(bf16[128,2048]{1,0:T(8,128)(2,1)S(1)} %convolution_convert_fusion.9), channel_id=1, source_target_pairs={{0,4},{4,8},{8,12},{12,0},{1,5},{5,9},{9,13},{13,1},{2,6},{6,10},{... | collective-permute-start | bytes 1572872 | tf_op jit(solution)/shard_map/ppermute | solution.py:36
  140.0 4.8 %fusion.4 = bf16[4,128,2048]{2,1,0:T(8,128)(2,1)S(1)} fusion(bf16[4,128,2048]{2,1,0:T(8,128)(2,1)S(1)} %broadcast_in_dim.63, s32[]{:T(128)S(6)} %select_n.166, bf16[128,2048]{1,0:T(8,128)(2,1)S(1)} %convolution_convert_fusion.9, bf16[2048,2048]{1,0:T(8,128)(2,1)} %param.14), kind=kOutput, calls=%fused_computation.14 | convolution fusion | flops 1074003968 | bytes 9437188 | tf_op jit(solution)/shard_map/dot_general | solution.py:222
  144.8 6.7 %collective-permute-done.13 = bf16[128,2048]{1,0:T(8,128)(2,1)S(1)} collective-permute-done((bf16[128,2048]{1,0:T(8,128)(2,1)S(1)}, bf16[128,2048]{1,0:T(8,128)(2,1)S(1)}, u32[]{:S(2)}, u32[]{:S(2)}) %collective-permute-start.13) | collective-permute-done | bytes 524320 | tf_op jit(solution)/shard_map/ppermute | solution.py:36
  152.8 31.0 %collective-permute-done.14 = bf16[128,2048]{1,0:T(8,128)(2,1)S(1)} collective-permute-done((bf16[128,2048]{1,0:T(8,128)(2,1)S(1)}, bf16[128,2048]{1,0:T(8,128)(2,1)S(1)}, u32[]{:S(2)}, u32[]{:S(2)}) %collective-permute-start.14) | collective-permute-done | bytes 524320 | tf_op jit(solution)/shard_map/ppermute | solution.py:36
  186.6 2.8 %collective-permute-done.16 = bf16[256,2048]{1,0:T(8,128)(2,1)} collective-permute-done((bf16[256,2048]{1,0:T(8,128)(2,1)S(1)}, bf16[256,2048]{1,0:T(8,128)(2,1)}, u32[]{:S(2)}, u32[]{:S(2)}) %collective-permute-start.16) | collective-permute-done | bytes 1048608 | tf_op jit(solution)/shard_map/ppermute | solution.py:47
  191.7 13.4 %collective-permute-done.17 = bf16[128,2048]{1,0:T(8,128)(2,1)S(1)} collective-permute-done((bf16[128,2048]{1,0:T(8,128)(2,1)S(1)}, bf16[128,2048]{1,0:T(8,128)(2,1)S(1)}, u32[]{:S(2)}, u32[]{:S(2)}) %collective-permute-start.17) | collective-permute-done | bytes 524320 | tf_op jit(solution)/shard_map/ppermute | solution.py:47
  205.2 1.9 collective-permute-start.18
  207.2 19.6 %collective-permute-done.18 = bf16[128,2048]{1,0:T(8,128)(2,1)S(1)} collective-permute-done((bf16[128,2048]{1,0:T(8,128)(2,1)S(1)}, bf16[128,2048]{1,0:T(8,128)(2,1)S(1)}, u32[]{:S(2)}, u32[]{:S(2)}) %collective-permute-start.18) | collective-permute-done | bytes 524320 | tf_op jit(solution)/shard_map/ppermute | solution.py:250
  226.8 2.0 add_convert_fusion
  (97 shorter events, 30.8 us)
Async XLA Ops:
  0.0 40.5 %copy-start = (f32[128]{0:T(128)S(1)}, f32[128]{0:T(128)}, u32[]{:S(2)}) copy-start(f32[128]{0:T(128)} %param.11) | copy-start | bytes 1540
  0.0 26.6 %copy-start.4 = (s32[4]{0:T(128)S(1)}, s32[4]{0:T(128)}, u32[]{:S(2)}) copy-start(s32[4]{0:T(128)} %param.17) | copy-start | bytes 52
  0.0 26.6 %copy-start.5 = (s32[128]{0:T(128)S(1)}, s32[128]{0:T(128)}, u32[]{:S(2)}) copy-start(s32[128]{0:T(128)} %param.15) | copy-start | bytes 1540
  0.0 26.8 %copy-start.6 = (s32[128]{0:T(128)S(1)}, s32[128]{0:T(128)}, u32[]{:S(2)}) copy-start(s32[128]{0:T(128)} %param.16) | copy-start | bytes 1540
  1.6 8.5 %collective-permute-start = (bf16[64,2048]{1,0:T(8,128)(2,1)S(1)}, bf16[64,2048]{1,0:T(8,128)(2,1)S(1)}, u32[]{:S(2)}, u32[]{:S(2)}) collective-permute-start(bf16[64,2048]{1,0:T(8,128)(2,1)S(1)} %get-tuple-element.10), channel_id=1, source_target_pairs={{0,4},{4,8},{8,12},{12,0},{1,5},{5,9},{9,13},{13,1},{2,6},{6,10},{... | collective-permute-start | bytes 786440 | tf_op jit(solution)/shard_map/ppermute | solution.py:134
  1.9 24.5 %collective-permute-start.1 = (bf16[64,2048]{1,0:T(8,128)(2,1)S(1)}, bf16[64,2048]{1,0:T(8,128)(2,1)S(1)}, u32[]{:S(2)}, u32[]{:S(2)}) collective-permute-start(bf16[64,2048]{1,0:T(8,128)(2,1)S(1)} %get-tuple-element.11), channel_id=1, source_target_pairs={{0,8},{4,12},{8,0},{12,4},{1,9},{5,13},{9,1},{13,5},{2,10},{6,14},... | collective-permute-start | bytes 786440 | tf_op jit(solution)/shard_map/ppermute | solution.py:134
  3.6 22.9 %collective-permute-start.2 = (bf16[64,2048]{1,0:T(8,128)(2,1)S(1)}, bf16[64,2048]{1,0:T(8,128)(2,1)S(1)}, u32[]{:S(2)}, u32[]{:S(2)}) collective-permute-start(bf16[64,2048]{1,0:T(8,128)(2,1)S(1)} %get-tuple-element.9), channel_id=1, source_target_pairs={{0,12},{4,0},{8,4},{12,8},{1,13},{5,1},{9,5},{13,9},{2,14},{6,2},{... | collective-permute-start | bytes 786440 | tf_op jit(solution)/shard_map/ppermute | solution.py:134
  26.5 2.7 %collective-permute-start.3 = (bf16[4,64,2048]{2,1,0:T(8,128)(2,1)S(1)}, bf16[4,64,2048]{2,1,0:T(8,128)(2,1)S(1)}, u32[]{:S(2)}, u32[]{:S(2)}) collective-permute-start(bf16[4,64,2048]{2,1,0:T(8,128)(2,1)S(1)} %bitcast_dynamic-update-slice_fusion.2), channel_id=1, source_target_pairs={{0,1},{1,0},{2,3},{3,2},{4,5},{5,4},{6,7},{7,6},{8,9},{9,8},{10,11... | collective-permute-start | bytes 3145736 | tf_op jit(solution)/shard_map/ppermute | solution.py:145
  34.2 14.8 %collective-permute-start.4 = (bf16[128,2048]{1,0:T(8,128)(2,1)S(1)}, bf16[128,2048]{1,0:T(8,128)(2,1)S(1)}, u32[]{:S(2)}, u32[]{:S(2)}) collective-permute-start(bf16[128,2048]{1,0:T(8,128)(2,1)S(1)} %convolution_convert_fusion.7), channel_id=1, source_target_pairs={{0,4},{4,8},{8,12},{12,0},{1,5},{5,9},{9,13},{13,1},{2,6},{6,10},{... | collective-permute-start | bytes 1572872 | tf_op jit(solution)/shard_map/ppermute | solution.py:24
  36.4 45.1 %collective-permute-start.5 = (bf16[128,2048]{1,0:T(8,128)(2,1)S(1)}, bf16[128,2048]{1,0:T(8,128)(2,1)S(1)}, u32[]{:S(2)}, u32[]{:S(2)}) collective-permute-start(bf16[128,2048]{1,0:T(8,128)(2,1)S(1)} %convolution_convert_fusion.6), channel_id=1, source_target_pairs={{0,8},{4,12},{8,0},{12,4},{1,9},{5,13},{9,1},{13,5},{2,10},{6,14},... | collective-permute-start | bytes 1572872 | tf_op jit(solution)/shard_map/ppermute | solution.py:24
  39.1 42.4 %collective-permute-start.6 = (bf16[128,2048]{1,0:T(8,128)(2,1)S(1)}, bf16[128,2048]{1,0:T(8,128)(2,1)S(1)}, u32[]{:S(2)}, u32[]{:S(2)}) collective-permute-start(bf16[128,2048]{1,0:T(8,128)(2,1)S(1)} %convolution_convert_fusion.5), channel_id=1, source_target_pairs={{0,12},{4,0},{8,4},{12,8},{1,13},{5,1},{9,5},{13,9},{2,14},{6,2},{... | collective-permute-start | bytes 1572872 | tf_op jit(solution)/shard_map/ppermute | solution.py:24
  86.2 14.6 %collective-permute-start.7 = (bf16[2,512,128]{2,1,0:T(8,128)(2,1)S(1)}, bf16[2,512,128]{2,1,0:T(8,128)(2,1)}, u32[]{:S(2)}, u32[]{:S(2)}) collective-permute-start(bf16[2,512,128]{2,1,0:T(8,128)(2,1)S(1)} %bitcast.125), channel_id=1, source_target_pairs={{0,4},{4,8},{8,12},{12,0},{1,5},{5,9},{9,13},{13,1},{2,6},{6,10},{... | collective-permute-start | bytes 786440 | tf_op jit(solution)/shard_map/ppermute | solution.py:193
  86.2 25.1 %collective-permute-start.9 = (bf16[2,512,128]{2,1,0:T(8,128)(2,1)S(1)}, bf16[2,512,128]{2,1,0:T(8,128)(2,1)}, u32[]{:S(2)}, u32[]{:S(2)}) collective-permute-start(bf16[2,512,128]{2,1,0:T(8,128)(2,1)S(1)} %bitcast.123), channel_id=1, source_target_pairs={{0,8},{4,12},{8,0},{12,4},{1,9},{5,13},{9,1},{13,5},{2,10},{6,14},... | collective-permute-start | bytes 786440 | tf_op jit(solution)/shard_map/ppermute | solution.py:193
  87.8 30.2 %collective-permute-start.11 = (bf16[2,512,128]{2,1,0:T(8,128)(2,1)S(1)}, bf16[2,512,128]{2,1,0:T(8,128)(2,1)}, u32[]{:S(2)}, u32[]{:S(2)}) collective-permute-start(bf16[2,512,128]{2,1,0:T(8,128)(2,1)S(1)} %bitcast.122), channel_id=1, source_target_pairs={{0,12},{4,0},{8,4},{12,8},{1,13},{5,1},{9,5},{13,9},{2,14},{6,2},{... | collective-permute-start | bytes 786440 | tf_op jit(solution)/shard_map/ppermute | solution.py:193
  107.6 17.9 %collective-permute-start.8 = (bf16[2,512,128]{2,1,0:T(8,128)(2,1)}, bf16[2,512,128]{2,1,0:T(8,128)(2,1)S(1)}, u32[]{:S(2)}, u32[]{:S(2)}) collective-permute-start(bf16[2,512,128]{2,1,0:T(8,128)(2,1)} %shard_map.92), channel_id=1, source_target_pairs={{0,12},{4,0},{8,4},{12,8},{1,13},{5,1},{9,5},{13,9},{2,14},{6,2},{... | collective-permute-start | bytes 786440 | tf_op jit(solution)/shard_map/ppermute | solution.py:207
  118.0 11.5 %collective-permute-start.10 = (bf16[2,512,128]{2,1,0:T(8,128)(2,1)}, bf16[2,512,128]{2,1,0:T(8,128)(2,1)S(1)}, u32[]{:S(2)}, u32[]{:S(2)}) collective-permute-start(bf16[2,512,128]{2,1,0:T(8,128)(2,1)} %shard_map.93), channel_id=1, source_target_pairs={{0,8},{4,12},{8,0},{12,4},{1,9},{5,13},{9,1},{13,5},{2,10},{6,14},... | collective-permute-start | bytes 786440 | tf_op jit(solution)/shard_map/ppermute | solution.py:207
  124.9 10.1 %collective-permute-start.12 = (bf16[2,512,128]{2,1,0:T(8,128)(2,1)}, bf16[2,512,128]{2,1,0:T(8,128)(2,1)S(1)}, u32[]{:S(2)}, u32[]{:S(2)}) collective-permute-start(bf16[2,512,128]{2,1,0:T(8,128)(2,1)} %shard_map.94), channel_id=1, source_target_pairs={{0,4},{4,8},{8,12},{12,0},{1,5},{5,9},{9,13},{13,1},{2,6},{6,10},{... | collective-permute-start | bytes 786440 | tf_op jit(solution)/shard_map/ppermute | solution.py:207
  136.2 15.3 %collective-permute-start.13 = (bf16[128,2048]{1,0:T(8,128)(2,1)S(1)}, bf16[128,2048]{1,0:T(8,128)(2,1)S(1)}, u32[]{:S(2)}, u32[]{:S(2)}) collective-permute-start(bf16[128,2048]{1,0:T(8,128)(2,1)S(1)} %convolution_convert_fusion.9), channel_id=1, source_target_pairs={{0,4},{4,8},{8,12},{12,0},{1,5},{5,9},{9,13},{13,1},{2,6},{6,10},{... | collective-permute-start | bytes 1572872 | tf_op jit(solution)/shard_map/ppermute | solution.py:36
  139.0 44.8 %collective-permute-start.14 = (bf16[128,2048]{1,0:T(8,128)(2,1)S(1)}, bf16[128,2048]{1,0:T(8,128)(2,1)S(1)}, u32[]{:S(2)}, u32[]{:S(2)}) collective-permute-start(bf16[128,2048]{1,0:T(8,128)(2,1)S(1)} %convolution_convert_fusion.9), channel_id=1, source_target_pairs={{0,8},{4,12},{8,0},{12,4},{1,9},{5,13},{9,1},{13,5},{2,10},{6,14},... | collective-permute-start | bytes 1572872 | tf_op jit(solution)/shard_map/ppermute | solution.py:36
  139.0 46.1 %collective-permute-start.15 = (bf16[128,2048]{1,0:T(8,128)(2,1)S(1)}, bf16[128,2048]{1,0:T(8,128)(2,1)S(1)}, u32[]{:S(2)}, u32[]{:S(2)}) collective-permute-start(bf16[128,2048]{1,0:T(8,128)(2,1)S(1)} %convolution_convert_fusion.9), channel_id=1, source_target_pairs={{0,12},{4,0},{8,4},{12,8},{1,13},{5,1},{9,5},{13,9},{2,14},{6,2},{... | collective-permute-start | bytes 1572872 | tf_op jit(solution)/shard_map/ppermute | solution.py:36
  139.7 11.8 %slice-start = ((s8[8388608]{0:T(1024)(128)(4,1)}), s8[4194304]{0:T(1024)(128)(4,1)S(1)}, s32[]{:S(2)}) async-start(s8[8388608]{0:T(1024)(128)(4,1)} %bitcast.90), calls=%async_computation | async-start | bytes 8388608
  186.5 2.9 %collective-permute-start.16 = (bf16[256,2048]{1,0:T(8,128)(2,1)S(1)}, bf16[256,2048]{1,0:T(8,128)(2,1)}, u32[]{:S(2)}, u32[]{:S(2)}) collective-permute-start(bf16[256,2048]{1,0:T(8,128)(2,1)S(1)} %dynamic-slice_bitcast_fusion), channel_id=1, source_target_pairs={{0,1},{1,0},{2,3},{3,2},{4,5},{5,4},{6,7},{7,6},{8,9},{9,8},{10,11... | collective-permute-start | bytes 3145736 | tf_op jit(solution)/shard_map/ppermute | solution.py:47
  191.1 14.0 %collective-permute-start.17 = (bf16[128,2048]{1,0:T(8,128)(2,1)S(1)}, bf16[128,2048]{1,0:T(8,128)(2,1)S(1)}, u32[]{:S(2)}, u32[]{:S(2)}) collective-permute-start(bf16[128,2048]{1,0:T(8,128)(2,1)S(1)} %dynamic-slice_bitcast_fusion.1), channel_id=1, source_target_pairs={{0,2},{2,0},{1,3},{3,1},{4,6},{6,4},{5,7},{7,5},{8,10},{10,8},{9,1... | collective-permute-start | bytes 1572872 | tf_op jit(solution)/shard_map/ppermute | solution.py:47
  205.2 21.5 %collective-permute-start.18 = (bf16[128,2048]{1,0:T(8,128)(2,1)S(1)}, bf16[128,2048]{1,0:T(8,128)(2,1)S(1)}, u32[]{:S(2)}, u32[]{:S(2)}) collective-permute-start(bf16[128,2048]{1,0:T(8,128)(2,1)S(1)} %fusion.16), channel_id=1, source_target_pairs={{0,0},{1,8},{2,4},{3,12},{4,1},{5,9},{6,5},{7,13},{8,2},{9,10},{10... | collective-permute-start | bytes 1572872 | tf_op jit(solution)/shard_map/ppermute | solution.py:250
  (6 other events, 39.1 us)

commit v22 on v19

--- a/solution.py
+++ b/solution.py
@@ -233,9 +233,12 @@
     out_block = partial_cols.shape[1]
     sub_sums = sub_sums.reshape(head_count, per_hs, local_rows, out_block)
     head_index = lax.axis_index("head")
-    head_total = jnp.zeros((local_rows, per_hs * out_block), jnp.float32)
+    out_width = per_hs * out_block
+    residual = lax.dynamic_slice_in_dim(hidden_in, hs_index * out_width, out_width, 1)
+    head_total = jnp.zeros((local_rows, out_width), jnp.float32)
     for step in range(per_hs):
-        gathered = None
+        offset = ((req_index % per_hs - step) % per_hs) * out_block
+        gathered = lax.dynamic_slice_in_dim(residual, offset, out_block, 1).astype(jnp.float32)
         for turn in range(head_count):
             group = (head_index + turn) % head_count
             chunk = lax.dynamic_index_in_dim(sub_sums, group, 0, keepdims=False)
@@ -251,14 +254,9 @@
                         src = c * hs_count + h * sub_count + u
                         pairs.append((src, k * hs_count + c // per_hs))
             got = lax.ppermute(chunk, ("req", "head", "sub"), pairs).astype(jnp.float32)
-            gathered = got if gathered is None else gathered + got
-        head_total = lax.dynamic_update_slice_in_dim(
-            head_total, gathered, ((req_index % per_hs - step) % per_hs) * out_block, 1
-        )
-    head_total = head_total.astype(jnp.float32)
-    out_width = head_total.shape[1]
-    residual = lax.dynamic_slice_in_dim(hidden_in, hs_index * out_width, out_width, 1)
-    return (residual.astype(jnp.float32) + head_total).astype(jnp.bfloat16)
+            gathered = gathered + got
+        head_total = lax.dynamic_update_slice_in_dim(head_total, gathered, offset, 1)
+    return head_total.astype(jnp.bfloat16)
 
 
 def solution(mesh):

time: 223 us -> 223 us (level)
  no operation moved by 1% of the time
where the time goes in v22:
time: 223 us; the launch traced here: 222 us
  waiting for transfers between devices  109 us (49%)
  starting transfers between devices  51 us (23%)
  Pallas kernels  27.1 us (12%)
  matrix products  18.6 us (8%)
  local copies, waits for them, and re-layouts  11.2 us (5%)
  other arithmetic  4.94 us (2%)
    ppermute x3, waiting for transfers between devices, direct_reduce_scatter(): lax.ppermute(outgoing, axis, [(i, (i + shift) % count) for i in range(cou...  29.7 us
    pallas_call x4, Pallas kernels, attend(): pl.pallas_call(kernel, grid=(kv_count,), in_specs=[pl.BlockSpec((1, stack...  27.1 us
    ppermute x3, waiting for transfers between devices, direct_gather_apply(): lax.ppermute(block, axis, [(i, (i + shift) % count) for i in range(count)])  26.4 us
    ppermute x2, waiting for transfers between devices, local(): got = lax.ppermute(chunk, ('req', 'head', 'sub'), pairs).astype(jnp.float32)  25.4 us
    ppermute x3, waiting for transfers between devices, local(): lax.ppermute(my_block((req_index + shift) % req_count), 'req', [(i, (i +...  14.5 us
    ppermute x3, starting transfers between devices, local(): lax.ppermute(outgoing[shift], 'req', [(i, (i + shift) % req_count) for i...  14.1 us
    ppermute x2, starting transfers between devices, local(): got = lax.ppermute(chunk, ('req', 'head', 'sub'), pairs).astype(jnp.float32)  11.7 us
    ppermute x3, starting transfers between devices, direct_reduce_scatter(): lax.ppermute(outgoing, axis, [(i, (i + shift) % count) for i in range(cou...  9.44 us
  transfers between devices with their start and end apart: 19, of which 11 were waited for; matrix products, arithmetic and copies ran while one was open for 8% of the time, Pallas kernels for 12%

profile of v22, /device:TPU:6, one launch (start us, length us, event | category | flops | bytes accessed | tf_op | source)
XLA Modules:
  0.0 222.0 jit_solution(16831303110723377804)
XLA Ops:
  3.3 2.6 %collective-permute-start.1 = (bf16[64,2048]{1,0:T(8,128)(2,1)S(1)}, bf16[64,2048]{1,0:T(8,128)(2,1)S(1)}, u32[]{:S(2)}, u32[]{:S(2)}) collective-permute-start(bf16[64,2048]{1,0:T(8,128)(2,1)S(1)} %get-tuple-element.11), channel_id=1, source_target_pairs={{0,8},{4,12},{8,0},{12,4},{1,9},{5,13},{9,1},{13,5},{2,10},{6,14},... | collective-permute-start | bytes 786440 | tf_op jit(solution)/shard_map/ppermute | solution.py:134
  8.5 4.4 %collective-permute-done = bf16[64,2048]{1,0:T(8,128)(2,1)S(1)} collective-permute-done((bf16[64,2048]{1,0:T(8,128)(2,1)S(1)}, bf16[64,2048]{1,0:T(8,128)(2,1)S(1)}, u32[]{:S(2)}, u32[]{:S(2)}) %collective-permute-start) | collective-permute-done | bytes 262176 | tf_op jit(solution)/shard_map/ppermute | solution.py:134
  12.8 10.1 %collective-permute-done.1 = bf16[64,2048]{1,0:T(8,128)(2,1)S(1)} collective-permute-done((bf16[64,2048]{1,0:T(8,128)(2,1)S(1)}, bf16[64,2048]{1,0:T(8,128)(2,1)S(1)}, u32[]{:S(2)}, u32[]{:S(2)}) %collective-permute-start.1) | collective-permute-done | bytes 262176 | tf_op jit(solution)/shard_map/ppermute | solution.py:134
  25.9 4.8 %convolution_convert_fusion.7 = bf16[128,2048]{1,0:T(8,128)(2,1)S(1)} fusion(bf16[2048,2048]{1,0:T(8,128)(2,1)} %param.10, bf16[512,2048]{1,0:T(8,128)(2,1)S(1)} %bitcast.95, s32[]{:T(128)S(6)} %select_n.194), kind=kOutput, calls=%fused_computation.7 | convolution fusion | flops 1074003968 | bytes 9437188 | tf_op jit(solution)/shard_map/dot_general | solution.py:154
  30.7 6.1 %collective-permute-start.4 = (bf16[128,2048]{1,0:T(8,128)(2,1)S(1)}, bf16[128,2048]{1,0:T(8,128)(2,1)S(1)}, u32[]{:S(2)}, u32[]{:S(2)}) collective-permute-start(bf16[128,2048]{1,0:T(8,128)(2,1)S(1)} %convolution_convert_fusion.7), channel_id=1, source_target_pairs={{0,4},{4,8},{8,12},{12,0},{1,5},{5,9},{9,13},{13,1},{2,6},{6,10},{... | collective-permute-start | bytes 1572872 | tf_op jit(solution)/shard_map/ppermute | solution.py:24
  43.0 7.7 %collective-permute-done.4 = bf16[128,2048]{1,0:T(8,128)(2,1)S(1)} collective-permute-done((bf16[128,2048]{1,0:T(8,128)(2,1)S(1)}, bf16[128,2048]{1,0:T(8,128)(2,1)S(1)}, u32[]{:S(2)}, u32[]{:S(2)}) %collective-permute-start.4) | collective-permute-done | bytes 524320 | tf_op jit(solution)/shard_map/ppermute | solution.py:24
  50.7 22.0 %collective-permute-done.5 = bf16[128,2048]{1,0:T(8,128)(2,1)S(1)} collective-permute-done((bf16[128,2048]{1,0:T(8,128)(2,1)S(1)}, bf16[128,2048]{1,0:T(8,128)(2,1)S(1)}, u32[]{:S(2)}, u32[]{:S(2)}) %collective-permute-start.5) | collective-permute-done | bytes 524320 | tf_op jit(solution)/shard_map/ppermute | solution.py:24
  77.4 11.7 %collective-permute-start.7 = (bf16[2,512,128]{2,1,0:T(8,128)(2,1)S(1)}, bf16[2,512,128]{2,1,0:T(8,128)(2,1)}, u32[]{:S(2)}, u32[]{:S(2)}) collective-permute-start(bf16[2,512,128]{2,1,0:T(8,128)(2,1)S(1)} %bitcast.123), channel_id=1, source_target_pairs={{0,4},{4,8},{8,12},{12,0},{1,5},{5,9},{9,13},{13,1},{2,6},{6,10},{... | collective-permute-start | bytes 786440 | tf_op jit(solution)/shard_map/ppermute | solution.py:193
  95.6 6.8 %shard_map.91 = bf16[2,512,128]{2,1,0:T(8,128)(2,1)} custom-call(bf16[2,512,128]{2,1,0:T(8,128)(2,1)} %bitcast.122, bf16[2,1664,128]{2,1,0:T(8,128)(2,1)} %bitcast.108, bf16[2,1664,128]{2,1,0:T(8,128)(2,1)} %bitcast.112), custom_call_target="tpu_custom_call" | custom-call | flops 872415232 | bytes 2228224 | tf_op jit(solution)/shard_map/pallas_call | solution.py:86
  102.4 6.8 %shard_map.92 = bf16[2,512,128]{2,1,0:T(8,128)(2,1)} custom-call(bf16[2,512,128]{2,1,0:T(8,128)(2,1)} %collective-permute-done.7.q_ref, bf16[2,1664,128]{2,1,0:T(8,128)(2,1)} %bitcast.109, bf16[2,1664,128]{2,1,0:T(8,128)(2,1)} %bitcast.113), custom_call_target="tpu_custom_call" | custom-call | flops 872415232 | bytes 2228224 | tf_op jit(solution)/shard_map/pallas_call | solution.py:86
  109.2 2.0 collective-permute-start.8
  111.2 6.8 %shard_map.93 = bf16[2,512,128]{2,1,0:T(8,128)(2,1)} custom-call(bf16[2,512,128]{2,1,0:T(8,128)(2,1)} %collective-permute-done.9.q_ref, bf16[2,1664,128]{2,1,0:T(8,128)(2,1)} %bitcast.110, bf16[2,1664,128]{2,1,0:T(8,128)(2,1)} %bitcast.114), custom_call_target="tpu_custom_call" | custom-call | flops 872415232 | bytes 2228224 | tf_op jit(solution)/shard_map/pallas_call | solution.py:86
  118.3 6.8 %shard_map.94 = bf16[2,512,128]{2,1,0:T(8,128)(2,1)} custom-call(bf16[2,512,128]{2,1,0:T(8,128)(2,1)} %collective-permute-done.11.q_ref, bf16[2,1664,128]{2,1,0:T(8,128)(2,1)} %bitcast.111, bf16[2,1664,128]{2,1,0:T(8,128)(2,1)} %bitcast.115), custom_call_target="tpu_custom_call" | custom-call | flops 872415232 | bytes 2228224 | tf_op jit(solution)/shard_map/pallas_call | solution.py:86
  125.1 3.9 %collective-permute-start.12 = (bf16[2,512,128]{2,1,0:T(8,128)(2,1)}, bf16[2,512,128]{2,1,0:T(8,128)(2,1)S(1)}, u32[]{:S(2)}, u32[]{:S(2)}) collective-permute-start(bf16[2,512,128]{2,1,0:T(8,128)(2,1)} %shard_map.94), channel_id=1, source_target_pairs={{0,4},{4,8},{8,12},{12,0},{1,5},{5,9},{9,13},{13,1},{2,6},{6,10},{... | collective-permute-start | bytes 786440 | tf_op jit(solution)/shard_map/ppermute | solution.py:207
  129.4 8.1 %collective-permute-done.10 = bf16[2,512,128]{2,1,0:T(8,128)(2,1)S(1)} collective-permute-done((bf16[2,512,128]{2,1,0:T(8,128)(2,1)}, bf16[2,512,128]{2,1,0:T(8,128)(2,1)S(1)}, u32[]{:S(2)}, u32[]{:S(2)}) %collective-permute-start.10) | collective-permute-done | bytes 262176 | tf_op jit(solution)/shard_map/ppermute | solution.py:207
  140.4 2.3 %collective-permute-start.15 = (bf16[128,2048]{1,0:T(8,128)(2,1)S(1)}, bf16[128,2048]{1,0:T(8,128)(2,1)S(1)}, u32[]{:S(2)}, u32[]{:S(2)}) collective-permute-start(bf16[128,2048]{1,0:T(8,128)(2,1)S(1)} %convolution_convert_fusion.9), channel_id=1, source_target_pairs={{0,12},{4,0},{8,4},{12,8},{1,13},{5,1},{9,5},{13,9},{2,14},{6,2},{... | collective-permute-start | bytes 1572872 | tf_op jit(solution)/shard_map/ppermute | solution.py:36
  142.9 4.8 %fusion.4 = bf16[4,128,2048]{2,1,0:T(8,128)(2,1)S(1)} fusion(bf16[4,128,2048]{2,1,0:T(8,128)(2,1)S(1)} %broadcast_in_dim.63, s32[]{:T(128)S(6)} %select_n.174, bf16[128,2048]{1,0:T(8,128)(2,1)S(1)} %convolution_convert_fusion.9, bf16[2048,2048]{1,0:T(8,128)(2,1)} %param.14), kind=kOutput, calls=%fused_computation.14 | convolution fusion | flops 1074003968 | bytes 9437188 | tf_op jit(solution)/shard_map/dot_general | solution.py:222
  147.8 7.8 %collective-permute-done.13 = bf16[128,2048]{1,0:T(8,128)(2,1)S(1)} collective-permute-done((bf16[128,2048]{1,0:T(8,128)(2,1)S(1)}, bf16[128,2048]{1,0:T(8,128)(2,1)S(1)}, u32[]{:S(2)}, u32[]{:S(2)}) %collective-permute-start.13) | collective-permute-done | bytes 524320 | tf_op jit(solution)/shard_map/ppermute | solution.py:36
  156.9 18.6 %collective-permute-done.14 = bf16[128,2048]{1,0:T(8,128)(2,1)S(1)} collective-permute-done((bf16[128,2048]{1,0:T(8,128)(2,1)S(1)}, bf16[128,2048]{1,0:T(8,128)(2,1)S(1)}, u32[]{:S(2)}, u32[]{:S(2)}) %collective-permute-start.14) | collective-permute-done | bytes 524320 | tf_op jit(solution)/shard_map/ppermute | solution.py:36
  178.3 2.8 %collective-permute-done.16 = bf16[256,2048]{1,0:T(8,128)(2,1)} collective-permute-done((bf16[256,2048]{1,0:T(8,128)(2,1)S(1)}, bf16[256,2048]{1,0:T(8,128)(2,1)}, u32[]{:S(2)}, u32[]{:S(2)}) %collective-permute-start.16) | collective-permute-done | bytes 1048608 | tf_op jit(solution)/shard_map/ppermute | solution.py:47
  182.8 11.6 %collective-permute-start.17 = (bf16[128,2048]{1,0:T(8,128)(2,1)S(1)}, bf16[128,2048]{1,0:T(8,128)(2,1)S(1)}, u32[]{:S(2)}, u32[]{:S(2)}) collective-permute-start(bf16[128,2048]{1,0:T(8,128)(2,1)S(1)} %get-tuple-element.12), channel_id=1, source_target_pairs={{0,0},{1,8},{2,4},{3,12},{4,1},{5,9},{6,5},{7,13},{8,2},{9,10},{10... | collective-permute-start | bytes 1572872 | tf_op jit(solution)/shard_map/ppermute | solution.py:256
  194.5 10.6 %collective-permute-done.17 = bf16[128,2048]{1,0:T(8,128)(2,1)S(1)} collective-permute-done((bf16[128,2048]{1,0:T(8,128)(2,1)S(1)}, bf16[128,2048]{1,0:T(8,128)(2,1)S(1)}, u32[]{:S(2)}, u32[]{:S(2)}) %collective-permute-start.17) | collective-permute-done | bytes 524320 | tf_op jit(solution)/shard_map/ppermute | solution.py:256
  205.1 14.8 %collective-permute-done.18 = bf16[128,2048]{1,0:T(8,128)(2,1)S(1)} collective-permute-done((bf16[128,2048]{1,0:T(8,128)(2,1)S(1)}, bf16[128,2048]{1,0:T(8,128)(2,1)S(1)}, u32[]{:S(2)}, u32[]{:S(2)}) %collective-permute-start.18) | collective-permute-done | bytes 524320 | tf_op jit(solution)/shard_map/ppermute | solution.py:256
  219.9 2.1 add_convert_fusion
  (96 shorter events, 35.6 us)
Async XLA Ops:
  0.0 42.9 %copy-start = (f32[128]{0:T(128)S(1)}, f32[128]{0:T(128)}, u32[]{:S(2)}) copy-start(f32[128]{0:T(128)} %param.11) | copy-start | bytes 1540
  0.0 23.1 %copy-start.4 = (s32[4]{0:T(128)S(1)}, s32[4]{0:T(128)}, u32[]{:S(2)}) copy-start(s32[4]{0:T(128)} %param.17) | copy-start | bytes 52
  0.0 23.1 %copy-start.5 = (s32[128]{0:T(128)S(1)}, s32[128]{0:T(128)}, u32[]{:S(2)}) copy-start(s32[128]{0:T(128)} %param.15) | copy-start | bytes 1540
  0.0 23.3 %copy-start.6 = (s32[128]{0:T(128)S(1)}, s32[128]{0:T(128)}, u32[]{:S(2)}) copy-start(s32[128]{0:T(128)} %param.16) | copy-start | bytes 1540
  1.6 11.2 %collective-permute-start = (bf16[64,2048]{1,0:T(8,128)(2,1)S(1)}, bf16[64,2048]{1,0:T(8,128)(2,1)S(1)}, u32[]{:S(2)}, u32[]{:S(2)}) collective-permute-start(bf16[64,2048]{1,0:T(8,128)(2,1)S(1)} %get-tuple-element.10), channel_id=1, source_target_pairs={{0,4},{4,8},{8,12},{12,0},{1,5},{5,9},{9,13},{13,1},{2,6},{6,10},{... | collective-permute-start | bytes 786440 | tf_op jit(solution)/shard_map/ppermute | solution.py:134
  3.3 19.7 %collective-permute-start.1 = (bf16[64,2048]{1,0:T(8,128)(2,1)S(1)}, bf16[64,2048]{1,0:T(8,128)(2,1)S(1)}, u32[]{:S(2)}, u32[]{:S(2)}) collective-permute-start(bf16[64,2048]{1,0:T(8,128)(2,1)S(1)} %get-tuple-element.11), channel_id=1, source_target_pairs={{0,8},{4,12},{8,0},{12,4},{1,9},{5,13},{9,1},{13,5},{2,10},{6,14},... | collective-permute-start | bytes 786440 | tf_op jit(solution)/shard_map/ppermute | solution.py:134
  5.9 17.1 %collective-permute-start.2 = (bf16[64,2048]{1,0:T(8,128)(2,1)S(1)}, bf16[64,2048]{1,0:T(8,128)(2,1)S(1)}, u32[]{:S(2)}, u32[]{:S(2)}) collective-permute-start(bf16[64,2048]{1,0:T(8,128)(2,1)S(1)} %get-tuple-element.9), channel_id=1, source_target_pairs={{0,12},{4,0},{8,4},{12,8},{1,13},{5,1},{9,5},{13,9},{2,14},{6,2},{... | collective-permute-start | bytes 786440 | tf_op jit(solution)/shard_map/ppermute | solution.py:134
  23.0 2.7 %collective-permute-start.3 = (bf16[4,64,2048]{2,1,0:T(8,128)(2,1)S(1)}, bf16[4,64,2048]{2,1,0:T(8,128)(2,1)S(1)}, u32[]{:S(2)}, u32[]{:S(2)}) collective-permute-start(bf16[4,64,2048]{2,1,0:T(8,128)(2,1)S(1)} %bitcast_dynamic-update-slice_fusion.2), channel_id=1, source_target_pairs={{0,1},{1,0},{2,3},{3,2},{4,5},{5,4},{6,7},{7,6},{8,9},{9,8},{10,11... | collective-permute-start | bytes 3145736 | tf_op jit(solution)/shard_map/ppermute | solution.py:145
  30.7 20.0 %collective-permute-start.4 = (bf16[128,2048]{1,0:T(8,128)(2,1)S(1)}, bf16[128,2048]{1,0:T(8,128)(2,1)S(1)}, u32[]{:S(2)}, u32[]{:S(2)}) collective-permute-start(bf16[128,2048]{1,0:T(8,128)(2,1)S(1)} %convolution_convert_fusion.7), channel_id=1, source_target_pairs={{0,4},{4,8},{8,12},{12,0},{1,5},{5,9},{9,13},{13,1},{2,6},{6,10},{... | collective-permute-start | bytes 1572872 | tf_op jit(solution)/shard_map/ppermute | solution.py:24
  38.1 34.6 %collective-permute-start.5 = (bf16[128,2048]{1,0:T(8,128)(2,1)S(1)}, bf16[128,2048]{1,0:T(8,128)(2,1)S(1)}, u32[]{:S(2)}, u32[]{:S(2)}) collective-permute-start(bf16[128,2048]{1,0:T(8,128)(2,1)S(1)} %convolution_convert_fusion.6), channel_id=1, source_target_pairs={{0,8},{4,12},{8,0},{12,4},{1,9},{5,13},{9,1},{13,5},{2,10},{6,14},... | collective-permute-start | bytes 1572872 | tf_op jit(solution)/shard_map/ppermute | solution.py:24
  41.1 31.6 %collective-permute-start.6 = (bf16[128,2048]{1,0:T(8,128)(2,1)S(1)}, bf16[128,2048]{1,0:T(8,128)(2,1)S(1)}, u32[]{:S(2)}, u32[]{:S(2)}) collective-permute-start(bf16[128,2048]{1,0:T(8,128)(2,1)S(1)} %convolution_convert_fusion.5), channel_id=1, source_target_pairs={{0,12},{4,0},{8,4},{12,8},{1,13},{5,1},{9,5},{13,9},{2,14},{6,2},{... | collective-permute-start | bytes 1572872 | tf_op jit(solution)/shard_map/ppermute | solution.py:24
  76.3 15.1 %copy-start.1 = (bf16[1,1601,512]{2,1,0:T(8,128)(2,1)S(1)}, bf16[1,1601,512]{2,1,0:T(8,128)(2,1)}, u32[]{:S(2)}) copy-start(bf16[1,1601,512]{2,1,0:T(8,128)(2,1)} %param.13) | copy-start | bytes 4918276
  77.4 25.0 %collective-permute-start.7 = (bf16[2,512,128]{2,1,0:T(8,128)(2,1)S(1)}, bf16[2,512,128]{2,1,0:T(8,128)(2,1)}, u32[]{:S(2)}, u32[]{:S(2)}) collective-permute-start(bf16[2,512,128]{2,1,0:T(8,128)(2,1)S(1)} %bitcast.123), channel_id=1, source_target_pairs={{0,4},{4,8},{8,12},{12,0},{1,5},{5,9},{9,13},{13,1},{2,6},{6,10},{... | collective-permute-start | bytes 786440 | tf_op jit(solution)/shard_map/ppermute | solution.py:193
  89.1 22.1 %collective-permute-start.9 = (bf16[2,512,128]{2,1,0:T(8,128)(2,1)S(1)}, bf16[2,512,128]{2,1,0:T(8,128)(2,1)}, u32[]{:S(2)}, u32[]{:S(2)}) collective-permute-start(bf16[2,512,128]{2,1,0:T(8,128)(2,1)S(1)} %bitcast.121), channel_id=1, source_target_pairs={{0,8},{4,12},{8,0},{12,4},{1,9},{5,13},{9,1},{13,5},{2,10},{6,14},... | collective-permute-start | bytes 786440 | tf_op jit(solution)/shard_map/ppermute | solution.py:193
  90.3 28.0 %collective-permute-start.11 = (bf16[2,512,128]{2,1,0:T(8,128)(2,1)S(1)}, bf16[2,512,128]{2,1,0:T(8,128)(2,1)}, u32[]{:S(2)}, u32[]{:S(2)}) collective-permute-start(bf16[2,512,128]{2,1,0:T(8,128)(2,1)S(1)} %bitcast.120), channel_id=1, source_target_pairs={{0,12},{4,0},{8,4},{12,8},{1,13},{5,1},{9,5},{13,9},{2,14},{6,2},{... | collective-permute-start | bytes 786440 | tf_op jit(solution)/shard_map/ppermute | solution.py:193
  109.2 20.0 %collective-permute-start.8 = (bf16[2,512,128]{2,1,0:T(8,128)(2,1)}, bf16[2,512,128]{2,1,0:T(8,128)(2,1)S(1)}, u32[]{:S(2)}, u32[]{:S(2)}) collective-permute-start(bf16[2,512,128]{2,1,0:T(8,128)(2,1)} %shard_map.92), channel_id=1, source_target_pairs={{0,12},{4,0},{8,4},{12,8},{1,13},{5,1},{9,5},{13,9},{2,14},{6,2},{... | collective-permute-start | bytes 786440 | tf_op jit(solution)/shard_map/ppermute | solution.py:207
  118.0 19.5 %collective-permute-start.10 = (bf16[2,512,128]{2,1,0:T(8,128)(2,1)}, bf16[2,512,128]{2,1,0:T(8,128)(2,1)S(1)}, u32[]{:S(2)}, u32[]{:S(2)}) collective-permute-start(bf16[2,512,128]{2,1,0:T(8,128)(2,1)} %shard_map.93), channel_id=1, source_target_pairs={{0,8},{4,12},{8,0},{12,4},{1,9},{5,13},{9,1},{13,5},{2,10},{6,14},... | collective-permute-start | bytes 786440 | tf_op jit(solution)/shard_map/ppermute | solution.py:207
  125.1 12.5 %collective-permute-start.12 = (bf16[2,512,128]{2,1,0:T(8,128)(2,1)}, bf16[2,512,128]{2,1,0:T(8,128)(2,1)S(1)}, u32[]{:S(2)}, u32[]{:S(2)}) collective-permute-start(bf16[2,512,128]{2,1,0:T(8,128)(2,1)} %shard_map.94), channel_id=1, source_target_pairs={{0,4},{4,8},{8,12},{12,0},{1,5},{5,9},{9,13},{13,1},{2,6},{6,10},{... | collective-permute-start | bytes 786440 | tf_op jit(solution)/shard_map/ppermute | solution.py:207
  138.8 16.8 %collective-permute-start.13 = (bf16[128,2048]{1,0:T(8,128)(2,1)S(1)}, bf16[128,2048]{1,0:T(8,128)(2,1)S(1)}, u32[]{:S(2)}, u32[]{:S(2)}) collective-permute-start(bf16[128,2048]{1,0:T(8,128)(2,1)S(1)} %convolution_convert_fusion.9), channel_id=1, source_target_pairs={{0,4},{4,8},{8,12},{12,0},{1,5},{5,9},{9,13},{13,1},{2,6},{6,10},{... | collective-permute-start | bytes 1572872 | tf_op jit(solution)/shard_map/ppermute | solution.py:36
  138.9 36.6 %collective-permute-start.14 = (bf16[128,2048]{1,0:T(8,128)(2,1)S(1)}, bf16[128,2048]{1,0:T(8,128)(2,1)S(1)}, u32[]{:S(2)}, u32[]{:S(2)}) collective-permute-start(bf16[128,2048]{1,0:T(8,128)(2,1)S(1)} %convolution_convert_fusion.9), channel_id=1, source_target_pairs={{0,8},{4,12},{8,0},{12,4},{1,9},{5,13},{9,1},{13,5},{2,10},{6,14},... | collective-permute-start | bytes 1572872 | tf_op jit(solution)/shard_map/ppermute | solution.py:36
  140.4 36.4 %collective-permute-start.15 = (bf16[128,2048]{1,0:T(8,128)(2,1)S(1)}, bf16[128,2048]{1,0:T(8,128)(2,1)S(1)}, u32[]{:S(2)}, u32[]{:S(2)}) collective-permute-start(bf16[128,2048]{1,0:T(8,128)(2,1)S(1)} %convolution_convert_fusion.9), channel_id=1, source_target_pairs={{0,12},{4,0},{8,4},{12,8},{1,13},{5,1},{9,5},{13,9},{2,14},{6,2},{... | collective-permute-start | bytes 1572872 | tf_op jit(solution)/shard_map/ppermute | solution.py:36
  178.2 2.9 %collective-permute-start.16 = (bf16[256,2048]{1,0:T(8,128)(2,1)S(1)}, bf16[256,2048]{1,0:T(8,128)(2,1)}, u32[]{:S(2)}, u32[]{:S(2)}) collective-permute-start(bf16[256,2048]{1,0:T(8,128)(2,1)S(1)} %dynamic-slice_bitcast_fusion), channel_id=1, source_target_pairs={{0,1},{1,0},{2,3},{3,2},{4,5},{5,4},{6,7},{7,6},{8,9},{9,8},{10,11... | collective-permute-start | bytes 3145736 | tf_op jit(solution)/shard_map/ppermute | solution.py:47
  182.8 22.3 %collective-permute-start.17 = (bf16[128,2048]{1,0:T(8,128)(2,1)S(1)}, bf16[128,2048]{1,0:T(8,128)(2,1)S(1)}, u32[]{:S(2)}, u32[]{:S(2)}) collective-permute-start(bf16[128,2048]{1,0:T(8,128)(2,1)S(1)} %get-tuple-element.12), channel_id=1, source_target_pairs={{0,0},{1,8},{2,4},{3,12},{4,1},{5,9},{6,5},{7,13},{8,2},{9,10},{10... | collective-permute-start | bytes 1572872 | tf_op jit(solution)/shard_map/ppermute | solution.py:256
  194.4 25.5 %collective-permute-start.18 = (bf16[128,2048]{1,0:T(8,128)(2,1)S(1)}, bf16[128,2048]{1,0:T(8,128)(2,1)S(1)}, u32[]{:S(2)}, u32[]{:S(2)}) collective-permute-start(bf16[128,2048]{1,0:T(8,128)(2,1)S(1)} %get-tuple-element.13), channel_id=1, source_target_pairs={{0,4},{1,12},{2,0},{3,8},{4,5},{5,13},{6,1},{7,9},{8,6},{9,14},{10... | collective-permute-start | bytes 1572872 | tf_op jit(solution)/shard_map/ppermute | solution.py:256
  (6 other events, 73.8 us)

commit v23 on v19

--- a/solution.py
+++ b/solution.py
@@ -18,13 +18,15 @@
 
 
 def direct_reduce_scatter(chunk_of, axis, count, index):
+    own = chunk_of(index)
     total = None
     for shift in range(1, count):
         outgoing = chunk_of((index + shift) % count).astype(jnp.bfloat16)
+        if shift == count - 1:
+            own, outgoing = lax.optimization_barrier((own, outgoing))
         incoming = lax.ppermute(outgoing, axis, [(i, (i + shift) % count) for i in range(count)])
         incoming = incoming.astype(jnp.float32)
         total = incoming if total is None else total + incoming
-    own = chunk_of(index)
     return own if total is None else own + total
 
 

time: 223 us -> 226 us (1.013)
  waiting for transfers between devices: 109 us -> 122 us
  starting transfers between devices: 51 us -> 39.7 us
    ppermute x3, waiting for transfers between devices: 29.7 us -> 42.5 us  [direct_reduce_scatter(): lax.ppermute(outgoing, axis, [(i, (i + shift) % count) for i in range(cou...]
    ppermute x3, starting transfers between devices: 14.1 us -> 3.99 us  [local(): lax.ppermute(outgoing[shift], 'req', [(i, (i + shift) % req_count) for i...]
  transfers between devices with their start and end apart: 19 -> 19, of which waited for: 11 -> 12; matrix products, arithmetic and copies ran while one was open for 8% -> 8% of each run, Pallas kernels for 12% -> 12%
where the time goes in v23:
time: 226 us; the launch traced here: 225 us
  waiting for transfers between devices  122 us (54%)
  starting transfers between devices  39.7 us (18%)
  Pallas kernels  27.1 us (12%)
  matrix products  18.3 us (8%)
  local copies, waits for them, and re-layouts  12.1 us (5%)
  other arithmetic  5.21 us (2%)
    ppermute x3, waiting for transfers between devices, direct_reduce_scatter(): lax.ppermute(outgoing, axis, [(i, (i + shift) % count) for i in range(cou...  42.5 us
    pallas_call x4, Pallas kernels, attend(): pl.pallas_call(kernel, grid=(kv_count,), in_specs=[pl.BlockSpec((1, stack...  27.1 us
    ppermute x3, waiting for transfers between devices, direct_gather_apply(): lax.ppermute(block, axis, [(i, (i + shift) % count) for i in range(count)])  26.4 us
    ppermute x2, waiting for transfers between devices, local(): got = lax.ppermute(chunk, ('req', 'head', 'sub'), pairs).astype(jnp.float32)  25.4 us
    ppermute x3, waiting for transfers between devices, local(): lax.ppermute(my_block((req_index + shift) % req_count), 'req', [(i, (i +...  14.5 us
    ppermute x2, starting transfers between devices, local(): got = lax.ppermute(chunk, ('req', 'head', 'sub'), pairs).astype(jnp.float32)  12.4 us
    ppermute x3, waiting for transfers between devices, local(): lax.ppermute(mixed_block, 'req', [(i, (i - shift) % req_count) for i in r...  8.8 us
    dot_general x4, matrix products, out_part(): product = jnp.dot(rows, out_weight, preferred_element_type=jnp.float32)  8.71 us
  transfers between devices with their start and end apart: 19, of which 12 were waited for; matrix products, arithmetic and copies ran while one was open for 8% of the time, Pallas kernels for 12%

profile of v23, /device:TPU:6, one launch (start us, length us, event | category | flops | bytes accessed | tf_op | source)
XLA Modules:
  0.0 225.1 jit_solution(10995029118434166158)
XLA Ops:
  3.3 2.6 %collective-permute-start.1 = (bf16[64,2048]{1,0:T(8,128)(2,1)S(1)}, bf16[64,2048]{1,0:T(8,128)(2,1)S(1)}, u32[]{:S(2)}, u32[]{:S(2)}) collective-permute-start(bf16[64,2048]{1,0:T(8,128)(2,1)S(1)} %get-tuple-element.15), channel_id=1, source_target_pairs={{0,8},{4,12},{8,0},{12,4},{1,9},{5,13},{9,1},{13,5},{2,10},{6,14},... | collective-permute-start | bytes 786440 | tf_op jit(solution)/shard_map/ppermute | solution.py:136
  8.5 4.4 %collective-permute-done = bf16[64,2048]{1,0:T(8,128)(2,1)S(1)} collective-permute-done((bf16[64,2048]{1,0:T(8,128)(2,1)S(1)}, bf16[64,2048]{1,0:T(8,128)(2,1)S(1)}, u32[]{:S(2)}, u32[]{:S(2)}) %collective-permute-start) | collective-permute-done | bytes 262176 | tf_op jit(solution)/shard_map/ppermute | solution.py:136
  12.8 10.1 %collective-permute-done.1 = bf16[64,2048]{1,0:T(8,128)(2,1)S(1)} collective-permute-done((bf16[64,2048]{1,0:T(8,128)(2,1)S(1)}, bf16[64,2048]{1,0:T(8,128)(2,1)S(1)}, u32[]{:S(2)}, u32[]{:S(2)}) %collective-permute-start.1) | collective-permute-done | bytes 262176 | tf_op jit(solution)/shard_map/ppermute | solution.py:136
  25.9 4.8 %fusion = f32[128,2048]{1,0:T(8,128)S(1)} fusion(bf16[2048,2048]{1,0:T(8,128)(2,1)} %param.10, bf16[512,2048]{1,0:T(8,128)(2,1)S(1)} %bitcast.95, s32[]{:T(128)S(6)} %select_n.192), kind=kOutput, calls=%fused_computation.9 | convolution fusion | flops 1074266112 | bytes 9961476 | tf_op jit(solution)/shard_map/dot_general | solution.py:156
  32.9 7.2 %collective-permute-start.6 = (bf16[128,2048]{1,0:T(8,128)(2,1)S(1)}, bf16[128,2048]{1,0:T(8,128)(2,1)S(1)}, u32[]{:S(2)}, u32[]{:S(2)}) collective-permute-start(bf16[128,2048]{1,0:T(8,128)(2,1)S(1)} %convolution_convert_fusion.7), channel_id=1, source_target_pairs={{0,12},{4,0},{8,4},{12,8},{1,13},{5,1},{9,5},{13,9},{2,14},{6,2},{... | collective-permute-start | bytes 1572872 | tf_op jit(solution)/shard_map/ppermute | solution.py:27
  43.6 8.8 %collective-permute-done.6 = bf16[128,2048]{1,0:T(8,128)(2,1)S(1)} collective-permute-done((bf16[128,2048]{1,0:T(8,128)(2,1)S(1)}, bf16[128,2048]{1,0:T(8,128)(2,1)S(1)}, u32[]{:S(2)}, u32[]{:S(2)}) %collective-permute-start.6) | collective-permute-done | bytes 524320 | tf_op jit(solution)/shard_map/ppermute | solution.py:27
  52.4 11.7 %collective-permute-done.4 = bf16[128,2048]{1,0:T(8,128)(2,1)S(1)} collective-permute-done((bf16[128,2048]{1,0:T(8,128)(2,1)S(1)}, bf16[128,2048]{1,0:T(8,128)(2,1)S(1)}, u32[]{:S(2)}, u32[]{:S(2)}) %collective-permute-start.4) | collective-permute-done | bytes 524320 | tf_op jit(solution)/shard_map/ppermute | solution.py:27
  64.1 22.0 %collective-permute-done.5 = bf16[128,2048]{1,0:T(8,128)(2,1)S(1)} collective-permute-done((bf16[128,2048]{1,0:T(8,128)(2,1)S(1)}, bf16[128,2048]{1,0:T(8,128)(2,1)S(1)}, u32[]{:S(2)}, u32[]{:S(2)}) %collective-permute-start.5) | collective-permute-done | bytes 524320 | tf_op jit(solution)/shard_map/ppermute | solution.py:27
  90.1 3.4 %collective-permute-start.9 = (bf16[2,512,128]{2,1,0:T(8,128)(2,1)S(1)}, bf16[2,512,128]{2,1,0:T(8,128)(2,1)}, u32[]{:S(2)}, u32[]{:S(2)}) collective-permute-start(bf16[2,512,128]{2,1,0:T(8,128)(2,1)S(1)} %bitcast.121), channel_id=1, source_target_pairs={{0,8},{4,12},{8,0},{12,4},{1,9},{5,13},{9,1},{13,5},{2,10},{6,14},... | collective-permute-start | bytes 786440 | tf_op jit(solution)/shard_map/ppermute | solution.py:195
  97.7 6.8 %shard_map.91 = bf16[2,512,128]{2,1,0:T(8,128)(2,1)} custom-call(bf16[2,512,128]{2,1,0:T(8,128)(2,1)} %bitcast.122, bf16[2,1664,128]{2,1,0:T(8,128)(2,1)} %bitcast.108, bf16[2,1664,128]{2,1,0:T(8,128)(2,1)} %bitcast.112), custom_call_target="tpu_custom_call" | custom-call | flops 872415232 | bytes 2228224 | tf_op jit(solution)/shard_map/pallas_call | solution.py:88
  104.5 6.8 %shard_map.92 = bf16[2,512,128]{2,1,0:T(8,128)(2,1)} custom-call(bf16[2,512,128]{2,1,0:T(8,128)(2,1)} %collective-permute-done.7.q_ref, bf16[2,1664,128]{2,1,0:T(8,128)(2,1)} %bitcast.109, bf16[2,1664,128]{2,1,0:T(8,128)(2,1)} %bitcast.113), custom_call_target="tpu_custom_call" | custom-call | flops 872415232 | bytes 2228224 | tf_op jit(solution)/shard_map/pallas_call | solution.py:88
  112.7 6.8 %shard_map.93 = bf16[2,512,128]{2,1,0:T(8,128)(2,1)} custom-call(bf16[2,512,128]{2,1,0:T(8,128)(2,1)} %collective-permute-done.9.q_ref, bf16[2,1664,128]{2,1,0:T(8,128)(2,1)} %bitcast.110, bf16[2,1664,128]{2,1,0:T(8,128)(2,1)} %bitcast.114), custom_call_target="tpu_custom_call" | custom-call | flops 872415232 | bytes 2228224 | tf_op jit(solution)/shard_map/pallas_call | solution.py:88
  119.5 2.0 collective-permute-start.10
  121.5 6.8 %shard_map.94 = bf16[2,512,128]{2,1,0:T(8,128)(2,1)} custom-call(bf16[2,512,128]{2,1,0:T(8,128)(2,1)} %collective-permute-done.11.q_ref, bf16[2,1664,128]{2,1,0:T(8,128)(2,1)} %bitcast.111, bf16[2,1664,128]{2,1,0:T(8,128)(2,1)} %bitcast.115), custom_call_target="tpu_custom_call" | custom-call | flops 872415232 | bytes 2228224 | tf_op jit(solution)/shard_map/pallas_call | solution.py:88
  130.4 8.8 %collective-permute-done.10 = bf16[2,512,128]{2,1,0:T(8,128)(2,1)S(1)} collective-permute-done((bf16[2,512,128]{2,1,0:T(8,128)(2,1)}, bf16[2,512,128]{2,1,0:T(8,128)(2,1)S(1)}, u32[]{:S(2)}, u32[]{:S(2)}) %collective-permute-start.10) | collective-permute-done | bytes 262176 | tf_op jit(solution)/shard_map/ppermute | solution.py:209
  140.6 3.0 %collective-permute-start.14 = (bf16[128,2048]{1,0:T(8,128)(2,1)S(1)}, bf16[128,2048]{1,0:T(8,128)(2,1)S(1)}, u32[]{:S(2)}, u32[]{:S(2)}) collective-permute-start(bf16[128,2048]{1,0:T(8,128)(2,1)S(1)} %convolution_convert_fusion.9), channel_id=1, source_target_pairs={{0,8},{4,12},{8,0},{12,4},{1,9},{5,13},{9,1},{13,5},{2,10},{6,14},... | collective-permute-start | bytes 1572872 | tf_op jit(solution)/shard_map/ppermute | solution.py:38
  145.4 4.8 %fusion.2 = bf16[4,128,2048]{2,1,0:T(8,128)(2,1)S(1)} fusion(bf16[4,128,2048]{2,1,0:T(8,128)(2,1)S(1)} %broadcast_in_dim.63, s32[]{:T(128)S(6)} %select_n.173, bf16[128,2048]{1,0:T(8,128)(2,1)S(1)} %convolution_convert_fusion.9, bf16[2048,2048]{1,0:T(8,128)(2,1)} %param.14), kind=kOutput, calls=%fused_computation.12 | convolution fusion | flops 1074003968 | bytes 9437188 | tf_op jit(solution)/shard_map/dot_general | solution.py:224
  150.2 7.2 %collective-permute-done.13 = bf16[128,2048]{1,0:T(8,128)(2,1)S(1)} collective-permute-done((bf16[128,2048]{1,0:T(8,128)(2,1)S(1)}, bf16[128,2048]{1,0:T(8,128)(2,1)S(1)}, u32[]{:S(2)}, u32[]{:S(2)}) %collective-permute-start.13) | collective-permute-done | bytes 524320 | tf_op jit(solution)/shard_map/ppermute | solution.py:38
  158.7 19.2 %collective-permute-done.14 = bf16[128,2048]{1,0:T(8,128)(2,1)S(1)} collective-permute-done((bf16[128,2048]{1,0:T(8,128)(2,1)S(1)}, bf16[128,2048]{1,0:T(8,128)(2,1)S(1)}, u32[]{:S(2)}, u32[]{:S(2)}) %collective-permute-start.14) | collective-permute-done | bytes 524320 | tf_op jit(solution)/shard_map/ppermute | solution.py:38
  180.8 2.8 %collective-permute-done.16 = bf16[256,2048]{1,0:T(8,128)(2,1)} collective-permute-done((bf16[256,2048]{1,0:T(8,128)(2,1)S(1)}, bf16[256,2048]{1,0:T(8,128)(2,1)}, u32[]{:S(2)}, u32[]{:S(2)}) %collective-permute-start.16) | collective-permute-done | bytes 1048608 | tf_op jit(solution)/shard_map/ppermute | solution.py:49
  185.2 12.3 %collective-permute-start.17 = (bf16[128,2048]{1,0:T(8,128)(2,1)S(1)}, bf16[128,2048]{1,0:T(8,128)(2,1)S(1)}, u32[]{:S(2)}, u32[]{:S(2)}) collective-permute-start(bf16[128,2048]{1,0:T(8,128)(2,1)S(1)} %get-tuple-element.16), channel_id=1, source_target_pairs={{0,0},{1,8},{2,4},{3,12},{4,1},{5,9},{6,5},{7,13},{8,2},{9,10},{10... | collective-permute-start | bytes 1572872 | tf_op jit(solution)/shard_map/ppermute | solution.py:255
  197.6 10.5 %collective-permute-done.17 = bf16[128,2048]{1,0:T(8,128)(2,1)S(1)} collective-permute-done((bf16[128,2048]{1,0:T(8,128)(2,1)S(1)}, bf16[128,2048]{1,0:T(8,128)(2,1)S(1)}, u32[]{:S(2)}, u32[]{:S(2)}) %collective-permute-start.17) | collective-permute-done | bytes 524320 | tf_op jit(solution)/shard_map/ppermute | solution.py:255
  208.1 14.9 %collective-permute-done.18 = bf16[128,2048]{1,0:T(8,128)(2,1)S(1)} collective-permute-done((bf16[128,2048]{1,0:T(8,128)(2,1)S(1)}, bf16[128,2048]{1,0:T(8,128)(2,1)S(1)}, u32[]{:S(2)}, u32[]{:S(2)}) %collective-permute-start.18) | collective-permute-done | bytes 524320 | tf_op jit(solution)/shard_map/ppermute | solution.py:255
  223.0 2.1 add_convert_fusion
  (97 shorter events, 35.0 us)
Async XLA Ops:
  0.0 43.6 %copy-start = (f32[128]{0:T(128)S(1)}, f32[128]{0:T(128)}, u32[]{:S(2)}) copy-start(f32[128]{0:T(128)} %param.11) | copy-start | bytes 1540
  0.0 23.1 %copy-start.4 = (s32[4]{0:T(128)S(1)}, s32[4]{0:T(128)}, u32[]{:S(2)}) copy-start(s32[4]{0:T(128)} %param.17) | copy-start | bytes 52
  0.0 23.1 %copy-start.5 = (s32[128]{0:T(128)S(1)}, s32[128]{0:T(128)}, u32[]{:S(2)}) copy-start(s32[128]{0:T(128)} %param.15) | copy-start | bytes 1540
  0.0 23.3 %copy-start.6 = (s32[128]{0:T(128)S(1)}, s32[128]{0:T(128)}, u32[]{:S(2)}) copy-start(s32[128]{0:T(128)} %param.16) | copy-start | bytes 1540
  1.6 11.2 %collective-permute-start = (bf16[64,2048]{1,0:T(8,128)(2,1)S(1)}, bf16[64,2048]{1,0:T(8,128)(2,1)S(1)}, u32[]{:S(2)}, u32[]{:S(2)}) collective-permute-start(bf16[64,2048]{1,0:T(8,128)(2,1)S(1)} %get-tuple-element.14), channel_id=1, source_target_pairs={{0,4},{4,8},{8,12},{12,0},{1,5},{5,9},{9,13},{13,1},{2,6},{6,10},{... | collective-permute-start | bytes 786440 | tf_op jit(solution)/shard_map/ppermute | solution.py:136
  3.3 19.7 %collective-permute-start.1 = (bf16[64,2048]{1,0:T(8,128)(2,1)S(1)}, bf16[64,2048]{1,0:T(8,128)(2,1)S(1)}, u32[]{:S(2)}, u32[]{:S(2)}) collective-permute-start(bf16[64,2048]{1,0:T(8,128)(2,1)S(1)} %get-tuple-element.15), channel_id=1, source_target_pairs={{0,8},{4,12},{8,0},{12,4},{1,9},{5,13},{9,1},{13,5},{2,10},{6,14},... | collective-permute-start | bytes 786440 | tf_op jit(solution)/shard_map/ppermute | solution.py:136
  5.9 17.1 %collective-permute-start.2 = (bf16[64,2048]{1,0:T(8,128)(2,1)S(1)}, bf16[64,2048]{1,0:T(8,128)(2,1)S(1)}, u32[]{:S(2)}, u32[]{:S(2)}) collective-permute-start(bf16[64,2048]{1,0:T(8,128)(2,1)S(1)} %get-tuple-element.13), channel_id=1, source_target_pairs={{0,12},{4,0},{8,4},{12,8},{1,13},{5,1},{9,5},{13,9},{2,14},{6,2},{... | collective-permute-start | bytes 786440 | tf_op jit(solution)/shard_map/ppermute | solution.py:136
  23.0 2.7 %collective-permute-start.3 = (bf16[4,64,2048]{2,1,0:T(8,128)(2,1)S(1)}, bf16[4,64,2048]{2,1,0:T(8,128)(2,1)S(1)}, u32[]{:S(2)}, u32[]{:S(2)}) collective-permute-start(bf16[4,64,2048]{2,1,0:T(8,128)(2,1)S(1)} %bitcast_dynamic-update-slice_fusion.2), channel_id=1, source_target_pairs={{0,1},{1,0},{2,3},{3,2},{4,5},{5,4},{6,7},{7,6},{8,9},{9,8},{10,11... | collective-permute-start | bytes 3145736 | tf_op jit(solution)/shard_map/ppermute | solution.py:147
  32.9 19.5 %collective-permute-start.6 = (bf16[128,2048]{1,0:T(8,128)(2,1)S(1)}, bf16[128,2048]{1,0:T(8,128)(2,1)S(1)}, u32[]{:S(2)}, u32[]{:S(2)}) collective-permute-start(bf16[128,2048]{1,0:T(8,128)(2,1)S(1)} %convolution_convert_fusion.7), channel_id=1, source_target_pairs={{0,12},{4,0},{8,4},{12,8},{1,13},{5,1},{9,5},{13,9},{2,14},{6,2},{... | collective-permute-start | bytes 1572872 | tf_op jit(solution)/shard_map/ppermute | solution.py:27
  41.4 22.7 %collective-permute-start.4 = (bf16[128,2048]{1,0:T(8,128)(2,1)S(1)}, bf16[128,2048]{1,0:T(8,128)(2,1)S(1)}, u32[]{:S(2)}, u32[]{:S(2)}) collective-permute-start(bf16[128,2048]{1,0:T(8,128)(2,1)S(1)} %convolution_convert_fusion.6), channel_id=1, source_target_pairs={{0,4},{4,8},{8,12},{12,0},{1,5},{5,9},{9,13},{13,1},{2,6},{6,10},{... | collective-permute-start | bytes 1572872 | tf_op jit(solution)/shard_map/ppermute | solution.py:27
  42.7 43.4 %collective-permute-start.5 = (bf16[128,2048]{1,0:T(8,128)(2,1)S(1)}, bf16[128,2048]{1,0:T(8,128)(2,1)S(1)}, u32[]{:S(2)}, u32[]{:S(2)}) collective-permute-start(bf16[128,2048]{1,0:T(8,128)(2,1)S(1)} %convolution_convert_fusion.5), channel_id=1, source_target_pairs={{0,8},{4,12},{8,0},{12,4},{1,9},{5,13},{9,1},{13,5},{2,10},{6,14},... | collective-permute-start | bytes 1572872 | tf_op jit(solution)/shard_map/ppermute | solution.py:27
  89.5 15.0 %collective-permute-start.7 = (bf16[2,512,128]{2,1,0:T(8,128)(2,1)S(1)}, bf16[2,512,128]{2,1,0:T(8,128)(2,1)}, u32[]{:S(2)}, u32[]{:S(2)}) collective-permute-start(bf16[2,512,128]{2,1,0:T(8,128)(2,1)S(1)} %bitcast.123), channel_id=1, source_target_pairs={{0,4},{4,8},{8,12},{12,0},{1,5},{5,9},{9,13},{13,1},{2,6},{6,10},{... | collective-permute-start | bytes 786440 | tf_op jit(solution)/shard_map/ppermute | solution.py:195
  90.1 22.6 %collective-permute-start.9 = (bf16[2,512,128]{2,1,0:T(8,128)(2,1)S(1)}, bf16[2,512,128]{2,1,0:T(8,128)(2,1)}, u32[]{:S(2)}, u32[]{:S(2)}) collective-permute-start(bf16[2,512,128]{2,1,0:T(8,128)(2,1)S(1)} %bitcast.121), channel_id=1, source_target_pairs={{0,8},{4,12},{8,0},{12,4},{1,9},{5,13},{9,1},{13,5},{2,10},{6,14},... | collective-permute-start | bytes 786440 | tf_op jit(solution)/shard_map/ppermute | solution.py:195
  93.5 28.0 %collective-permute-start.11 = (bf16[2,512,128]{2,1,0:T(8,128)(2,1)S(1)}, bf16[2,512,128]{2,1,0:T(8,128)(2,1)}, u32[]{:S(2)}, u32[]{:S(2)}) collective-permute-start(bf16[2,512,128]{2,1,0:T(8,128)(2,1)S(1)} %bitcast.120), channel_id=1, source_target_pairs={{0,12},{4,0},{8,4},{12,8},{1,13},{5,1},{9,5},{13,9},{2,14},{6,2},{... | collective-permute-start | bytes 786440 | tf_op jit(solution)/shard_map/ppermute | solution.py:195
  111.2 19.0 %collective-permute-start.8 = (bf16[2,512,128]{2,1,0:T(8,128)(2,1)}, bf16[2,512,128]{2,1,0:T(8,128)(2,1)S(1)}, u32[]{:S(2)}, u32[]{:S(2)}) collective-permute-start(bf16[2,512,128]{2,1,0:T(8,128)(2,1)} %shard_map.92), channel_id=1, source_target_pairs={{0,12},{4,0},{8,4},{12,8},{1,13},{5,1},{9,5},{13,9},{2,14},{6,2},{... | collective-permute-start | bytes 786440 | tf_op jit(solution)/shard_map/ppermute | solution.py:209
  119.5 19.7 %collective-permute-start.10 = (bf16[2,512,128]{2,1,0:T(8,128)(2,1)}, bf16[2,512,128]{2,1,0:T(8,128)(2,1)S(1)}, u32[]{:S(2)}, u32[]{:S(2)}) collective-permute-start(bf16[2,512,128]{2,1,0:T(8,128)(2,1)} %shard_map.93), channel_id=1, source_target_pairs={{0,8},{4,12},{8,0},{12,4},{1,9},{5,13},{9,1},{13,5},{2,10},{6,14},... | collective-permute-start | bytes 786440 | tf_op jit(solution)/shard_map/ppermute | solution.py:209
  128.3 11.1 %collective-permute-start.12 = (bf16[2,512,128]{2,1,0:T(8,128)(2,1)}, bf16[2,512,128]{2,1,0:T(8,128)(2,1)S(1)}, u32[]{:S(2)}, u32[]{:S(2)}) collective-permute-start(bf16[2,512,128]{2,1,0:T(8,128)(2,1)} %shard_map.94), channel_id=1, source_target_pairs={{0,4},{4,8},{8,12},{12,0},{1,5},{5,9},{9,13},{13,1},{2,6},{6,10},{... | collective-permute-start | bytes 786440 | tf_op jit(solution)/shard_map/ppermute | solution.py:209
  140.6 16.8 %collective-permute-start.13 = (bf16[128,2048]{1,0:T(8,128)(2,1)S(1)}, bf16[128,2048]{1,0:T(8,128)(2,1)S(1)}, u32[]{:S(2)}, u32[]{:S(2)}) collective-permute-start(bf16[128,2048]{1,0:T(8,128)(2,1)S(1)} %convolution_convert_fusion.9), channel_id=1, source_target_pairs={{0,4},{4,8},{8,12},{12,0},{1,5},{5,9},{9,13},{13,1},{2,6},{6,10},{... | collective-permute-start | bytes 1572872 | tf_op jit(solution)/shard_map/ppermute | solution.py:38
  140.6 37.3 %collective-permute-start.14 = (bf16[128,2048]{1,0:T(8,128)(2,1)S(1)}, bf16[128,2048]{1,0:T(8,128)(2,1)S(1)}, u32[]{:S(2)}, u32[]{:S(2)}) collective-permute-start(bf16[128,2048]{1,0:T(8,128)(2,1)S(1)} %convolution_convert_fusion.9), channel_id=1, source_target_pairs={{0,8},{4,12},{8,0},{12,4},{1,9},{5,13},{9,1},{13,5},{2,10},{6,14},... | collective-permute-start | bytes 1572872 | tf_op jit(solution)/shard_map/ppermute | solution.py:38
  143.6 35.6 %collective-permute-start.15 = (bf16[128,2048]{1,0:T(8,128)(2,1)S(1)}, bf16[128,2048]{1,0:T(8,128)(2,1)S(1)}, u32[]{:S(2)}, u32[]{:S(2)}) collective-permute-start(bf16[128,2048]{1,0:T(8,128)(2,1)S(1)} %convolution_convert_fusion.9), channel_id=1, source_target_pairs={{0,12},{4,0},{8,4},{12,8},{1,13},{5,1},{9,5},{13,9},{2,14},{6,2},{... | collective-permute-start | bytes 1572872 | tf_op jit(solution)/shard_map/ppermute | solution.py:38
  145.2 12.3 %slice-start = ((s8[8388608]{0:T(1024)(128)(4,1)}), s8[4194304]{0:T(1024)(128)(4,1)S(1)}, s32[]{:S(2)}) async-start(s8[8388608]{0:T(1024)(128)(4,1)} %bitcast.89), calls=%async_computation | async-start | bytes 8388608
  180.6 2.9 %collective-permute-start.16 = (bf16[256,2048]{1,0:T(8,128)(2,1)S(1)}, bf16[256,2048]{1,0:T(8,128)(2,1)}, u32[]{:S(2)}, u32[]{:S(2)}) collective-permute-start(bf16[256,2048]{1,0:T(8,128)(2,1)S(1)} %dynamic-slice_bitcast_fusion), channel_id=1, source_target_pairs={{0,1},{1,0},{2,3},{3,2},{4,5},{5,4},{6,7},{7,6},{8,9},{9,8},{10,11... | collective-permute-start | bytes 3145736 | tf_op jit(solution)/shard_map/ppermute | solution.py:49
  185.2 22.8 %collective-permute-start.17 = (bf16[128,2048]{1,0:T(8,128)(2,1)S(1)}, bf16[128,2048]{1,0:T(8,128)(2,1)S(1)}, u32[]{:S(2)}, u32[]{:S(2)}) collective-permute-start(bf16[128,2048]{1,0:T(8,128)(2,1)S(1)} %get-tuple-element.16), channel_id=1, source_target_pairs={{0,0},{1,8},{2,4},{3,12},{4,1},{5,9},{6,5},{7,13},{8,2},{9,10},{10... | collective-permute-start | bytes 1572872 | tf_op jit(solution)/shard_map/ppermute | solution.py:255
  197.5 25.5 %collective-permute-start.18 = (bf16[128,2048]{1,0:T(8,128)(2,1)S(1)}, bf16[128,2048]{1,0:T(8,128)(2,1)S(1)}, u32[]{:S(2)}, u32[]{:S(2)}) collective-permute-start(bf16[128,2048]{1,0:T(8,128)(2,1)S(1)} %get-tuple-element.17), channel_id=1, source_target_pairs={{0,4},{1,12},{2,0},{3,8},{4,5},{5,13},{6,1},{7,9},{8,6},{9,14},{10... | collective-permute-start | bytes 1572872 | tf_op jit(solution)/shard_map/ppermute | solution.py:255
  (6 other events, 43.4 us)

commit v24 on v19

--- a/solution.py
+++ b/solution.py
@@ -155,7 +155,7 @@
         return product.astype(jnp.bfloat16).astype(jnp.float32)
 
     query_sum = direct_reduce_scatter(query_chunk, "req", req_count, req_index)
-    queries = lax.optimization_barrier(query_sum.astype(jnp.bfloat16))
+    queries = query_sum.astype(jnp.bfloat16)
     normalized = normalize_heads(queries, q_gain, head_dim)
     capacity = 2 * local_rows // req_count
     slot_total = req_count * capacity

time: 223 us -> 223 us (level)
  no operation moved by 1% of the time
where the time goes in v24:
time: 223 us; the launch traced here: 222 us
  waiting for transfers between devices  109 us (49%)
  starting transfers between devices  51 us (23%)
  Pallas kernels  27.1 us (12%)
  matrix products  18.6 us (8%)
  local copies, waits for them, and re-layouts  11.2 us (5%)
  other arithmetic  4.91 us (2%)
    ppermute x3, waiting for transfers between devices, direct_reduce_scatter(): lax.ppermute(outgoing, axis, [(i, (i + shift) % count) for i in range(cou...  29.7 us
    pallas_call x4, Pallas kernels, attend(): pl.pallas_call(kernel, grid=(kv_count,), in_specs=[pl.BlockSpec((1, stack...  27.1 us
    ppermute x3, waiting for transfers between devices, direct_gather_apply(): lax.ppermute(block, axis, [(i, (i + shift) % count) for i in range(count)])  26.4 us
    ppermute x2, waiting for transfers between devices, local(): got = lax.ppermute(chunk, ('req', 'head', 'sub'), pairs).astype(jnp.float32)  25.4 us
    ppermute x3, waiting for transfers between devices, local(): lax.ppermute(my_block((req_index + shift) % req_count), 'req', [(i, (i +...  14.5 us
    ppermute x3, starting transfers between devices, local(): lax.ppermute(outgoing[shift], 'req', [(i, (i + shift) % req_count) for i...  14.1 us
    ppermute x2, starting transfers between devices, local(): got = lax.ppermute(chunk, ('req', 'head', 'sub'), pairs).astype(jnp.float32)  11.7 us
    ppermute x3, starting transfers between devices, direct_reduce_scatter(): lax.ppermute(outgoing, axis, [(i, (i + shift) % count) for i in range(cou...  9.46 us
  transfers between devices with their start and end apart: 19, of which 11 were waited for; matrix products, arithmetic and copies ran while one was open for 8% of the time, Pallas kernels for 12%

profile of v24, /device:TPU:6, one launch (start us, length us, event | category | flops | bytes accessed | tf_op | source)
XLA Modules:
  0.0 221.9 jit_solution(6111716176604969130)
XLA Ops:
  3.3 2.6 %collective-permute-start.1 = (bf16[64,2048]{1,0:T(8,128)(2,1)S(1)}, bf16[64,2048]{1,0:T(8,128)(2,1)S(1)}, u32[]{:S(2)}, u32[]{:S(2)}) collective-permute-start(bf16[64,2048]{1,0:T(8,128)(2,1)S(1)} %get-tuple-element.11), channel_id=1, source_target_pairs={{0,8},{4,12},{8,0},{12,4},{1,9},{5,13},{9,1},{13,5},{2,10},{6,14},... | collective-permute-start | bytes 786440 | tf_op jit(solution)/shard_map/ppermute | solution.py:134
  8.5 4.4 %collective-permute-done = bf16[64,2048]{1,0:T(8,128)(2,1)S(1)} collective-permute-done((bf16[64,2048]{1,0:T(8,128)(2,1)S(1)}, bf16[64,2048]{1,0:T(8,128)(2,1)S(1)}, u32[]{:S(2)}, u32[]{:S(2)}) %collective-permute-start) | collective-permute-done | bytes 262176 | tf_op jit(solution)/shard_map/ppermute | solution.py:134
  12.8 10.1 %collective-permute-done.1 = bf16[64,2048]{1,0:T(8,128)(2,1)S(1)} collective-permute-done((bf16[64,2048]{1,0:T(8,128)(2,1)S(1)}, bf16[64,2048]{1,0:T(8,128)(2,1)S(1)}, u32[]{:S(2)}, u32[]{:S(2)}) %collective-permute-start.1) | collective-permute-done | bytes 262176 | tf_op jit(solution)/shard_map/ppermute | solution.py:134
  25.9 4.8 %convolution_convert_fusion.7 = bf16[128,2048]{1,0:T(8,128)(2,1)S(1)} fusion(bf16[2048,2048]{1,0:T(8,128)(2,1)} %param.10, bf16[512,2048]{1,0:T(8,128)(2,1)S(1)} %bitcast.99, s32[]{:T(128)S(6)} %select_n.193), kind=kOutput, calls=%fused_computation.7 | convolution fusion | flops 1074003968 | bytes 9437188 | tf_op jit(solution)/shard_map/dot_general | solution.py:154
  30.7 6.1 %collective-permute-start.4 = (bf16[128,2048]{1,0:T(8,128)(2,1)S(1)}, bf16[128,2048]{1,0:T(8,128)(2,1)S(1)}, u32[]{:S(2)}, u32[]{:S(2)}) collective-permute-start(bf16[128,2048]{1,0:T(8,128)(2,1)S(1)} %convolution_convert_fusion.7), channel_id=1, source_target_pairs={{0,4},{4,8},{8,12},{12,0},{1,5},{5,9},{9,13},{13,1},{2,6},{6,10},{... | collective-permute-start | bytes 1572872 | tf_op jit(solution)/shard_map/ppermute | solution.py:24
  43.0 7.7 %collective-permute-done.4 = bf16[128,2048]{1,0:T(8,128)(2,1)S(1)} collective-permute-done((bf16[128,2048]{1,0:T(8,128)(2,1)S(1)}, bf16[128,2048]{1,0:T(8,128)(2,1)S(1)}, u32[]{:S(2)}, u32[]{:S(2)}) %collective-permute-start.4) | collective-permute-done | bytes 524320 | tf_op jit(solution)/shard_map/ppermute | solution.py:24
  50.7 22.0 %collective-permute-done.5 = bf16[128,2048]{1,0:T(8,128)(2,1)S(1)} collective-permute-done((bf16[128,2048]{1,0:T(8,128)(2,1)S(1)}, bf16[128,2048]{1,0:T(8,128)(2,1)S(1)}, u32[]{:S(2)}, u32[]{:S(2)}) %collective-permute-start.5) | collective-permute-done | bytes 524320 | tf_op jit(solution)/shard_map/ppermute | solution.py:24
  77.3 11.7 %collective-permute-start.7 = (bf16[2,512,128]{2,1,0:T(8,128)(2,1)S(1)}, bf16[2,512,128]{2,1,0:T(8,128)(2,1)}, u32[]{:S(2)}, u32[]{:S(2)}) collective-permute-start(bf16[2,512,128]{2,1,0:T(8,128)(2,1)S(1)} %bitcast.127), channel_id=1, source_target_pairs={{0,4},{4,8},{8,12},{12,0},{1,5},{5,9},{9,13},{13,1},{2,6},{6,10},{... | collective-permute-start | bytes 786440 | tf_op jit(solution)/shard_map/ppermute | solution.py:193
  95.5 6.8 %shard_map.91 = bf16[2,512,128]{2,1,0:T(8,128)(2,1)} custom-call(bf16[2,512,128]{2,1,0:T(8,128)(2,1)} %bitcast.126, bf16[2,1664,128]{2,1,0:T(8,128)(2,1)} %bitcast.112, bf16[2,1664,128]{2,1,0:T(8,128)(2,1)} %bitcast.116), custom_call_target="tpu_custom_call" | custom-call | flops 872415232 | bytes 2228224 | tf_op jit(solution)/shard_map/pallas_call | solution.py:86
  102.3 6.8 %shard_map.92 = bf16[2,512,128]{2,1,0:T(8,128)(2,1)} custom-call(bf16[2,512,128]{2,1,0:T(8,128)(2,1)} %collective-permute-done.7.q_ref, bf16[2,1664,128]{2,1,0:T(8,128)(2,1)} %bitcast.113, bf16[2,1664,128]{2,1,0:T(8,128)(2,1)} %bitcast.117), custom_call_target="tpu_custom_call" | custom-call | flops 872415232 | bytes 2228224 | tf_op jit(solution)/shard_map/pallas_call | solution.py:86
  109.1 2.0 collective-permute-start.8
  111.1 6.8 %shard_map.93 = bf16[2,512,128]{2,1,0:T(8,128)(2,1)} custom-call(bf16[2,512,128]{2,1,0:T(8,128)(2,1)} %collective-permute-done.9.q_ref, bf16[2,1664,128]{2,1,0:T(8,128)(2,1)} %bitcast.114, bf16[2,1664,128]{2,1,0:T(8,128)(2,1)} %bitcast.118), custom_call_target="tpu_custom_call" | custom-call | flops 872415232 | bytes 2228224 | tf_op jit(solution)/shard_map/pallas_call | solution.py:86
  118.3 6.8 %shard_map.94 = bf16[2,512,128]{2,1,0:T(8,128)(2,1)} custom-call(bf16[2,512,128]{2,1,0:T(8,128)(2,1)} %collective-permute-done.11.q_ref, bf16[2,1664,128]{2,1,0:T(8,128)(2,1)} %bitcast.115, bf16[2,1664,128]{2,1,0:T(8,128)(2,1)} %bitcast.119), custom_call_target="tpu_custom_call" | custom-call | flops 872415232 | bytes 2228224 | tf_op jit(solution)/shard_map/pallas_call | solution.py:86
  125.0 3.9 %collective-permute-start.12 = (bf16[2,512,128]{2,1,0:T(8,128)(2,1)}, bf16[2,512,128]{2,1,0:T(8,128)(2,1)S(1)}, u32[]{:S(2)}, u32[]{:S(2)}) collective-permute-start(bf16[2,512,128]{2,1,0:T(8,128)(2,1)} %shard_map.94), channel_id=1, source_target_pairs={{0,4},{4,8},{8,12},{12,0},{1,5},{5,9},{9,13},{13,1},{2,6},{6,10},{... | collective-permute-start | bytes 786440 | tf_op jit(solution)/shard_map/ppermute | solution.py:207
  129.3 8.1 %collective-permute-done.10 = bf16[2,512,128]{2,1,0:T(8,128)(2,1)S(1)} collective-permute-done((bf16[2,512,128]{2,1,0:T(8,128)(2,1)}, bf16[2,512,128]{2,1,0:T(8,128)(2,1)S(1)}, u32[]{:S(2)}, u32[]{:S(2)}) %collective-permute-start.10) | collective-permute-done | bytes 262176 | tf_op jit(solution)/shard_map/ppermute | solution.py:207
  140.3 2.3 %collective-permute-start.15 = (bf16[128,2048]{1,0:T(8,128)(2,1)S(1)}, bf16[128,2048]{1,0:T(8,128)(2,1)S(1)}, u32[]{:S(2)}, u32[]{:S(2)}) collective-permute-start(bf16[128,2048]{1,0:T(8,128)(2,1)S(1)} %convolution_convert_fusion.9), channel_id=1, source_target_pairs={{0,12},{4,0},{8,4},{12,8},{1,13},{5,1},{9,5},{13,9},{2,14},{6,2},{... | collective-permute-start | bytes 1572872 | tf_op jit(solution)/shard_map/ppermute | solution.py:36
  142.8 4.8 %fusion.5 = bf16[4,128,2048]{2,1,0:T(8,128)(2,1)S(1)} fusion(bf16[4,128,2048]{2,1,0:T(8,128)(2,1)S(1)} %broadcast_in_dim.63, s32[]{:T(128)S(6)} %select_n.173, bf16[128,2048]{1,0:T(8,128)(2,1)S(1)} %convolution_convert_fusion.9, bf16[2048,2048]{1,0:T(8,128)(2,1)} %param.14), kind=kOutput, calls=%fused_computation.15 | convolution fusion | flops 1074003968 | bytes 9437188 | tf_op jit(solution)/shard_map/dot_general | solution.py:222
  147.7 7.8 %collective-permute-done.13 = bf16[128,2048]{1,0:T(8,128)(2,1)S(1)} collective-permute-done((bf16[128,2048]{1,0:T(8,128)(2,1)S(1)}, bf16[128,2048]{1,0:T(8,128)(2,1)S(1)}, u32[]{:S(2)}, u32[]{:S(2)}) %collective-permute-start.13) | collective-permute-done | bytes 524320 | tf_op jit(solution)/shard_map/ppermute | solution.py:36
  156.8 18.6 %collective-permute-done.14 = bf16[128,2048]{1,0:T(8,128)(2,1)S(1)} collective-permute-done((bf16[128,2048]{1,0:T(8,128)(2,1)S(1)}, bf16[128,2048]{1,0:T(8,128)(2,1)S(1)}, u32[]{:S(2)}, u32[]{:S(2)}) %collective-permute-start.14) | collective-permute-done | bytes 524320 | tf_op jit(solution)/shard_map/ppermute | solution.py:36
  178.2 2.8 %collective-permute-done.16 = bf16[256,2048]{1,0:T(8,128)(2,1)} collective-permute-done((bf16[256,2048]{1,0:T(8,128)(2,1)S(1)}, bf16[256,2048]{1,0:T(8,128)(2,1)}, u32[]{:S(2)}, u32[]{:S(2)}) %collective-permute-start.16) | collective-permute-done | bytes 1048608 | tf_op jit(solution)/shard_map/ppermute | solution.py:47
  182.7 11.6 %collective-permute-start.17 = (bf16[128,2048]{1,0:T(8,128)(2,1)S(1)}, bf16[128,2048]{1,0:T(8,128)(2,1)S(1)}, u32[]{:S(2)}, u32[]{:S(2)}) collective-permute-start(bf16[128,2048]{1,0:T(8,128)(2,1)S(1)} %get-tuple-element.12), channel_id=1, source_target_pairs={{0,0},{1,8},{2,4},{3,12},{4,1},{5,9},{6,5},{7,13},{8,2},{9,10},{10... | collective-permute-start | bytes 1572872 | tf_op jit(solution)/shard_map/ppermute | solution.py:253
  194.4 10.6 %collective-permute-done.17 = bf16[128,2048]{1,0:T(8,128)(2,1)S(1)} collective-permute-done((bf16[128,2048]{1,0:T(8,128)(2,1)S(1)}, bf16[128,2048]{1,0:T(8,128)(2,1)S(1)}, u32[]{:S(2)}, u32[]{:S(2)}) %collective-permute-start.17) | collective-permute-done | bytes 524320 | tf_op jit(solution)/shard_map/ppermute | solution.py:253
  205.0 14.8 %collective-permute-done.18 = bf16[128,2048]{1,0:T(8,128)(2,1)S(1)} collective-permute-done((bf16[128,2048]{1,0:T(8,128)(2,1)S(1)}, bf16[128,2048]{1,0:T(8,128)(2,1)S(1)}, u32[]{:S(2)}, u32[]{:S(2)}) %collective-permute-start.18) | collective-permute-done | bytes 524320 | tf_op jit(solution)/shard_map/ppermute | solution.py:253
  219.8 2.1 add_convert_fusion
  (96 shorter events, 35.6 us)
Async XLA Ops:
  0.0 42.9 %copy-start = (f32[128]{0:T(128)S(1)}, f32[128]{0:T(128)}, u32[]{:S(2)}) copy-start(f32[128]{0:T(128)} %param.11) | copy-start | bytes 1540
  0.0 23.1 %copy-start.4 = (s32[4]{0:T(128)S(1)}, s32[4]{0:T(128)}, u32[]{:S(2)}) copy-start(s32[4]{0:T(128)} %param.17) | copy-start | bytes 52
  0.0 23.1 %copy-start.5 = (s32[128]{0:T(128)S(1)}, s32[128]{0:T(128)}, u32[]{:S(2)}) copy-start(s32[128]{0:T(128)} %param.15) | copy-start | bytes 1540
  0.0 23.3 %copy-start.6 = (s32[128]{0:T(128)S(1)}, s32[128]{0:T(128)}, u32[]{:S(2)}) copy-start(s32[128]{0:T(128)} %param.16) | copy-start | bytes 1540
  1.6 11.2 %collective-permute-start = (bf16[64,2048]{1,0:T(8,128)(2,1)S(1)}, bf16[64,2048]{1,0:T(8,128)(2,1)S(1)}, u32[]{:S(2)}, u32[]{:S(2)}) collective-permute-start(bf16[64,2048]{1,0:T(8,128)(2,1)S(1)} %get-tuple-element.10), channel_id=1, source_target_pairs={{0,4},{4,8},{8,12},{12,0},{1,5},{5,9},{9,13},{13,1},{2,6},{6,10},{... | collective-permute-start | bytes 786440 | tf_op jit(solution)/shard_map/ppermute | solution.py:134
  3.3 19.7 %collective-permute-start.1 = (bf16[64,2048]{1,0:T(8,128)(2,1)S(1)}, bf16[64,2048]{1,0:T(8,128)(2,1)S(1)}, u32[]{:S(2)}, u32[]{:S(2)}) collective-permute-start(bf16[64,2048]{1,0:T(8,128)(2,1)S(1)} %get-tuple-element.11), channel_id=1, source_target_pairs={{0,8},{4,12},{8,0},{12,4},{1,9},{5,13},{9,1},{13,5},{2,10},{6,14},... | collective-permute-start | bytes 786440 | tf_op jit(solution)/shard_map/ppermute | solution.py:134
  5.9 17.1 %collective-permute-start.2 = (bf16[64,2048]{1,0:T(8,128)(2,1)S(1)}, bf16[64,2048]{1,0:T(8,128)(2,1)S(1)}, u32[]{:S(2)}, u32[]{:S(2)}) collective-permute-start(bf16[64,2048]{1,0:T(8,128)(2,1)S(1)} %get-tuple-element.9), channel_id=1, source_target_pairs={{0,12},{4,0},{8,4},{12,8},{1,13},{5,1},{9,5},{13,9},{2,14},{6,2},{... | collective-permute-start | bytes 786440 | tf_op jit(solution)/shard_map/ppermute | solution.py:134
  23.0 2.7 %collective-permute-start.3 = (bf16[4,64,2048]{2,1,0:T(8,128)(2,1)S(1)}, bf16[4,64,2048]{2,1,0:T(8,128)(2,1)S(1)}, u32[]{:S(2)}, u32[]{:S(2)}) collective-permute-start(bf16[4,64,2048]{2,1,0:T(8,128)(2,1)S(1)} %bitcast_dynamic-update-slice_fusion.2), channel_id=1, source_target_pairs={{0,1},{1,0},{2,3},{3,2},{4,5},{5,4},{6,7},{7,6},{8,9},{9,8},{10,11... | collective-permute-start | bytes 3145736 | tf_op jit(solution)/shard_map/ppermute | solution.py:145
  30.7 20.0 %collective-permute-start.4 = (bf16[128,2048]{1,0:T(8,128)(2,1)S(1)}, bf16[128,2048]{1,0:T(8,128)(2,1)S(1)}, u32[]{:S(2)}, u32[]{:S(2)}) collective-permute-start(bf16[128,2048]{1,0:T(8,128)(2,1)S(1)} %convolution_convert_fusion.7), channel_id=1, source_target_pairs={{0,4},{4,8},{8,12},{12,0},{1,5},{5,9},{9,13},{13,1},{2,6},{6,10},{... | collective-permute-start | bytes 1572872 | tf_op jit(solution)/shard_map/ppermute | solution.py:24
  38.1 34.6 %collective-permute-start.5 = (bf16[128,2048]{1,0:T(8,128)(2,1)S(1)}, bf16[128,2048]{1,0:T(8,128)(2,1)S(1)}, u32[]{:S(2)}, u32[]{:S(2)}) collective-permute-start(bf16[128,2048]{1,0:T(8,128)(2,1)S(1)} %convolution_convert_fusion.6), channel_id=1, source_target_pairs={{0,8},{4,12},{8,0},{12,4},{1,9},{5,13},{9,1},{13,5},{2,10},{6,14},... | collective-permute-start | bytes 1572872 | tf_op jit(solution)/shard_map/ppermute | solution.py:24
  41.1 31.6 %collective-permute-start.6 = (bf16[128,2048]{1,0:T(8,128)(2,1)S(1)}, bf16[128,2048]{1,0:T(8,128)(2,1)S(1)}, u32[]{:S(2)}, u32[]{:S(2)}) collective-permute-start(bf16[128,2048]{1,0:T(8,128)(2,1)S(1)} %convolution_convert_fusion.5), channel_id=1, source_target_pairs={{0,12},{4,0},{8,4},{12,8},{1,13},{5,1},{9,5},{13,9},{2,14},{6,2},{... | collective-permute-start | bytes 1572872 | tf_op jit(solution)/shard_map/ppermute | solution.py:24
  76.2 15.1 %copy-start.1 = (bf16[1,1601,512]{2,1,0:T(8,128)(2,1)S(1)}, bf16[1,1601,512]{2,1,0:T(8,128)(2,1)}, u32[]{:S(2)}) copy-start(bf16[1,1601,512]{2,1,0:T(8,128)(2,1)} %param.13) | copy-start | bytes 4918276
  77.3 25.0 %collective-permute-start.7 = (bf16[2,512,128]{2,1,0:T(8,128)(2,1)S(1)}, bf16[2,512,128]{2,1,0:T(8,128)(2,1)}, u32[]{:S(2)}, u32[]{:S(2)}) collective-permute-start(bf16[2,512,128]{2,1,0:T(8,128)(2,1)S(1)} %bitcast.127), channel_id=1, source_target_pairs={{0,4},{4,8},{8,12},{12,0},{1,5},{5,9},{9,13},{13,1},{2,6},{6,10},{... | collective-permute-start | bytes 786440 | tf_op jit(solution)/shard_map/ppermute | solution.py:193
  89.0 22.1 %collective-permute-start.9 = (bf16[2,512,128]{2,1,0:T(8,128)(2,1)S(1)}, bf16[2,512,128]{2,1,0:T(8,128)(2,1)}, u32[]{:S(2)}, u32[]{:S(2)}) collective-permute-start(bf16[2,512,128]{2,1,0:T(8,128)(2,1)S(1)} %bitcast.125), channel_id=1, source_target_pairs={{0,8},{4,12},{8,0},{12,4},{1,9},{5,13},{9,1},{13,5},{2,10},{6,14},... | collective-permute-start | bytes 786440 | tf_op jit(solution)/shard_map/ppermute | solution.py:193
  90.2 28.0 %collective-permute-start.11 = (bf16[2,512,128]{2,1,0:T(8,128)(2,1)S(1)}, bf16[2,512,128]{2,1,0:T(8,128)(2,1)}, u32[]{:S(2)}, u32[]{:S(2)}) collective-permute-start(bf16[2,512,128]{2,1,0:T(8,128)(2,1)S(1)} %bitcast.124), channel_id=1, source_target_pairs={{0,12},{4,0},{8,4},{12,8},{1,13},{5,1},{9,5},{13,9},{2,14},{6,2},{... | collective-permute-start | bytes 786440 | tf_op jit(solution)/shard_map/ppermute | solution.py:193
  109.1 20.0 %collective-permute-start.8 = (bf16[2,512,128]{2,1,0:T(8,128)(2,1)}, bf16[2,512,128]{2,1,0:T(8,128)(2,1)S(1)}, u32[]{:S(2)}, u32[]{:S(2)}) collective-permute-start(bf16[2,512,128]{2,1,0:T(8,128)(2,1)} %shard_map.92), channel_id=1, source_target_pairs={{0,12},{4,0},{8,4},{12,8},{1,13},{5,1},{9,5},{13,9},{2,14},{6,2},{... | collective-permute-start | bytes 786440 | tf_op jit(solution)/shard_map/ppermute | solution.py:207
  117.9 19.5 %collective-permute-start.10 = (bf16[2,512,128]{2,1,0:T(8,128)(2,1)}, bf16[2,512,128]{2,1,0:T(8,128)(2,1)S(1)}, u32[]{:S(2)}, u32[]{:S(2)}) collective-permute-start(bf16[2,512,128]{2,1,0:T(8,128)(2,1)} %shard_map.93), channel_id=1, source_target_pairs={{0,8},{4,12},{8,0},{12,4},{1,9},{5,13},{9,1},{13,5},{2,10},{6,14},... | collective-permute-start | bytes 786440 | tf_op jit(solution)/shard_map/ppermute | solution.py:207
  125.0 12.5 %collective-permute-start.12 = (bf16[2,512,128]{2,1,0:T(8,128)(2,1)}, bf16[2,512,128]{2,1,0:T(8,128)(2,1)S(1)}, u32[]{:S(2)}, u32[]{:S(2)}) collective-permute-start(bf16[2,512,128]{2,1,0:T(8,128)(2,1)} %shard_map.94), channel_id=1, source_target_pairs={{0,4},{4,8},{8,12},{12,0},{1,5},{5,9},{9,13},{13,1},{2,6},{6,10},{... | collective-permute-start | bytes 786440 | tf_op jit(solution)/shard_map/ppermute | solution.py:207
  138.7 16.8 %collective-permute-start.13 = (bf16[128,2048]{1,0:T(8,128)(2,1)S(1)}, bf16[128,2048]{1,0:T(8,128)(2,1)S(1)}, u32[]{:S(2)}, u32[]{:S(2)}) collective-permute-start(bf16[128,2048]{1,0:T(8,128)(2,1)S(1)} %convolution_convert_fusion.9), channel_id=1, source_target_pairs={{0,4},{4,8},{8,12},{12,0},{1,5},{5,9},{9,13},{13,1},{2,6},{6,10},{... | collective-permute-start | bytes 1572872 | tf_op jit(solution)/shard_map/ppermute | solution.py:36
  138.8 36.6 %collective-permute-start.14 = (bf16[128,2048]{1,0:T(8,128)(2,1)S(1)}, bf16[128,2048]{1,0:T(8,128)(2,1)S(1)}, u32[]{:S(2)}, u32[]{:S(2)}) collective-permute-start(bf16[128,2048]{1,0:T(8,128)(2,1)S(1)} %convolution_convert_fusion.9), channel_id=1, source_target_pairs={{0,8},{4,12},{8,0},{12,4},{1,9},{5,13},{9,1},{13,5},{2,10},{6,14},... | collective-permute-start | bytes 1572872 | tf_op jit(solution)/shard_map/ppermute | solution.py:36
  140.3 36.4 %collective-permute-start.15 = (bf16[128,2048]{1,0:T(8,128)(2,1)S(1)}, bf16[128,2048]{1,0:T(8,128)(2,1)S(1)}, u32[]{:S(2)}, u32[]{:S(2)}) collective-permute-start(bf16[128,2048]{1,0:T(8,128)(2,1)S(1)} %convolution_convert_fusion.9), channel_id=1, source_target_pairs={{0,12},{4,0},{8,4},{12,8},{1,13},{5,1},{9,5},{13,9},{2,14},{6,2},{... | collective-permute-start | bytes 1572872 | tf_op jit(solution)/shard_map/ppermute | solution.py:36
  178.1 2.9 %collective-permute-start.16 = (bf16[256,2048]{1,0:T(8,128)(2,1)S(1)}, bf16[256,2048]{1,0:T(8,128)(2,1)}, u32[]{:S(2)}, u32[]{:S(2)}) collective-permute-start(bf16[256,2048]{1,0:T(8,128)(2,1)S(1)} %dynamic-slice_bitcast_fusion), channel_id=1, source_target_pairs={{0,1},{1,0},{2,3},{3,2},{4,5},{5,4},{6,7},{7,6},{8,9},{9,8},{10,11... | collective-permute-start | bytes 3145736 | tf_op jit(solution)/shard_map/ppermute | solution.py:47
  182.7 22.3 %collective-permute-start.17 = (bf16[128,2048]{1,0:T(8,128)(2,1)S(1)}, bf16[128,2048]{1,0:T(8,128)(2,1)S(1)}, u32[]{:S(2)}, u32[]{:S(2)}) collective-permute-start(bf16[128,2048]{1,0:T(8,128)(2,1)S(1)} %get-tuple-element.12), channel_id=1, source_target_pairs={{0,0},{1,8},{2,4},{3,12},{4,1},{5,9},{6,5},{7,13},{8,2},{9,10},{10... | collective-permute-start | bytes 1572872 | tf_op jit(solution)/shard_map/ppermute | solution.py:253
  194.3 25.5 %collective-permute-start.18 = (bf16[128,2048]{1,0:T(8,128)(2,1)S(1)}, bf16[128,2048]{1,0:T(8,128)(2,1)S(1)}, u32[]{:S(2)}, u32[]{:S(2)}) collective-permute-start(bf16[128,2048]{1,0:T(8,128)(2,1)S(1)} %get-tuple-element.13), channel_id=1, source_target_pairs={{0,4},{1,12},{2,0},{3,8},{4,5},{5,13},{6,1},{7,9},{8,6},{9,14},{10... | collective-permute-start | bytes 1572872 | tf_op jit(solution)/shard_map/ppermute | solution.py:253
  (6 other events, 73.8 us)

commit v25 on v19

--- a/solution.py
+++ b/solution.py
@@ -170,9 +170,7 @@
     )
     slot_ids = lax.broadcasted_iota(jnp.int32, (slot_total, local_rows), 0)
     dispatch = ((slot_ids == position[None, :]) & wanted[None, :]).astype(jnp.bfloat16)
-    outgoing = jnp.dot(dispatch, normalized, preferred_element_type=jnp.float32).astype(
-        jnp.bfloat16
-    )
+    outgoing = jnp.dot(dispatch, normalized, preferred_element_type=jnp.bfloat16)
     kv_count = max(1, heads_here // group_size)
     per_kv = heads_here // kv_count
     outgoing = outgoing.reshape(req_count, capacity, kv_count, per_kv, head_dim)
@@ -216,8 +214,8 @@
         dispatch,
         returned.reshape(slot_total, q_cols),
         (((0,), (0,)), ((), ())),
-        preferred_element_type=jnp.float32,
-    ).astype(jnp.bfloat16)
+        preferred_element_type=jnp.bfloat16,
+    )
     def out_part(rows):
         product = jnp.dot(rows, out_weight, preferred_element_type=jnp.float32)
         return product.astype(jnp.bfloat16)

time: 223 us -> 223 us (level)
  no operation moved by 1% of the time
where the time goes in v25:
time: 223 us; the launch traced here: 222 us
  waiting for transfers between devices  108 us (48%)
  starting transfers between devices  51.1 us (23%)
  Pallas kernels  27.1 us (12%)
  matrix products  18.5 us (8%)
  local copies, waits for them, and re-layouts  11 us (5%)
  other arithmetic  6.07 us (3%)
    ppermute x3, waiting for transfers between devices, direct_reduce_scatter(): lax.ppermute(outgoing, axis, [(i, (i + shift) % count) for i in range(cou...  29.9 us
    pallas_call x4, Pallas kernels, attend(): pl.pallas_call(kernel, grid=(kv_count,), in_specs=[pl.BlockSpec((1, stack...  27.1 us
    ppermute x3, waiting for transfers between devices, direct_gather_apply(): lax.ppermute(block, axis, [(i, (i + shift) % count) for i in range(count)])  26.4 us
    ppermute x2, waiting for transfers between devices, local(): got = lax.ppermute(chunk, ('req', 'head', 'sub'), pairs).astype(jnp.float32)  25.4 us
    ppermute x3, starting transfers between devices, local(): lax.ppermute(outgoing[shift], 'req', [(i, (i + shift) % req_count) for i...  14.1 us
    ppermute x3, waiting for transfers between devices, local(): lax.ppermute(my_block((req_index + shift) % req_count), 'req', [(i, (i +...  13.5 us
    ppermute x2, starting transfers between devices, local(): got = lax.ppermute(chunk, ('req', 'head', 'sub'), pairs).astype(jnp.float32)  11.7 us
    ppermute x3, starting transfers between devices, direct_reduce_scatter(): lax.ppermute(outgoing, axis, [(i, (i + shift) % count) for i in range(cou...  9.46 us
  transfers between devices with their start and end apart: 19, of which 11 were waited for; matrix products, arithmetic and copies ran while one was open for 8% of the time, Pallas kernels for 12%

profile of v25, /device:TPU:6, one launch (start us, length us, event | category | flops | bytes accessed | tf_op | source)
XLA Modules:
  0.0 222.1 jit_solution(13175157012634336210)
XLA Ops:
  3.2 2.6 %collective-permute-start.1 = (bf16[64,2048]{1,0:T(8,128)(2,1)S(1)}, bf16[64,2048]{1,0:T(8,128)(2,1)S(1)}, u32[]{:S(2)}, u32[]{:S(2)}) collective-permute-start(bf16[64,2048]{1,0:T(8,128)(2,1)S(1)} %get-tuple-element.11), channel_id=1, source_target_pairs={{0,8},{4,12},{8,0},{12,4},{1,9},{5,13},{9,1},{13,5},{2,10},{6,14},... | collective-permute-start | bytes 786440 | tf_op jit(solution)/shard_map/ppermute | solution.py:134
  9.4 3.4 %collective-permute-done = bf16[64,2048]{1,0:T(8,128)(2,1)S(1)} collective-permute-done((bf16[64,2048]{1,0:T(8,128)(2,1)S(1)}, bf16[64,2048]{1,0:T(8,128)(2,1)S(1)}, u32[]{:S(2)}, u32[]{:S(2)}) %collective-permute-start) | collective-permute-done | bytes 262176 | tf_op jit(solution)/shard_map/ppermute | solution.py:134
  12.8 10.1 %collective-permute-done.1 = bf16[64,2048]{1,0:T(8,128)(2,1)S(1)} collective-permute-done((bf16[64,2048]{1,0:T(8,128)(2,1)S(1)}, bf16[64,2048]{1,0:T(8,128)(2,1)S(1)}, u32[]{:S(2)}, u32[]{:S(2)}) %collective-permute-start.1) | collective-permute-done | bytes 262176 | tf_op jit(solution)/shard_map/ppermute | solution.py:134
  25.8 4.8 %convolution_convert_fusion.6 = bf16[128,2048]{1,0:T(8,128)(2,1)S(1)} fusion(bf16[2048,2048]{1,0:T(8,128)(2,1)} %param.10, bf16[512,2048]{1,0:T(8,128)(2,1)S(1)} %bitcast.102, s32[]{:T(128)S(6)} %select_n.193), kind=kOutput, calls=%fused_computation.6 | convolution fusion | flops 1074003968 | bytes 9437188 | tf_op jit(solution)/shard_map/dot_general | solution.py:154
  30.6 6.1 %collective-permute-start.4 = (bf16[128,2048]{1,0:T(8,128)(2,1)S(1)}, bf16[128,2048]{1,0:T(8,128)(2,1)S(1)}, u32[]{:S(2)}, u32[]{:S(2)}) collective-permute-start(bf16[128,2048]{1,0:T(8,128)(2,1)S(1)} %convolution_convert_fusion.6), channel_id=1, source_target_pairs={{0,4},{4,8},{8,12},{12,0},{1,5},{5,9},{9,13},{13,1},{2,6},{6,10},{... | collective-permute-start | bytes 1572872 | tf_op jit(solution)/shard_map/ppermute | solution.py:24
  42.7 7.9 %collective-permute-done.4 = bf16[128,2048]{1,0:T(8,128)(2,1)S(1)} collective-permute-done((bf16[128,2048]{1,0:T(8,128)(2,1)S(1)}, bf16[128,2048]{1,0:T(8,128)(2,1)S(1)}, u32[]{:S(2)}, u32[]{:S(2)}) %collective-permute-start.4) | collective-permute-done | bytes 524320 | tf_op jit(solution)/shard_map/ppermute | solution.py:24
  50.7 22.0 %collective-permute-done.5 = bf16[128,2048]{1,0:T(8,128)(2,1)S(1)} collective-permute-done((bf16[128,2048]{1,0:T(8,128)(2,1)S(1)}, bf16[128,2048]{1,0:T(8,128)(2,1)S(1)}, u32[]{:S(2)}, u32[]{:S(2)}) %collective-permute-start.5) | collective-permute-done | bytes 524320 | tf_op jit(solution)/shard_map/ppermute | solution.py:24
  77.5 11.7 %collective-permute-start.7 = (bf16[2,512,128]{2,1,0:T(8,128)(2,1)S(1)}, bf16[2,512,128]{2,1,0:T(8,128)(2,1)}, u32[]{:S(2)}, u32[]{:S(2)}) collective-permute-start(bf16[2,512,128]{2,1,0:T(8,128)(2,1)S(1)} %bitcast.129), channel_id=1, source_target_pairs={{0,4},{4,8},{8,12},{12,0},{1,5},{5,9},{9,13},{13,1},{2,6},{6,10},{... | collective-permute-start | bytes 786440 | tf_op jit(solution)/shard_map/ppermute | solution.py:191
  95.7 6.8 %shard_map.91 = bf16[2,512,128]{2,1,0:T(8,128)(2,1)} custom-call(bf16[2,512,128]{2,1,0:T(8,128)(2,1)} %bitcast.128, bf16[2,1664,128]{2,1,0:T(8,128)(2,1)} %bitcast.114, bf16[2,1664,128]{2,1,0:T(8,128)(2,1)} %bitcast.118), custom_call_target="tpu_custom_call" | custom-call | flops 872415232 | bytes 2228224 | tf_op jit(solution)/shard_map/pallas_call | solution.py:86
  102.5 6.8 %shard_map.92 = bf16[2,512,128]{2,1,0:T(8,128)(2,1)} custom-call(bf16[2,512,128]{2,1,0:T(8,128)(2,1)} %collective-permute-done.7.q_ref, bf16[2,1664,128]{2,1,0:T(8,128)(2,1)} %bitcast.115, bf16[2,1664,128]{2,1,0:T(8,128)(2,1)} %bitcast.119), custom_call_target="tpu_custom_call" | custom-call | flops 872415232 | bytes 2228224 | tf_op jit(solution)/shard_map/pallas_call | solution.py:86
  109.3 2.0 collective-permute-start.8
  111.3 6.8 %shard_map.93 = bf16[2,512,128]{2,1,0:T(8,128)(2,1)} custom-call(bf16[2,512,128]{2,1,0:T(8,128)(2,1)} %collective-permute-done.9.q_ref, bf16[2,1664,128]{2,1,0:T(8,128)(2,1)} %bitcast.116, bf16[2,1664,128]{2,1,0:T(8,128)(2,1)} %bitcast.120), custom_call_target="tpu_custom_call" | custom-call | flops 872415232 | bytes 2228224 | tf_op jit(solution)/shard_map/pallas_call | solution.py:86
  118.4 6.8 %shard_map.94 = bf16[2,512,128]{2,1,0:T(8,128)(2,1)} custom-call(bf16[2,512,128]{2,1,0:T(8,128)(2,1)} %collective-permute-done.11.q_ref, bf16[2,1664,128]{2,1,0:T(8,128)(2,1)} %bitcast.117, bf16[2,1664,128]{2,1,0:T(8,128)(2,1)} %bitcast.121), custom_call_target="tpu_custom_call" | custom-call | flops 872415232 | bytes 2228224 | tf_op jit(solution)/shard_map/pallas_call | solution.py:86
  125.2 3.9 %collective-permute-start.12 = (bf16[2,512,128]{2,1,0:T(8,128)(2,1)}, bf16[2,512,128]{2,1,0:T(8,128)(2,1)S(1)}, u32[]{:S(2)}, u32[]{:S(2)}) collective-permute-start(bf16[2,512,128]{2,1,0:T(8,128)(2,1)} %shard_map.94), channel_id=1, source_target_pairs={{0,4},{4,8},{8,12},{12,0},{1,5},{5,9},{9,13},{13,1},{2,6},{6,10},{... | collective-permute-start | bytes 786440 | tf_op jit(solution)/shard_map/ppermute | solution.py:205
  129.5 8.1 %collective-permute-done.10 = bf16[2,512,128]{2,1,0:T(8,128)(2,1)S(1)} collective-permute-done((bf16[2,512,128]{2,1,0:T(8,128)(2,1)}, bf16[2,512,128]{2,1,0:T(8,128)(2,1)S(1)}, u32[]{:S(2)}, u32[]{:S(2)}) %collective-permute-start.10) | collective-permute-done | bytes 262176 | tf_op jit(solution)/shard_map/ppermute | solution.py:205
  140.5 2.3 %collective-permute-start.15 = (bf16[128,2048]{1,0:T(8,128)(2,1)S(1)}, bf16[128,2048]{1,0:T(8,128)(2,1)S(1)}, u32[]{:S(2)}, u32[]{:S(2)}) collective-permute-start(bf16[128,2048]{1,0:T(8,128)(2,1)S(1)} %fusion.21), channel_id=1, source_target_pairs={{0,12},{4,0},{8,4},{12,8},{1,13},{5,1},{9,5},{13,9},{2,14},{6,2},{... | collective-permute-start | bytes 1572872 | tf_op jit(solution)/shard_map/ppermute | solution.py:36
  143.0 4.8 %fusion.4 = bf16[4,128,2048]{2,1,0:T(8,128)(2,1)S(1)} fusion(bf16[4,128,2048]{2,1,0:T(8,128)(2,1)S(1)} %broadcast_in_dim.63, s32[]{:T(128)S(6)} %select_n.173, bf16[128,2048]{1,0:T(8,128)(2,1)S(1)} %fusion.21, bf16[2048,2048]{1,0:T(8,128)(2,1)} %param.14), kind=kOutput, calls=%fused_computation.12 | convolution fusion | flops 1074003968 | bytes 9437188 | tf_op jit(solution)/shard_map/dot_general | solution.py:220
  147.9 7.8 %collective-permute-done.13 = bf16[128,2048]{1,0:T(8,128)(2,1)S(1)} collective-permute-done((bf16[128,2048]{1,0:T(8,128)(2,1)S(1)}, bf16[128,2048]{1,0:T(8,128)(2,1)S(1)}, u32[]{:S(2)}, u32[]{:S(2)}) %collective-permute-start.13) | collective-permute-done | bytes 524320 | tf_op jit(solution)/shard_map/ppermute | solution.py:36
  157.0 18.6 %collective-permute-done.14 = bf16[128,2048]{1,0:T(8,128)(2,1)S(1)} collective-permute-done((bf16[128,2048]{1,0:T(8,128)(2,1)S(1)}, bf16[128,2048]{1,0:T(8,128)(2,1)S(1)}, u32[]{:S(2)}, u32[]{:S(2)}) %collective-permute-start.14) | collective-permute-done | bytes 524320 | tf_op jit(solution)/shard_map/ppermute | solution.py:36
  178.4 2.8 %collective-permute-done.16 = bf16[256,2048]{1,0:T(8,128)(2,1)} collective-permute-done((bf16[256,2048]{1,0:T(8,128)(2,1)S(1)}, bf16[256,2048]{1,0:T(8,128)(2,1)}, u32[]{:S(2)}, u32[]{:S(2)}) %collective-permute-start.16) | collective-permute-done | bytes 1048608 | tf_op jit(solution)/shard_map/ppermute | solution.py:47
  182.9 11.6 %collective-permute-start.17 = (bf16[128,2048]{1,0:T(8,128)(2,1)S(1)}, bf16[128,2048]{1,0:T(8,128)(2,1)S(1)}, u32[]{:S(2)}, u32[]{:S(2)}) collective-permute-start(bf16[128,2048]{1,0:T(8,128)(2,1)S(1)} %get-tuple-element.12), channel_id=1, source_target_pairs={{0,0},{1,8},{2,4},{3,12},{4,1},{5,9},{6,5},{7,13},{8,2},{9,10},{10... | collective-permute-start | bytes 1572872 | tf_op jit(solution)/shard_map/ppermute | solution.py:251
  194.6 10.6 %collective-permute-done.17 = bf16[128,2048]{1,0:T(8,128)(2,1)S(1)} collective-permute-done((bf16[128,2048]{1,0:T(8,128)(2,1)S(1)}, bf16[128,2048]{1,0:T(8,128)(2,1)S(1)}, u32[]{:S(2)}, u32[]{:S(2)}) %collective-permute-start.17) | collective-permute-done | bytes 524320 | tf_op jit(solution)/shard_map/ppermute | solution.py:251
  205.2 14.8 %collective-permute-done.18 = bf16[128,2048]{1,0:T(8,128)(2,1)S(1)} collective-permute-done((bf16[128,2048]{1,0:T(8,128)(2,1)S(1)}, bf16[128,2048]{1,0:T(8,128)(2,1)S(1)}, u32[]{:S(2)}, u32[]{:S(2)}) %collective-permute-start.18) | collective-permute-done | bytes 524320 | tf_op jit(solution)/shard_map/ppermute | solution.py:251
  220.0 2.1 add_convert_fusion
  (93 shorter events, 36.5 us)
Async XLA Ops:
  0.0 42.7 %copy-start = (f32[128]{0:T(128)S(1)}, f32[128]{0:T(128)}, u32[]{:S(2)}) copy-start(f32[128]{0:T(128)} %param.11) | copy-start | bytes 1540
  0.0 23.1 %copy-start.4 = (s32[128]{0:T(128)S(1)}, s32[128]{0:T(128)}, u32[]{:S(2)}) copy-start(s32[128]{0:T(128)} %param.16) | copy-start | bytes 1540
  1.6 11.2 %collective-permute-start = (bf16[64,2048]{1,0:T(8,128)(2,1)S(1)}, bf16[64,2048]{1,0:T(8,128)(2,1)S(1)}, u32[]{:S(2)}, u32[]{:S(2)}) collective-permute-start(bf16[64,2048]{1,0:T(8,128)(2,1)S(1)} %get-tuple-element.10), channel_id=1, source_target_pairs={{0,4},{4,8},{8,12},{12,0},{1,5},{5,9},{9,13},{13,1},{2,6},{6,10},{... | collective-permute-start | bytes 786440 | tf_op jit(solution)/shard_map/ppermute | solution.py:134
  3.2 19.7 %collective-permute-start.1 = (bf16[64,2048]{1,0:T(8,128)(2,1)S(1)}, bf16[64,2048]{1,0:T(8,128)(2,1)S(1)}, u32[]{:S(2)}, u32[]{:S(2)}) collective-permute-start(bf16[64,2048]{1,0:T(8,128)(2,1)S(1)} %get-tuple-element.11), channel_id=1, source_target_pairs={{0,8},{4,12},{8,0},{12,4},{1,9},{5,13},{9,1},{13,5},{2,10},{6,14},... | collective-permute-start | bytes 786440 | tf_op jit(solution)/shard_map/ppermute | solution.py:134
  5.8 17.1 %collective-permute-start.2 = (bf16[64,2048]{1,0:T(8,128)(2,1)S(1)}, bf16[64,2048]{1,0:T(8,128)(2,1)S(1)}, u32[]{:S(2)}, u32[]{:S(2)}) collective-permute-start(bf16[64,2048]{1,0:T(8,128)(2,1)S(1)} %get-tuple-element.9), channel_id=1, source_target_pairs={{0,12},{4,0},{8,4},{12,8},{1,13},{5,1},{9,5},{13,9},{2,14},{6,2},{... | collective-permute-start | bytes 786440 | tf_op jit(solution)/shard_map/ppermute | solution.py:134
  23.0 2.7 %collective-permute-start.3 = (bf16[4,64,2048]{2,1,0:T(8,128)(2,1)S(1)}, bf16[4,64,2048]{2,1,0:T(8,128)(2,1)S(1)}, u32[]{:S(2)}, u32[]{:S(2)}) collective-permute-start(bf16[4,64,2048]{2,1,0:T(8,128)(2,1)S(1)} %bitcast_dynamic-update-slice_fusion.2), channel_id=1, source_target_pairs={{0,1},{1,0},{2,3},{3,2},{4,5},{5,4},{6,7},{7,6},{8,9},{9,8},{10,11... | collective-permute-start | bytes 3145736 | tf_op jit(solution)/shard_map/ppermute | solution.py:145
  30.6 20.0 %collective-permute-start.4 = (bf16[128,2048]{1,0:T(8,128)(2,1)S(1)}, bf16[128,2048]{1,0:T(8,128)(2,1)S(1)}, u32[]{:S(2)}, u32[]{:S(2)}) collective-permute-start(bf16[128,2048]{1,0:T(8,128)(2,1)S(1)} %convolution_convert_fusion.6), channel_id=1, source_target_pairs={{0,4},{4,8},{8,12},{12,0},{1,5},{5,9},{9,13},{13,1},{2,6},{6,10},{... | collective-permute-start | bytes 1572872 | tf_op jit(solution)/shard_map/ppermute | solution.py:24
  38.1 34.6 %collective-permute-start.5 = (bf16[128,2048]{1,0:T(8,128)(2,1)S(1)}, bf16[128,2048]{1,0:T(8,128)(2,1)S(1)}, u32[]{:S(2)}, u32[]{:S(2)}) collective-permute-start(bf16[128,2048]{1,0:T(8,128)(2,1)S(1)} %convolution_convert_fusion.5), channel_id=1, source_target_pairs={{0,8},{4,12},{8,0},{12,4},{1,9},{5,13},{9,1},{13,5},{2,10},{6,14},... | collective-permute-start | bytes 1572872 | tf_op jit(solution)/shard_map/ppermute | solution.py:24
  41.1 31.6 %collective-permute-start.6 = (bf16[128,2048]{1,0:T(8,128)(2,1)S(1)}, bf16[128,2048]{1,0:T(8,128)(2,1)S(1)}, u32[]{:S(2)}, u32[]{:S(2)}) collective-permute-start(bf16[128,2048]{1,0:T(8,128)(2,1)S(1)} %convolution_convert_fusion.4), channel_id=1, source_target_pairs={{0,12},{4,0},{8,4},{12,8},{1,13},{5,1},{9,5},{13,9},{2,14},{6,2},{... | collective-permute-start | bytes 1572872 | tf_op jit(solution)/shard_map/ppermute | solution.py:24
  76.1 15.4 %copy-start.1 = (bf16[1,1601,512]{2,1,0:T(8,128)(2,1)S(1)}, bf16[1,1601,512]{2,1,0:T(8,128)(2,1)}, u32[]{:S(2)}) copy-start(bf16[1,1601,512]{2,1,0:T(8,128)(2,1)} %param.13) | copy-start | bytes 4918276
  76.2 15.4 %copy-start.2 = (bf16[1,1601,512]{2,1,0:T(8,128)(2,1)S(1)}, bf16[1,1601,512]{2,1,0:T(8,128)(2,1)}, u32[]{:S(2)}) copy-start(bf16[1,1601,512]{2,1,0:T(8,128)(2,1)} %param.12) | copy-start | bytes 4918276
  77.5 25.0 %collective-permute-start.7 = (bf16[2,512,128]{2,1,0:T(8,128)(2,1)S(1)}, bf16[2,512,128]{2,1,0:T(8,128)(2,1)}, u32[]{:S(2)}, u32[]{:S(2)}) collective-permute-start(bf16[2,512,128]{2,1,0:T(8,128)(2,1)S(1)} %bitcast.129), channel_id=1, source_target_pairs={{0,4},{4,8},{8,12},{12,0},{1,5},{5,9},{9,13},{13,1},{2,6},{6,10},{... | collective-permute-start | bytes 786440 | tf_op jit(solution)/shard_map/ppermute | solution.py:191
  89.2 22.1 %collective-permute-start.9 = (bf16[2,512,128]{2,1,0:T(8,128)(2,1)S(1)}, bf16[2,512,128]{2,1,0:T(8,128)(2,1)}, u32[]{:S(2)}, u32[]{:S(2)}) collective-permute-start(bf16[2,512,128]{2,1,0:T(8,128)(2,1)S(1)} %bitcast.127), channel_id=1, source_target_pairs={{0,8},{4,12},{8,0},{12,4},{1,9},{5,13},{9,1},{13,5},{2,10},{6,14},... | collective-permute-start | bytes 786440 | tf_op jit(solution)/shard_map/ppermute | solution.py:191
  90.4 28.0 %collective-permute-start.11 = (bf16[2,512,128]{2,1,0:T(8,128)(2,1)S(1)}, bf16[2,512,128]{2,1,0:T(8,128)(2,1)}, u32[]{:S(2)}, u32[]{:S(2)}) collective-permute-start(bf16[2,512,128]{2,1,0:T(8,128)(2,1)S(1)} %bitcast.126), channel_id=1, source_target_pairs={{0,12},{4,0},{8,4},{12,8},{1,13},{5,1},{9,5},{13,9},{2,14},{6,2},{... | collective-permute-start | bytes 786440 | tf_op jit(solution)/shard_map/ppermute | solution.py:191
  109.3 20.0 %collective-permute-start.8 = (bf16[2,512,128]{2,1,0:T(8,128)(2,1)}, bf16[2,512,128]{2,1,0:T(8,128)(2,1)S(1)}, u32[]{:S(2)}, u32[]{:S(2)}) collective-permute-start(bf16[2,512,128]{2,1,0:T(8,128)(2,1)} %shard_map.92), channel_id=1, source_target_pairs={{0,12},{4,0},{8,4},{12,8},{1,13},{5,1},{9,5},{13,9},{2,14},{6,2},{... | collective-permute-start | bytes 786440 | tf_op jit(solution)/shard_map/ppermute | solution.py:205
  118.1 19.4 %collective-permute-start.10 = (bf16[2,512,128]{2,1,0:T(8,128)(2,1)}, bf16[2,512,128]{2,1,0:T(8,128)(2,1)S(1)}, u32[]{:S(2)}, u32[]{:S(2)}) collective-permute-start(bf16[2,512,128]{2,1,0:T(8,128)(2,1)} %shard_map.93), channel_id=1, source_target_pairs={{0,8},{4,12},{8,0},{12,4},{1,9},{5,13},{9,1},{13,5},{2,10},{6,14},... | collective-permute-start | bytes 786440 | tf_op jit(solution)/shard_map/ppermute | solution.py:205
  125.2 12.5 %collective-permute-start.12 = (bf16[2,512,128]{2,1,0:T(8,128)(2,1)}, bf16[2,512,128]{2,1,0:T(8,128)(2,1)S(1)}, u32[]{:S(2)}, u32[]{:S(2)}) collective-permute-start(bf16[2,512,128]{2,1,0:T(8,128)(2,1)} %shard_map.94), channel_id=1, source_target_pairs={{0,4},{4,8},{8,12},{12,0},{1,5},{5,9},{9,13},{13,1},{2,6},{6,10},{... | collective-permute-start | bytes 786440 | tf_op jit(solution)/shard_map/ppermute | solution.py:205
  138.9 16.8 %collective-permute-start.13 = (bf16[128,2048]{1,0:T(8,128)(2,1)S(1)}, bf16[128,2048]{1,0:T(8,128)(2,1)S(1)}, u32[]{:S(2)}, u32[]{:S(2)}) collective-permute-start(bf16[128,2048]{1,0:T(8,128)(2,1)S(1)} %fusion.21), channel_id=1, source_target_pairs={{0,4},{4,8},{8,12},{12,0},{1,5},{5,9},{9,13},{13,1},{2,6},{6,10},{... | collective-permute-start | bytes 1572872 | tf_op jit(solution)/shard_map/ppermute | solution.py:36
  139.0 36.6 %collective-permute-start.14 = (bf16[128,2048]{1,0:T(8,128)(2,1)S(1)}, bf16[128,2048]{1,0:T(8,128)(2,1)S(1)}, u32[]{:S(2)}, u32[]{:S(2)}) collective-permute-start(bf16[128,2048]{1,0:T(8,128)(2,1)S(1)} %fusion.21), channel_id=1, source_target_pairs={{0,8},{4,12},{8,0},{12,4},{1,9},{5,13},{9,1},{13,5},{2,10},{6,14},... | collective-permute-start | bytes 1572872 | tf_op jit(solution)/shard_map/ppermute | solution.py:36
  140.5 36.4 %collective-permute-start.15 = (bf16[128,2048]{1,0:T(8,128)(2,1)S(1)}, bf16[128,2048]{1,0:T(8,128)(2,1)S(1)}, u32[]{:S(2)}, u32[]{:S(2)}) collective-permute-start(bf16[128,2048]{1,0:T(8,128)(2,1)S(1)} %fusion.21), channel_id=1, source_target_pairs={{0,12},{4,0},{8,4},{12,8},{1,13},{5,1},{9,5},{13,9},{2,14},{6,2},{... | collective-permute-start | bytes 1572872 | tf_op jit(solution)/shard_map/ppermute | solution.py:36
  142.8 12.9 %slice-start = ((s8[8388608]{0:T(1024)(128)(4,1)}), s8[4194304]{0:T(1024)(128)(4,1)S(1)}, s32[]{:S(2)}) async-start(s8[8388608]{0:T(1024)(128)(4,1)} %bitcast.96), calls=%async_computation | async-start | bytes 8388608
  178.3 2.9 %collective-permute-start.16 = (bf16[256,2048]{1,0:T(8,128)(2,1)S(1)}, bf16[256,2048]{1,0:T(8,128)(2,1)}, u32[]{:S(2)}, u32[]{:S(2)}) collective-permute-start(bf16[256,2048]{1,0:T(8,128)(2,1)S(1)} %dynamic-slice_bitcast_fusion), channel_id=1, source_target_pairs={{0,1},{1,0},{2,3},{3,2},{4,5},{5,4},{6,7},{7,6},{8,9},{9,8},{10,11... | collective-permute-start | bytes 3145736 | tf_op jit(solution)/shard_map/ppermute | solution.py:47
  182.9 22.3 %collective-permute-start.17 = (bf16[128,2048]{1,0:T(8,128)(2,1)S(1)}, bf16[128,2048]{1,0:T(8,128)(2,1)S(1)}, u32[]{:S(2)}, u32[]{:S(2)}) collective-permute-start(bf16[128,2048]{1,0:T(8,128)(2,1)S(1)} %get-tuple-element.12), channel_id=1, source_target_pairs={{0,0},{1,8},{2,4},{3,12},{4,1},{5,9},{6,5},{7,13},{8,2},{9,10},{10... | collective-permute-start | bytes 1572872 | tf_op jit(solution)/shard_map/ppermute | solution.py:251
  194.5 25.5 %collective-permute-start.18 = (bf16[128,2048]{1,0:T(8,128)(2,1)S(1)}, bf16[128,2048]{1,0:T(8,128)(2,1)S(1)}, u32[]{:S(2)}, u32[]{:S(2)}) collective-permute-start(bf16[128,2048]{1,0:T(8,128)(2,1)S(1)} %get-tuple-element.13), channel_id=1, source_target_pairs={{0,4},{1,12},{2,0},{3,8},{4,5},{5,13},{6,1},{7,9},{8,6},{9,14},{10... | collective-permute-start | bytes 1572872 | tf_op jit(solution)/shard_map/ppermute | solution.py:251
  (4 other events, 45.7 us)
